TPU v7x, 32 devices: a whole 2x2x4 slice. The times are simulated.
32 devices in a mesh: pix: 16 (over z, y, core), ch: 2 (over x).
Axes of the slice: x: 2, y: 2, z: 4, core: 2. Of those that a mesh axis runs over, the one named last changes fastest.
Arguments:
- fine_pixels: bfloat16 [16384, 768], P('pix', 'ch'), as said below
- pool_kernel: bfloat16 [768, 384], P('ch'), may hold values from -0.21875 to 0.21875
- projections: bfloat16 [3, 384, 384], P(None, None, 'ch'), may hold values from -0.3125 to 0.3125
- mixing_weight: bfloat16 [384, 384], P('ch'), may hold values from -1.25 to 1.25
- send_list: int32 [256, 32], P('pix'), may hold values from 0 to 1023, as said below
- neighbours: int32 [16384, 8], P('pix'), may hold values from -1 to 1535, as said below
- cotangent: bfloat16 [16384, 384], P('pix', 'ch'), may hold values from -6 to 6
Outputs:
- section_output: bfloat16 [16384, 384], P('pix', 'ch')
- fine_gradient: bfloat16 [16384, 768], P('pix', 'ch')
- kernel_gradient: float32 [768, 384], P('ch')
- projection_gradient: float32 [3, 384, 384], P(None, None, 'ch')
- mixing_gradient: float32 [384, 384], P('ch')
Inputs may be any that keep to these rules, and one draw needn't show every extreme that they name: `send_list`: row s * 16 + d lists rows of block s read by block d; the first n of its 32 slots are used (n from 2 to 32, 0 when s = d) and the others hold 0. Some block reads 32 rows from every other block, and block 15 sends 32 rows to block 0. `neighbours`: in block b, -1 marks a missing neighbour, which occurs only in the last slot of 8 pixels of each block; values under 1024 are rows of block b; 1024 + s * 32 + k names used slot k of send_list row s * 16 + b, and every used slot is named exactly once. `fine_pixels`: fine activations, finite, of order one in most rows.
All inputs are finite; a program needn't handle non-finite values.
Results may differ from a plain program's by a relative error of at most 0.012.
The roundings to bfloat16 on the way count: a program that leaves them out, or rounds other values in their place, can miss the bound.
Values may be sent and summed in bfloat16 or wider, within the bound.
No kernel may reach another device: no remote copies, remote signals or barrier semaphores. Data moves between devices by JAX's collectives and lax.ppermute only.
A program may use at most 64 MiB of HBM per device.

v0:
```python
import math

import jax
import jax.numpy as jnp
from jax import lax
from jax.sharding import PartitionSpec as P

HD = 64


def pick_table(row_ids, total):
    return (row_ids[:, None] == jnp.arange(total, dtype=jnp.int32)[None, :]).astype(jnp.bfloat16)


def slot_index(neighbour_block, first_row, block_rows):
    present = neighbour_block >= 0
    own_rows = first_row + jnp.arange(block_rows, dtype=jnp.int32)
    slot_rows = jnp.concatenate([own_rows[:, None], jnp.where(present, neighbour_block, 0)], axis=1)
    slot_live = jnp.concatenate([jnp.ones((block_rows, 1), bool), present], axis=1)
    return (slot_rows, slot_live)


def attention_forward(queries, extended, neighbours, row_offset):
    f32 = jnp.float32
    bf16 = jnp.bfloat16
    row_count = queries.shape[0]
    span = queries.shape[1]
    ext_rows = extended.shape[0]
    heads_here = span // HD
    slot_width = neighbours.shape[1] + 1
    score_scale = 1.0 / math.sqrt(HD)
    block_rows = math.gcd(row_count, 512)
    block_count = row_count // block_rows
    block_starts = row_offset + jnp.arange(block_count, dtype=jnp.int32) * block_rows
    query_blocks = queries.reshape(block_count, block_rows, span)
    neighbour_blocks = neighbours.reshape(block_count, block_rows, slot_width - 1)
    flattened = extended.reshape(ext_rows, 2 * span)

    def forward_block(inputs):
        query_block, neighbour_block, first_row = inputs
        slot_rows, slot_live = slot_index(neighbour_block, first_row, block_rows)
        pieces = [
            jnp.dot(
                pick_table(slot_rows[:, slot], ext_rows), flattened, preferred_element_type=f32
            ).astype(bf16)
            for slot in range(slot_width)
        ]
        gathered = jnp.stack(pieces, axis=1).reshape(block_rows, slot_width, 2, span)
        block_keys = gathered[:, :, 0].reshape(block_rows, slot_width, heads_here, HD)
        block_values = gathered[:, :, 1].reshape(block_rows, slot_width, heads_here, HD)
        scores = (
            jnp.einsum(
                "bhd,bmhd->bhm",
                query_block.reshape(block_rows, heads_here, HD),
                block_keys,
                preferred_element_type=f32,
            )
            * score_scale
        )
        shut = slot_live[:, None, :]
        masked = jnp.where(shut, scores, -1e30)
        largest = jnp.max(masked, axis=2, keepdims=True)
        raised = jnp.where(shut, jnp.exp(masked - largest), 0.0)
        probabilities = raised / jnp.sum(raised, axis=2, keepdims=True)
        weights = probabilities.astype(bf16)
        mixture = jnp.einsum("bhm,bmhd->bhd", weights, block_values, preferred_element_type=f32)
        return (mixture.reshape(block_rows, span).astype(bf16), probabilities, gathered)

    attn_blocks, prob_blocks, kv_blocks = lax.map(
        forward_block, (query_blocks, neighbour_blocks, block_starts)
    )
    return (attn_blocks.reshape(row_count, span), prob_blocks, kv_blocks)


def attention_backward(
    queries, ext_rows, neighbours, row_offset, grad_attended, prob_blocks, kv_blocks
):
    f32 = jnp.float32
    bf16 = jnp.bfloat16
    row_count = queries.shape[0]
    span = queries.shape[1]
    heads_here = span // HD
    slot_width = neighbours.shape[1] + 1
    score_scale = 1.0 / math.sqrt(HD)
    block_rows = math.gcd(row_count, 512)
    block_count = row_count // block_rows
    block_starts = row_offset + jnp.arange(block_count, dtype=jnp.int32) * block_rows
    query_blocks = queries.reshape(block_count, block_rows, span)
    neighbour_blocks = neighbours.reshape(block_count, block_rows, slot_width - 1)
    grad_blocks = grad_attended.reshape(block_count, block_rows, span)

    def backward_block(carried, inputs):
        query_block, neighbour_block, first_row, grad_block, probabilities, gathered = inputs
        slot_rows, slot_live = slot_index(neighbour_block, first_row, block_rows)
        block_keys = gathered[:, :, 0].reshape(block_rows, slot_width, heads_here, HD).astype(f32)
        block_values = gathered[:, :, 1].reshape(block_rows, slot_width, heads_here, HD).astype(f32)
        grad_mix = grad_block.reshape(block_rows, heads_here, HD).astype(f32)
        grad_weights = jnp.einsum("bhd,bmhd->bhm", grad_mix, block_values)
        grad_scores = (
            probabilities
            * (grad_weights - jnp.sum(probabilities * grad_weights, axis=2, keepdims=True))
            * score_scale
        )
        grad_query = jnp.einsum("bhm,bmhd->bhd", grad_scores, block_keys).reshape(block_rows, span)
        query_wide = query_block.reshape(block_rows, heads_here, HD).astype(f32)
        grad_keys = jnp.einsum("bhm,bhd->bmhd", grad_scores, query_wide)
        rounded = lax.optimization_barrier(probabilities.astype(bf16))
        grad_values = jnp.einsum("bhm,bhd->bmhd", rounded.astype(f32), grad_mix)
        contribution = (
            jnp.stack([grad_keys, grad_values], axis=2)
            .reshape(block_rows, slot_width, 2 * span)
            .astype(bf16)
        )
        for slot in range(slot_width):
            carried = carried + jnp.einsum(
                "bx,bc->xc",
                pick_table(slot_rows[:, slot], ext_rows),
                contribution[:, slot],
                preferred_element_type=f32,
            )
        return (carried, grad_query)

    start_grads = jnp.zeros((ext_rows, 2 * span), f32)
    carried, query_grads = lax.scan(
        backward_block,
        start_grads,
        (query_blocks, neighbour_blocks, block_starts, grad_blocks, prob_blocks, kv_blocks),
    )
    return (carried.reshape(ext_rows, 2, span), query_grads.reshape(row_count, span))


def ch_exchange(value):
    size = lax.axis_size("ch")
    return [
        lax.ppermute(value, "ch", [(i, (i + shift) % size) for i in range(size)])
        for shift in range(1, size)
    ]


def ch_assemble(own, others, axis):
    size = len(others) + 1
    index = lax.axis_index("ch")
    pieces = [own] + others
    result = None
    for case in range(size):
        ordered = jnp.concatenate([pieces[(case - j) % size] for j in range(size)], axis=axis)
        result = ordered if result is None else jnp.where(index == case, ordered, result)
    return result


def per_device(
    fine_pixels, pool_kernel, projections, mixing_weight, send_list, neighbours, cotangent
):
    f32 = jnp.float32
    bf16 = jnp.bfloat16
    row_count = fine_pixels.shape[0]
    half_width = projections.shape[2]
    ch_size = lax.axis_size("ch")
    ch_index = lax.axis_index("ch")
    peer_count = lax.axis_size("pix")
    slot_count = send_list.shape[1]
    grad_scale = 1.0 / math.sqrt(row_count * peer_count)
    send_pick = pick_table(send_list.reshape(-1), row_count)
    fine_others = ch_exchange(fine_pixels)
    kernel_others = ch_exchange(pool_kernel)
    cot_others = ch_exchange(cotangent)
    proj_others = ch_exchange(projections)
    mix_pieces = mixing_weight.reshape(mixing_weight.shape[0], ch_size, half_width)
    mix_others = [
        lax.ppermute(
            jnp.take(mix_pieces, (ch_index + shift) % ch_size, axis=1),
            "ch",
            [(i, (i + shift) % ch_size) for i in range(ch_size)],
        )
        for shift in range(1, ch_size)
    ]
    mix_own = jnp.take(mix_pieces, ch_index, axis=1)
    pooled_sum = jnp.dot(fine_pixels, pool_kernel, preferred_element_type=f32)
    for fine_other, kernel_other in zip(fine_others, kernel_others):
        pooled_sum = pooled_sum + jnp.dot(fine_other, kernel_other, preferred_element_type=f32)
    pooled_all = pooled_sum.astype(bf16)
    pooled = lax.dynamic_slice_in_dim(pooled_all, ch_index * half_width, half_width, axis=1)
    upstream = ch_assemble(cotangent, cot_others, axis=1)
    projected = jnp.einsum(
        "rc,kcd->rkd", pooled_all, projections, preferred_element_type=f32
    ).astype(bf16)
    queries = projected[:, 0]
    key_value = projected[:, 1:]
    outgoing = (
        jnp.dot(send_pick, key_value.reshape(row_count, 2 * half_width), preferred_element_type=f32)
        .astype(bf16)
        .reshape(peer_count, slot_count, 2, half_width)
    )
    incoming = lax.all_to_all(outgoing, "pix", split_axis=0, concat_axis=0, tiled=True)
    extended = jnp.concatenate(
        [key_value, incoming.reshape(peer_count * slot_count, 2, half_width)], axis=0
    )
    attended, prob_blocks, kv_blocks = attention_forward(queries, extended, neighbours, 0)
    attended_others = ch_exchange(attended)
    branch = jnp.dot(attended, mix_own, preferred_element_type=f32)
    for attended_other, mix_other in zip(attended_others, mix_others):
        branch = branch + jnp.dot(attended_other, mix_other, preferred_element_type=f32)
    section_output = (pooled.astype(f32) + branch).astype(bf16)
    grad_attended = jnp.dot(upstream, mixing_weight.T, preferred_element_type=f32).astype(bf16)
    mixing_term = jnp.dot(attended.T, upstream, preferred_element_type=f32) * grad_scale
    mixing_gradient = lax.psum(mixing_term, "pix")
    carried, query_grads = attention_backward(
        queries, extended.shape[0], neighbours, 0, grad_attended, prob_blocks, kv_blocks
    )
    remote_grads = carried[row_count:].reshape(peer_count, slot_count, 2, half_width)
    returned = lax.all_to_all(remote_grads, "pix", split_axis=0, concat_axis=0, tiled=True)
    returned_rows = jnp.einsum(
        "px,pc->xc",
        send_pick,
        returned.reshape(peer_count * slot_count, 2 * half_width).astype(bf16),
        preferred_element_type=f32,
    )
    local_grads = carried[:row_count] + returned_rows.reshape(row_count, 2, half_width)
    grad_projected = jnp.concatenate(
        [query_grads.reshape(row_count, 1, half_width), local_grads], axis=1
    ).astype(bf16)
    grad_others = ch_exchange(grad_projected)
    projection_term = (
        jnp.einsum("rc,rkd->kcd", pooled_all, grad_projected, preferred_element_type=f32)
        * grad_scale
    )
    mixing_gradient, projection_term = lax.optimization_barrier((mixing_gradient, projection_term))
    projection_gradient = lax.psum(projection_term, "pix")
    pooled_sum = upstream.astype(f32) + jnp.einsum(
        "rkd,kcd->rc", grad_projected, projections, preferred_element_type=f32
    )
    for grad_other, proj_other in zip(grad_others, proj_others):
        pooled_sum = pooled_sum + jnp.einsum(
            "rkd,kcd->rc", grad_other, proj_other, preferred_element_type=f32
        )
    grad_pooled = pooled_sum.astype(bf16)
    kernel_term = jnp.dot(fine_pixels.T, grad_pooled, preferred_element_type=f32) * grad_scale
    fine_gradient = jnp.dot(grad_pooled, pool_kernel.T, preferred_element_type=f32).astype(bf16)
    projection_gradient, kernel_term = lax.optimization_barrier((projection_gradient, kernel_term))
    kernel_gradient = lax.psum(kernel_term, "pix")
    return (section_output, fine_gradient, kernel_gradient, projection_gradient, mixing_gradient)


def solution(mesh):
    placed = (
        P("pix", "ch"),
        P("ch", None),
        P(None, None, "ch"),
        P("ch", None),
        P("pix", None),
        P("pix", None),
        P("pix", "ch"),
    )
    return jax.shard_map(
        per_device,
        mesh=mesh,
        in_specs=placed,
        out_specs=(
            P("pix", "ch"),
            P("pix", "ch"),
            P("ch", None),
            P(None, None, "ch"),
            P("ch", None),
        ),
        check_vma=False,
    )
```

profile of v0, /device:TPU:0, one launch (start us, length us, event | category | flops | bytes accessed | tf_op | source)
XLA Modules:
  0.0 499.7 jit_solution(882570962671841157)
XLA Ops:
  7.2 3.0 collective-permute-start
  11.0 1.8 fusion.81
  12.8 21.4 %collective-permute-done.1 = bf16[384,384]{1,0:T(8,128)(2,1)S(1)} collective-permute-done((bf16[384,384]{1,0:T(8,128)(2,1)}, bf16[384,384]{1,0:T(8,128)(2,1)S(1)}, u32[]{:S(2)}, u32[]{:S(2)}) %collective-permute-start.1) | collective-permute-done | bytes 294944 | tf_op jit(solution)/shard_map/ppermute | solution.py:135
  35.0 1.6 add_convert_fusion.1
  37.4 1.8 fusion.82
  39.4 1.1 copy-done.3
  42.2 1.1 reshape.126
  43.3 6.2 %all-to-all-start = ((bf16[16,32,2,192]{3,2,1,0:T(2,128)(2,1)}), bf16[16,32,2,192]{3,2,1,0:T(2,128)(2,1)}, u32[]{:S(2)}, u32[]{:S(2)}) async-start(bf16[16,32,2,192]{3,2,1,0:T(2,128)(2,1)} %reshape.126), calls=%async_computation | async-start | bytes 1048576 | tf_op jit(solution)/shard_map/all_to_all | solution.py:194
  49.8 1.6 collective-permute-start.4
  51.3 12.8 %collective-permute-done.4 = bf16[1024,192]{1,0:T(8,128)(2,1)} collective-permute-done((bf16[1024,192]{1,0:T(8,128)(2,1)S(1)}, bf16[1024,192]{1,0:T(8,128)(2,1)}, u32[]{:S(2)}, u32[]{:S(2)}) %collective-permute-start.4) | collective-permute-done | bytes 393248 | tf_op jit(solution)/shard_map/ppermute | solution.py:135
  64.1 1.9 convolution_convert_fusion.1
  66.1 2.4 copy.62
  70.6 2.1 concatenate.24
  72.7 2.5 pad_maximum_fusion.1
  75.2 39.0 %while.28 = (s32[]{:T(128)}, bf16[2,512,192]{1,2,0:T(8,128)(2,1)}, f32[2,512,3,9]{1,2,3,0:T(4,128)S(1)}, bf16[2,512,9,2,192]{1,4,3,2,0:T(8,128)(2,1)}, s32[2,512...) while((s32[]{:T(128)}, bf16[2,512,192]{1,2,0:T(8,128)(2,1)}, ...), condition=%wide.region_3.4_spmd, body=%wide.region_0.0_spmd.sunk | while | flops 5450242048 | bytes 106029360 | solution.py:69
  76.8 2.4 fusion.157
  82.6 1.1 fusion.162
  87.0 1.1 fusion.166
  92.0 2.9 copy-done
  96.1 2.4 fusion.157
  104.1 1.1 fusion.164
  106.3 1.1 fusion.166
  111.3 2.9 copy-done
  114.2 61.1 %while.29 = (s32[]{:T(128)}, f32[1536,384]{1,0:T(8,128)S(1)}, bf16[2,512,192]{1,2,0:T(8,128)(2,1)}, s32[2]{0:T(128)S(1)}, bf16[2,512,192]{1,2,0:T(8,128)(2,1)S(1...) while((s32[]{:T(128)}, f32[1536,384]{1,0:T(8,128)S(1)}, ...), condition=%wide.region_6.8_spmd.clone, body=%wide.region_4.7_spmd.clone.sunk | while | flops 5459585536 | bytes 81540312 | solution.py:124
  128.7 2.3 copy_bitcast_fusion.4
  133.7 2.0 fusion.174
  135.7 1.9 fusion.176
  137.7 1.9 fusion.177
  139.6 1.9 fusion.178
  141.5 1.9 fusion.179
  143.5 1.9 fusion.180
  145.4 1.9 fusion.181
  147.4 1.9 fusion.182
  149.3 1.9 fusion.183
  152.5 2.3 copy_bitcast_fusion.4
  157.5 1.9 fusion.174
  159.5 1.9 fusion.176
  161.4 1.9 fusion.177
  163.4 1.9 fusion.178
  165.3 1.9 fusion.179
  167.3 1.9 fusion.180
  169.2 1.9 fusion.181
  171.2 1.9 fusion.182
  173.1 1.9 fusion.183
  175.3 1.1 reshape.130
  176.4 5.7 %all-to-all-start.1 = ((bf16[16,32,2,192]{3,2,1,0:T(2,128)(2,1)}), bf16[16,32,2,192]{3,2,1,0:T(2,128)(2,1)S(1)}, u32[]{:S(2)}, u32[]{:S(2)}) async-start(bf16[16,32,2,192]{3,2,1,0:T(2,128)(2,1)} %reshape.130), calls=%async_computation.1 | async-start | bytes 1048576 | tf_op jit(solution)/shard_map/all_to_all | solution.py:211
  182.2 1.3 slice.105
  183.5 1.9 copy.72
  186.1 10.5 %all-to-all-done.1 = bf16[16,32,2,192]{3,2,1,0:T(2,128)(2,1)S(1)} async-done(((bf16[16,32,2,192]{3,2,1,0:T(2,128)(2,1)}), bf16[16,32,2,192]{3,2,1,0:T(2,128)(2,1)S(1)}, u32[]{:S(2)}, u32[]{:S(2)}) %all-to-all-start.1) | async-done | bytes 393248 | tf_op jit(solution)/shard_map/all_to_all | solution.py:211
  197.8 1.8 add_convert_fusion
  199.6 1.1 pad_maximum_fusion.2
  200.8 1.5 collective-permute-start.5
  204.1 1.5 collective-permute-start.3
  206.3 2.6 convolution_multiply_fusion.2
  209.3 1.7 fusion.67
  211.0 87.8 %all-reduce.5.cloned.1.call-done = f32[192,384]{1,0:T(8,128)} async-done(((f32[192,384]{1,0:T(8,128)}), f32[192,384]{1,0:T(8,128)}) %all-reduce.5.cloned.1.call-update) | async-done | bytes 294928 | tf_op jit(solution)/shard_map/psum | solution.py:206
  298.9 2.0 fusion.76
  301.0 3.1 fusion.64
  304.1 1.4 fusion.68
  305.5 89.3 %all-reduce.7.cloned.1.call-done = f32[3,384,192]{1,2,0:T(8,128)} async-done(((f32[3,384,192]{1,2,0:T(8,128)}), f32[3,384,192]{1,2,0:T(8,128)}) %all-reduce.7.cloned.1.call-update) | async-done | bytes 884752 | tf_op jit(solution)/shard_map/psum | solution.py:228
  394.8 2.2 add_convert_fusion.2
  397.0 2.7 convolution_convert_fusion
  399.7 89.5 %all-reduce.9.cloned.1.call-done = f32[384,384]{0,1:T(8,128)} async-done(((f32[384,384]{0,1:T(8,128)}), f32[384,384]{0,1:T(8,128)}) %all-reduce.9.cloned.1.call-update) | async-done | bytes 589840 | tf_op jit(solution)/shard_map/psum | solution.py:240
  489.2 2.1 copy.75
  (230 shorter events, 43.9 us)
Async XLA Ops:
  7.2 27.8 %collective-permute-start = (bf16[1024,384]{1,0:T(8,128)(2,1)}, bf16[1024,384]{1,0:T(8,128)(2,1)S(1)}, u32[]{:S(2)}, u32[]{:S(2)}) collective-permute-start(bf16[1024,384]{1,0:T(8,128)(2,1)} %param.13), channel_id=1, source_target_pairs={{0,1},{1,0},{2,3},{3,2},{4,5},{5,4},{6,7},{7,6},{8,9},{9,8},{10,11... | collective-permute-start | bytes 2359304 | tf_op jit(solution)/shard_map/ppermute | solution.py:135
  10.2 24.1 %collective-permute-start.1 = (bf16[384,384]{1,0:T(8,128)(2,1)}, bf16[384,384]{1,0:T(8,128)(2,1)S(1)}, u32[]{:S(2)}, u32[]{:S(2)}) collective-permute-start(bf16[384,384]{1,0:T(8,128)(2,1)} %param.14), channel_id=1, source_target_pairs={{0,1},{1,0},{2,3},{3,2},{4,5},{5,4},{6,7},{7,6},{8,9},{9,8},{10,11... | collective-permute-start | bytes 884744 | tf_op jit(solution)/shard_map/ppermute | solution.py:135
  11.0 29.6 %copy-start.25 = (s32[512]{0:T(512)}, s32[512]{0:T(512)S(1)}, u32[]{:S(2)}) copy-start(s32[512]{0:T(512)S(1)} %eq.286) | copy-start | bytes 6148
  34.2 0.7 copy-start.22
  36.5 0.9 copy-start.1
  39.4 1.1 copy-start.3
  40.6 0.9 copy-start.4
  40.6 9.0 %copy-start.14 = (bf16[1024,192]{0,1:T(8,128)(2,1)S(1)}, bf16[1024,192]{0,1:T(8,128)(2,1)}, u32[]{:S(2)}) copy-start(bf16[1024,192]{0,1:T(8,128)(2,1)} %param.19) | copy-start | bytes 1179652
  41.4 22.7 %copy-start.23 = (bf16[192,384]{1,0:T(8,128)(2,1)S(1)}, bf16[192,384]{1,0:T(8,128)(2,1)}, u32[]{:S(2)}) copy-start(bf16[192,384]{1,0:T(8,128)(2,1)} %param.16) | copy-start | bytes 442372
  43.3 27.3 %all-to-all-start = ((bf16[16,32,2,192]{3,2,1,0:T(2,128)(2,1)}), bf16[16,32,2,192]{3,2,1,0:T(2,128)(2,1)}, u32[]{:S(2)}, u32[]{:S(2)}) async-start(bf16[16,32,2,192]{3,2,1,0:T(2,128)(2,1)} %reshape.126), calls=%async_computation | async-start | bytes 1048576 | tf_op jit(solution)/shard_map/all_to_all | solution.py:194
  49.8 14.4 %copy-start.11 = (bf16[1024,192]{1,0:T(8,128)(2,1)}, bf16[1024,192]{1,0:T(8,128)(2,1)S(1)}, u32[]{:S(2)}) copy-start(bf16[1024,192]{1,0:T(8,128)(2,1)S(1)} %copy.65) | copy-start | bytes 1179652
  49.8 14.4 %collective-permute-start.4 = (bf16[1024,192]{1,0:T(8,128)(2,1)S(1)}, bf16[1024,192]{1,0:T(8,128)(2,1)}, u32[]{:S(2)}, u32[]{:S(2)}) collective-permute-start(bf16[1024,192]{1,0:T(8,128)(2,1)S(1)} %copy.65), channel_id=1, source_target_pairs={{0,1},{1,0},{2,3},{3,2},{4,5},{5,4},{6,7},{7,6},{8,9},{9,8},{10,11... | collective-permute-start | bytes 1179656 | tf_op jit(solution)/shard_map/ppermute | solution.py:135
  66.1 2.5 slice-start.2
  68.5 6.7 %copy-start.8 = (s32[1024,8]{0,1:T(8,128)S(1)}, s32[1024,8]{0,1:T(8,128)}, u32[]{:S(2)}) copy-start(s32[1024,8]{0,1:T(8,128)} %param.18) | copy-start | bytes 98308
  76.8 2.5 copy-start.5
  88.1 2.5 slice-start
  88.5 1.2 copy-start.18
  88.5 3.0 slice-start.1
  89.7 0.7 copy-start.19
  92.0 2.9 copy-start
  96.1 2.5 copy-start.5
  107.4 2.5 slice-start
  107.8 1.2 copy-start.18
  107.8 3.0 slice-start.1
  109.0 0.7 copy-start.19
  111.3 2.9 copy-start
  131.5 1.3 copy-start.15
  132.8 0.9 copy-start.16
  155.3 1.3 copy-start.15
  156.6 0.9 copy-start.16
  176.4 20.2 %all-to-all-start.1 = ((bf16[16,32,2,192]{3,2,1,0:T(2,128)(2,1)}), bf16[16,32,2,192]{3,2,1,0:T(2,128)(2,1)S(1)}, u32[]{:S(2)}, u32[]{:S(2)}) async-start(bf16[16,32,2,192]{3,2,1,0:T(2,128)(2,1)} %reshape.130), calls=%async_computation.1 | async-start | bytes 1048576 | tf_op jit(solution)/shard_map/all_to_all | solution.py:211
  182.1 116.7 %all-reduce.5.cloned.1.call-start = ((), (), s32[]{:S(2)}) async-start(), calls=%async_computation.2 | async-start | bytes 589824 | tf_op jit(solution)/shard_map/psum | solution.py:206
  183.5 1.9 copy-start.17
  185.4 12.4 %copy-start.26 = (s32[512]{0:T(512)S(1)}, s32[512]{0:T(512)}, u32[]{:S(2)}) copy-start(s32[512]{0:T(512)} %copy-done.25) | copy-start | bytes 6148
  197.8 5.0 copy-start.24
  199.6 6.0 %copy-start.20 = (bf16[2,512,192]{1,2,0:T(8,128)(2,1)S(1)}, bf16[2,512,192]{1,2,0:T(8,128)(2,1)}, u32[]{:S(2)}) copy-start(bf16[2,512,192]{1,2,0:T(8,128)(2,1)} %get-tuple-element.102) | copy-start | bytes 1179652
  199.6 6.7 %copy-start.12 = (bf16[1024,192]{1,0:T(8,128)(2,1)S(1)}, bf16[1024,192]{1,0:T(8,128)(2,1)}, u32[]{:S(2)}) copy-start(bf16[1024,192]{1,0:T(8,128)(2,1)} %copy-done.11) | copy-start | bytes 1179652
  200.8 100.2 %collective-permute-start.5 = (bf16[1024,3,192]{0,2,1:T(8,128)(2,1)}, bf16[1024,3,192]{0,2,1:T(8,128)(2,1)}, u32[]{:S(2)}, u32[]{:S(2)}) collective-permute-start(bf16[1024,3,192]{0,2,1:T(8,128)(2,1)} %pad_maximum_fusion.2), channel_id=1, source_target_pairs={{0,1},{1,0},{2,3},{3,2},{4,5},{5,4},{6,7},{7,6},{8,9},{9,8},{10,11... | collective-permute-start | bytes 3538952 | tf_op jit(solution)/shard_map/ppermute | solution.py:135
  202.2 98.7 %collective-permute-start.6 = (bf16[3,384,192]{1,2,0:T(8,128)(2,1)}, bf16[3,384,192]{1,2,0:T(8,128)(2,1)}, u32[]{:S(2)}, u32[]{:S(2)}) collective-permute-start(bf16[3,384,192]{1,2,0:T(8,128)(2,1)} %param.15), channel_id=1, source_target_pairs={{0,1},{1,0},{2,3},{3,2},{4,5},{5,4},{6,7},{7,6},{8,9},{9,8},{10,11... | collective-permute-start | bytes 1327112 | tf_op jit(solution)/shard_map/ppermute | solution.py:135
  204.1 190.7 %collective-permute-start.3 = (bf16[192,192]{1,0:T(8,128)(2,1)}, bf16[192,192]{1,0:T(8,128)(2,1)}, u32[]{:S(2)}, u32[]{:S(2)}) collective-permute-start(bf16[192,192]{1,0:T(8,128)(2,1)} %bitcast.190), channel_id=1, source_target_pairs={{0,1},{1,0},{2,3},{3,2},{4,5},{5,4},{6,7},{7,6},{8,9},{9,8},{10,11... | collective-permute-start | bytes 221192 | tf_op jit(solution)/shard_map/ppermute | solution.py:170
  205.6 3.7 copy-start.2
  205.7 189.1 %collective-permute-start.2 = (bf16[1024,192]{0,1:T(8,128)(2,1)S(1)}, bf16[1024,192]{0,1:T(8,128)(2,1)}, u32[]{:S(2)}, u32[]{:S(2)}) collective-permute-start(bf16[1024,192]{0,1:T(8,128)(2,1)S(1)} %bitcast.377), channel_id=1, source_target_pairs={{0,1},{1,0},{2,3},{3,2},{4,5},{5,4},{6,7},{7,6},{8,9},{9,8},{10,11... | collective-permute-start | bytes 1179656 | tf_op jit(solution)/shard_map/ppermute | solution.py:135
  208.9 185.8 %all-reduce.7.cloned.1.call-start = ((), (), s32[]{:S(2)}) async-start(), calls=%async_computation.3 | async-start | bytes 1769472 | tf_op jit(solution)/shard_map/psum | solution.py:228
  298.8 190.4 %all-reduce.9.cloned.1.call-start = ((), (), s32[]{:S(2)}) async-start(), calls=%async_computation.4 | async-start | bytes 1179648 | tf_op jit(solution)/shard_map/psum | solution.py:240
  298.9 2.1 copy-start.13
  300.9 3.1 copy-start.10
  304.1 90.7 %copy-start.9 = (bf16[1024,384]{1,0:T(8,128)(2,1)}, bf16[1024,384]{1,0:T(8,128)(2,1)S(1)}, u32[]{:S(2)}) copy-start(bf16[1024,384]{1,0:T(8,128)(2,1)S(1)} %fusion.64) | copy-start | bytes 2359300
  304.1 92.9 %copy-start.6 = (bf16[384,384]{1,0:T(8,128)(2,1)S(1)}, bf16[384,384]{1,0:T(8,128)(2,1)}, u32[]{:S(2)}) copy-start(bf16[384,384]{1,0:T(8,128)(2,1)} %param.14) | copy-start | bytes 884740
  394.8 96.5 %copy-start.7 = (f32[3,384,192]{1,2,0:T(8,128)S(1)}, f32[3,384,192]{1,2,0:T(8,128)}, u32[]{:S(2)}) copy-start(f32[3,384,192]{1,2,0:T(8,128)} %all-reduce.7.cloned.1.call-done) | copy-start | bytes 2654212
  397.0 95.3 %copy-start.21 = (f32[192,384]{1,0:T(8,128)S(1)}, f32[192,384]{1,0:T(8,128)}, u32[]{:S(2)}) copy-start(f32[192,384]{1,0:T(8,128)} %all-reduce.5.cloned.1.call-done) | copy-start | bytes 884740
Sparse Core Ops, SparseCore 0:
  209.1 89.6 all-reduce.4
  302.8 91.8 all-reduce.6
  398.7 90.4 all-reduce.8
where the time goes:
time: 498 us; the launch traced here: 500 us
  waiting for transfers between devices  311 us (62%)
  matrix products  82.3 us (17%)
  local copies, waits for them, and re-layouts  42.4 us (9%)
  starting transfers between devices  20.9 us (4%)
  loops' own time  15 us (3%)
  between operations  14.4 us (3%)
  other arithmetic  13.4 us (3%)
    psum x1, waiting for transfers between devices, per_device(): kernel_gradient = lax.psum(kernel_term, 'pix')  89.5 us
    psum x1, waiting for transfers between devices, per_device(): projection_gradient = lax.psum(projection_term, 'pix')  89.3 us
    psum x1, waiting for transfers between devices, per_device(): mixing_gradient = lax.psum(mixing_term, 'pix')  87.8 us
    dot_general x18, matrix products, backward_block(): jnp.einsum('bx,bc->xc', pick_table(slot_rows[:, slot], ext_rows), contrib...  34.9 us
    ppermute x6, waiting for transfers between devices, ch_exchange(): lax.ppermute(value, 'ch', [(i, (i + shift) % size) for i in range(size)])  34.2 us
    dot_general x18, matrix products, forward_block(): jnp.dot(pick_table(slot_rows[:, slot], ext_rows), flattened, preferred_el...  21.6 us
    another operation x1, loops' own time, attention_backward(): lax.scan(backward_block, start_grads, (query_blocks, neighbour_blocks, bl...  13.9 us
    all_to_all x1, waiting for transfers between devices, per_device(): lax.all_to_all(remote_grads, 'pix', split_axis=0, concat_axis=0, tiled=True)  10.5 us
  transfers between devices with their start and end apart: 12, of which 6 were waited for; matrix products, arithmetic and copies ran while one was open for 6% of the time, Pallas kernels for 0%

commit v1 on v0

--- a/solution.py
+++ b/solution.py
@@ -146,6 +146,26 @@
         ordered = jnp.concatenate([pieces[(case - j) % size] for j in range(size)], axis=axis)
         result = ordered if result is None else jnp.where(index == case, ordered, result)
     return result
+
+
+def pix_sum(terms):
+    size = lax.axis_size("pix")
+    width = terms[0].shape[-1]
+    flat = jnp.concatenate([term.reshape(-1, width) for term in terms], axis=0)
+    rows = flat.shape[0]
+    chunk = -(-rows // size)
+    flat = jnp.pad(flat, ((0, chunk * size - rows), (0, 0)))
+    parts = lax.all_to_all(flat.reshape(size, chunk, width), "pix", 0, 0, tiled=True)
+    reduced = jnp.sum(parts, axis=0)
+    spread = jnp.broadcast_to(reduced[None], (size, chunk, width))
+    gathered = lax.all_to_all(spread, "pix", 0, 0, tiled=True).reshape(size * chunk, width)
+    results = []
+    offset = 0
+    for term in terms:
+        count = term.size // width
+        results.append(gathered[offset : offset + count].reshape(term.shape))
+        offset += count
+    return results
 
 
 def per_device(
@@ -203,7 +223,6 @@
     section_output = (pooled.astype(f32) + branch).astype(bf16)
     grad_attended = jnp.dot(upstream, mixing_weight.T, preferred_element_type=f32).astype(bf16)
     mixing_term = jnp.dot(attended.T, upstream, preferred_element_type=f32) * grad_scale
-    mixing_gradient = lax.psum(mixing_term, "pix")
     carried, query_grads = attention_backward(
         queries, extended.shape[0], neighbours, 0, grad_attended, prob_blocks, kv_blocks
     )
@@ -224,8 +243,6 @@
         jnp.einsum("rc,rkd->kcd", pooled_all, grad_projected, preferred_element_type=f32)
         * grad_scale
     )
-    mixing_gradient, projection_term = lax.optimization_barrier((mixing_gradient, projection_term))
-    projection_gradient = lax.psum(projection_term, "pix")
     pooled_sum = upstream.astype(f32) + jnp.einsum(
         "rkd,kcd->rc", grad_projected, projections, preferred_element_type=f32
     )
@@ -236,8 +253,9 @@
     grad_pooled = pooled_sum.astype(bf16)
     kernel_term = jnp.dot(fine_pixels.T, grad_pooled, preferred_element_type=f32) * grad_scale
     fine_gradient = jnp.dot(grad_pooled, pool_kernel.T, preferred_element_type=f32).astype(bf16)
-    projection_gradient, kernel_term = lax.optimization_barrier((projection_gradient, kernel_term))
-    kernel_gradient = lax.psum(kernel_term, "pix")
+    kernel_gradient, projection_gradient, mixing_gradient = pix_sum(
+        (kernel_term, projection_term, mixing_term)
+    )
     return (section_output, fine_gradient, kernel_gradient, projection_gradient, mixing_gradient)
 
 

time: 498 us -> 332 us (0.67)
  the two profiles are of different devices: /device:TPU:0 before, /device:TPU:13 now
where the time goes in v1:
time: 332 us; the launch traced here: 326 us
  waiting for transfers between devices  102 us (31%)
  matrix products  79 us (24%)
  blocking collectives  45.9 us (14%)
  local copies, waits for them, and re-layouts  43.1 us (13%)
  starting transfers between devices  25.2 us (8%)
  loops' own time  15 us (5%)
  other arithmetic  14.4 us (4%)
    ppermute x6, waiting for transfers between devices, ch_exchange(): lax.ppermute(value, 'ch', [(i, (i + shift) % size) for i in range(size)])  61.3 us
    all_to_all x1, blocking collectives, pix_sum(): lax.all_to_all(flat.reshape(size, chunk, width), 'pix', 0, 0, tiled=True)  45.9 us
    dot_general x18, matrix products, backward_block(): jnp.einsum('bx,bc->xc', pick_table(slot_rows[:, slot], ext_rows), contrib...  34.9 us
    all_to_all x1, waiting for transfers between devices, pix_sum(): lax.all_to_all(spread, 'pix', 0, 0, tiled=True).reshape(size * chunk, width)  24.1 us
    dot_general x18, matrix products, forward_block(): jnp.dot(pick_table(slot_rows[:, slot], ext_rows), flattened, preferred_el...  21.6 us
    another operation x1, loops' own time, attention_backward(): lax.scan(backward_block, start_grads, (query_blocks, neighbour_blocks, bl...  14 us
    while x64, local copies, waits for them, and re-layouts  9.77 us
    all_to_all x1, waiting for transfers between devices, per_device(): lax.all_to_all(remote_grads, 'pix', split_axis=0, concat_axis=0, tiled=True)  9.65 us
  transfers between devices with their start and end apart: 10, of which 6 were waited for; matrix products, arithmetic and copies ran while one was open for 8% of the time, Pallas kernels for 0%

profile of v1, /device:TPU:13, one launch (start us, length us, event | category | flops | bytes accessed | tf_op | source)
XLA Modules:
  0.0 326.3 jit_solution(6360506680200122142)
XLA Ops:
  0.6 1.3 collective-permute-start
  2.9 1.8 fusion.81
  4.8 20.9 %collective-permute-done.1 = bf16[384,384]{1,0:T(8,128)(2,1)S(1)} collective-permute-done((bf16[384,384]{1,0:T(8,128)(2,1)}, bf16[384,384]{1,0:T(8,128)(2,1)S(1)}, u32[]{:S(2)}, u32[]{:S(2)}) %collective-permute-start.1) | collective-permute-done | bytes 294944 | tf_op jit(solution)/shard_map/ppermute | solution.py:135
  26.3 2.1 fusion.82
  31.3 1.1 reshape.139
  32.4 7.4 %all-to-all-start = ((bf16[16,32,2,192]{3,2,1,0:T(2,128)(2,1)}), bf16[16,32,2,192]{3,2,1,0:T(2,128)(2,1)}, u32[]{:S(2)}, u32[]{:S(2)}) async-start(bf16[16,32,2,192]{3,2,1,0:T(2,128)(2,1)} %reshape.139), calls=%async_computation | async-start | bytes 1048576 | tf_op jit(solution)/shard_map/all_to_all | solution.py:214
  40.0 1.3 collective-permute-start.4
  41.3 12.0 %collective-permute-done.4 = bf16[1024,192]{1,0:T(8,128)(2,1)} collective-permute-done((bf16[1024,192]{1,0:T(8,128)(2,1)S(1)}, bf16[1024,192]{1,0:T(8,128)(2,1)}, u32[]{:S(2)}, u32[]{:S(2)}) %collective-permute-start.4) | collective-permute-done | bytes 393248 | tf_op jit(solution)/shard_map/ppermute | solution.py:135
  53.4 1.9 convolution_convert_fusion.1
  55.4 2.4 copy.62
  59.8 2.1 concatenate.27
  61.9 2.5 pad_maximum_fusion.2
  64.4 38.8 %while.28 = (s32[]{:T(128)}, bf16[2,512,192]{1,2,0:T(8,128)(2,1)}, f32[2,512,3,9]{1,2,3,0:T(4,128)S(1)}, bf16[2,512,9,2,192]{1,4,3,2,0:T(8,128)(2,1)}, s32[2,512...) while((s32[]{:T(128)}, bf16[2,512,192]{1,2,0:T(8,128)(2,1)}, ...), condition=%wide.region_3.4_spmd, body=%wide.region_0.0_spmd.sunk | while | flops 5450242048 | bytes 106029360 | solution.py:69
  65.9 2.4 fusion.157
  76.1 1.1 fusion.166
  81.1 2.9 copy-done
  85.2 2.4 fusion.157
  93.2 1.1 fusion.164
  95.4 1.1 fusion.166
  100.4 2.9 copy-done
  103.2 61.1 %while.29 = (s32[]{:T(128)}, f32[1536,384]{1,0:T(8,128)S(1)}, bf16[2,512,192]{1,2,0:T(8,128)(2,1)}, s32[2]{0:T(128)S(1)}, bf16[2,512,192]{1,2,0:T(8,128)(2,1)S(1...) while((s32[]{:T(128)}, f32[1536,384]{1,0:T(8,128)S(1)}, ...), condition=%wide.region_6.8_spmd.clone, body=%wide.region_4.7_spmd.clone.sunk | while | flops 5459585536 | bytes 81540312 | solution.py:124
  117.9 2.3 copy_bitcast_fusion.4
  122.8 1.9 fusion.174
  124.8 1.9 fusion.176
  126.8 1.9 fusion.177
  128.7 1.9 fusion.178
  130.7 1.9 fusion.179
  132.6 1.9 fusion.180
  134.5 1.9 fusion.181
  136.5 1.9 fusion.182
  138.4 1.9 fusion.183
  141.6 2.3 copy_bitcast_fusion.4
  146.6 2.0 fusion.174
  148.6 1.9 fusion.176
  150.6 1.9 fusion.177
  152.5 1.9 fusion.178
  154.4 1.9 fusion.179
  156.4 1.9 fusion.180
  158.3 1.9 fusion.181
  160.3 1.9 fusion.182
  162.2 1.9 fusion.183
  164.4 1.1 reshape.143
  165.5 6.8 %all-to-all-start.1 = ((bf16[16,32,2,192]{3,2,1,0:T(2,128)(2,1)}), bf16[16,32,2,192]{3,2,1,0:T(2,128)(2,1)S(1)}, u32[]{:S(2)}, u32[]{:S(2)}) async-start(bf16[16,32,2,192]{3,2,1,0:T(2,128)(2,1)} %reshape.143), calls=%async_computation.1 | async-start | bytes 1048576 | tf_op jit(solution)/shard_map/all_to_all | solution.py:230
  172.4 1.3 slice.114
  173.7 1.9 copy.72
  176.3 9.7 %all-to-all-done.1 = bf16[16,32,2,192]{3,2,1,0:T(2,128)(2,1)S(1)} async-done(((bf16[16,32,2,192]{3,2,1,0:T(2,128)(2,1)}), bf16[16,32,2,192]{3,2,1,0:T(2,128)(2,1)S(1)}, u32[]{:S(2)}, u32[]{:S(2)}) %all-to-all-start.1) | async-done | bytes 393248 | tf_op jit(solution)/shard_map/all_to_all | solution.py:230
  187.2 1.2 pad_maximum_fusion.3
  188.4 1.2 collective-permute-start.5
  190.7 2.8 convolution_multiply_fusion.2
  194.9 2.3 fusion.76
  197.2 28.4 %collective-permute-done.6 = bf16[3,384,192]{1,2,0:T(8,128)(2,1)} collective-permute-done((bf16[3,384,192]{1,2,0:T(8,128)(2,1)}, bf16[3,384,192]{1,2,0:T(8,128)(2,1)}, u32[]{:S(2)}, u32[]{:S(2)}) %collective-permute-start.6) | collective-permute-done | bytes 442400 | tf_op jit(solution)/shard_map/ppermute | solution.py:135
  225.6 3.0 fusion.64
  230.0 45.9 %all_to_all.20 = f32[16,72,384]{2,1,0:T(8,128)S(1)} all-to-all(f32[16,72,384]{2,1,0:T(8,128)S(1)} %bitcast.374), channel_id=1, replica_groups=mesh['pix'=16,'ch'=2] {'pix'}, dimensions={0} | all-to-all | bytes 3538944 | tf_op jit(solution)/shard_map/all_to_all | solution.py:158
  275.9 1.3 broadcast_in_dim.93
  277.3 5.1 %all-to-all-start.3 = ((f32[16,72,384]{2,1,0:T(8,128)}), f32[16,72,384]{2,1,0:T(8,128)S(1)}, u32[]{:S(2)}, u32[]{:S(2)}) async-start(f32[16,72,384]{2,1,0:T(8,128)} %broadcast_in_dim.93), calls=%async_computation.3 | async-start | bytes 3538944 | tf_op jit(solution)/shard_map/all_to_all | solution.py:161
  282.4 1.2 collective-permute-start.2
  283.6 1.1 reshape.141
  284.7 1.2 broadcast_select_fusion
  286.3 1.4 fusion.73
  287.7 7.4 %collective-permute-done.3 = bf16[192,192]{1,0:T(8,128)(2,1)S(1)} collective-permute-done((bf16[192,192]{1,0:T(8,128)(2,1)S(1)}, bf16[192,192]{1,0:T(8,128)(2,1)S(1)}, u32[]{:S(2)}, u32[]{:S(2)}) %collective-permute-start.3) | collective-permute-done | bytes 73760 | tf_op jit(solution)/shard_map/ppermute | solution.py:190
  295.0 2.1 add_convert_fusion.2
  297.1 1.5 convolution_convert_fusion
  298.6 24.1 %all-to-all-done.3 = f32[16,72,384]{2,1,0:T(8,128)S(1)} async-done(((f32[16,72,384]{2,1,0:T(8,128)}), f32[16,72,384]{2,1,0:T(8,128)S(1)}, u32[]{:S(2)}, u32[]{:S(2)}) %all-to-all-start.3) | async-done | bytes 1769504 | tf_op jit(solution)/shard_map/all_to_all | solution.py:161
  324.7 1.3 copy.76
  (229 shorter events, 46.7 us)
Async XLA Ops:
  0.6 25.0 %collective-permute-start = (bf16[1024,384]{1,0:T(8,128)(2,1)}, bf16[1024,384]{1,0:T(8,128)(2,1)S(1)}, u32[]{:S(2)}, u32[]{:S(2)}) collective-permute-start(bf16[1024,384]{1,0:T(8,128)(2,1)} %param.13), channel_id=1, source_target_pairs={{0,1},{1,0},{2,3},{3,2},{4,5},{5,4},{6,7},{7,6},{8,9},{9,8},{10,11... | collective-permute-start | bytes 2359304 | tf_op jit(solution)/shard_map/ppermute | solution.py:135
  1.9 23.7 %collective-permute-start.1 = (bf16[384,384]{1,0:T(8,128)(2,1)}, bf16[384,384]{1,0:T(8,128)(2,1)S(1)}, u32[]{:S(2)}, u32[]{:S(2)}) collective-permute-start(bf16[384,384]{1,0:T(8,128)(2,1)} %param.14), channel_id=1, source_target_pairs={{0,1},{1,0},{2,3},{3,2},{4,5},{5,4},{6,7},{7,6},{8,9},{9,8},{10,11... | collective-permute-start | bytes 884744 | tf_op jit(solution)/shard_map/ppermute | solution.py:135
  2.9 26.7 %copy-start.24 = (s32[512]{0:T(512)}, s32[512]{0:T(512)S(1)}, u32[]{:S(2)}) copy-start(s32[512]{0:T(512)S(1)} %eq.286) | copy-start | bytes 6148
  26.3 2.3 copy-start.1
  28.6 1.1 copy-start.3
  29.7 0.9 copy-start.6
  29.7 10.1 %copy-start.15 = (bf16[1024,192]{0,1:T(8,128)(2,1)S(1)}, bf16[1024,192]{0,1:T(8,128)(2,1)}, u32[]{:S(2)}) copy-start(bf16[1024,192]{0,1:T(8,128)(2,1)} %param.19) | copy-start | bytes 1179652
  30.5 22.8 %copy-start.23 = (bf16[192,384]{1,0:T(8,128)(2,1)S(1)}, bf16[192,384]{1,0:T(8,128)(2,1)}, u32[]{:S(2)}) copy-start(bf16[192,384]{1,0:T(8,128)(2,1)} %param.16) | copy-start | bytes 442372
  32.4 27.4 %all-to-all-start = ((bf16[16,32,2,192]{3,2,1,0:T(2,128)(2,1)}), bf16[16,32,2,192]{3,2,1,0:T(2,128)(2,1)}, u32[]{:S(2)}, u32[]{:S(2)}) async-start(bf16[16,32,2,192]{3,2,1,0:T(2,128)(2,1)} %reshape.139), calls=%async_computation | async-start | bytes 1048576 | tf_op jit(solution)/shard_map/all_to_all | solution.py:214
  40.0 13.3 %copy-start.12 = (bf16[1024,192]{1,0:T(8,128)(2,1)}, bf16[1024,192]{1,0:T(8,128)(2,1)S(1)}, u32[]{:S(2)}) copy-start(bf16[1024,192]{1,0:T(8,128)(2,1)S(1)} %copy.65) | copy-start | bytes 1179652
  40.0 13.3 %collective-permute-start.4 = (bf16[1024,192]{1,0:T(8,128)(2,1)S(1)}, bf16[1024,192]{1,0:T(8,128)(2,1)}, u32[]{:S(2)}, u32[]{:S(2)}) collective-permute-start(bf16[1024,192]{1,0:T(8,128)(2,1)S(1)} %copy.65), channel_id=1, source_target_pairs={{0,1},{1,0},{2,3},{3,2},{4,5},{5,4},{6,7},{7,6},{8,9},{9,8},{10,11... | collective-permute-start | bytes 1179656 | tf_op jit(solution)/shard_map/ppermute | solution.py:135
  55.3 2.5 slice-start.2
  57.8 6.7 %copy-start.10 = (s32[1024,8]{0,1:T(8,128)S(1)}, s32[1024,8]{0,1:T(8,128)}, u32[]{:S(2)}) copy-start(s32[1024,8]{0,1:T(8,128)} %param.18) | copy-start | bytes 98308
  65.9 2.5 copy-start.8
  77.2 2.5 slice-start
  77.6 1.2 copy-start.19
  77.6 3.0 slice-start.1
  78.8 0.7 copy-start.20
  81.1 2.9 copy-start
  85.2 2.5 copy-start.8
  96.5 2.5 slice-start
  96.9 1.2 copy-start.19
  96.9 3.0 slice-start.1
  98.1 0.7 copy-start.20
  100.4 2.9 copy-start
  120.6 1.3 copy-start.16
  121.9 0.9 copy-start.17
  144.4 1.3 copy-start.16
  145.7 0.9 copy-start.17
  165.5 20.4 %all-to-all-start.1 = ((bf16[16,32,2,192]{3,2,1,0:T(2,128)(2,1)}), bf16[16,32,2,192]{3,2,1,0:T(2,128)(2,1)S(1)}, u32[]{:S(2)}, u32[]{:S(2)}) async-start(bf16[16,32,2,192]{3,2,1,0:T(2,128)(2,1)} %reshape.143), calls=%async_computation.1 | async-start | bytes 1048576 | tf_op jit(solution)/shard_map/all_to_all | solution.py:230
  173.7 1.9 copy-start.18
  175.6 10.8 %copy-start.25 = (s32[512]{0:T(512)S(1)}, s32[512]{0:T(512)}, u32[]{:S(2)}) copy-start(s32[512]{0:T(512)} %copy-done.24) | copy-start | bytes 6148
  186.5 3.5 %copy-start.21 = (bf16[2,512,192]{1,2,0:T(8,128)(2,1)S(1)}, bf16[2,512,192]{1,2,0:T(8,128)(2,1)}, u32[]{:S(2)}) copy-start(bf16[2,512,192]{1,2,0:T(8,128)(2,1)} %get-tuple-element.98) | copy-start | bytes 1179652
  186.5 4.2 %copy-start.13 = (bf16[1024,192]{1,0:T(8,128)(2,1)S(1)}, bf16[1024,192]{1,0:T(8,128)(2,1)}, u32[]{:S(2)}) copy-start(bf16[1024,192]{1,0:T(8,128)(2,1)} %copy-done.12) | copy-start | bytes 1179652
  187.2 6.3 %copy-start.11 = (bf16[1024,2,192]{0,2,1:T(8,128)(2,1)}, bf16[1024,2,192]{0,2,1:T(8,128)(2,1)S(1)}, u32[]{:S(2)}) copy-start(bf16[1024,2,192]{0,2,1:T(8,128)(2,1)S(1)} %add_convert_fusion) | copy-start | bytes 2359300
  188.4 5.0 %copy-start.2 = (bf16[1024,384]{0,1:T(8,128)(2,1)S(1)}, bf16[1024,384]{0,1:T(8,128)(2,1)}, u32[]{:S(2)}) copy-start(bf16[1024,384]{0,1:T(8,128)(2,1)} %copy-done.1) | copy-start | bytes 2359300
  188.4 37.2 %collective-permute-start.5 = (bf16[1024,3,192]{0,2,1:T(8,128)(2,1)}, bf16[1024,3,192]{0,2,1:T(8,128)(2,1)}, u32[]{:S(2)}, u32[]{:S(2)}) collective-permute-start(bf16[1024,3,192]{0,2,1:T(8,128)(2,1)} %pad_maximum_fusion.3), channel_id=1, source_target_pairs={{0,1},{1,0},{2,3},{3,2},{4,5},{5,4},{6,7},{7,6},{8,9},{9,8},{10,11... | collective-permute-start | bytes 3538952 | tf_op jit(solution)/shard_map/ppermute | solution.py:135
  189.7 35.9 %collective-permute-start.6 = (bf16[3,384,192]{1,2,0:T(8,128)(2,1)}, bf16[3,384,192]{1,2,0:T(8,128)(2,1)}, u32[]{:S(2)}, u32[]{:S(2)}) collective-permute-start(bf16[3,384,192]{1,2,0:T(8,128)(2,1)} %param.15), channel_id=1, source_target_pairs={{0,1},{1,0},{2,3},{3,2},{4,5},{5,4},{6,7},{7,6},{8,9},{9,8},{10,11... | collective-permute-start | bytes 1327112 | tf_op jit(solution)/shard_map/ppermute | solution.py:135
  194.9 30.7 %copy-start.14 = (bf16[1024,192]{1,0:T(8,128)(2,1)S(1)}, bf16[1024,192]{1,0:T(8,128)(2,1)}, u32[]{:S(2)}) copy-start(bf16[1024,192]{1,0:T(8,128)(2,1)} %copy-done.12) | copy-start | bytes 1179652
  197.2 31.4 %copy-start.7 = (bf16[1024,384]{1,0:T(8,128)(2,1)S(1)}, bf16[1024,384]{1,0:T(8,128)(2,1)}, u32[]{:S(2)}) copy-start(bf16[1024,384]{1,0:T(8,128)(2,1)} %param.13) | copy-start | bytes 2359300
  228.6 1.3 copy-start.4
  228.7 1.2 copy-start.22
  277.3 45.5 %all-to-all-start.3 = ((f32[16,72,384]{2,1,0:T(8,128)}), f32[16,72,384]{2,1,0:T(8,128)S(1)}, u32[]{:S(2)}, u32[]{:S(2)}) async-start(f32[16,72,384]{2,1,0:T(8,128)} %broadcast_in_dim.93), calls=%async_computation.3 | async-start | bytes 3538944 | tf_op jit(solution)/shard_map/all_to_all | solution.py:161
  282.4 12.7 %collective-permute-start.2 = (bf16[1024,192]{0,1:T(8,128)(2,1)}, bf16[1024,192]{0,1:T(8,128)(2,1)}, u32[]{:S(2)}, u32[]{:S(2)}) collective-permute-start(bf16[1024,192]{0,1:T(8,128)(2,1)} %bitcast.106), channel_id=1, source_target_pairs={{0,1},{1,0},{2,3},{3,2},{4,5},{5,4},{6,7},{7,6},{8,9},{9,8},{10,11... | collective-permute-start | bytes 1179656 | tf_op jit(solution)/shard_map/ppermute | solution.py:135
  283.6 13.5 %copy-start.5 = (bf16[1024,384]{1,0:T(8,128)(2,1)S(1)}, bf16[1024,384]{1,0:T(8,128)(2,1)}, u32[]{:S(2)}) copy-start(bf16[1024,384]{1,0:T(8,128)(2,1)} %copy-done.4) | copy-start | bytes 2359300
  285.9 9.1 %collective-permute-start.3 = (bf16[192,192]{1,0:T(8,128)(2,1)S(1)}, bf16[192,192]{1,0:T(8,128)(2,1)S(1)}, u32[]{:S(2)}, u32[]{:S(2)}) collective-permute-start(bf16[192,192]{1,0:T(8,128)(2,1)S(1)} %bitcast.395), channel_id=1, source_target_pairs={{0,1},{1,0},{2,3},{3,2},{4,5},{5,4},{6,7},{7,6},{8,9},{9,8},{10,11... | collective-permute-start | bytes 221192 | tf_op jit(solution)/shard_map/ppermute | solution.py:190
  286.3 10.8 %copy-start.9 = (bf16[384,384]{1,0:T(8,128)(2,1)S(1)}, bf16[384,384]{1,0:T(8,128)(2,1)}, u32[]{:S(2)}) copy-start(bf16[384,384]{1,0:T(8,128)(2,1)} %param.14) | copy-start | bytes 884740

commit v2 on v1

--- a/solution.py
+++ b/solution.py
@@ -66,14 +66,18 @@
         mixture = jnp.einsum("bhm,bmhd->bhd", weights, block_values, preferred_element_type=f32)
         return (mixture.reshape(block_rows, span).astype(bf16), probabilities, gathered)
 
-    attn_blocks, prob_blocks, kv_blocks = lax.map(
-        forward_block, (query_blocks, neighbour_blocks, block_starts)
-    )
+    outputs = [
+        forward_block((query_blocks[b], neighbour_blocks[b], block_starts[b]))
+        for b in range(block_count)
+    ]
+    attn_blocks = jnp.stack([out[0] for out in outputs])
+    prob_blocks = [out[1] for out in outputs]
+    kv_blocks = [out[2] for out in outputs]
     return (attn_blocks.reshape(row_count, span), prob_blocks, kv_blocks)
 
 
 def attention_backward(
-    queries, ext_rows, neighbours, row_offset, grad_attended, prob_blocks, kv_blocks
+    queries, ext_rows, neighbours, row_offset, grad_attended, prob_blocks, kv_blocks, riders
 ):
     f32 = jnp.float32
     bf16 = jnp.bfloat16
@@ -120,13 +124,19 @@
             )
         return (carried, grad_query)
 
-    start_grads = jnp.zeros((ext_rows, 2 * span), f32)
-    carried, query_grads = lax.scan(
-        backward_block,
-        start_grads,
-        (query_blocks, neighbour_blocks, block_starts, grad_blocks, prob_blocks, kv_blocks),
-    )
-    return (carried.reshape(ext_rows, 2, span), query_grads.reshape(row_count, span))
+    carried = jnp.zeros((ext_rows, 2 * span), f32)
+    query_grads = []
+    for b in range(block_count):
+        carried, grad_query = backward_block(
+            carried,
+            (query_blocks[b], neighbour_blocks[b], block_starts[b], grad_blocks[b],
+             prob_blocks[b], kv_blocks[b]),
+        )
+        query_grads.append(grad_query)
+        if b == 0:
+            carried, riders = lax.optimization_barrier((carried, riders))
+    query_grads = jnp.stack(query_grads)
+    return (carried.reshape(ext_rows, 2, span), query_grads.reshape(row_count, span), riders)
 
 
 def ch_exchange(value):
@@ -217,15 +227,17 @@
     )
     attended, prob_blocks, kv_blocks = attention_forward(queries, extended, neighbours, 0)
     attended_others = ch_exchange(attended)
+    grad_attended = jnp.dot(upstream, mixing_weight.T, preferred_element_type=f32).astype(bf16)
+    grad_attended, proj_others = lax.optimization_barrier((grad_attended, proj_others))
+    mixing_term = jnp.dot(attended.T, upstream, preferred_element_type=f32) * grad_scale
+    carried, query_grads, (attended_others, mix_others) = attention_backward(
+        queries, extended.shape[0], neighbours, 0, grad_attended, prob_blocks, kv_blocks,
+        (attended_others, mix_others),
+    )
     branch = jnp.dot(attended, mix_own, preferred_element_type=f32)
     for attended_other, mix_other in zip(attended_others, mix_others):
         branch = branch + jnp.dot(attended_other, mix_other, preferred_element_type=f32)
     section_output = (pooled.astype(f32) + branch).astype(bf16)
-    grad_attended = jnp.dot(upstream, mixing_weight.T, preferred_element_type=f32).astype(bf16)
-    mixing_term = jnp.dot(attended.T, upstream, preferred_element_type=f32) * grad_scale
-    carried, query_grads = attention_backward(
-        queries, extended.shape[0], neighbours, 0, grad_attended, prob_blocks, kv_blocks
-    )
     remote_grads = carried[row_count:].reshape(peer_count, slot_count, 2, half_width)
     returned = lax.all_to_all(remote_grads, "pix", split_axis=0, concat_axis=0, tiled=True)
     returned_rows = jnp.einsum(

time: 332 us -> 303 us (0.913)
  local copies, waits for them, and re-layouts: 43.1 us -> 23.9 us
  loops' own time: 15 us -> 0 us
  waiting for transfers between devices: 102 us -> 111 us
    another operation x2 -> x0, loops' own time: 15 us -> none  [the longest x1 14 us: attention_backward(): lax.scan(backward_block, start_grads, (query_blocks, neighbour_blocks, bl...]
    all_to_all x1, waiting for transfers between devices: 24.1 us -> 35.4 us  [pix_sum(): lax.all_to_all(spread, 'pix', 0, 0, tiled=True).reshape(size * chunk, width)]
    while x65 -> x0, local copies, waits for them, and re-layouts: 10.8 us -> none
    all_to_all x1, waiting for transfers between devices: 0.01 us -> 8.35 us  [per_device(): lax.all_to_all(outgoing, 'pix', split_axis=0, concat_axis=0, tiled=True)]
    ppermute x1, waiting for transfers between devices: 7.35 us -> 0.01 us  [per_device(): lax.ppermute(jnp.take(mix_pieces, (ch_index + shift) % ch_size, axis=1),...]
    squeeze x2 -> x0, local copies, waits for them, and re-layouts: 4.6 us -> none  [attention_backward(): lax.scan(backward_block, start_grads, (query_blocks, neighbour_blocks, bl...]
    unnamed x43 -> x123, local copies, waits for them, and re-layouts: 4.01 us -> 8.46 us
    concatenate x2, local copies, waits for them, and re-layouts: 4.52 us -> 0.46 us  [per_device(): jnp.concatenate([key_value, incoming.reshape(peer_count * slot_count, 2,...]
  transfers between devices with their start and end apart: 10 -> 10, of which waited for: 6 -> 6; matrix products, arithmetic and copies ran while one was open for 8% -> 29% of each run, Pallas kernels for 0% -> 0%
where the time goes in v2:
time: 303 us; the launch traced here: 298 us
  waiting for transfers between devices  111 us (37%)
  matrix products  76.7 us (25%)
  blocking collectives  45.9 us (15%)
  starting transfers between devices  24.1 us (8%)
  local copies, waits for them, and re-layouts  23.9 us (8%)
  other arithmetic  14 us (5%)
    ppermute x6, waiting for transfers between devices, ch_exchange(): lax.ppermute(value, 'ch', [(i, (i + shift) % size) for i in range(size)])  58.3 us
    all_to_all x1, blocking collectives, pix_sum(): lax.all_to_all(flat.reshape(size, chunk, width), 'pix', 0, 0, tiled=True)  45.9 us
    dot_general x18, matrix products, backward_block(): jnp.einsum('bx,bc->xc', pick_table(slot_rows[:, slot], ext_rows), contrib...  37.3 us
    all_to_all x1, waiting for transfers between devices, pix_sum(): lax.all_to_all(spread, 'pix', 0, 0, tiled=True).reshape(size * chunk, width)  35.4 us
    dot_general x18, matrix products, forward_block(): jnp.dot(pick_table(slot_rows[:, slot], ext_rows), flattened, preferred_el...  17.8 us
    all_to_all x1, waiting for transfers between devices, per_device(): lax.all_to_all(remote_grads, 'pix', split_axis=0, concat_axis=0, tiled=True)  9.12 us
    unnamed x123, local copies, waits for them, and re-layouts  8.46 us
    all_to_all x1, waiting for transfers between devices, per_device(): lax.all_to_all(outgoing, 'pix', split_axis=0, concat_axis=0, tiled=True)  8.35 us
  transfers between devices with their start and end apart: 10, of which 6 were waited for; matrix products, arithmetic and copies ran while one was open for 29% of the time, Pallas kernels for 0%

profile of v2, /device:TPU:13, one launch (start us, length us, event | category | flops | bytes accessed | tf_op | source)
XLA Modules:
  0.0 298.1 jit_solution(9822541826003201611)
XLA Ops:
  0.7 1.1 reshape.150
  1.9 1.2 broadcast_select_fusion
  3.7 1.2 collective-permute-start.5
  5.2 1.2 collective-permute-start.3
  6.4 2.0 copy.76
  8.6 1.2 collective-permute-start
  12.0 2.2 collective-permute-done.1
  14.2 37.6 %collective-permute-done = bf16[1024,384]{1,0:T(8,128)(2,1)S(1)} collective-permute-done((bf16[1024,384]{1,0:T(8,128)(2,1)S(1)}, bf16[1024,384]{1,0:T(8,128)(2,1)S(1)}, u32[]{:S(2)}, u32[]{:S(2)}) %collective-permute-start) | collective-permute-done | bytes 786464 | tf_op jit(solution)/shard_map/ppermute | solution.py:145
  54.2 1.1 reshape.148
  55.3 7.8 %all-to-all-start = ((bf16[16,32,2,192]{3,2,1,0:T(2,128)(2,1)}), bf16[16,32,2,192]{3,2,1,0:T(2,128)(2,1)S(1)}, u32[]{:S(2)}, u32[]{:S(2)}) async-start(bf16[16,32,2,192]{3,2,1,0:T(2,128)(2,1)} %reshape.148), calls=%async_computation | async-start | bytes 1048576 | tf_op jit(solution)/shard_map/all_to_all | solution.py:224
  63.8 2.3 convolution_convert_fusion.1
  67.8 8.4 %all-to-all-done = bf16[16,32,2,192]{3,2,1,0:T(2,128)(2,1)S(1)} async-done(((bf16[16,32,2,192]{3,2,1,0:T(2,128)(2,1)}), bf16[16,32,2,192]{3,2,1,0:T(2,128)(2,1)S(1)}, u32[]{:S(2)}, u32[]{:S(2)}) %all-to-all-start) | async-done | bytes 393248 | tf_op jit(solution)/shard_map/all_to_all | solution.py:224
  76.6 1.0 fusion.101
  77.6 1.0 fusion.102
  78.6 1.0 fusion.103
  79.6 1.0 fusion.104
  81.6 1.0 fusion.106
  82.6 1.0 fusion.107
  83.6 1.0 fusion.108
  88.8 2.1 fusion.18
  90.9 1.9 fusion.22
  92.8 1.9 fusion.26
  94.7 1.9 fusion.30
  96.6 1.9 fusion.32
  98.5 1.0 fusion.109
  100.5 1.0 fusion.111
  102.5 1.2 fusion.113
  106.6 1.0 fusion.117
  111.9 1.9 fusion
  113.9 1.9 fusion.4
  115.8 1.9 fusion.8
  117.7 3.7 %fusion.12 = f32[1536,384]{1,0:T(8,128)} fusion(s32[512]{0:T(512)S(1)} %bitcast.313, bf16[512,9,384]{0,2,1:T(8,128)(2,1)S(1)} %bitcast.241), kind=kOutput, calls=%fused_computation.33 | convolution fusion | flops 604766208 | bytes 2754560 | tf_op jit(solution)/shard_map/bx,bc->xc/dot_general | solution.py:119
  122.3 1.2 collective-permute-start.4
  123.5 2.0 fusion.37
  125.5 2.0 fusion.39
  127.5 2.0 fusion.41
  129.6 2.0 fusion.43
  131.6 1.9 fusion.14
  133.5 2.1 fusion.16
  135.7 2.2 fusion.45
  137.9 2.0 fusion.47
  139.9 2.0 fusion.49
  141.9 1.4 copy-done
  144.1 2.1 reshape.151
  146.2 5.6 %all-to-all-start.1 = ((bf16[16,32,2,192]{3,2,1,0:T(2,128)(2,1)}), bf16[16,32,2,192]{3,2,1,0:T(2,128)(2,1)}, u32[]{:S(2)}, u32[]{:S(2)}) async-start(bf16[16,32,2,192]{3,2,1,0:T(2,128)(2,1)} %reshape.151), calls=%async_computation.1 | async-start | bytes 1048576 | tf_op jit(solution)/shard_map/all_to_all | solution.py:242
  151.8 1.2 multiply_reduce_fusion.2
  153.1 1.2 multiply_reduce_fusion
  156.3 9.1 %all-to-all-done.1 = bf16[16,32,2,192]{3,2,1,0:T(2,128)(2,1)} async-done(((bf16[16,32,2,192]{3,2,1,0:T(2,128)(2,1)}), bf16[16,32,2,192]{3,2,1,0:T(2,128)(2,1)}, u32[]{:S(2)}, u32[]{:S(2)}) %all-to-all-start.1) | async-done | bytes 393248 | tf_op jit(solution)/shard_map/all_to_all | solution.py:242
  165.4 1.4 convert_element_type.211
  167.7 1.2 pad_maximum_fusion.4
  169.3 3.0 convolution_multiply_fusion.2
  172.2 1.7 fusion.97
  173.9 1.6 copy.110
  175.8 2.2 fusion.128
  178.0 18.6 %collective-permute-done.6 = bf16[1024,3,192]{0,2,1:T(8,128)(2,1)} collective-permute-done((bf16[1024,3,192]{0,2,1:T(8,128)(2,1)}, bf16[1024,3,192]{0,2,1:T(8,128)(2,1)}, u32[]{:S(2)}, u32[]{:S(2)}) %collective-permute-start.6) | collective-permute-done | bytes 1179680 | tf_op jit(solution)/shard_map/ppermute | solution.py:145
  196.6 3.3 %fusion.58 = bf16[1024,384]{1,0:T(8,128)(2,1)S(1)} fusion(f32[1024,384,1]{1,0,2:T(8,128)S(1)} %fusion.128, bf16[1024,3,192]{0,2,1:T(8,128)(2,1)} %collective-permute-done.6, bf16[3,384,192]{1,2,0:T(8,128)(2,1)} %collective-permute-done.3, bf16[1024,192]{1,0:T(8,128)(2,1)} %collective-permute-done.2, bf16[1024,192]{1,0:T(8,128)(2,1)} %copy.76, pred[]{:T(512)S(6)} %eq.238), kind=kOutput, calls=%fused_computation.92 | convolution fusion | flops 458096640 | bytes 4767745 | tf_op jit(solution)/shard_map/rkd,kcd->rc/dot_general | solution.py:262
  201.9 45.9 %all_to_all.20 = f32[16,72,384]{2,1,0:T(8,128)S(1)} all-to-all(f32[16,72,384]{2,1,0:T(8,128)S(1)} %bitcast.234), channel_id=1, replica_groups=mesh['pix'=16,'ch'=2] {'pix'}, dimensions={0} | all-to-all | bytes 3538944 | tf_op jit(solution)/shard_map/all_to_all | solution.py:168
  247.8 1.4 broadcast_in_dim.48
  249.2 5.1 %all-to-all-start.3 = ((f32[16,72,384]{2,1,0:T(8,128)}), f32[16,72,384]{2,1,0:T(8,128)S(1)}, u32[]{:S(2)}, u32[]{:S(2)}) async-start(f32[16,72,384]{2,1,0:T(8,128)} %broadcast_in_dim.48), calls=%async_computation.3 | async-start | bytes 3538944 | tf_op jit(solution)/shard_map/all_to_all | solution.py:171
  254.3 1.4 fusion.121
  255.7 2.1 add_convert_fusion.2
  257.8 1.5 convolution_convert_fusion
  259.3 35.4 %all-to-all-done.3 = f32[16,72,384]{2,1,0:T(8,128)S(1)} async-done(((f32[16,72,384]{2,1,0:T(8,128)}), f32[16,72,384]{2,1,0:T(8,128)S(1)}, u32[]{:S(2)}, u32[]{:S(2)}) %all-to-all-start.3) | async-done | bytes 1769504 | tf_op jit(solution)/shard_map/all_to_all | solution.py:171
  296.6 1.3 copy.111
  (202 shorter events, 31.5 us)
Async XLA Ops:
  0.6 10.7 %copy-start.14 = (bf16[384,384]{1,0:T(8,128)(2,1)S(1)}, bf16[384,384]{1,0:T(8,128)(2,1)}, u32[]{:S(2)}) copy-start(bf16[384,384]{1,0:T(8,128)(2,1)} %param.10) | copy-start | bytes 884740
  0.6 8.0 %copy-start.7 = (bf16[1024,384]{1,0:T(8,128)(2,1)S(1)}, bf16[1024,384]{1,0:T(8,128)(2,1)}, u32[]{:S(2)}) copy-start(bf16[1024,384]{1,0:T(8,128)(2,1)} %param.9) | copy-start | bytes 2359300
  0.7 9.2 %copy-start.26 = (s32[1024,8]{0,1:T(8,128)S(1)}, s32[1024,8]{0,1:T(8,128)}, u32[]{:S(2)}) copy-start(s32[1024,8]{0,1:T(8,128)} %param.14) | copy-start | bytes 98308
  0.7 10.6 %copy-start.27 = (s32[16,32]{1,0:T(8,128)S(1)}, s32[16,32]{1,0:T(8,128)}, u32[]{:S(2)}) copy-start(s32[16,32]{1,0:T(8,128)} %param.13) | copy-start | bytes 6148
  3.7 131.9 %collective-permute-start.5 = (bf16[192,192]{1,0:T(8,128)(2,1)}, bf16[192,192]{1,0:T(8,128)(2,1)}, u32[]{:S(2)}, u32[]{:S(2)}) collective-permute-start(bf16[192,192]{1,0:T(8,128)(2,1)} %bitcast.215), channel_id=1, source_target_pairs={{0,1},{1,0},{2,3},{3,2},{4,5},{5,4},{6,7},{7,6},{8,9},{9,8},{10,11... | collective-permute-start | bytes 221192 | tf_op jit(solution)/shard_map/ppermute | solution.py:200
  4.9 9.2 %collective-permute-start.1 = (bf16[384,384]{1,0:T(8,128)(2,1)}, bf16[384,384]{1,0:T(8,128)(2,1)S(1)}, u32[]{:S(2)}, u32[]{:S(2)}) collective-permute-start(bf16[384,384]{1,0:T(8,128)(2,1)} %param.10), channel_id=1, source_target_pairs={{0,1},{1,0},{2,3},{3,2},{4,5},{5,4},{6,7},{7,6},{8,9},{9,8},{10,11... | collective-permute-start | bytes 884744 | tf_op jit(solution)/shard_map/ppermute | solution.py:145
  5.2 60.9 %collective-permute-start.3 = (bf16[3,384,192]{1,2,0:T(8,128)(2,1)}, bf16[3,384,192]{1,2,0:T(8,128)(2,1)}, u32[]{:S(2)}, u32[]{:S(2)}) collective-permute-start(bf16[3,384,192]{1,2,0:T(8,128)(2,1)} %param.11), channel_id=1, source_target_pairs={{0,1},{1,0},{2,3},{3,2},{4,5},{5,4},{6,7},{7,6},{8,9},{9,8},{10,11... | collective-permute-start | bytes 1327112 | tf_op jit(solution)/shard_map/ppermute | solution.py:145
  8.4 55.4 %collective-permute-start.2 = (bf16[1024,192]{1,0:T(8,128)(2,1)}, bf16[1024,192]{1,0:T(8,128)(2,1)}, u32[]{:S(2)}, u32[]{:S(2)}) collective-permute-start(bf16[1024,192]{1,0:T(8,128)(2,1)} %copy.76), channel_id=1, source_target_pairs={{0,1},{1,0},{2,3},{3,2},{4,5},{5,4},{6,7},{7,6},{8,9},{9,8},{10,11... | collective-permute-start | bytes 1179656 | tf_op jit(solution)/shard_map/ppermute | solution.py:145
  8.6 43.1 %collective-permute-start = (bf16[1024,384]{1,0:T(8,128)(2,1)S(1)}, bf16[1024,384]{1,0:T(8,128)(2,1)S(1)}, u32[]{:S(2)}, u32[]{:S(2)}) collective-permute-start(bf16[1024,384]{1,0:T(8,128)(2,1)S(1)} %copy-done.7), channel_id=1, source_target_pairs={{0,1},{1,0},{2,3},{3,2},{4,5},{5,4},{6,7},{7,6},{8,9},{9,8},{10,11... | collective-permute-start | bytes 2359304 | tf_op jit(solution)/shard_map/ppermute | solution.py:145
  10.5 68.1 %copy-start.32 = (s32[512,1]{0,1:T(1,128)}, s32[512,1]{0,1:T(1,128)S(1)}, u32[]{:S(2)}) copy-start(s32[512,1]{0,1:T(1,128)S(1)} %get-tuple-element.68) | copy-start | bytes 6148
  10.5 70.1 %copy-start.30 = (s32[512,1]{0,1:T(1,128)}, s32[512,1]{0,1:T(1,128)S(1)}, u32[]{:S(2)}) copy-start(s32[512,1]{0,1:T(1,128)S(1)} %get-tuple-element.66) | copy-start | bytes 6148
  10.5 72.1 %copy-start.28 = (s32[512,1]{0,1:T(1,128)}, s32[512,1]{0,1:T(1,128)S(1)}, u32[]{:S(2)}) copy-start(s32[512,1]{0,1:T(1,128)S(1)} %get-tuple-element.64) | copy-start | bytes 6148
  10.5 89.0 %copy-start.40 = (s32[512,1]{0,1:T(1,128)}, s32[512,1]{0,1:T(1,128)S(1)}, u32[]{:S(2)}) copy-start(s32[512,1]{0,1:T(1,128)S(1)} %get-tuple-element.81) | copy-start | bytes 6148
  10.5 90.0 %copy-start.42 = (s32[512,1]{0,1:T(1,128)}, s32[512,1]{0,1:T(1,128)S(1)}, u32[]{:S(2)}) copy-start(s32[512,1]{0,1:T(1,128)S(1)} %get-tuple-element.82) | copy-start | bytes 6148
  10.5 91.0 %copy-start.36 = (s32[512,1]{0,1:T(1,128)}, s32[512,1]{0,1:T(1,128)S(1)}, u32[]{:S(2)}) copy-start(s32[512,1]{0,1:T(1,128)S(1)} %get-tuple-element.83) | copy-start | bytes 6148
  10.6 92.0 %copy-start.44 = (s32[512,1]{0,1:T(1,128)}, s32[512,1]{0,1:T(1,128)S(1)}, u32[]{:S(2)}) copy-start(s32[512,1]{0,1:T(1,128)S(1)} %get-tuple-element.84) | copy-start | bytes 6148
  10.6 94.1 %copy-start.46 = (s32[512,1]{0,1:T(1,128)}, s32[512,1]{0,1:T(1,128)S(1)}, u32[]{:S(2)}) copy-start(s32[512,1]{0,1:T(1,128)S(1)} %get-tuple-element.86) | copy-start | bytes 6148
  10.6 96.1 %copy-start.48 = (s32[512,1]{0,1:T(1,128)}, s32[512,1]{0,1:T(1,128)S(1)}, u32[]{:S(2)}) copy-start(s32[512,1]{0,1:T(1,128)S(1)} %get-tuple-element.88) | copy-start | bytes 6148
  11.3 73.3 %copy-start.34 = (s32[512]{0:T(512)}, s32[512]{0:T(512)S(1)}, u32[]{:S(2)}) copy-start(s32[512]{0:T(512)S(1)} %iota_add_fusion.1) | copy-start | bytes 6148
  11.3 42.1 %copy-start.38 = (s32[512]{0:T(512)}, s32[512]{0:T(512)S(1)}, u32[]{:S(2)}) copy-start(s32[512]{0:T(512)S(1)} %eq.167) | copy-start | bytes 6148
  12.0 40.4 %copy-start.19 = (bf16[3,384,192]{1,2,0:T(8,128)(2,1)S(1)}, bf16[3,384,192]{1,2,0:T(8,128)(2,1)}, u32[]{:S(2)}) copy-start(bf16[3,384,192]{1,2,0:T(8,128)(2,1)} %param.11) | copy-start | bytes 1327108
  52.4 1.0 copy-start.1
  53.4 10.3 %copy-start.25 = (bf16[192,384]{1,0:T(8,128)(2,1)S(1)}, bf16[192,384]{1,0:T(8,128)(2,1)}, u32[]{:S(2)}) copy-start(bf16[192,384]{1,0:T(8,128)(2,1)} %param.12) | copy-start | bytes 442372
  55.3 20.9 %all-to-all-start = ((bf16[16,32,2,192]{3,2,1,0:T(2,128)(2,1)}), bf16[16,32,2,192]{3,2,1,0:T(2,128)(2,1)S(1)}, u32[]{:S(2)}, u32[]{:S(2)}) async-start(bf16[16,32,2,192]{3,2,1,0:T(2,128)(2,1)} %reshape.148), calls=%async_computation | async-start | bytes 1048576 | tf_op jit(solution)/shard_map/all_to_all | solution.py:224
  63.7 34.8 %copy-start.50 = (s32[512]{0:T(512)}, s32[512]{0:T(512)S(1)}, u32[]{:S(2)}) copy-start(s32[512]{0:T(512)S(1)} %iota_add_fusion) | copy-start | bytes 6148
  76.6 8.0 %copy-start.22 = (bf16[512,384]{0,1:T(8,128)(2,1)}, bf16[512,384]{0,1:T(8,128)(2,1)S(1)}, u32[]{:S(2)}) copy-start(bf16[512,384]{0,1:T(8,128)(2,1)S(1)} %copy.74) | copy-start | bytes 1179652
  87.3 0.6 copy-start.17
  96.6 1.9 copy-start.23
  108.0 1.0 copy-start.4
  108.2 1.3 copy-start.3
  110.1 0.6 copy-start.18
  111.3 0.7 copy-start.49
  111.6 2.2 copy-start.47
  113.8 1.9 copy-start.45
  115.8 1.9 copy-start.43
  121.4 2.0 copy-start.35
  122.3 3.2 %copy-start.12 = (bf16[2,24,8,512]{3,2,0,1:T(8,128)(2,1)}, bf16[2,24,8,512]{3,2,0,1:T(8,128)(2,1)S(1)}, u32[]{:S(2)}) copy-start(bf16[2,24,8,512]{3,2,0,1:T(8,128)(2,1)S(1)} %copy.180) | copy-start | bytes 1179652
  122.3 3.2 %copy-start.33 = (s32[512,1]{0,1:T(1,128)S(1)}, s32[512,1]{0,1:T(1,128)}, u32[]{:S(2)}) copy-start(s32[512,1]{0,1:T(1,128)} %copy-done.32) | copy-start | bytes 6148
  122.3 13.3 %collective-permute-start.4 = (bf16[1024,192]{0,1:T(8,128)(2,1)S(1)}, bf16[1024,192]{0,1:T(8,128)(2,1)S(1)}, u32[]{:S(2)}, u32[]{:S(2)}) collective-permute-start(bf16[1024,192]{0,1:T(8,128)(2,1)S(1)} %bitcast.248), channel_id=1, source_target_pairs={{0,1},{1,0},{2,3},{3,2},{4,5},{5,4},{6,7},{7,6},{8,9},{9,8},{10,11... | collective-permute-start | bytes 1179656 | tf_op jit(solution)/shard_map/ppermute | solution.py:145
  125.5 2.0 copy-start.31
  127.5 2.0 copy-start.29
  129.6 2.0 copy-start.41
  131.6 1.9 copy-start.51
  133.5 2.1 copy-start.9
  133.5 2.1 copy-start.37
  135.7 2.2 copy-start.21
  141.9 1.4 copy-start
  146.2 19.2 %all-to-all-start.1 = ((bf16[16,32,2,192]{3,2,1,0:T(2,128)(2,1)}), bf16[16,32,2,192]{3,2,1,0:T(2,128)(2,1)}, u32[]{:S(2)}, u32[]{:S(2)}) async-start(bf16[16,32,2,192]{3,2,1,0:T(2,128)(2,1)} %reshape.151), calls=%async_computation.1 | async-start | bytes 1048576 | tf_op jit(solution)/shard_map/all_to_all | solution.py:242
  154.4 1.4 slice-start
  155.1 17.2 %copy-start.10 = (bf16[1024,1,192]{0,2,1:T(8,128)(2,1)}, bf16[1024,1,192]{0,2,1:T(8,128)(2,1)S(1)}, u32[]{:S(2)}) copy-start(bf16[1024,1,192]{0,2,1:T(8,128)(2,1)S(1)} %reshape_reshape.4) | copy-start | bytes 1179652
  155.8 11.2 %copy-start.39 = (s32[512]{0:T(512)S(1)}, s32[512]{0:T(512)}, u32[]{:S(2)}) copy-start(s32[512]{0:T(512)} %copy-done.38) | copy-start | bytes 6148
  166.9 2.3 copy-start.13
  167.7 4.5 %copy-start.16 = (bf16[1024,2,192]{0,2,1:T(8,128)(2,1)}, bf16[1024,2,192]{0,2,1:T(8,128)(2,1)S(1)}, u32[]{:S(2)}) copy-start(bf16[1024,2,192]{0,2,1:T(8,128)(2,1)S(1)} %add_convert_fusion) | copy-start | bytes 2359300
  168.9 3.3 %copy-start.2 = (bf16[1024,384]{0,1:T(8,128)(2,1)S(1)}, bf16[1024,384]{0,1:T(8,128)(2,1)}, u32[]{:S(2)}) copy-start(bf16[1024,384]{0,1:T(8,128)(2,1)} %copy-done.1) | copy-start | bytes 2359300
  168.9 27.7 %collective-permute-start.6 = (bf16[1024,3,192]{0,2,1:T(8,128)(2,1)}, bf16[1024,3,192]{0,2,1:T(8,128)(2,1)}, u32[]{:S(2)}, u32[]{:S(2)}) collective-permute-start(bf16[1024,3,192]{0,2,1:T(8,128)(2,1)} %pad_maximum_fusion.4), channel_id=1, source_target_pairs={{0,1},{1,0},{2,3},{3,2},{4,5},{5,4},{6,7},{7,6},{8,9},{9,8},{10,11... | collective-permute-start | bytes 3538952 | tf_op jit(solution)/shard_map/ppermute | solution.py:145
  173.9 1.9 copy-start.11
  178.0 22.8 %copy-start.8 = (bf16[1024,384]{1,0:T(8,128)(2,1)S(1)}, bf16[1024,384]{1,0:T(8,128)(2,1)}, u32[]{:S(2)}) copy-start(bf16[1024,384]{1,0:T(8,128)(2,1)} %param.9) | copy-start | bytes 2359300
  199.9 0.9 copy-start.5
  200.8 1.0 copy-start.24
  247.8 6.5 %copy-start.20 = (bf16[192,1,192]{2,1,0:T(2,128)(2,1)S(1)}, bf16[192,1,192]{2,1,0:T(2,128)(2,1)}, u32[]{:S(2)}) copy-start(bf16[192,1,192]{2,1,0:T(2,128)(2,1)} %get-tuple-element.58) | copy-start | bytes 221188
  249.2 45.5 %all-to-all-start.3 = ((f32[16,72,384]{2,1,0:T(8,128)}), f32[16,72,384]{2,1,0:T(8,128)S(1)}, u32[]{:S(2)}, u32[]{:S(2)}) async-start(f32[16,72,384]{2,1,0:T(8,128)} %broadcast_in_dim.48), calls=%async_computation.3 | async-start | bytes 3538944 | tf_op jit(solution)/shard_map/all_to_all | solution.py:171
  254.3 3.5 %copy-start.6 = (bf16[1024,384]{1,0:T(8,128)(2,1)S(1)}, bf16[1024,384]{1,0:T(8,128)(2,1)}, u32[]{:S(2)}) copy-start(bf16[1024,384]{1,0:T(8,128)(2,1)} %copy-done.5) | copy-start | bytes 2359300
  254.3 3.5 %copy-start.15 = (bf16[384,384]{1,0:T(8,128)(2,1)S(1)}, bf16[384,384]{1,0:T(8,128)(2,1)}, u32[]{:S(2)}) copy-start(bf16[384,384]{1,0:T(8,128)(2,1)} %param.10) | copy-start | bytes 884740

commit v3 on v2

--- a/solution.py
+++ b/solution.py
@@ -158,23 +158,33 @@
     return result
 
 
-def pix_sum(terms):
+def pix_scatter(terms, width):
     size = lax.axis_size("pix")
-    width = terms[0].shape[-1]
     flat = jnp.concatenate([term.reshape(-1, width) for term in terms], axis=0)
     rows = flat.shape[0]
     chunk = -(-rows // size)
     flat = jnp.pad(flat, ((0, chunk * size - rows), (0, 0)))
     parts = lax.all_to_all(flat.reshape(size, chunk, width), "pix", 0, 0, tiled=True)
-    reduced = jnp.sum(parts, axis=0)
-    spread = jnp.broadcast_to(reduced[None], (size, chunk, width))
-    gathered = lax.all_to_all(spread, "pix", 0, 0, tiled=True).reshape(size * chunk, width)
+    return jnp.sum(parts, axis=0)
+
+
+def pix_gather(reduced_groups, term_groups):
+    size = lax.axis_size("pix")
+    width = reduced_groups[0].shape[-1]
+    joined = jnp.concatenate(reduced_groups, axis=0)
+    spread = jnp.broadcast_to(joined[None], (size,) + joined.shape)
+    gathered = lax.all_to_all(spread, "pix", 0, 0, tiled=True)
     results = []
     offset = 0
-    for term in terms:
-        count = term.size // width
-        results.append(gathered[offset : offset + count].reshape(term.shape))
-        offset += count
+    for reduced, terms in zip(reduced_groups, term_groups):
+        chunk = reduced.shape[0]
+        flat = gathered[:, offset : offset + chunk].reshape(size * chunk, width)
+        offset += chunk
+        row = 0
+        for term in terms:
+            count = term.size // width
+            results.append(flat[row : row + count].reshape(term.shape))
+            row += count
     return results
 
 
@@ -193,22 +203,24 @@
     send_pick = pick_table(send_list.reshape(-1), row_count)
     fine_others = ch_exchange(fine_pixels)
     kernel_others = ch_exchange(pool_kernel)
-    cot_others = ch_exchange(cotangent)
-    proj_others = ch_exchange(projections)
-    mix_pieces = mixing_weight.reshape(mixing_weight.shape[0], ch_size, half_width)
-    mix_others = [
-        lax.ppermute(
-            jnp.take(mix_pieces, (ch_index + shift) % ch_size, axis=1),
-            "ch",
-            [(i, (i + shift) % ch_size) for i in range(ch_size)],
-        )
-        for shift in range(1, ch_size)
-    ]
-    mix_own = jnp.take(mix_pieces, ch_index, axis=1)
     pooled_sum = jnp.dot(fine_pixels, pool_kernel, preferred_element_type=f32)
     for fine_other, kernel_other in zip(fine_others, kernel_others):
         pooled_sum = pooled_sum + jnp.dot(fine_other, kernel_other, preferred_element_type=f32)
     pooled_all = pooled_sum.astype(bf16)
+    mix_pieces = mixing_weight.reshape(mixing_weight.shape[0], ch_size, half_width)
+    mix_sends = [
+        jnp.take(mix_pieces, (ch_index + shift) % ch_size, axis=1) for shift in range(1, ch_size)
+    ]
+    pooled_all, cot_send, proj_send, mix_sends = lax.optimization_barrier(
+        (pooled_all, cotangent, projections, mix_sends)
+    )
+    cot_others = ch_exchange(cot_send)
+    proj_others = ch_exchange(proj_send)
+    mix_others = [
+        lax.ppermute(mix_send, "ch", [(i, (i + shift) % ch_size) for i in range(ch_size)])
+        for shift, mix_send in zip(range(1, ch_size), mix_sends)
+    ]
+    mix_own = jnp.take(mix_pieces, ch_index, axis=1)
     pooled = lax.dynamic_slice_in_dim(pooled_all, ch_index * half_width, half_width, axis=1)
     upstream = ch_assemble(cotangent, cot_others, axis=1)
     projected = jnp.einsum(
@@ -255,6 +267,8 @@
         jnp.einsum("rc,rkd->kcd", pooled_all, grad_projected, preferred_element_type=f32)
         * grad_scale
     )
+    early_reduced = pix_scatter((projection_term, mixing_term), mixing_weight.shape[1])
+    early_reduced, grad_others = lax.optimization_barrier((early_reduced, grad_others))
     pooled_sum = upstream.astype(f32) + jnp.einsum(
         "rkd,kcd->rc", grad_projected, projections, preferred_element_type=f32
     )
@@ -265,8 +279,9 @@
     grad_pooled = pooled_sum.astype(bf16)
     kernel_term = jnp.dot(fine_pixels.T, grad_pooled, preferred_element_type=f32) * grad_scale
     fine_gradient = jnp.dot(grad_pooled, pool_kernel.T, preferred_element_type=f32).astype(bf16)
-    kernel_gradient, projection_gradient, mixing_gradient = pix_sum(
-        (kernel_term, projection_term, mixing_term)
+    kernel_reduced = pix_scatter((kernel_term,), mixing_weight.shape[1])
+    projection_gradient, mixing_gradient, kernel_gradient = pix_gather(
+        (early_reduced, kernel_reduced), ((projection_term, mixing_term), (kernel_term,))
     )
     return (section_output, fine_gradient, kernel_gradient, projection_gradient, mixing_gradient)
 

time: 303 us -> 274 us (0.904)
  the two profiles are of different devices: /device:TPU:13 before, /device:TPU:15 now
where the time goes in v3:
time: 274 us; the launch traced here: 270 us
  waiting for transfers between devices  85.5 us (31%)
  matrix products  81.6 us (30%)
  starting transfers between devices  31.5 us (11%)
  local copies, waits for them, and re-layouts  30.1 us (11%)
  blocking collectives  21.8 us (8%)
  other arithmetic  16.9 us (6%)
    dot_general x18, matrix products, backward_block(): jnp.einsum('bx,bc->xc', pick_table(slot_rows[:, slot], ext_rows), contrib...  37.3 us
    all_to_all x1, waiting for transfers between devices, pix_gather(): gathered = lax.all_to_all(spread, 'pix', 0, 0, tiled=True)  32.3 us
    ppermute x6, waiting for transfers between devices, ch_exchange(): lax.ppermute(value, 'ch', [(i, (i + shift) % size) for i in range(size)])  25.2 us
    all_to_all x1, waiting for transfers between devices, pix_scatter(): lax.all_to_all(flat.reshape(size, chunk, width), 'pix', 0, 0, tiled=True)  23.6 us
    all_to_all x1, blocking collectives, pix_scatter(): lax.all_to_all(flat.reshape(size, chunk, width), 'pix', 0, 0, tiled=True)  21.8 us
    dot_general x18, matrix products, forward_block(): jnp.dot(pick_table(slot_rows[:, slot], ext_rows), flattened, preferred_el...  17.7 us
    unnamed x116, local copies, waits for them, and re-layouts  9.13 us
    all_to_all x1, starting transfers between devices, per_device(): lax.all_to_all(outgoing, 'pix', split_axis=0, concat_axis=0, tiled=True)  8.21 us
  transfers between devices with their start and end apart: 11, of which 6 were waited for; matrix products, arithmetic and copies ran while one was open for 34% of the time, Pallas kernels for 0%

profile of v3, /device:TPU:15, one launch (start us, length us, event | category | flops | bytes accessed | tf_op | source)
XLA Modules:
  0.0 269.6 jit_solution(1369244658740814188)
XLA Ops:
  1.0 1.2 collective-permute-start
  3.5 1.1 reshape.155
  4.6 1.2 broadcast_select_fusion
  8.0 1.8 fusion.139
  9.9 15.8 %collective-permute-done = bf16[1024,384]{1,0:T(8,128)(2,1)S(1)} collective-permute-done((bf16[1024,384]{1,0:T(8,128)(2,1)}, bf16[1024,384]{1,0:T(8,128)(2,1)S(1)}, u32[]{:S(2)}, u32[]{:S(2)}) %collective-permute-start) | collective-permute-done | bytes 786464 | tf_op jit(solution)/shard_map/ppermute | solution.py:145
  26.3 1.0 copy.77
  29.4 1.1 reshape.156
  30.5 8.2 %all-to-all-start = ((bf16[16,32,2,192]{3,2,1,0:T(2,128)(2,1)}), bf16[16,32,2,192]{3,2,1,0:T(2,128)(2,1)S(1)}, u32[]{:S(2)}, u32[]{:S(2)}) async-start(bf16[16,32,2,192]{3,2,1,0:T(2,128)(2,1)} %reshape.156), calls=%async_computation | async-start | bytes 1048576 | tf_op jit(solution)/shard_map/all_to_all | solution.py:236
  39.4 1.0 copy.78
  40.4 1.3 collective-permute-start.5
  42.9 2.3 convolution_convert_fusion.1
  45.2 9.0 %collective-permute-done.3 = bf16[3,384,192]{1,2,0:T(8,128)(2,1)S(1)} collective-permute-done((bf16[3,384,192]{1,2,0:T(8,128)(2,1)}, bf16[3,384,192]{1,2,0:T(8,128)(2,1)S(1)}, u32[]{:S(2)}, u32[]{:S(2)}) %collective-permute-start.3) | collective-permute-done | bytes 442400 | tf_op jit(solution)/shard_map/ppermute | solution.py:145
  58.6 1.0 fusion.105
  60.6 1.0 fusion.107
  67.7 2.1 fusion.18
  69.8 1.9 fusion.22
  71.7 1.9 fusion.26
  73.6 1.9 fusion.30
  75.6 1.9 fusion.32
  81.4 1.2 fusion.114
  84.6 1.0 fusion.117
  90.9 1.9 fusion
  92.8 1.9 fusion.4
  94.7 1.9 fusion.8
  96.7 3.7 %fusion.12 = f32[1536,384]{1,0:T(8,128)} fusion(s32[512]{0:T(512)S(1)} %bitcast.315, bf16[512,9,384]{0,2,1:T(8,128)(2,1)S(1)} %bitcast.239), kind=kOutput, calls=%fused_computation.33 | convolution fusion | flops 604766208 | bytes 2754560 | tf_op jit(solution)/shard_map/bx,bc->xc/dot_general | solution.py:119
  101.2 1.3 collective-permute-start.4
  102.5 2.0 fusion.37
  104.6 2.0 fusion.39
  106.6 2.0 fusion.41
  108.6 2.0 fusion.43
  110.7 2.1 fusion.14
  112.8 1.9 fusion.16
  114.7 2.2 fusion.45
  116.9 2.0 fusion.47
  119.0 2.0 fusion.49
  121.0 1.4 copy-done
  123.2 2.1 reshape.158
  125.3 7.5 %all-to-all-start.1 = ((bf16[16,32,2,192]{3,2,1,0:T(2,128)(2,1)}), bf16[16,32,2,192]{3,2,1,0:T(2,128)(2,1)}, u32[]{:S(2)}, u32[]{:S(2)}) async-start(bf16[16,32,2,192]{3,2,1,0:T(2,128)(2,1)} %reshape.158), calls=%async_computation.1 | async-start | bytes 1048576 | tf_op jit(solution)/shard_map/all_to_all | solution.py:254
  132.8 1.2 multiply_reduce_fusion.2
  134.1 1.3 multiply_reduce_fusion
  136.2 2.8 %convolution_multiply_fusion.2 = f32[192,384]{1,0:T(8,128)} fusion(bf16[1024,192]{0,1:T(8,128)(2,1)S(1)} %bitcast.250, bf16[1024,192]{1,0:T(8,128)(2,1)S(1)} %copy-done.16, bf16[1024,192]{1,0:T(8,128)(2,1)} %collective-permute-done.2, pred[]{:T(512)S(6)} %eq.238), kind=kOutput, calls=%fused_computation.161 | convolution fusion | flops 154607616 | bytes 1474561 | tf_op jit(solution)/shard_map/dot_general | solution.py:244
  139.0 1.4 slice-done
  140.4 1.7 copy.110
  142.0 4.3 %all-to-all-done.1 = bf16[16,32,2,192]{3,2,1,0:T(2,128)(2,1)} async-done(((bf16[16,32,2,192]{3,2,1,0:T(2,128)(2,1)}), bf16[16,32,2,192]{3,2,1,0:T(2,128)(2,1)}, u32[]{:S(2)}, u32[]{:S(2)}) %all-to-all-start.1) | async-done | bytes 393248 | tf_op jit(solution)/shard_map/all_to_all | solution.py:254
  146.4 1.4 convert_element_type.211
  147.9 2.1 add_convert_fusion
  151.0 1.7 fusion.98
  152.7 1.5 copy.112
  154.5 2.1 pad_maximum_fusion.4
  156.6 5.1 %all-to-all-start.2 = ((f32[16,48,384]{2,1,0:T(8,128)}), f32[16,48,384]{2,1,0:T(8,128)S(1)}, u32[]{:S(2)}, u32[]{:S(2)}) async-start(f32[16,48,384]{2,1,0:T(8,128)} %bitcast.245), calls=%async_computation.2 | async-start | bytes 2359296 | tf_op jit(solution)/shard_map/all_to_all | solution.py:167
  161.7 1.1 pad_maximum_fusion.3
  163.1 3.2 %fusion.129 = f32[1024,384,1]{1,0,2:T(8,128)} fusion(bf16[3,384,192]{1,2,0:T(8,128)(2,1)} %param.11, bf16[1024,2,192]{0,2,1:T(8,128)(2,1)S(1)} %copy-done.13, bf16[1024,1,192]{0,2,1:T(8,128)(2,1)S(1)} %copy-done.9), kind=kOutput, calls=%fused_computation.232 | convolution fusion | flops 453574656 | bytes 3194880 | tf_op jit(solution)/shard_map/rkd,kcd->rc/dot_general | solution.py:272
  166.3 23.6 %all-to-all-done.2 = f32[16,48,384]{2,1,0:T(8,128)S(1)} async-done(((f32[16,48,384]{2,1,0:T(8,128)}), f32[16,48,384]{2,1,0:T(8,128)S(1)}, u32[]{:S(2)}, u32[]{:S(2)}) %all-to-all-start.2) | async-done | bytes 1179680 | tf_op jit(solution)/shard_map/all_to_all | solution.py:167
  190.4 3.7 %fusion.58 = bf16[1024,384]{1,0:T(8,128)(2,1)S(1)} fusion(f32[1024,384,1]{1,0,2:T(8,128)} %fusion.129, bf16[1024,3,192]{0,2,1:T(8,128)(2,1)} %collective-permute-done.6, bf16[3,384,192]{1,2,0:T(8,128)(2,1)} %copy-done.47, bf16[1024,192]{1,0:T(8,128)(2,1)} %collective-permute-done.2, bf16[1024,192]{1,0:T(8,128)(2,1)} %copy.78, pred[]{:T(512)S(6)} %eq.238), kind=kOutput, calls=%fused_computation.91 | convolution fusion | flops 458096640 | bytes 4767745 | tf_op jit(solution)/shard_map/rkd,kcd->rc/dot_general | solution.py:276
  194.7 21.8 %all_to_all.25 = f32[16,24,384]{2,1,0:T(8,128)S(1)} all-to-all(f32[16,24,384]{2,1,0:T(8,128)S(1)} %bitcast.246), channel_id=1, replica_groups=mesh['pix'=16,'ch'=2] {'pix'}, dimensions={0} | all-to-all | bytes 1179648 | tf_op jit(solution)/shard_map/all_to_all | solution.py:167
  216.6 1.4 broadcast_in_dim.48
  217.9 5.8 %all-to-all-start.4 = ((f32[16,72,384]{2,1,0:T(8,128)}), f32[16,72,384]{2,1,0:T(8,128)S(1)}, u32[]{:S(2)}, u32[]{:S(2)}) async-start(f32[16,72,384]{2,1,0:T(8,128)} %broadcast_in_dim.48), calls=%async_computation.4 | async-start | bytes 3538944 | tf_op jit(solution)/shard_map/all_to_all | solution.py:176
  223.7 1.3 fusion.122
  225.1 2.3 fusion.99
  227.3 2.0 copy.113
  229.3 2.5 convolution_convert_fusion
  231.8 32.3 %all-to-all-done.4 = f32[16,72,384]{2,1,0:T(8,128)S(1)} async-done(((f32[16,72,384]{2,1,0:T(8,128)}), f32[16,72,384]{2,1,0:T(8,128)S(1)}, u32[]{:S(2)}, u32[]{:S(2)}) %all-to-all-start.4) | async-done | bytes 1769504 | tf_op jit(solution)/shard_map/all_to_all | solution.py:176
  265.1 1.4 reshape.163
  266.5 1.3 copy.114
  (200 shorter events, 38.2 us)
Async XLA Ops:
  0.6 9.2 %collective-permute-start.1 = (bf16[384,384]{1,0:T(8,128)(2,1)}, bf16[384,384]{1,0:T(8,128)(2,1)S(1)}, u32[]{:S(2)}, u32[]{:S(2)}) collective-permute-start(bf16[384,384]{1,0:T(8,128)(2,1)} %param.10), channel_id=1, source_target_pairs={{0,1},{1,0},{2,3},{3,2},{4,5},{5,4},{6,7},{7,6},{8,9},{9,8},{10,11... | collective-permute-start | bytes 884744 | tf_op jit(solution)/shard_map/ppermute | solution.py:145
  1.0 24.7 %collective-permute-start = (bf16[1024,384]{1,0:T(8,128)(2,1)}, bf16[1024,384]{1,0:T(8,128)(2,1)S(1)}, u32[]{:S(2)}, u32[]{:S(2)}) collective-permute-start(bf16[1024,384]{1,0:T(8,128)(2,1)} %param.9), channel_id=1, source_target_pairs={{0,1},{1,0},{2,3},{3,2},{4,5},{5,4},{6,7},{7,6},{8,9},{9,8},{10,11... | collective-permute-start | bytes 2359304 | tf_op jit(solution)/shard_map/ppermute | solution.py:145
  5.8 51.8 %copy-start.27 = (s32[512,1]{0,1:T(1,128)}, s32[512,1]{0,1:T(1,128)S(1)}, u32[]{:S(2)}) copy-start(s32[512,1]{0,1:T(1,128)S(1)} %get-tuple-element.85) | copy-start | bytes 6148
  5.8 53.7 %copy-start.25 = (s32[512,1]{0,1:T(1,128)}, s32[512,1]{0,1:T(1,128)S(1)}, u32[]{:S(2)}) copy-start(s32[512,1]{0,1:T(1,128)S(1)} %get-tuple-element.83) | copy-start | bytes 6148
  5.8 55.7 %copy-start.23 = (s32[512,1]{0,1:T(1,128)}, s32[512,1]{0,1:T(1,128)S(1)}, u32[]{:S(2)}) copy-start(s32[512,1]{0,1:T(1,128)S(1)} %get-tuple-element.81) | copy-start | bytes 6148
  5.8 72.6 %copy-start.35 = (s32[512,1]{0,1:T(1,128)}, s32[512,1]{0,1:T(1,128)S(1)}, u32[]{:S(2)}) copy-start(s32[512,1]{0,1:T(1,128)S(1)} %get-tuple-element.98) | copy-start | bytes 6148
  5.8 73.6 %copy-start.37 = (s32[512,1]{0,1:T(1,128)}, s32[512,1]{0,1:T(1,128)S(1)}, u32[]{:S(2)}) copy-start(s32[512,1]{0,1:T(1,128)S(1)} %get-tuple-element.99) | copy-start | bytes 6148
  5.9 74.6 %copy-start.31 = (s32[512,1]{0,1:T(1,128)}, s32[512,1]{0,1:T(1,128)S(1)}, u32[]{:S(2)}) copy-start(s32[512,1]{0,1:T(1,128)S(1)} %get-tuple-element.100) | copy-start | bytes 6148
  5.9 75.5 %copy-start.39 = (s32[512,1]{0,1:T(1,128)}, s32[512,1]{0,1:T(1,128)S(1)}, u32[]{:S(2)}) copy-start(s32[512,1]{0,1:T(1,128)S(1)} %get-tuple-element.101) | copy-start | bytes 6148
  5.9 77.7 %copy-start.41 = (s32[512,1]{0,1:T(1,128)}, s32[512,1]{0,1:T(1,128)S(1)}, u32[]{:S(2)}) copy-start(s32[512,1]{0,1:T(1,128)S(1)} %get-tuple-element.103) | copy-start | bytes 6148
  5.9 79.7 %copy-start.43 = (s32[512,1]{0,1:T(1,128)}, s32[512,1]{0,1:T(1,128)S(1)}, u32[]{:S(2)}) copy-start(s32[512,1]{0,1:T(1,128)S(1)} %get-tuple-element.105) | copy-start | bytes 6148
  6.6 57.0 %copy-start.29 = (s32[512]{0:T(512)}, s32[512]{0:T(512)S(1)}, u32[]{:S(2)}) copy-start(s32[512]{0:T(512)S(1)} %iota_add_fusion.1) | copy-start | bytes 6148
  7.3 21.3 %copy-start.33 = (s32[512]{0:T(512)}, s32[512]{0:T(512)S(1)}, u32[]{:S(2)}) copy-start(s32[512]{0:T(512)S(1)} %eq.167) | copy-start | bytes 6148
  9.8 16.5 %copy-start.7 = (bf16[1024,192]{0,1:T(8,128)(2,1)S(1)}, bf16[1024,192]{0,1:T(8,128)(2,1)}, u32[]{:S(2)}) copy-start(bf16[1024,192]{0,1:T(8,128)(2,1)} %param.15) | copy-start | bytes 1179652
  9.8 17.7 %copy-start.17 = (bf16[3,384,192]{1,2,0:T(8,128)(2,1)S(1)}, bf16[3,384,192]{1,2,0:T(8,128)(2,1)}, u32[]{:S(2)}) copy-start(bf16[3,384,192]{1,2,0:T(8,128)(2,1)} %param.11) | copy-start | bytes 1327108
  26.3 2.3 copy-start.1
  27.3 15.5 %collective-permute-start.2 = (bf16[1024,192]{1,0:T(8,128)(2,1)}, bf16[1024,192]{1,0:T(8,128)(2,1)}, u32[]{:S(2)}, u32[]{:S(2)}) collective-permute-start(bf16[1024,192]{1,0:T(8,128)(2,1)} %copy.77), channel_id=1, source_target_pairs={{0,1},{1,0},{2,3},{3,2},{4,5},{5,4},{6,7},{7,6},{8,9},{9,8},{10,11... | collective-permute-start | bytes 1179656 | tf_op jit(solution)/shard_map/ppermute | solution.py:145
  29.4 13.5 %copy-start.22 = (bf16[192,384]{1,0:T(8,128)(2,1)S(1)}, bf16[192,384]{1,0:T(8,128)(2,1)}, u32[]{:S(2)}) copy-start(bf16[192,384]{1,0:T(8,128)(2,1)} %param.12) | copy-start | bytes 442372
  30.5 24.6 %all-to-all-start = ((bf16[16,32,2,192]{3,2,1,0:T(2,128)(2,1)}), bf16[16,32,2,192]{3,2,1,0:T(2,128)(2,1)S(1)}, u32[]{:S(2)}, u32[]{:S(2)}) async-start(bf16[16,32,2,192]{3,2,1,0:T(2,128)(2,1)} %reshape.156), calls=%async_computation | async-start | bytes 1048576 | tf_op jit(solution)/shard_map/all_to_all | solution.py:236
  39.4 38.1 %copy-start.45 = (s32[512]{0:T(512)}, s32[512]{0:T(512)S(1)}, u32[]{:S(2)}) copy-start(s32[512]{0:T(512)S(1)} %iota_add_fusion) | copy-start | bytes 6148
  40.4 74.3 %collective-permute-start.5 = (bf16[192,192]{1,0:T(8,128)(2,1)}, bf16[192,192]{1,0:T(8,128)(2,1)}, u32[]{:S(2)}, u32[]{:S(2)}) collective-permute-start(bf16[192,192]{1,0:T(8,128)(2,1)} %bitcast.217), channel_id=1, source_target_pairs={{0,1},{1,0},{2,3},{3,2},{4,5},{5,4},{6,7},{7,6},{8,9},{9,8},{10,11... | collective-permute-start | bytes 221192 | tf_op jit(solution)/shard_map/ppermute | solution.py:220
  41.7 12.5 %collective-permute-start.3 = (bf16[3,384,192]{1,2,0:T(8,128)(2,1)}, bf16[3,384,192]{1,2,0:T(8,128)(2,1)S(1)}, u32[]{:S(2)}, u32[]{:S(2)}) collective-permute-start(bf16[3,384,192]{1,2,0:T(8,128)(2,1)} %param.11), channel_id=1, source_target_pairs={{0,1},{1,0},{2,3},{3,2},{4,5},{5,4},{6,7},{7,6},{8,9},{9,8},{10,11... | collective-permute-start | bytes 1327112 | tf_op jit(solution)/shard_map/ppermute | solution.py:145
  54.2 0.9 copy-start.47
  55.6 7.9 %copy-start.19 = (bf16[512,384]{0,1:T(8,128)(2,1)}, bf16[512,384]{0,1:T(8,128)(2,1)S(1)}, u32[]{:S(2)}) copy-start(bf16[512,384]{0,1:T(8,128)(2,1)S(1)} %copy.75) | copy-start | bytes 1179652
  66.3 0.6 copy-start.14
  75.5 1.9 copy-start.20
  86.9 1.0 copy-start.3
  87.1 1.3 copy-start.4
  89.1 0.6 copy-start.15
  90.2 0.7 copy-start.44
  90.5 2.3 copy-start.42
  92.8 1.9 copy-start.40
  94.7 1.9 copy-start.38
  100.4 2.1 copy-start.30
  101.2 3.3 %copy-start.10 = (bf16[2,24,8,512]{3,2,0,1:T(8,128)(2,1)}, bf16[2,24,8,512]{3,2,0,1:T(8,128)(2,1)S(1)}, u32[]{:S(2)}) copy-start(bf16[2,24,8,512]{3,2,0,1:T(8,128)(2,1)S(1)} %copy.182) | copy-start | bytes 1179652
  101.2 3.3 %copy-start.28 = (s32[512,1]{0,1:T(1,128)S(1)}, s32[512,1]{0,1:T(1,128)}, u32[]{:S(2)}) copy-start(s32[512,1]{0,1:T(1,128)} %copy-done.27) | copy-start | bytes 6148
  101.2 13.5 %collective-permute-start.4 = (bf16[1024,192]{0,1:T(8,128)(2,1)S(1)}, bf16[1024,192]{0,1:T(8,128)(2,1)S(1)}, u32[]{:S(2)}, u32[]{:S(2)}) collective-permute-start(bf16[1024,192]{0,1:T(8,128)(2,1)S(1)} %bitcast.248), channel_id=1, source_target_pairs={{0,1},{1,0},{2,3},{3,2},{4,5},{5,4},{6,7},{7,6},{8,9},{9,8},{10,11... | collective-permute-start | bytes 1179656 | tf_op jit(solution)/shard_map/ppermute | solution.py:145
  104.5 2.0 copy-start.26
  106.6 2.0 copy-start.24
  108.6 2.0 copy-start.36
  110.7 2.1 copy-start.46
  112.8 2.0 copy-start.6
  112.8 2.0 copy-start.32
  114.7 2.2 copy-start.21
  121.0 1.4 copy-start
  125.3 21.1 %all-to-all-start.1 = ((bf16[16,32,2,192]{3,2,1,0:T(2,128)(2,1)}), bf16[16,32,2,192]{3,2,1,0:T(2,128)(2,1)}, u32[]{:S(2)}, u32[]{:S(2)}) async-start(bf16[16,32,2,192]{3,2,1,0:T(2,128)(2,1)} %reshape.158), calls=%async_computation.1 | async-start | bytes 1048576 | tf_op jit(solution)/shard_map/all_to_all | solution.py:254
  134.1 2.1 copy-start.11
  134.1 2.1 copy-start.16
  136.2 13.9 %copy-start.8 = (bf16[1024,1,192]{0,2,1:T(8,128)(2,1)}, bf16[1024,1,192]{0,2,1:T(8,128)(2,1)S(1)}, u32[]{:S(2)}) copy-start(bf16[1024,1,192]{0,2,1:T(8,128)(2,1)S(1)} %reshape_reshape.4) | copy-start | bytes 1179652
  139.0 1.4 slice-start
  140.4 7.5 %copy-start.34 = (s32[512]{0:T(512)S(1)}, s32[512]{0:T(512)}, u32[]{:S(2)}) copy-start(s32[512]{0:T(512)} %copy-done.33) | copy-start | bytes 6148
  142.0 9.0 %copy-start.2 = (bf16[1024,384]{1,0:T(8,128)(2,1)S(1)}, bf16[1024,384]{1,0:T(8,128)(2,1)}, u32[]{:S(2)}) copy-start(bf16[1024,384]{1,0:T(8,128)(2,1)} %copy-done.1) | copy-start | bytes 2359300
  150.1 0.9 copy-start.12
  154.5 7.2 %copy-start.9 = (bf16[1024,1,192]{0,2,1:T(8,128)(2,1)S(1)}, bf16[1024,1,192]{0,2,1:T(8,128)(2,1)}, u32[]{:S(2)}) copy-start(bf16[1024,1,192]{0,2,1:T(8,128)(2,1)} %copy-done.8) | copy-start | bytes 1179652
  156.6 5.1 %copy-start.13 = (bf16[1024,2,192]{0,2,1:T(8,128)(2,1)S(1)}, bf16[1024,2,192]{0,2,1:T(8,128)(2,1)}, u32[]{:S(2)}) copy-start(bf16[1024,2,192]{0,2,1:T(8,128)(2,1)} %copy-done.12) | copy-start | bytes 2359300
  156.6 33.2 %all-to-all-start.2 = ((f32[16,48,384]{2,1,0:T(8,128)}), f32[16,48,384]{2,1,0:T(8,128)S(1)}, u32[]{:S(2)}, u32[]{:S(2)}) async-start(f32[16,48,384]{2,1,0:T(8,128)} %bitcast.245), calls=%async_computation.2 | async-start | bytes 2359296 | tf_op jit(solution)/shard_map/all_to_all | solution.py:167
  162.8 27.5 %collective-permute-start.6 = (bf16[1024,3,192]{0,2,1:T(8,128)(2,1)}, bf16[1024,3,192]{0,2,1:T(8,128)(2,1)}, u32[]{:S(2)}, u32[]{:S(2)}) collective-permute-start(bf16[1024,3,192]{0,2,1:T(8,128)(2,1)} %pad_maximum_fusion.3), channel_id=1, source_target_pairs={{0,1},{1,0},{2,3},{3,2},{4,5},{5,4},{6,7},{7,6},{8,9},{9,8},{10,11... | collective-permute-start | bytes 3538952 | tf_op jit(solution)/shard_map/ppermute | solution.py:145
  189.9 4.2 %copy-start.5 = (bf16[1024,384]{1,0:T(8,128)(2,1)S(1)}, bf16[1024,384]{1,0:T(8,128)(2,1)}, u32[]{:S(2)}) copy-start(bf16[1024,384]{1,0:T(8,128)(2,1)} %param.9) | copy-start | bytes 2359300
  216.5 7.2 %copy-start.18 = (bf16[192,1,192]{2,1,0:T(2,128)(2,1)S(1)}, bf16[192,1,192]{2,1,0:T(2,128)(2,1)}, u32[]{:S(2)}) copy-start(bf16[192,1,192]{2,1,0:T(2,128)(2,1)} %get-tuple-element.74) | copy-start | bytes 221188
  217.9 46.2 %all-to-all-start.4 = ((f32[16,72,384]{2,1,0:T(8,128)}), f32[16,72,384]{2,1,0:T(8,128)S(1)}, u32[]{:S(2)}, u32[]{:S(2)}) async-start(f32[16,72,384]{2,1,0:T(8,128)} %broadcast_in_dim.48), calls=%async_computation.4 | async-start | bytes 3538944 | tf_op jit(solution)/shard_map/all_to_all | solution.py:176

commit v4 on v3

--- a/solution.py
+++ b/solution.py
@@ -158,27 +158,48 @@
     return result
 
 
+def core_swap(value):
+    size = lax.axis_size("pix")
+    return lax.ppermute(value, "pix", [(i, i ^ 1) for i in range(size)])
+
+
 def pix_scatter(terms, width):
     size = lax.axis_size("pix")
+    core = lax.axis_index("pix") % 2
     flat = jnp.concatenate([term.reshape(-1, width) for term in terms], axis=0)
     rows = flat.shape[0]
-    chunk = -(-rows // size)
-    flat = jnp.pad(flat, ((0, chunk * size - rows), (0, 0)))
-    parts = lax.all_to_all(flat.reshape(size, chunk, width), "pix", 0, 0, tiled=True)
-    return jnp.sum(parts, axis=0)
+    chunk = -(-rows // (2 * size))
+    flat = jnp.pad(flat, ((0, 2 * size * chunk - rows), (0, 0)))
+    halves = flat.reshape(2, size * chunk, width)
+    keep = jnp.where(core == 0, halves[0], halves[1])
+    send = jnp.where(core == 0, halves[1], halves[0])
+    mine = keep + core_swap(send)
+    parts = lax.all_to_all(mine.reshape(size, chunk, width), "pix", 0, 0, tiled=True)
+    return jnp.sum(parts.reshape(size // 2, 2, chunk, width), axis=0)
 
 
 def pix_gather(reduced_groups, term_groups):
     size = lax.axis_size("pix")
+    core = lax.axis_index("pix") % 2
     width = reduced_groups[0].shape[-1]
-    joined = jnp.concatenate(reduced_groups, axis=0)
-    spread = jnp.broadcast_to(joined[None], (size,) + joined.shape)
-    gathered = lax.all_to_all(spread, "pix", 0, 0, tiled=True)
+    joined = jnp.concatenate(reduced_groups, axis=1)
+    total = joined.shape[1]
+    spread = jnp.broadcast_to(joined[None], (size // 2, 2, total, width))
+    got = lax.all_to_all(spread.reshape(size, total, width), "pix", 0, 0, tiled=True)
+    other = core_swap(got)
+    first = jnp.where(core == 0, got, other)
+    second = jnp.where(core == 0, other, got)
     results = []
     offset = 0
     for reduced, terms in zip(reduced_groups, term_groups):
-        chunk = reduced.shape[0]
-        flat = gathered[:, offset : offset + chunk].reshape(size * chunk, width)
+        chunk = reduced.shape[1]
+        flat = jnp.concatenate(
+            [
+                first[:, offset : offset + chunk].reshape(size * chunk, width),
+                second[:, offset : offset + chunk].reshape(size * chunk, width),
+            ],
+            axis=0,
+        )
         offset += chunk
         row = 0
         for term in terms:

time: 274 us -> 252 us (0.920)
  the two profiles are of different devices: /device:TPU:15 before, /device:TPU:0 now
where the time goes in v4:
time: 252 us; the launch traced here: 247 us
  matrix products  78.7 us (31%)
  waiting for transfers between devices  52 us (21%)
  blocking collectives  43.5 us (17%)
  starting transfers between devices  26.4 us (10%)
  local copies, waits for them, and re-layouts  24.2 us (10%)
  other arithmetic  19.3 us (8%)
  between operations  2.74 us (1%)
    dot_general x18, matrix products, backward_block(): jnp.einsum('bx,bc->xc', pick_table(slot_rows[:, slot], ext_rows), contrib...  37.2 us
    ppermute x6, waiting for transfers between devices, ch_exchange(): lax.ppermute(value, 'ch', [(i, (i + shift) % size) for i in range(size)])  32.2 us
    all_to_all x1, blocking collectives, pix_gather(): lax.all_to_all(spread.reshape(size, total, width), 'pix', 0, 0, tiled=True)  27.4 us
    dot_general x18, matrix products, forward_block(): jnp.dot(pick_table(slot_rows[:, slot], ext_rows), flattened, preferred_el...  18 us
    all_to_all x1, blocking collectives, pix_scatter(): lax.all_to_all(mine.reshape(size, chunk, width), 'pix', 0, 0, tiled=True)  16.1 us
    all_to_all x1, waiting for transfers between devices, pix_scatter(): lax.all_to_all(mine.reshape(size, chunk, width), 'pix', 0, 0, tiled=True)  12.4 us
    ppermute x6, starting transfers between devices, ch_exchange(): lax.ppermute(value, 'ch', [(i, (i + shift) % size) for i in range(size)])  8.45 us
    unnamed x118, local copies, waits for them, and re-layouts  7.27 us
  transfers between devices with their start and end apart: 13, of which 7 were waited for; matrix products, arithmetic and copies ran while one was open for 36% of the time, Pallas kernels for 0%

profile of v4, /device:TPU:0, one launch (start us, length us, event | category | flops | bytes accessed | tf_op | source)
XLA Modules:
  0.0 246.8 jit_solution(13783201367864865338)
XLA Ops:
  0.6 3.0 %collective-permute-start.1 = (bf16[384,384]{1,0:T(8,128)(2,1)}, bf16[384,384]{1,0:T(8,128)(2,1)S(1)}, u32[]{:S(2)}, u32[]{:S(2)}) collective-permute-start(bf16[384,384]{1,0:T(8,128)(2,1)} %param.10), channel_id=1, source_target_pairs={{0,1},{1,0},{2,3},{3,2},{4,5},{5,4},{6,7},{7,6},{8,9},{9,8},{10,11... | collective-permute-start | bytes 884744 | tf_op jit(solution)/shard_map/ppermute | solution.py:145
  5.0 1.1 reshape.181
  6.1 1.2 broadcast_select_fusion
  9.5 1.8 fusion.140
  11.7 16.0 %collective-permute-done = bf16[1024,384]{1,0:T(8,128)(2,1)S(1)} collective-permute-done((bf16[1024,384]{1,0:T(8,128)(2,1)}, bf16[1024,384]{1,0:T(8,128)(2,1)S(1)}, u32[]{:S(2)}, u32[]{:S(2)}) %collective-permute-start) | collective-permute-done | bytes 786464 | tf_op jit(solution)/shard_map/ppermute | solution.py:145
  28.4 1.0 copy.162
  29.4 1.7 collective-permute-start.2
  33.0 1.1 reshape.182
  34.1 6.1 %all-to-all-start = ((bf16[16,32,2,192]{3,2,1,0:T(2,128)(2,1)}), bf16[16,32,2,192]{3,2,1,0:T(2,128)(2,1)S(1)}, u32[]{:S(2)}, u32[]{:S(2)}) async-start(bf16[16,32,2,192]{3,2,1,0:T(2,128)(2,1)} %reshape.182), calls=%async_computation | async-start | bytes 1048576 | tf_op jit(solution)/shard_map/all_to_all | solution.py:257
  40.9 1.0 copy.163
  42.5 1.5 collective-permute-start.3
  44.9 2.3 convolution_convert_fusion.1
  47.2 9.6 %collective-permute-done.3 = bf16[3,384,192]{1,2,0:T(8,128)(2,1)S(1)} collective-permute-done((bf16[3,384,192]{1,2,0:T(8,128)(2,1)}, bf16[3,384,192]{1,2,0:T(8,128)(2,1)S(1)}, u32[]{:S(2)}, u32[]{:S(2)}) %collective-permute-start.3) | collective-permute-done | bytes 442400 | tf_op jit(solution)/shard_map/ppermute | solution.py:145
  61.1 1.0 fusion.106
  63.1 1.0 fusion.108
  70.3 2.1 fusion.18
  72.4 1.9 fusion.22
  74.3 1.9 fusion.26
  76.2 1.9 fusion.30
  78.2 1.9 fusion.32
  84.1 1.4 fusion.115
  85.5 1.0 fusion.116
  87.5 1.0 fusion.118
  93.8 1.9 fusion
  95.7 1.9 fusion.4
  97.6 1.9 fusion.8
  99.6 3.5 %fusion.12 = f32[1536,384]{1,0:T(8,128)} fusion(s32[512]{0:T(512)S(1)} %bitcast.320, bf16[512,9,384]{0,2,1:T(8,128)(2,1)S(1)} %bitcast.242), kind=kOutput, calls=%fused_computation.33 | convolution fusion | flops 604766208 | bytes 2754560 | tf_op jit(solution)/shard_map/bx,bc->xc/dot_general | solution.py:119
  104.5 2.0 fusion.37
  106.6 2.0 fusion.39
  108.6 2.0 fusion.41
  110.6 2.0 fusion.43
  112.7 2.1 fusion.14
  114.8 1.9 fusion.16
  116.8 2.2 fusion.45
  119.0 2.0 fusion.47
  121.0 2.0 fusion.49
  123.0 1.4 copy-done
  125.2 2.1 reshape.184
  127.3 6.0 %all-to-all-start.1 = ((bf16[16,32,2,192]{3,2,1,0:T(2,128)(2,1)}), bf16[16,32,2,192]{3,2,1,0:T(2,128)(2,1)}, u32[]{:S(2)}, u32[]{:S(2)}) async-start(bf16[16,32,2,192]{3,2,1,0:T(2,128)(2,1)} %reshape.184), calls=%async_computation.1 | async-start | bytes 1048576 | tf_op jit(solution)/shard_map/all_to_all | solution.py:275
  133.3 1.2 multiply_reduce_fusion.2
  134.6 1.3 multiply_reduce_fusion
  136.4 1.0 reshape_reshape.4
  137.4 2.6 %convolution_multiply_fusion.2 = f32[192,384]{1,0:T(8,128)} fusion(bf16[1024,192]{0,1:T(8,128)(2,1)S(1)} %bitcast.255, bf16[1024,192]{1,0:T(8,128)(2,1)S(1)} %copy-done.18, bf16[1024,192]{1,0:T(8,128)(2,1)} %collective-permute-done.2, pred[]{:T(512)S(6)} %eq.243), kind=kOutput, calls=%fused_computation.161 | convolution fusion | flops 154607616 | bytes 1474561 | tf_op jit(solution)/shard_map/dot_general | solution.py:265
  140.1 1.4 slice-done
  142.0 5.9 %all-to-all-done.1 = bf16[16,32,2,192]{3,2,1,0:T(2,128)(2,1)} async-done(((bf16[16,32,2,192]{3,2,1,0:T(2,128)(2,1)}), bf16[16,32,2,192]{3,2,1,0:T(2,128)(2,1)}, u32[]{:S(2)}, u32[]{:S(2)}) %all-to-all-start.1) | async-done | bytes 393248 | tf_op jit(solution)/shard_map/all_to_all | solution.py:275
  147.8 1.4 convert_element_type.211
  150.2 2.1 fusion.98
  153.4 1.1 broadcast_select_fusion.2
  154.7 1.2 pad_maximum_fusion.3
  155.9 1.5 collective-permute-start.7
  158.3 4.3 %all-to-all-start.2 = ((f32[16,24,384]{2,1,0:T(8,128)}), f32[16,24,384]{2,1,0:T(8,128)S(1)}, u32[]{:S(2)}, u32[]{:S(2)}) async-start(f32[16,24,384]{2,1,0:T(8,128)} %bitcast.103), calls=%async_computation.2 | async-start | bytes 1179648 | tf_op jit(solution)/shard_map/all_to_all | solution.py:177
  162.6 3.2 %fusion.130 = f32[1024,384,1]{1,0,2:T(8,128)} fusion(bf16[3,384,192]{1,2,0:T(8,128)(2,1)} %param.11, bf16[1024,2,192]{0,2,1:T(8,128)(2,1)S(1)} %copy-done.15, bf16[1024,1,192]{0,2,1:T(8,128)(2,1)S(1)} %copy-done.8), kind=kOutput, calls=%fused_computation.241 | convolution fusion | flops 453574656 | bytes 3194880 | tf_op jit(solution)/shard_map/rkd,kcd->rc/dot_general | solution.py:293
  165.8 12.4 %all-to-all-done.2 = f32[16,24,384]{2,1,0:T(8,128)S(1)} async-done(((f32[16,24,384]{2,1,0:T(8,128)}), f32[16,24,384]{2,1,0:T(8,128)S(1)}, u32[]{:S(2)}, u32[]{:S(2)}) %all-to-all-start.2) | async-done | bytes 589856 | tf_op jit(solution)/shard_map/all_to_all | solution.py:177
  178.2 6.3 %collective-permute-done.7 = bf16[1024,3,192]{0,2,1:T(8,128)(2,1)} collective-permute-done((bf16[1024,3,192]{0,2,1:T(8,128)(2,1)}, bf16[1024,3,192]{0,2,1:T(8,128)(2,1)}, u32[]{:S(2)}, u32[]{:S(2)}) %collective-permute-start.7) | collective-permute-done | bytes 1179680 | tf_op jit(solution)/shard_map/ppermute | solution.py:145
  184.5 3.7 %fusion.58 = bf16[1024,384]{1,0:T(8,128)(2,1)S(1)} fusion(f32[1024,384,1]{1,0,2:T(8,128)} %fusion.130, bf16[1024,3,192]{0,2,1:T(8,128)(2,1)} %collective-permute-done.7, bf16[3,384,192]{1,2,0:T(8,128)(2,1)} %copy-done.48, bf16[1024,192]{1,0:T(8,128)(2,1)} %collective-permute-done.2, bf16[1024,192]{1,0:T(8,128)(2,1)} %copy.163, pred[]{:T(512)S(6)} %eq.243), kind=kOutput, calls=%fused_computation.91 | convolution fusion | flops 458096640 | bytes 4767745 | tf_op jit(solution)/shard_map/rkd,kcd->rc/dot_general | solution.py:297
  189.0 1.6 collective-permute-done.8
  190.7 16.1 %all_to_all.25 = f32[16,12,384]{2,1,0:T(8,128)S(1)} all-to-all(f32[16,12,384]{2,1,0:T(8,128)S(1)} %reshape.188), channel_id=1, replica_groups=mesh['pix'=16,'ch'=2] {'pix'}, dimensions={0} | all-to-all | bytes 589824 | tf_op jit(solution)/shard_map/all_to_all | solution.py:177
  206.9 27.4 %all_to_all.26 = f32[16,36,384]{2,1,0:T(8,128)S(1)} all-to-all(f32[16,36,384]{2,1,0:T(8,128)S(1)} %bitcast.248), channel_id=1, replica_groups=mesh['pix'=16,'ch'=2] {'pix'}, dimensions={0} | all-to-all | bytes 1769472 | tf_op jit(solution)/shard_map/all_to_all | solution.py:188
  234.3 1.1 copy.199
  236.2 1.3 fusion.123
  237.5 1.5 fusion.99
  239.9 1.5 convolution_convert_fusion
  241.4 1.5 copy_select_fusion.1
  244.2 1.3 copy.203
  (222 shorter events, 40.9 us)
Async XLA Ops:
  0.6 11.1 %collective-permute-start.1 = (bf16[384,384]{1,0:T(8,128)(2,1)}, bf16[384,384]{1,0:T(8,128)(2,1)S(1)}, u32[]{:S(2)}, u32[]{:S(2)}) collective-permute-start(bf16[384,384]{1,0:T(8,128)(2,1)} %param.10), channel_id=1, source_target_pairs={{0,1},{1,0},{2,3},{3,2},{4,5},{5,4},{6,7},{7,6},{8,9},{9,8},{10,11... | collective-permute-start | bytes 884744 | tf_op jit(solution)/shard_map/ppermute | solution.py:145
  3.6 24.1 %collective-permute-start = (bf16[1024,384]{1,0:T(8,128)(2,1)}, bf16[1024,384]{1,0:T(8,128)(2,1)S(1)}, u32[]{:S(2)}, u32[]{:S(2)}) collective-permute-start(bf16[1024,384]{1,0:T(8,128)(2,1)} %param.9), channel_id=1, source_target_pairs={{0,1},{1,0},{2,3},{3,2},{4,5},{5,4},{6,7},{7,6},{8,9},{9,8},{10,11... | collective-permute-start | bytes 2359304 | tf_op jit(solution)/shard_map/ppermute | solution.py:145
  7.4 52.8 %copy-start.28 = (s32[512,1]{0,1:T(1,128)}, s32[512,1]{0,1:T(1,128)S(1)}, u32[]{:S(2)}) copy-start(s32[512,1]{0,1:T(1,128)S(1)} %get-tuple-element.97) | copy-start | bytes 6148
  7.4 54.8 %copy-start.26 = (s32[512,1]{0,1:T(1,128)}, s32[512,1]{0,1:T(1,128)S(1)}, u32[]{:S(2)}) copy-start(s32[512,1]{0,1:T(1,128)S(1)} %get-tuple-element.95) | copy-start | bytes 6148
  7.4 56.7 %copy-start.24 = (s32[512,1]{0,1:T(1,128)}, s32[512,1]{0,1:T(1,128)S(1)}, u32[]{:S(2)}) copy-start(s32[512,1]{0,1:T(1,128)S(1)} %get-tuple-element.93) | copy-start | bytes 6148
  7.4 73.7 %copy-start.36 = (s32[512,1]{0,1:T(1,128)}, s32[512,1]{0,1:T(1,128)S(1)}, u32[]{:S(2)}) copy-start(s32[512,1]{0,1:T(1,128)S(1)} %get-tuple-element.110) | copy-start | bytes 6148
  7.4 74.7 %copy-start.38 = (s32[512,1]{0,1:T(1,128)}, s32[512,1]{0,1:T(1,128)S(1)}, u32[]{:S(2)}) copy-start(s32[512,1]{0,1:T(1,128)S(1)} %get-tuple-element.111) | copy-start | bytes 6148
  7.4 75.7 %copy-start.32 = (s32[512,1]{0,1:T(1,128)}, s32[512,1]{0,1:T(1,128)S(1)}, u32[]{:S(2)}) copy-start(s32[512,1]{0,1:T(1,128)S(1)} %get-tuple-element.112) | copy-start | bytes 6148
  7.4 76.7 %copy-start.40 = (s32[512,1]{0,1:T(1,128)}, s32[512,1]{0,1:T(1,128)S(1)}, u32[]{:S(2)}) copy-start(s32[512,1]{0,1:T(1,128)S(1)} %get-tuple-element.113) | copy-start | bytes 6148
  7.4 79.1 %copy-start.42 = (s32[512,1]{0,1:T(1,128)}, s32[512,1]{0,1:T(1,128)S(1)}, u32[]{:S(2)}) copy-start(s32[512,1]{0,1:T(1,128)S(1)} %get-tuple-element.115) | copy-start | bytes 6148
  7.4 81.0 %copy-start.44 = (s32[512,1]{0,1:T(1,128)}, s32[512,1]{0,1:T(1,128)S(1)}, u32[]{:S(2)}) copy-start(s32[512,1]{0,1:T(1,128)S(1)} %get-tuple-element.117) | copy-start | bytes 6148
  8.1 58.0 %copy-start.30 = (s32[512]{0:T(512)}, s32[512]{0:T(512)S(1)}, u32[]{:S(2)}) copy-start(s32[512]{0:T(512)S(1)} %iota_add_fusion.1) | copy-start | bytes 6148
  8.9 23.3 %copy-start.34 = (s32[512]{0:T(512)}, s32[512]{0:T(512)S(1)}, u32[]{:S(2)}) copy-start(s32[512]{0:T(512)S(1)} %eq.172) | copy-start | bytes 6148
  11.4 17.0 %copy-start.7 = (bf16[1024,192]{0,1:T(8,128)(2,1)S(1)}, bf16[1024,192]{0,1:T(8,128)(2,1)}, u32[]{:S(2)}) copy-start(bf16[1024,192]{0,1:T(8,128)(2,1)} %param.15) | copy-start | bytes 1179652
  11.4 19.8 %copy-start.19 = (bf16[3,384,192]{1,2,0:T(8,128)(2,1)S(1)}, bf16[3,384,192]{1,2,0:T(8,128)(2,1)}, u32[]{:S(2)}) copy-start(bf16[3,384,192]{1,2,0:T(8,128)(2,1)} %param.11) | copy-start | bytes 1327108
  28.3 3.8 %copy-start.1 = (bf16[1024,384]{1,0:T(8,128)(2,1)}, bf16[1024,384]{1,0:T(8,128)(2,1)S(1)}, u32[]{:S(2)}) copy-start(bf16[1024,384]{1,0:T(8,128)(2,1)S(1)} %add_convert_fusion.1) | copy-start | bytes 2359300
  29.4 15.5 %collective-permute-start.2 = (bf16[1024,192]{1,0:T(8,128)(2,1)}, bf16[1024,192]{1,0:T(8,128)(2,1)}, u32[]{:S(2)}, u32[]{:S(2)}) collective-permute-start(bf16[1024,192]{1,0:T(8,128)(2,1)} %copy.162), channel_id=1, source_target_pairs={{0,1},{1,0},{2,3},{3,2},{4,5},{5,4},{6,7},{7,6},{8,9},{9,8},{10,11... | collective-permute-start | bytes 1179656 | tf_op jit(solution)/shard_map/ppermute | solution.py:145
  33.0 11.9 %copy-start.23 = (bf16[192,384]{1,0:T(8,128)(2,1)S(1)}, bf16[192,384]{1,0:T(8,128)(2,1)}, u32[]{:S(2)}) copy-start(bf16[192,384]{1,0:T(8,128)(2,1)} %param.12) | copy-start | bytes 442372
  34.1 23.6 %all-to-all-start = ((bf16[16,32,2,192]{3,2,1,0:T(2,128)(2,1)}), bf16[16,32,2,192]{3,2,1,0:T(2,128)(2,1)S(1)}, u32[]{:S(2)}, u32[]{:S(2)}) async-start(bf16[16,32,2,192]{3,2,1,0:T(2,128)(2,1)} %reshape.182), calls=%async_computation | async-start | bytes 1048576 | tf_op jit(solution)/shard_map/all_to_all | solution.py:257
  40.9 39.2 %copy-start.46 = (s32[512]{0:T(512)}, s32[512]{0:T(512)S(1)}, u32[]{:S(2)}) copy-start(s32[512]{0:T(512)S(1)} %iota_add_fusion) | copy-start | bytes 6148
  41.9 74.8 %collective-permute-start.5 = (bf16[192,192]{1,0:T(8,128)(2,1)}, bf16[192,192]{1,0:T(8,128)(2,1)}, u32[]{:S(2)}, u32[]{:S(2)}) collective-permute-start(bf16[192,192]{1,0:T(8,128)(2,1)} %bitcast.220), channel_id=1, source_target_pairs={{0,1},{1,0},{2,3},{3,2},{4,5},{5,4},{6,7},{7,6},{8,9},{9,8},{10,11... | collective-permute-start | bytes 221192 | tf_op jit(solution)/shard_map/ppermute | solution.py:241
  42.5 14.2 %collective-permute-start.3 = (bf16[3,384,192]{1,2,0:T(8,128)(2,1)}, bf16[3,384,192]{1,2,0:T(8,128)(2,1)S(1)}, u32[]{:S(2)}, u32[]{:S(2)}) collective-permute-start(bf16[3,384,192]{1,2,0:T(8,128)(2,1)} %param.11), channel_id=1, source_target_pairs={{0,1},{1,0},{2,3},{3,2},{4,5},{5,4},{6,7},{7,6},{8,9},{9,8},{10,11... | collective-permute-start | bytes 1327112 | tf_op jit(solution)/shard_map/ppermute | solution.py:145
  56.8 0.9 copy-start.48
  58.2 7.9 %copy-start.20 = (bf16[512,384]{0,1:T(8,128)(2,1)}, bf16[512,384]{0,1:T(8,128)(2,1)S(1)}, u32[]{:S(2)}) copy-start(bf16[512,384]{0,1:T(8,128)(2,1)S(1)} %copy.160) | copy-start | bytes 1179652
  68.8 0.6 copy-start.16
  78.2 1.9 copy-start.21
  89.8 1.0 copy-start.3
  90.0 1.3 copy-start.4
  92.0 0.6 copy-start.17
  93.1 0.7 copy-start.45
  93.4 2.2 copy-start.43
  95.7 1.9 copy-start.41
  97.6 1.9 copy-start.39
  103.0 1.5 copy-start.31
  103.9 2.7 %copy-start.9 = (bf16[2,24,8,512]{3,2,0,1:T(8,128)(2,1)}, bf16[2,24,8,512]{3,2,0,1:T(8,128)(2,1)S(1)}, u32[]{:S(2)}) copy-start(bf16[2,24,8,512]{3,2,0,1:T(8,128)(2,1)S(1)} %copy.271) | copy-start | bytes 1179652
  103.9 2.7 %copy-start.29 = (s32[512,1]{0,1:T(1,128)S(1)}, s32[512,1]{0,1:T(1,128)}, u32[]{:S(2)}) copy-start(s32[512,1]{0,1:T(1,128)} %copy-done.28) | copy-start | bytes 6148
  103.9 12.9 %collective-permute-start.4 = (bf16[1024,192]{0,1:T(8,128)(2,1)S(1)}, bf16[1024,192]{0,1:T(8,128)(2,1)S(1)}, u32[]{:S(2)}, u32[]{:S(2)}) collective-permute-start(bf16[1024,192]{0,1:T(8,128)(2,1)S(1)} %bitcast.254), channel_id=1, source_target_pairs={{0,1},{1,0},{2,3},{3,2},{4,5},{5,4},{6,7},{7,6},{8,9},{9,8},{10,11... | collective-permute-start | bytes 1179656 | tf_op jit(solution)/shard_map/ppermute | solution.py:145
  106.6 2.0 copy-start.27
  108.6 2.0 copy-start.25
  110.6 2.0 copy-start.37
  112.7 2.1 copy-start.47
  114.8 2.0 copy-start.6
  114.8 2.0 copy-start.33
  116.8 2.2 copy-start.22
  123.0 1.4 copy-start
  127.3 20.5 %all-to-all-start.1 = ((bf16[16,32,2,192]{3,2,1,0:T(2,128)(2,1)}), bf16[16,32,2,192]{3,2,1,0:T(2,128)(2,1)}, u32[]{:S(2)}, u32[]{:S(2)}) async-start(bf16[16,32,2,192]{3,2,1,0:T(2,128)(2,1)} %reshape.184), calls=%async_computation.1 | async-start | bytes 1048576 | tf_op jit(solution)/shard_map/all_to_all | solution.py:275
  134.6 2.8 %copy-start.10 = (bf16[2,24,8,512]{3,2,0,1:T(8,128)(2,1)S(1)}, bf16[2,24,8,512]{3,2,0,1:T(8,128)(2,1)}, u32[]{:S(2)}) copy-start(bf16[2,24,8,512]{3,2,0,1:T(8,128)(2,1)} %copy-done.9) | copy-start | bytes 1179652
  134.6 2.8 %copy-start.18 = (bf16[1024,192]{1,0:T(8,128)(2,1)S(1)}, bf16[1024,192]{1,0:T(8,128)(2,1)}, u32[]{:S(2)}) copy-start(bf16[1024,192]{1,0:T(8,128)(2,1)} %copy.163) | copy-start | bytes 1179652
  140.1 1.4 slice-start
  141.5 7.9 %copy-start.35 = (s32[512]{0:T(512)S(1)}, s32[512]{0:T(512)}, u32[]{:S(2)}) copy-start(s32[512]{0:T(512)} %copy-done.34) | copy-start | bytes 6148
  142.0 8.2 %copy-start.2 = (bf16[1024,384]{1,0:T(8,128)(2,1)S(1)}, bf16[1024,384]{1,0:T(8,128)(2,1)}, u32[]{:S(2)}) copy-start(bf16[1024,384]{1,0:T(8,128)(2,1)} %copy-done.1) | copy-start | bytes 2359300
  150.2 2.1 copy-start.14
  153.4 1.3 copy-start.8
  153.4 1.3 copy-start.15
  153.4 4.0 %copy-start.12 = (f32[192,384]{1,0:T(8,128)S(1)}, f32[192,384]{1,0:T(8,128)}, u32[]{:S(2)}) copy-start(f32[192,384]{1,0:T(8,128)} %convolution_multiply_fusion.2) | copy-start | bytes 884740
  154.5 2.8 %collective-permute-start.6 = (f32[384,384]{1,0:T(8,128)S(1)}, f32[384,384]{1,0:T(8,128)S(1)}, u32[]{:S(2)}, u32[]{:S(2)}) collective-permute-start(f32[384,384]{1,0:T(8,128)S(1)} %broadcast_select_fusion.2), channel_id=1, source_target_pairs={{0,2},{2,0},{4,6},{6,4},{8,10},{10,8},{12,14},{14,12},{16,18},{18,... | collective-permute-start | bytes 1769480 | tf_op jit(solution)/shard_map/ppermute | solution.py:163
  155.9 28.6 %collective-permute-start.7 = (bf16[1024,3,192]{0,2,1:T(8,128)(2,1)}, bf16[1024,3,192]{0,2,1:T(8,128)(2,1)}, u32[]{:S(2)}, u32[]{:S(2)}) collective-permute-start(bf16[1024,3,192]{0,2,1:T(8,128)(2,1)} %pad_maximum_fusion.3), channel_id=1, source_target_pairs={{0,1},{1,0},{2,3},{3,2},{4,5},{5,4},{6,7},{7,6},{8,9},{9,8},{10,11... | collective-permute-start | bytes 3538952 | tf_op jit(solution)/shard_map/ppermute | solution.py:145
  158.3 19.9 %all-to-all-start.2 = ((f32[16,24,384]{2,1,0:T(8,128)}), f32[16,24,384]{2,1,0:T(8,128)S(1)}, u32[]{:S(2)}, u32[]{:S(2)}) async-start(f32[16,24,384]{2,1,0:T(8,128)} %bitcast.103), calls=%async_computation.2 | async-start | bytes 1179648 | tf_op jit(solution)/shard_map/all_to_all | solution.py:177
  178.2 10.1 %copy-start.5 = (bf16[1024,384]{1,0:T(8,128)(2,1)S(1)}, bf16[1024,384]{1,0:T(8,128)(2,1)}, u32[]{:S(2)}) copy-start(bf16[1024,384]{1,0:T(8,128)(2,1)} %param.9) | copy-start | bytes 2359300
  188.9 1.6 collective-permute-start.8
  206.8 29.4 %copy-start.11 = (bf16[2,24,8,512]{3,2,0,1:T(8,128)(2,1)S(1)}, bf16[2,24,8,512]{3,2,0,1:T(8,128)(2,1)}, u32[]{:S(2)}) copy-start(bf16[2,24,8,512]{3,2,0,1:T(8,128)(2,1)} %copy-done.9) | copy-start | bytes 1179652
  235.4 6.0 %collective-permute-start.9 = (f32[16,36,384]{2,0,1:T(8,128)}, f32[16,36,384]{2,0,1:T(8,128)}, u32[]{:S(2)}, u32[]{:S(2)}) collective-permute-start(f32[16,36,384]{2,0,1:T(8,128)} %copy.199), channel_id=1, source_target_pairs={{0,2},{2,0},{4,6},{6,4},{8,10},{10,8},{12,14},{14,12},{16,18},{18,... | collective-permute-start | bytes 2654216 | tf_op jit(solution)/shard_map/ppermute | solution.py:163
  236.2 3.7 %copy-start.13 = (bf16[384,384]{1,0:T(8,128)(2,1)S(1)}, bf16[384,384]{1,0:T(8,128)(2,1)}, u32[]{:S(2)}) copy-start(bf16[384,384]{1,0:T(8,128)(2,1)} %param.10) | copy-start | bytes 884740

commit v5 on v4

--- a/solution.py
+++ b/solution.py
@@ -20,7 +20,7 @@
     return (slot_rows, slot_live)
 
 
-def attention_forward(queries, extended, neighbours, row_offset):
+def attention_forward(queries, extended, neighbours, row_offset, riders):
     f32 = jnp.float32
     bf16 = jnp.bfloat16
     row_count = queries.shape[0]
@@ -66,14 +66,16 @@
         mixture = jnp.einsum("bhm,bmhd->bhd", weights, block_values, preferred_element_type=f32)
         return (mixture.reshape(block_rows, span).astype(bf16), probabilities, gathered)
 
-    outputs = [
-        forward_block((query_blocks[b], neighbour_blocks[b], block_starts[b]))
-        for b in range(block_count)
-    ]
+    outputs = []
+    for b in range(block_count):
+        out = forward_block((query_blocks[b], neighbour_blocks[b], block_starts[b]))
+        if b == 0:
+            out, riders = lax.optimization_barrier((out, riders))
+        outputs.append(out)
     attn_blocks = jnp.stack([out[0] for out in outputs])
     prob_blocks = [out[1] for out in outputs]
     kv_blocks = [out[2] for out in outputs]
-    return (attn_blocks.reshape(row_count, span), prob_blocks, kv_blocks)
+    return (attn_blocks.reshape(row_count, span), prob_blocks, kv_blocks, riders)
 
 
 def attention_backward(
@@ -243,7 +245,6 @@
     ]
     mix_own = jnp.take(mix_pieces, ch_index, axis=1)
     pooled = lax.dynamic_slice_in_dim(pooled_all, ch_index * half_width, half_width, axis=1)
-    upstream = ch_assemble(cotangent, cot_others, axis=1)
     projected = jnp.einsum(
         "rc,kcd->rkd", pooled_all, projections, preferred_element_type=f32
     ).astype(bf16)
@@ -258,10 +259,12 @@
     extended = jnp.concatenate(
         [key_value, incoming.reshape(peer_count * slot_count, 2, half_width)], axis=0
     )
-    attended, prob_blocks, kv_blocks = attention_forward(queries, extended, neighbours, 0)
+    attended, prob_blocks, kv_blocks, (cot_others, proj_others) = attention_forward(
+        queries, extended, neighbours, 0, (cot_others, proj_others)
+    )
+    upstream = ch_assemble(cotangent, cot_others, axis=1)
     attended_others = ch_exchange(attended)
     grad_attended = jnp.dot(upstream, mixing_weight.T, preferred_element_type=f32).astype(bf16)
-    grad_attended, proj_others = lax.optimization_barrier((grad_attended, proj_others))
     mixing_term = jnp.dot(attended.T, upstream, preferred_element_type=f32) * grad_scale
     carried, query_grads, (attended_others, mix_others) = attention_backward(
         queries, extended.shape[0], neighbours, 0, grad_attended, prob_blocks, kv_blocks,
@@ -289,7 +292,12 @@
         * grad_scale
     )
     early_reduced = pix_scatter((projection_term, mixing_term), mixing_weight.shape[1])
-    early_reduced, grad_others = lax.optimization_barrier((early_reduced, grad_others))
+    projection_gradient, mixing_gradient = pix_gather(
+        (early_reduced,), ((projection_term, mixing_term),)
+    )
+    projection_gradient, mixing_gradient, grad_others = lax.optimization_barrier(
+        (projection_gradient, mixing_gradient, grad_others)
+    )
     pooled_sum = upstream.astype(f32) + jnp.einsum(
         "rkd,kcd->rc", grad_projected, projections, preferred_element_type=f32
     )
@@ -301,9 +309,7 @@
     kernel_term = jnp.dot(fine_pixels.T, grad_pooled, preferred_element_type=f32) * grad_scale
     fine_gradient = jnp.dot(grad_pooled, pool_kernel.T, preferred_element_type=f32).astype(bf16)
     kernel_reduced = pix_scatter((kernel_term,), mixing_weight.shape[1])
-    projection_gradient, mixing_gradient, kernel_gradient = pix_gather(
-        (early_reduced, kernel_reduced), ((projection_term, mixing_term), (kernel_term,))
-    )
+    (kernel_gradient,) = pix_gather((kernel_reduced,), ((kernel_term,),))
     return (section_output, fine_gradient, kernel_gradient, projection_gradient, mixing_gradient)
 
 

time: 252 us -> 270 us (1.071)
  waiting for transfers between devices: 52 us -> 69.5 us
  local copies, waits for them, and re-layouts: 24.2 us -> 30.7 us
  blocking collectives: 43.5 us -> 39.3 us
  other arithmetic: 19.3 us -> 15.4 us
  starting transfers between devices: 26.4 us -> 29.5 us
    all_to_all x1 -> x0, blocking collectives: 27.4 us -> none  [pix_gather(): lax.all_to_all(spread.reshape(size, total, width), 'pix', 0, 0, tiled=True)]
    all_to_all x1 -> x2, blocking collectives: 16.1 us -> 39.3 us  [pix_scatter(): lax.all_to_all(mine.reshape(size, chunk, width), 'pix', 0, 0, tiled=True)]
    all_to_all x1 -> x2, waiting for transfers between devices: 12.4 us -> 23.7 us  [pix_gather(): lax.all_to_all(spread.reshape(size, total, width), 'pix', 0, 0, tiled=True)]
    all_to_all x1, waiting for transfers between devices: 0.01 us -> 6.48 us  [per_device(): lax.all_to_all(outgoing, 'pix', split_axis=0, concat_axis=0, tiled=True)]
    all_to_all x1 -> x2, starting transfers between devices: 4.29 us -> 7.79 us  [pix_gather(): lax.all_to_all(spread.reshape(size, total, width), 'pix', 0, 0, tiled=True)]
    unnamed x118 -> x106, local copies, waits for them, and re-layouts: 7.27 us -> 6.84 us
  transfers between devices with their start and end apart: 13 -> 15, of which waited for: 7 -> 9; matrix products, arithmetic and copies ran while one was open for 36% -> 34% of each run, Pallas kernels for 0% -> 0%
where the time goes in v5:
time: 270 us; the launch traced here: 265 us
  matrix products  78.3 us (29%)
  waiting for transfers between devices  69.5 us (26%)
  blocking collectives  39.3 us (15%)
  local copies, waits for them, and re-layouts  30.7 us (11%)
  starting transfers between devices  29.5 us (11%)
  other arithmetic  15.4 us (6%)
    all_to_all x2, blocking collectives, pix_scatter(): lax.all_to_all(mine.reshape(size, chunk, width), 'pix', 0, 0, tiled=True)  39.3 us
    dot_general x18, matrix products, backward_block(): jnp.einsum('bx,bc->xc', pick_table(slot_rows[:, slot], ext_rows), contrib...  37.3 us
    ppermute x6, waiting for transfers between devices, ch_exchange(): lax.ppermute(value, 'ch', [(i, (i + shift) % size) for i in range(size)])  31.9 us
    all_to_all x2, waiting for transfers between devices, pix_gather(): lax.all_to_all(spread.reshape(size, total, width), 'pix', 0, 0, tiled=True)  23.7 us
    dot_general x18, matrix products, forward_block(): jnp.dot(pick_table(slot_rows[:, slot], ext_rows), flattened, preferred_el...  17.7 us
    all_to_all x2, starting transfers between devices, pix_gather(): lax.all_to_all(spread.reshape(size, total, width), 'pix', 0, 0, tiled=True)  7.79 us
    ppermute x6, starting transfers between devices, ch_exchange(): lax.ppermute(value, 'ch', [(i, (i + shift) % size) for i in range(size)])  7.23 us
    unnamed x106, local copies, waits for them, and re-layouts  6.84 us
  transfers between devices with their start and end apart: 15, of which 9 were waited for; matrix products, arithmetic and copies ran while one was open for 34% of the time, Pallas kernels for 0%

profile of v5, /device:TPU:0, one launch (start us, length us, event | category | flops | bytes accessed | tf_op | source)
XLA Modules:
  0.0 265.4 jit_solution(15343463725021713811)
XLA Ops:
  0.6 3.0 %collective-permute-start = (bf16[1024,384]{1,0:T(8,128)(2,1)}, bf16[1024,384]{1,0:T(8,128)(2,1)S(1)}, u32[]{:S(2)}, u32[]{:S(2)}) collective-permute-start(bf16[1024,384]{1,0:T(8,128)(2,1)} %param.9), channel_id=1, source_target_pairs={{0,1},{1,0},{2,3},{3,2},{4,5},{5,4},{6,7},{7,6},{8,9},{9,8},{10,11... | collective-permute-start | bytes 2359304 | tf_op jit(solution)/shard_map/ppermute | solution.py:147
  3.7 1.1 reshape.175
  4.8 1.2 broadcast_select_fusion
  8.2 1.8 fusion.140
  10.0 17.7 %collective-permute-done.1 = bf16[384,384]{1,0:T(8,128)(2,1)S(1)} collective-permute-done((bf16[384,384]{1,0:T(8,128)(2,1)}, bf16[384,384]{1,0:T(8,128)(2,1)S(1)}, u32[]{:S(2)}, u32[]{:S(2)}) %collective-permute-start.1) | collective-permute-done | bytes 294944 | tf_op jit(solution)/shard_map/ppermute | solution.py:147
  31.1 1.1 reshape.176
  32.1 6.4 %all-to-all-start = ((bf16[16,32,2,192]{3,2,1,0:T(2,128)(2,1)}), bf16[16,32,2,192]{3,2,1,0:T(2,128)(2,1)S(1)}, u32[]{:S(2)}, u32[]{:S(2)}) async-start(bf16[16,32,2,192]{3,2,1,0:T(2,128)(2,1)} %reshape.176), calls=%async_computation | async-start | bytes 1048576 | tf_op jit(solution)/shard_map/all_to_all | solution.py:258
  39.1 1.0 copy.79
  41.7 1.0 copy.77
  42.7 1.5 collective-permute-start.2
  44.8 1.6 collective-permute-start.5
  46.3 6.5 %all-to-all-done = bf16[16,32,2,192]{3,2,1,0:T(2,128)(2,1)S(1)} async-done(((bf16[16,32,2,192]{3,2,1,0:T(2,128)(2,1)}), bf16[16,32,2,192]{3,2,1,0:T(2,128)(2,1)S(1)}, u32[]{:S(2)}, u32[]{:S(2)}) %all-to-all-start) | async-done | bytes 393248 | tf_op jit(solution)/shard_map/all_to_all | solution.py:258
  63.8 3.4 %collective-permute-done.3 = bf16[3,384,192]{1,2,0:T(8,128)(2,1)} collective-permute-done((bf16[3,384,192]{1,2,0:T(8,128)(2,1)}, bf16[3,384,192]{1,2,0:T(8,128)(2,1)}, u32[]{:S(2)}, u32[]{:S(2)}) %collective-permute-start.3) | collective-permute-done | bytes 442400 | tf_op jit(solution)/shard_map/ppermute | solution.py:147
  67.2 2.0 convolution_convert_fusion.1
  71.2 1.2 fusion.111
  81.5 1.9 fusion.12
  83.4 1.9 fusion.14
  85.3 2.3 fusion.8
  87.7 1.9 fusion.16
  92.2 1.9 fusion.30
  94.1 1.9 fusion.32
  96.0 1.9 fusion.26
  98.0 2.1 fusion.22
  100.0 1.9 fusion.18
  102.4 1.6 collective-permute-start.4
  104.0 2.0 fusion.37
  106.1 2.0 fusion.39
  108.0 2.0 fusion.41
  110.0 2.0 fusion.43
  112.1 2.1 fusion.4
  114.2 1.9 fusion
  116.1 2.3 fusion.45
  118.4 2.0 fusion.47
  120.4 3.4 %fusion.49 = f32[1536,384]{1,0:T(8,128)} fusion(f32[1536,384]{1,0:T(8,128)S(1)} %fusion, f32[1536,384]{1,0:T(8,128)S(1)} %fusion.47, s32[512]{0:T(512)S(1)} %bitcast.310, bf16[512,9,384]{0,2,1:T(8,128)(2,1)S(1)} %bitcast.251), kind=kOutput, calls=%fused_computation.81 | convolution fusion | flops 605945856 | bytes 7473152 | tf_op jit(solution)/shard_map/bx,bc->xc/dot_general | solution.py:121
  123.8 1.9 slice.336
  125.7 2.1 reshape.178
  127.8 6.3 %all-to-all-start.1 = ((bf16[16,32,2,192]{3,2,1,0:T(2,128)(2,1)}), bf16[16,32,2,192]{3,2,1,0:T(2,128)(2,1)}, u32[]{:S(2)}, u32[]{:S(2)}) async-start(bf16[16,32,2,192]{3,2,1,0:T(2,128)(2,1)} %reshape.178), calls=%async_computation.1 | async-start | bytes 1048576 | tf_op jit(solution)/shard_map/all_to_all | solution.py:278
  134.1 1.2 multiply_reduce_fusion.2
  135.4 1.3 multiply_reduce_fusion
  137.2 1.0 reshape_reshape.4
  138.2 1.9 convolution_multiply_fusion.2
  140.1 2.7 %slice.335 = f32[1024,384]{1,0:T(8,128)} slice(f32[1536,384]{1,0:T(8,128)} %fusion.49), slice={[0:1024], [0:384]} | slice | bytes 3145728 | tf_op jit(solution)/shard_map/slice | solution.py:285
  142.8 1.9 copy.111
  144.7 3.9 %all-to-all-done.1 = bf16[16,32,2,192]{3,2,1,0:T(2,128)(2,1)} async-done(((bf16[16,32,2,192]{3,2,1,0:T(2,128)(2,1)}), bf16[16,32,2,192]{3,2,1,0:T(2,128)(2,1)}, u32[]{:S(2)}, u32[]{:S(2)}) %all-to-all-start.1) | async-done | bytes 393248 | tf_op jit(solution)/shard_map/all_to_all | solution.py:278
  148.6 1.4 convert_element_type.207
  151.8 1.8 fusion.98
  155.1 1.3 copy.113
  156.7 2.0 collective-permute-done.6
  158.8 21.3 %all_to_all.30 = f32[16,24,384]{2,1,0:T(8,128)S(1)} all-to-all(f32[16,24,384]{2,1,0:T(8,128)S(1)} %bitcast.255), channel_id=1, replica_groups=mesh['pix'=16,'ch'=2] {'pix'}, dimensions={0} | all-to-all | bytes 1179648 | tf_op jit(solution)/shard_map/all_to_all | solution.py:179
  181.0 3.6 %all-to-all-start.3 = ((f32[16,24,384]{2,1,0:T(8,128)}), f32[16,24,384]{2,1,0:T(8,128)S(1)}, u32[]{:S(2)}, u32[]{:S(2)}) async-start(f32[16,24,384]{2,1,0:T(8,128)} %bitcast.108), calls=%async_computation.3 | async-start | bytes 1179648 | tf_op jit(solution)/shard_map/all_to_all | solution.py:190
  184.6 1.1 pad_maximum_fusion.3
  186.3 13.8 %all-to-all-done.3 = f32[16,24,384]{2,1,0:T(8,128)S(1)} async-done(((f32[16,24,384]{2,1,0:T(8,128)}), f32[16,24,384]{2,1,0:T(8,128)S(1)}, u32[]{:S(2)}, u32[]{:S(2)}) %all-to-all-start.3) | async-done | bytes 589856 | tf_op jit(solution)/shard_map/all_to_all | solution.py:190
  200.2 2.1 fusion.130
  203.5 10.8 %collective-permute-done.8 = bf16[1024,3,192]{0,2,1:T(8,128)(2,1)} collective-permute-done((bf16[1024,3,192]{0,2,1:T(8,128)(2,1)}, bf16[1024,3,192]{0,2,1:T(8,128)(2,1)}, u32[]{:S(2)}, u32[]{:S(2)}) %collective-permute-start.8) | collective-permute-done | bytes 1179680 | tf_op jit(solution)/shard_map/ppermute | solution.py:147
  214.3 3.5 %fusion.58 = bf16[1024,384]{1,0:T(8,128)(2,1)S(1)} fusion(f32[1024,384,1]{1,0,2:T(8,128)} %fusion.130, bf16[1024,3,192]{0,2,1:T(8,128)(2,1)} %collective-permute-done.8, bf16[3,384,192]{1,2,0:T(8,128)(2,1)} %collective-permute-done.3, bf16[1024,192]{1,0:T(8,128)(2,1)} %collective-permute-done.2, bf16[1024,192]{1,0:T(8,128)(2,1)S(1)} %copy-done.15, pred[]{:T(512)S(6)} %eq.244), kind=kOutput, calls=%fused_computation.91 | convolution fusion | flops 458096640 | bytes 4767745 | tf_op jit(solution)/shard_map/rkd,kcd->rc/dot_general | solution.py:305
  218.5 1.6 collective-permute-done.9
  220.9 18.0 %all_to_all.31 = f32[16,12,384]{2,1,0:T(8,128)S(1)} all-to-all(f32[16,12,384]{2,1,0:T(8,128)} %reshape.186), channel_id=1, replica_groups=mesh['pix'=16,'ch'=2] {'pix'}, dimensions={0} | all-to-all | bytes 589824 | tf_op jit(solution)/shard_map/all_to_all | solution.py:179
  239.8 4.2 %all-to-all-start.5 = ((f32[16,12,384]{2,1,0:T(8,128)}), f32[16,12,384]{2,1,0:T(8,128)}, u32[]{:S(2)}, u32[]{:S(2)}) async-start(f32[16,12,384]{2,1,0:T(8,128)} %bitcast.115), calls=%async_computation.5 | async-start | bytes 786432 | tf_op jit(solution)/shard_map/all_to_all | solution.py:190
  244.0 2.3 fusion.123
  246.3 9.9 %all-to-all-done.5 = f32[16,12,384]{2,1,0:T(8,128)} async-done(((f32[16,12,384]{2,1,0:T(8,128)}), f32[16,12,384]{2,1,0:T(8,128)}, u32[]{:S(2)}, u32[]{:S(2)}) %all-to-all-start.5) | async-done | bytes 294944 | tf_op jit(solution)/shard_map/all_to_all | solution.py:190
  256.3 1.8 fusion.99
  259.1 1.3 copy.116
  260.3 2.5 convolution_convert_fusion
  262.8 1.2 broadcast_select_fusion.6
  (211 shorter events, 43.9 us)
Async XLA Ops:
  0.6 27.1 %collective-permute-start = (bf16[1024,384]{1,0:T(8,128)(2,1)}, bf16[1024,384]{1,0:T(8,128)(2,1)S(1)}, u32[]{:S(2)}, u32[]{:S(2)}) collective-permute-start(bf16[1024,384]{1,0:T(8,128)(2,1)} %param.9), channel_id=1, source_target_pairs={{0,1},{1,0},{2,3},{3,2},{4,5},{5,4},{6,7},{7,6},{8,9},{9,8},{10,11... | collective-permute-start | bytes 2359304 | tf_op jit(solution)/shard_map/ppermute | solution.py:147
  3.6 24.1 %collective-permute-start.1 = (bf16[384,384]{1,0:T(8,128)(2,1)}, bf16[384,384]{1,0:T(8,128)(2,1)S(1)}, u32[]{:S(2)}, u32[]{:S(2)}) collective-permute-start(bf16[384,384]{1,0:T(8,128)(2,1)} %param.10), channel_id=1, source_target_pairs={{0,1},{1,0},{2,3},{3,2},{4,5},{5,4},{6,7},{7,6},{8,9},{9,8},{10,11... | collective-permute-start | bytes 884744 | tf_op jit(solution)/shard_map/ppermute | solution.py:147
  8.2 22.1 %copy-start.27 = (s32[512]{0:T(512)}, s32[512]{0:T(512)S(1)}, u32[]{:S(2)}) copy-start(s32[512]{0:T(512)S(1)} %eq.173) | copy-start | bytes 6148
  10.0 19.2 %copy-start.16 = (bf16[3,384,192]{1,2,0:T(8,128)(2,1)S(1)}, bf16[3,384,192]{1,2,0:T(8,128)(2,1)}, u32[]{:S(2)}) copy-start(bf16[3,384,192]{1,2,0:T(8,128)(2,1)} %param.11) | copy-start | bytes 1327108
  28.3 0.9 copy-start
  30.3 8.8 %copy-start.5 = (bf16[1024,192]{0,1:T(8,128)(2,1)S(1)}, bf16[1024,192]{0,1:T(8,128)(2,1)}, u32[]{:S(2)}) copy-start(bf16[1024,192]{0,1:T(8,128)(2,1)} %param.15) | copy-start | bytes 1179652
  32.1 20.7 %all-to-all-start = ((bf16[16,32,2,192]{3,2,1,0:T(2,128)(2,1)}), bf16[16,32,2,192]{3,2,1,0:T(2,128)(2,1)S(1)}, u32[]{:S(2)}, u32[]{:S(2)}) async-start(bf16[16,32,2,192]{3,2,1,0:T(2,128)(2,1)} %reshape.176), calls=%async_computation | async-start | bytes 1048576 | tf_op jit(solution)/shard_map/all_to_all | solution.py:258
  40.8 13.5 %copy-start.23 = (s32[512]{0:T(512)}, s32[512]{0:T(512)S(1)}, u32[]{:S(2)}) copy-start(s32[512]{0:T(512)S(1)} %iota_add_fusion.1) | copy-start | bytes 6148
  41.5 12.8 %copy-start.39 = (s32[512,1]{0,1:T(1,128)}, s32[512,1]{0,1:T(1,128)S(1)}, u32[]{:S(2)}) copy-start(s32[512,1]{0,1:T(1,128)S(1)} %get-tuple-element.100) | copy-start | bytes 6148
  41.5 13.8 %copy-start.41 = (s32[512,1]{0,1:T(1,128)}, s32[512,1]{0,1:T(1,128)S(1)}, u32[]{:S(2)}) copy-start(s32[512,1]{0,1:T(1,128)S(1)} %get-tuple-element.99) | copy-start | bytes 6148
  41.5 14.8 %copy-start.21 = (s32[512,1]{0,1:T(1,128)}, s32[512,1]{0,1:T(1,128)S(1)}, u32[]{:S(2)}) copy-start(s32[512,1]{0,1:T(1,128)S(1)} %get-tuple-element.98) | copy-start | bytes 6148
  41.5 15.8 %copy-start.37 = (s32[512,1]{0,1:T(1,128)}, s32[512,1]{0,1:T(1,128)S(1)}, u32[]{:S(2)}) copy-start(s32[512,1]{0,1:T(1,128)S(1)} %get-tuple-element.97) | copy-start | bytes 6148
  41.5 17.7 %copy-start.35 = (s32[512,1]{0,1:T(1,128)}, s32[512,1]{0,1:T(1,128)S(1)}, u32[]{:S(2)}) copy-start(s32[512,1]{0,1:T(1,128)S(1)} %get-tuple-element.95) | copy-start | bytes 6148
  41.5 19.7 %copy-start.33 = (s32[512,1]{0,1:T(1,128)}, s32[512,1]{0,1:T(1,128)S(1)}, u32[]{:S(2)}) copy-start(s32[512,1]{0,1:T(1,128)S(1)} %get-tuple-element.93) | copy-start | bytes 6148
  41.6 30.8 %copy-start.25 = (s32[512,1]{0,1:T(1,128)}, s32[512,1]{0,1:T(1,128)S(1)}, u32[]{:S(2)}) copy-start(s32[512,1]{0,1:T(1,128)S(1)} %get-tuple-element.113) | copy-start | bytes 6148
  41.6 33.8 %copy-start.31 = (s32[512,1]{0,1:T(1,128)}, s32[512,1]{0,1:T(1,128)S(1)}, u32[]{:S(2)}) copy-start(s32[512,1]{0,1:T(1,128)S(1)} %get-tuple-element.116) | copy-start | bytes 6148
  41.6 35.8 %copy-start.29 = (s32[512,1]{0,1:T(1,128)}, s32[512,1]{0,1:T(1,128)S(1)}, u32[]{:S(2)}) copy-start(s32[512,1]{0,1:T(1,128)S(1)} %get-tuple-element.118) | copy-start | bytes 6148
  41.7 21.1 %copy-start.2 = (f32[512,3,64]{0,2,1:T(8,128)}, f32[512,3,64]{0,2,1:T(8,128)S(1)}, u32[]{:S(2)}) copy-start(f32[512,3,64]{0,2,1:T(8,128)S(1)} %convert.64) | copy-start | bytes 1179652
  42.7 21.1 %collective-permute-start.2 = (bf16[1024,192]{1,0:T(8,128)(2,1)}, bf16[1024,192]{1,0:T(8,128)(2,1)}, u32[]{:S(2)}, u32[]{:S(2)}) collective-permute-start(bf16[1024,192]{1,0:T(8,128)(2,1)} %copy.77), channel_id=1, source_target_pairs={{0,1},{1,0},{2,3},{3,2},{4,5},{5,4},{6,7},{7,6},{8,9},{9,8},{10,11... | collective-permute-start | bytes 1179656 | tf_op jit(solution)/shard_map/ppermute | solution.py:147
  44.2 23.0 %collective-permute-start.3 = (bf16[3,384,192]{1,2,0:T(8,128)(2,1)}, bf16[3,384,192]{1,2,0:T(8,128)(2,1)}, u32[]{:S(2)}, u32[]{:S(2)}) collective-permute-start(bf16[3,384,192]{1,2,0:T(8,128)(2,1)} %param.11), channel_id=1, source_target_pairs={{0,1},{1,0},{2,3},{3,2},{4,5},{5,4},{6,7},{7,6},{8,9},{9,8},{10,11... | collective-permute-start | bytes 1327112 | tf_op jit(solution)/shard_map/ppermute | solution.py:147
  44.8 71.3 %collective-permute-start.5 = (bf16[192,192]{1,0:T(8,128)(2,1)}, bf16[192,192]{1,0:T(8,128)(2,1)}, u32[]{:S(2)}, u32[]{:S(2)}) collective-permute-start(bf16[192,192]{1,0:T(8,128)(2,1)} %bitcast.224), channel_id=1, source_target_pairs={{0,1},{1,0},{2,3},{3,2},{4,5},{5,4},{6,7},{7,6},{8,9},{9,8},{10,11... | collective-permute-start | bytes 221192 | tf_op jit(solution)/shard_map/ppermute | solution.py:243
  62.8 4.5 %copy-start.13 = (bf16[1024,192]{1,0:T(8,128)(2,1)S(1)}, bf16[1024,192]{1,0:T(8,128)(2,1)}, u32[]{:S(2)}) copy-start(bf16[1024,192]{1,0:T(8,128)(2,1)} %copy.79) | copy-start | bytes 1179652
  62.8 4.5 %copy-start.20 = (bf16[192,384]{1,0:T(8,128)(2,1)S(1)}, bf16[192,384]{1,0:T(8,128)(2,1)}, u32[]{:S(2)}) copy-start(bf16[192,384]{1,0:T(8,128)(2,1)} %param.12) | copy-start | bytes 442372
  80.0 0.6 copy-start.12
  89.9 1.0 copy-start.3
  90.9 0.6 copy-start.11
  91.5 0.7 copy-start.42
  91.8 2.3 copy-start.40
  94.1 1.9 copy-start.38
  96.0 1.9 copy-start.36
  97.9 2.1 copy-start.34
  102.0 2.0 copy-start.24
  102.4 3.6 %copy-start.7 = (bf16[2,24,8,512]{3,2,0,1:T(8,128)(2,1)}, bf16[2,24,8,512]{3,2,0,1:T(8,128)(2,1)S(1)}, u32[]{:S(2)}) copy-start(bf16[2,24,8,512]{3,2,0,1:T(8,128)(2,1)S(1)} %copy.184) | copy-start | bytes 1179652
  102.4 3.6 %copy-start.22 = (s32[512,1]{0,1:T(1,128)S(1)}, s32[512,1]{0,1:T(1,128)}, u32[]{:S(2)}) copy-start(s32[512,1]{0,1:T(1,128)} %copy-done.21) | copy-start | bytes 6148
  102.4 13.7 %collective-permute-start.4 = (bf16[1024,192]{0,1:T(8,128)(2,1)S(1)}, bf16[1024,192]{0,1:T(8,128)(2,1)S(1)}, u32[]{:S(2)}, u32[]{:S(2)}) collective-permute-start(bf16[1024,192]{0,1:T(8,128)(2,1)S(1)} %bitcast.258), channel_id=1, source_target_pairs={{0,1},{1,0},{2,3},{3,2},{4,5},{5,4},{6,7},{7,6},{8,9},{9,8},{10,11... | collective-permute-start | bytes 1179656 | tf_op jit(solution)/shard_map/ppermute | solution.py:147
  110.0 2.0 copy-start.32
  112.1 2.1 copy-start.30
  114.2 1.9 copy-start.26
  116.1 2.3 copy-start.19
  127.8 20.8 %all-to-all-start.1 = ((bf16[16,32,2,192]{3,2,1,0:T(2,128)(2,1)}), bf16[16,32,2,192]{3,2,1,0:T(2,128)(2,1)}, u32[]{:S(2)}, u32[]{:S(2)}) async-start(bf16[16,32,2,192]{3,2,1,0:T(2,128)(2,1)} %reshape.178), calls=%async_computation.1 | async-start | bytes 1048576 | tf_op jit(solution)/shard_map/all_to_all | solution.py:278
  135.3 2.8 %copy-start.8 = (bf16[2,24,8,512]{3,2,0,1:T(8,128)(2,1)S(1)}, bf16[2,24,8,512]{3,2,0,1:T(8,128)(2,1)}, u32[]{:S(2)}) copy-start(bf16[2,24,8,512]{3,2,0,1:T(8,128)(2,1)} %copy-done.7) | copy-start | bytes 1179652
  135.4 2.8 %copy-start.14 = (bf16[1024,192]{1,0:T(8,128)(2,1)S(1)}, bf16[1024,192]{1,0:T(8,128)(2,1)}, u32[]{:S(2)}) copy-start(bf16[1024,192]{1,0:T(8,128)(2,1)} %copy.79) | copy-start | bytes 1179652
  142.8 7.4 %copy-start.28 = (s32[512]{0:T(512)S(1)}, s32[512]{0:T(512)}, u32[]{:S(2)}) copy-start(s32[512]{0:T(512)} %copy-done.27) | copy-start | bytes 6148
  144.7 7.1 %copy-start.1 = (bf16[1024,384]{1,0:T(8,128)(2,1)S(1)}, bf16[1024,384]{1,0:T(8,128)(2,1)}, u32[]{:S(2)}) copy-start(bf16[1024,384]{1,0:T(8,128)(2,1)} %copy-done) | copy-start | bytes 2359300
  150.9 0.9 copy-start.9
  156.6 2.1 collective-permute-start.6
  158.8 25.8 %copy-start.6 = (bf16[1024,1,192]{0,2,1:T(8,128)(2,1)S(1)}, bf16[1024,1,192]{0,2,1:T(8,128)(2,1)}, u32[]{:S(2)}) copy-start(bf16[1024,1,192]{0,2,1:T(8,128)(2,1)} %reshape_reshape.4) | copy-start | bytes 1179652
  158.8 25.8 %copy-start.10 = (bf16[1024,2,192]{0,2,1:T(8,128)(2,1)S(1)}, bf16[1024,2,192]{0,2,1:T(8,128)(2,1)}, u32[]{:S(2)}) copy-start(bf16[1024,2,192]{0,2,1:T(8,128)(2,1)} %copy-done.9) | copy-start | bytes 2359300
  180.1 20.0 %copy-start.17 = (bf16[3,384,192]{1,2,0:T(8,128)(2,1)S(1)}, bf16[3,384,192]{1,2,0:T(8,128)(2,1)}, u32[]{:S(2)}) copy-start(bf16[3,384,192]{1,2,0:T(8,128)(2,1)} %param.11) | copy-start | bytes 1327108
  181.0 19.1 %all-to-all-start.3 = ((f32[16,24,384]{2,1,0:T(8,128)}), f32[16,24,384]{2,1,0:T(8,128)S(1)}, u32[]{:S(2)}, u32[]{:S(2)}) async-start(f32[16,24,384]{2,1,0:T(8,128)} %bitcast.108), calls=%async_computation.3 | async-start | bytes 1179648 | tf_op jit(solution)/shard_map/all_to_all | solution.py:190
  185.8 28.5 %collective-permute-start.8 = (bf16[1024,3,192]{0,2,1:T(8,128)(2,1)}, bf16[1024,3,192]{0,2,1:T(8,128)(2,1)}, u32[]{:S(2)}, u32[]{:S(2)}) collective-permute-start(bf16[1024,3,192]{0,2,1:T(8,128)(2,1)} %pad_maximum_fusion.3), channel_id=1, source_target_pairs={{0,1},{1,0},{2,3},{3,2},{4,5},{5,4},{6,7},{7,6},{8,9},{9,8},{10,11... | collective-permute-start | bytes 3538952 | tf_op jit(solution)/shard_map/ppermute | solution.py:147
  200.1 2.2 collective-permute-start.7
  202.4 11.9 %copy-start.15 = (bf16[1024,192]{1,0:T(8,128)(2,1)S(1)}, bf16[1024,192]{1,0:T(8,128)(2,1)}, u32[]{:S(2)}) copy-start(bf16[1024,192]{1,0:T(8,128)(2,1)} %copy.79) | copy-start | bytes 1179652
  214.3 3.5 %copy-start.4 = (bf16[1024,384]{1,0:T(8,128)(2,1)S(1)}, bf16[1024,384]{1,0:T(8,128)(2,1)}, u32[]{:S(2)}) copy-start(bf16[1024,384]{1,0:T(8,128)(2,1)} %param.9) | copy-start | bytes 2359300
  218.4 25.5 %copy-start.18 = (bf16[192,1,192]{2,1,0:T(2,128)(2,1)S(1)}, bf16[192,1,192]{2,1,0:T(2,128)(2,1)}, u32[]{:S(2)}) copy-start(bf16[192,1,192]{2,1,0:T(2,128)(2,1)} %get-tuple-element.88) | copy-start | bytes 221188
  218.4 1.6 collective-permute-start.9
  239.8 16.4 %all-to-all-start.5 = ((f32[16,12,384]{2,1,0:T(8,128)}), f32[16,12,384]{2,1,0:T(8,128)}, u32[]{:S(2)}, u32[]{:S(2)}) async-start(f32[16,12,384]{2,1,0:T(8,128)} %bitcast.115), calls=%async_computation.5 | async-start | bytes 786432 | tf_op jit(solution)/shard_map/all_to_all | solution.py:190
  256.2 6.7 %collective-permute-start.10 = (f32[16,12,384]{2,1,0:T(8,128)}, f32[16,12,384]{2,1,0:T(8,128)}, u32[]{:S(2)}, u32[]{:S(2)}) collective-permute-start(f32[16,12,384]{2,1,0:T(8,128)} %all-to-all-done.5), channel_id=1, source_target_pairs={{0,2},{2,0},{4,6},{6,4},{8,10},{10,8},{12,14},{14,12},{16,18},{18,... | collective-permute-start | bytes 884744 | tf_op jit(solution)/shard_map/ppermute | solution.py:165

commit v6 on v5

--- a/solution.py
+++ b/solution.py
@@ -292,12 +292,7 @@
         * grad_scale
     )
     early_reduced = pix_scatter((projection_term, mixing_term), mixing_weight.shape[1])
-    projection_gradient, mixing_gradient = pix_gather(
-        (early_reduced,), ((projection_term, mixing_term),)
-    )
-    projection_gradient, mixing_gradient, grad_others = lax.optimization_barrier(
-        (projection_gradient, mixing_gradient, grad_others)
-    )
+    early_reduced, grad_others = lax.optimization_barrier((early_reduced, grad_others))
     pooled_sum = upstream.astype(f32) + jnp.einsum(
         "rkd,kcd->rc", grad_projected, projections, preferred_element_type=f32
     )
@@ -309,7 +304,9 @@
     kernel_term = jnp.dot(fine_pixels.T, grad_pooled, preferred_element_type=f32) * grad_scale
     fine_gradient = jnp.dot(grad_pooled, pool_kernel.T, preferred_element_type=f32).astype(bf16)
     kernel_reduced = pix_scatter((kernel_term,), mixing_weight.shape[1])
-    (kernel_gradient,) = pix_gather((kernel_reduced,), ((kernel_term,),))
+    projection_gradient, mixing_gradient, kernel_gradient = pix_gather(
+        (early_reduced, kernel_reduced), ((projection_term, mixing_term), (kernel_term,))
+    )
     return (section_output, fine_gradient, kernel_gradient, projection_gradient, mixing_gradient)
 
 

time: 270 us -> 254 us (0.941)
  waiting for transfers between devices: 69.5 us -> 52 us
  blocking collectives: 39.3 us -> 43.6 us
  starting transfers between devices: 29.5 us -> 26.5 us
    all_to_all x0 -> x1, blocking collectives: none -> 27.4 us  [pix_gather(): lax.all_to_all(spread.reshape(size, total, width), 'pix', 0, 0, tiled=True)]
    all_to_all x2 -> x1, blocking collectives: 39.3 us -> 16.1 us  [pix_scatter(): lax.all_to_all(mine.reshape(size, chunk, width), 'pix', 0, 0, tiled=True)]
    all_to_all x2 -> x1, waiting for transfers between devices: 23.7 us -> 12.1 us  [pix_scatter(): lax.all_to_all(mine.reshape(size, chunk, width), 'pix', 0, 0, tiled=True)]
    all_to_all x2 -> x1, starting transfers between devices: 7.79 us -> 4.1 us  [pix_scatter(): lax.all_to_all(mine.reshape(size, chunk, width), 'pix', 0, 0, tiled=True)]
    ppermute x6, waiting for transfers between devices: 31.9 us -> 28.3 us  [ch_exchange(): lax.ppermute(value, 'ch', [(i, (i + shift) % size) for i in range(size)])]
    unnamed x106 -> x108, local copies, waits for them, and re-layouts: 6.84 us -> 6.87 us
  transfers between devices with their start and end apart: 15 -> 13, of which waited for: 9 -> 8; matrix products, arithmetic and copies ran while one was open for 34% -> 36% of each run, Pallas kernels for 0% -> 0%
where the time goes in v6:
time: 254 us; the launch traced here: 250 us
  matrix products  78 us (31%)
  waiting for transfers between devices  52 us (20%)
  blocking collectives  43.6 us (17%)
  local copies, waits for them, and re-layouts  29.7 us (12%)
  starting transfers between devices  26.5 us (10%)
  other arithmetic  17.5 us (7%)
  between operations  2.66 us (1%)
    dot_general x18, matrix products, backward_block(): jnp.einsum('bx,bc->xc', pick_table(slot_rows[:, slot], ext_rows), contrib...  37.3 us
    ppermute x6, waiting for transfers between devices, ch_exchange(): lax.ppermute(value, 'ch', [(i, (i + shift) % size) for i in range(size)])  28.3 us
    all_to_all x1, blocking collectives, pix_gather(): lax.all_to_all(spread.reshape(size, total, width), 'pix', 0, 0, tiled=True)  27.4 us
    dot_general x18, matrix products, forward_block(): jnp.dot(pick_table(slot_rows[:, slot], ext_rows), flattened, preferred_el...  17.8 us
    all_to_all x1, blocking collectives, pix_scatter(): lax.all_to_all(mine.reshape(size, chunk, width), 'pix', 0, 0, tiled=True)  16.1 us
    all_to_all x1, waiting for transfers between devices, pix_scatter(): lax.all_to_all(mine.reshape(size, chunk, width), 'pix', 0, 0, tiled=True)  12.1 us
    ppermute x6, starting transfers between devices, ch_exchange(): lax.ppermute(value, 'ch', [(i, (i + shift) % size) for i in range(size)])  7.22 us
    unnamed x108, local copies, waits for them, and re-layouts  6.87 us
  transfers between devices with their start and end apart: 13, of which 8 were waited for; matrix products, arithmetic and copies ran while one was open for 36% of the time, Pallas kernels for 0%

profile of v6, /device:TPU:0, one launch (start us, length us, event | category | flops | bytes accessed | tf_op | source)
XLA Modules:
  0.0 249.7 jit_solution(17212079742729962591)
XLA Ops:
  0.6 3.0 %collective-permute-start = (bf16[1024,384]{1,0:T(8,128)(2,1)}, bf16[1024,384]{1,0:T(8,128)(2,1)S(1)}, u32[]{:S(2)}, u32[]{:S(2)}) collective-permute-start(bf16[1024,384]{1,0:T(8,128)(2,1)} %param.9), channel_id=1, source_target_pairs={{0,1},{1,0},{2,3},{3,2},{4,5},{5,4},{6,7},{7,6},{8,9},{9,8},{10,11... | collective-permute-start | bytes 2359304 | tf_op jit(solution)/shard_map/ppermute | solution.py:147
  3.7 1.1 reshape.171
  4.8 1.2 broadcast_select_fusion
  8.2 1.8 fusion.140
  10.0 17.7 %collective-permute-done.1 = bf16[384,384]{1,0:T(8,128)(2,1)S(1)} collective-permute-done((bf16[384,384]{1,0:T(8,128)(2,1)}, bf16[384,384]{1,0:T(8,128)(2,1)S(1)}, u32[]{:S(2)}, u32[]{:S(2)}) %collective-permute-start.1) | collective-permute-done | bytes 294944 | tf_op jit(solution)/shard_map/ppermute | solution.py:147
  31.1 1.1 reshape.172
  32.1 6.4 %all-to-all-start = ((bf16[16,32,2,192]{3,2,1,0:T(2,128)(2,1)}), bf16[16,32,2,192]{3,2,1,0:T(2,128)(2,1)S(1)}, u32[]{:S(2)}, u32[]{:S(2)}) async-start(bf16[16,32,2,192]{3,2,1,0:T(2,128)(2,1)} %reshape.172), calls=%async_computation | async-start | bytes 1048576 | tf_op jit(solution)/shard_map/all_to_all | solution.py:258
  39.1 1.0 copy.163
  41.7 1.0 copy.161
  42.7 1.5 collective-permute-start.2
  44.8 1.6 collective-permute-start.5
  46.3 6.5 %all-to-all-done = bf16[16,32,2,192]{3,2,1,0:T(2,128)(2,1)S(1)} async-done(((bf16[16,32,2,192]{3,2,1,0:T(2,128)(2,1)}), bf16[16,32,2,192]{3,2,1,0:T(2,128)(2,1)S(1)}, u32[]{:S(2)}, u32[]{:S(2)}) %all-to-all-start) | async-done | bytes 393248 | tf_op jit(solution)/shard_map/all_to_all | solution.py:258
  53.3 1.0 fusion.102
  63.8 3.4 %collective-permute-done.3 = bf16[3,384,192]{1,2,0:T(8,128)(2,1)} collective-permute-done((bf16[3,384,192]{1,2,0:T(8,128)(2,1)}, bf16[3,384,192]{1,2,0:T(8,128)(2,1)}, u32[]{:S(2)}, u32[]{:S(2)}) %collective-permute-start.3) | collective-permute-done | bytes 442400 | tf_op jit(solution)/shard_map/ppermute | solution.py:147
  67.3 2.0 convolution_convert_fusion.1
  71.2 1.2 fusion.111
  81.6 1.9 fusion.12
  83.5 1.9 fusion.14
  85.4 2.3 fusion.8
  87.7 1.9 fusion.16
  92.2 1.9 fusion.30
  94.1 1.9 fusion.32
  96.1 1.9 fusion.26
  98.0 2.1 fusion.22
  100.1 1.9 fusion.18
  102.5 1.5 collective-permute-start.4
  104.0 2.0 fusion.37
  106.1 2.0 fusion.39
  108.1 2.0 fusion.41
  110.0 2.0 fusion.43
  112.1 2.1 fusion.4
  114.2 1.9 fusion
  116.2 2.3 fusion.45
  118.4 2.0 fusion.47
  120.4 3.4 %fusion.49 = f32[1536,384]{1,0:T(8,128)} fusion(f32[1536,384]{1,0:T(8,128)S(1)} %fusion, f32[1536,384]{1,0:T(8,128)S(1)} %fusion.47, s32[512]{0:T(512)S(1)} %bitcast.309, bf16[512,9,384]{0,2,1:T(8,128)(2,1)S(1)} %bitcast.250), kind=kOutput, calls=%fused_computation.81 | convolution fusion | flops 605945856 | bytes 7473152 | tf_op jit(solution)/shard_map/bx,bc->xc/dot_general | solution.py:121
  123.8 1.9 slice.353
  125.7 2.1 reshape.174
  127.8 6.3 %all-to-all-start.1 = ((bf16[16,32,2,192]{3,2,1,0:T(2,128)(2,1)}), bf16[16,32,2,192]{3,2,1,0:T(2,128)(2,1)}, u32[]{:S(2)}, u32[]{:S(2)}) async-start(bf16[16,32,2,192]{3,2,1,0:T(2,128)(2,1)} %reshape.174), calls=%async_computation.1 | async-start | bytes 1048576 | tf_op jit(solution)/shard_map/all_to_all | solution.py:278
  134.1 1.2 multiply_reduce_fusion.2
  135.4 1.3 multiply_reduce_fusion
  137.2 1.0 reshape_reshape.4
  138.2 2.6 %convolution_multiply_fusion.2 = f32[192,384]{1,0:T(8,128)} fusion(bf16[1024,192]{0,1:T(8,128)(2,1)S(1)} %bitcast.258, bf16[1024,192]{1,0:T(8,128)(2,1)S(1)} %copy-done.17, bf16[1024,192]{1,0:T(8,128)(2,1)} %collective-permute-done.2, pred[]{:T(512)S(6)} %eq.243), kind=kOutput, calls=%fused_computation.161 | convolution fusion | flops 154607616 | bytes 1474561 | tf_op jit(solution)/shard_map/dot_general | solution.py:268
  140.9 2.7 %slice.352 = f32[1024,384]{1,0:T(8,128)} slice(f32[1536,384]{1,0:T(8,128)} %fusion.49), slice={[0:1024], [0:384]} | slice | bytes 3145728 | tf_op jit(solution)/shard_map/slice | solution.py:285
  143.5 1.9 copy.195
  145.4 3.2 %all-to-all-done.1 = bf16[16,32,2,192]{3,2,1,0:T(2,128)(2,1)} async-done(((bf16[16,32,2,192]{3,2,1,0:T(2,128)(2,1)}), bf16[16,32,2,192]{3,2,1,0:T(2,128)(2,1)}, u32[]{:S(2)}, u32[]{:S(2)}) %all-to-all-start.1) | async-done | bytes 393248 | tf_op jit(solution)/shard_map/all_to_all | solution.py:278
  148.6 1.4 convert_element_type.207
  151.8 1.8 fusion.98
  155.1 1.4 copy.197
  156.7 1.1 broadcast_select_fusion.2
  157.9 1.1 pad_maximum_fusion.3
  160.8 4.1 %all-to-all-start.2 = ((f32[16,24,384]{2,1,0:T(8,128)}), f32[16,24,384]{2,1,0:T(8,128)S(1)}, u32[]{:S(2)}, u32[]{:S(2)}) async-start(f32[16,24,384]{2,1,0:T(8,128)} %bitcast.106), calls=%async_computation.2 | async-start | bytes 1179648 | tf_op jit(solution)/shard_map/all_to_all | solution.py:179
  164.9 3.5 %fusion.130 = f32[1024,384,1]{1,0,2:T(8,128)} fusion(bf16[3,384,192]{1,2,0:T(8,128)(2,1)} %param.11, bf16[1024,2,192]{0,2,1:T(8,128)(2,1)} %copy-done.12, bf16[1024,1,192]{0,2,1:T(8,128)(2,1)S(1)} %copy-done.6), kind=kOutput, calls=%fused_computation.242 | convolution fusion | flops 453574656 | bytes 3194880 | tf_op jit(solution)/shard_map/rkd,kcd->rc/dot_general | solution.py:296
  168.4 12.1 %all-to-all-done.2 = f32[16,24,384]{2,1,0:T(8,128)S(1)} async-done(((f32[16,24,384]{2,1,0:T(8,128)}), f32[16,24,384]{2,1,0:T(8,128)S(1)}, u32[]{:S(2)}, u32[]{:S(2)}) %all-to-all-start.2) | async-done | bytes 589856 | tf_op jit(solution)/shard_map/all_to_all | solution.py:179
  180.5 7.2 %collective-permute-done.7 = bf16[1024,3,192]{0,2,1:T(8,128)(2,1)} collective-permute-done((bf16[1024,3,192]{0,2,1:T(8,128)(2,1)}, bf16[1024,3,192]{0,2,1:T(8,128)(2,1)}, u32[]{:S(2)}, u32[]{:S(2)}) %collective-permute-start.7) | collective-permute-done | bytes 1179680 | tf_op jit(solution)/shard_map/ppermute | solution.py:147
  187.7 3.4 %fusion.58 = bf16[1024,384]{1,0:T(8,128)(2,1)S(1)} fusion(f32[1024,384,1]{1,0,2:T(8,128)} %fusion.130, bf16[1024,3,192]{0,2,1:T(8,128)(2,1)} %collective-permute-done.7, bf16[3,384,192]{1,2,0:T(8,128)(2,1)} %collective-permute-done.3, bf16[1024,192]{1,0:T(8,128)(2,1)} %collective-permute-done.2, bf16[1024,192]{1,0:T(8,128)(2,1)S(1)} %copy-done.18, pred[]{:T(512)S(6)} %eq.243), kind=kOutput, calls=%fused_computation.91 | convolution fusion | flops 458096640 | bytes 4767745 | tf_op jit(solution)/shard_map/rkd,kcd->rc/dot_general | solution.py:300
  191.9 1.6 collective-permute-done.8
  193.6 16.1 %all_to_all.25 = f32[16,12,384]{2,1,0:T(8,128)S(1)} all-to-all(f32[16,12,384]{2,1,0:T(8,128)S(1)} %reshape.178), channel_id=1, replica_groups=mesh['pix'=16,'ch'=2] {'pix'}, dimensions={0} | all-to-all | bytes 589824 | tf_op jit(solution)/shard_map/all_to_all | solution.py:179
  209.8 27.4 %all_to_all.26 = f32[16,36,384]{2,1,0:T(8,128)S(1)} all-to-all(f32[16,36,384]{2,1,0:T(8,128)S(1)} %bitcast.251), channel_id=1, replica_groups=mesh['pix'=16,'ch'=2] {'pix'}, dimensions={0} | all-to-all | bytes 1769472 | tf_op jit(solution)/shard_map/all_to_all | solution.py:190
  237.2 1.1 copy.199
  239.1 1.3 fusion.123
  240.4 1.5 fusion.99
  242.8 1.5 convolution_convert_fusion
  244.3 1.5 copy_select_fusion.1
  247.0 1.3 copy.203
  (213 shorter events, 42.4 us)
Async XLA Ops:
  0.6 27.1 %collective-permute-start = (bf16[1024,384]{1,0:T(8,128)(2,1)}, bf16[1024,384]{1,0:T(8,128)(2,1)S(1)}, u32[]{:S(2)}, u32[]{:S(2)}) collective-permute-start(bf16[1024,384]{1,0:T(8,128)(2,1)} %param.9), channel_id=1, source_target_pairs={{0,1},{1,0},{2,3},{3,2},{4,5},{5,4},{6,7},{7,6},{8,9},{9,8},{10,11... | collective-permute-start | bytes 2359304 | tf_op jit(solution)/shard_map/ppermute | solution.py:147
  3.6 24.1 %collective-permute-start.1 = (bf16[384,384]{1,0:T(8,128)(2,1)}, bf16[384,384]{1,0:T(8,128)(2,1)S(1)}, u32[]{:S(2)}, u32[]{:S(2)}) collective-permute-start(bf16[384,384]{1,0:T(8,128)(2,1)} %param.10), channel_id=1, source_target_pairs={{0,1},{1,0},{2,3},{3,2},{4,5},{5,4},{6,7},{7,6},{8,9},{9,8},{10,11... | collective-permute-start | bytes 884744 | tf_op jit(solution)/shard_map/ppermute | solution.py:147
  8.2 22.1 %copy-start.28 = (s32[512]{0:T(512)}, s32[512]{0:T(512)S(1)}, u32[]{:S(2)}) copy-start(s32[512]{0:T(512)S(1)} %eq.172) | copy-start | bytes 6148
  10.0 19.2 %copy-start.19 = (bf16[3,384,192]{1,2,0:T(8,128)(2,1)S(1)}, bf16[3,384,192]{1,2,0:T(8,128)(2,1)}, u32[]{:S(2)}) copy-start(bf16[3,384,192]{1,2,0:T(8,128)(2,1)} %param.11) | copy-start | bytes 1327108
  28.3 0.9 copy-start
  30.3 8.8 %copy-start.5 = (bf16[1024,192]{0,1:T(8,128)(2,1)S(1)}, bf16[1024,192]{0,1:T(8,128)(2,1)}, u32[]{:S(2)}) copy-start(bf16[1024,192]{0,1:T(8,128)(2,1)} %param.15) | copy-start | bytes 1179652
  32.1 20.7 %all-to-all-start = ((bf16[16,32,2,192]{3,2,1,0:T(2,128)(2,1)}), bf16[16,32,2,192]{3,2,1,0:T(2,128)(2,1)S(1)}, u32[]{:S(2)}, u32[]{:S(2)}) async-start(bf16[16,32,2,192]{3,2,1,0:T(2,128)(2,1)} %reshape.172), calls=%async_computation | async-start | bytes 1048576 | tf_op jit(solution)/shard_map/all_to_all | solution.py:258
  40.8 13.5 %copy-start.24 = (s32[512]{0:T(512)}, s32[512]{0:T(512)S(1)}, u32[]{:S(2)}) copy-start(s32[512]{0:T(512)S(1)} %iota_add_fusion.1) | copy-start | bytes 6148
  41.5 12.8 %copy-start.40 = (s32[512,1]{0,1:T(1,128)}, s32[512,1]{0,1:T(1,128)S(1)}, u32[]{:S(2)}) copy-start(s32[512,1]{0,1:T(1,128)S(1)} %get-tuple-element.106) | copy-start | bytes 6148
  41.5 13.8 %copy-start.42 = (s32[512,1]{0,1:T(1,128)}, s32[512,1]{0,1:T(1,128)S(1)}, u32[]{:S(2)}) copy-start(s32[512,1]{0,1:T(1,128)S(1)} %get-tuple-element.105) | copy-start | bytes 6148
  41.5 14.8 %copy-start.22 = (s32[512,1]{0,1:T(1,128)}, s32[512,1]{0,1:T(1,128)S(1)}, u32[]{:S(2)}) copy-start(s32[512,1]{0,1:T(1,128)S(1)} %get-tuple-element.104) | copy-start | bytes 6148
  41.5 15.7 %copy-start.38 = (s32[512,1]{0,1:T(1,128)}, s32[512,1]{0,1:T(1,128)S(1)}, u32[]{:S(2)}) copy-start(s32[512,1]{0,1:T(1,128)S(1)} %get-tuple-element.103) | copy-start | bytes 6148
  41.5 17.7 %copy-start.36 = (s32[512,1]{0,1:T(1,128)}, s32[512,1]{0,1:T(1,128)S(1)}, u32[]{:S(2)}) copy-start(s32[512,1]{0,1:T(1,128)S(1)} %get-tuple-element.101) | copy-start | bytes 6148
  41.6 19.7 %copy-start.34 = (s32[512,1]{0,1:T(1,128)}, s32[512,1]{0,1:T(1,128)S(1)}, u32[]{:S(2)}) copy-start(s32[512,1]{0,1:T(1,128)S(1)} %get-tuple-element.99) | copy-start | bytes 6148
  41.6 30.9 %copy-start.26 = (s32[512,1]{0,1:T(1,128)}, s32[512,1]{0,1:T(1,128)S(1)}, u32[]{:S(2)}) copy-start(s32[512,1]{0,1:T(1,128)S(1)} %get-tuple-element.119) | copy-start | bytes 6148
  41.6 33.8 %copy-start.32 = (s32[512,1]{0,1:T(1,128)}, s32[512,1]{0,1:T(1,128)S(1)}, u32[]{:S(2)}) copy-start(s32[512,1]{0,1:T(1,128)S(1)} %get-tuple-element.122) | copy-start | bytes 6148
  41.6 35.8 %copy-start.30 = (s32[512,1]{0,1:T(1,128)}, s32[512,1]{0,1:T(1,128)S(1)}, u32[]{:S(2)}) copy-start(s32[512,1]{0,1:T(1,128)S(1)} %get-tuple-element.124) | copy-start | bytes 6148
  41.7 21.1 %copy-start.2 = (f32[512,3,64]{0,2,1:T(8,128)}, f32[512,3,64]{0,2,1:T(8,128)S(1)}, u32[]{:S(2)}) copy-start(f32[512,3,64]{0,2,1:T(8,128)S(1)} %convert.64) | copy-start | bytes 1179652
  42.7 21.1 %collective-permute-start.2 = (bf16[1024,192]{1,0:T(8,128)(2,1)}, bf16[1024,192]{1,0:T(8,128)(2,1)}, u32[]{:S(2)}, u32[]{:S(2)}) collective-permute-start(bf16[1024,192]{1,0:T(8,128)(2,1)} %copy.161), channel_id=1, source_target_pairs={{0,1},{1,0},{2,3},{3,2},{4,5},{5,4},{6,7},{7,6},{8,9},{9,8},{10,11... | collective-permute-start | bytes 1179656 | tf_op jit(solution)/shard_map/ppermute | solution.py:147
  44.2 23.0 %collective-permute-start.3 = (bf16[3,384,192]{1,2,0:T(8,128)(2,1)}, bf16[3,384,192]{1,2,0:T(8,128)(2,1)}, u32[]{:S(2)}, u32[]{:S(2)}) collective-permute-start(bf16[3,384,192]{1,2,0:T(8,128)(2,1)} %param.11), channel_id=1, source_target_pairs={{0,1},{1,0},{2,3},{3,2},{4,5},{5,4},{6,7},{7,6},{8,9},{9,8},{10,11... | collective-permute-start | bytes 1327112 | tf_op jit(solution)/shard_map/ppermute | solution.py:147
  44.8 71.3 %collective-permute-start.5 = (bf16[192,192]{1,0:T(8,128)(2,1)}, bf16[192,192]{1,0:T(8,128)(2,1)}, u32[]{:S(2)}, u32[]{:S(2)}) collective-permute-start(bf16[192,192]{1,0:T(8,128)(2,1)} %bitcast.223), channel_id=1, source_target_pairs={{0,1},{1,0},{2,3},{3,2},{4,5},{5,4},{6,7},{7,6},{8,9},{9,8},{10,11... | collective-permute-start | bytes 221192 | tf_op jit(solution)/shard_map/ppermute | solution.py:243
  62.8 4.5 %copy-start.16 = (bf16[1024,192]{1,0:T(8,128)(2,1)S(1)}, bf16[1024,192]{1,0:T(8,128)(2,1)}, u32[]{:S(2)}) copy-start(bf16[1024,192]{1,0:T(8,128)(2,1)} %copy.163) | copy-start | bytes 1179652
  62.8 4.5 %copy-start.21 = (bf16[192,384]{1,0:T(8,128)(2,1)S(1)}, bf16[192,384]{1,0:T(8,128)(2,1)}, u32[]{:S(2)}) copy-start(bf16[192,384]{1,0:T(8,128)(2,1)} %param.12) | copy-start | bytes 442372
  80.1 0.6 copy-start.15
  89.9 1.0 copy-start.3
  90.9 0.6 copy-start.14
  91.5 0.7 copy-start.43
  91.9 2.3 copy-start.41
  94.1 1.9 copy-start.39
  96.0 1.9 copy-start.37
  98.0 2.1 copy-start.35
  102.0 2.0 copy-start.25
  102.5 3.6 %copy-start.7 = (bf16[2,24,8,512]{3,2,0,1:T(8,128)(2,1)}, bf16[2,24,8,512]{3,2,0,1:T(8,128)(2,1)S(1)}, u32[]{:S(2)}) copy-start(bf16[2,24,8,512]{3,2,0,1:T(8,128)(2,1)S(1)} %copy.271) | copy-start | bytes 1179652
  102.5 3.6 %copy-start.23 = (s32[512,1]{0,1:T(1,128)S(1)}, s32[512,1]{0,1:T(1,128)}, u32[]{:S(2)}) copy-start(s32[512,1]{0,1:T(1,128)} %copy-done.22) | copy-start | bytes 6148
  102.5 13.7 %collective-permute-start.4 = (bf16[1024,192]{0,1:T(8,128)(2,1)S(1)}, bf16[1024,192]{0,1:T(8,128)(2,1)S(1)}, u32[]{:S(2)}, u32[]{:S(2)}) collective-permute-start(bf16[1024,192]{0,1:T(8,128)(2,1)S(1)} %bitcast.257), channel_id=1, source_target_pairs={{0,1},{1,0},{2,3},{3,2},{4,5},{5,4},{6,7},{7,6},{8,9},{9,8},{10,11... | collective-permute-start | bytes 1179656 | tf_op jit(solution)/shard_map/ppermute | solution.py:147
  110.0 2.0 copy-start.33
  112.1 2.1 copy-start.31
  114.2 1.9 copy-start.27
  116.2 2.3 copy-start.20
  127.8 20.8 %all-to-all-start.1 = ((bf16[16,32,2,192]{3,2,1,0:T(2,128)(2,1)}), bf16[16,32,2,192]{3,2,1,0:T(2,128)(2,1)}, u32[]{:S(2)}, u32[]{:S(2)}) async-start(bf16[16,32,2,192]{3,2,1,0:T(2,128)(2,1)} %reshape.174), calls=%async_computation.1 | async-start | bytes 1048576 | tf_op jit(solution)/shard_map/all_to_all | solution.py:278
  135.4 2.8 %copy-start.8 = (bf16[2,24,8,512]{3,2,0,1:T(8,128)(2,1)S(1)}, bf16[2,24,8,512]{3,2,0,1:T(8,128)(2,1)}, u32[]{:S(2)}) copy-start(bf16[2,24,8,512]{3,2,0,1:T(8,128)(2,1)} %copy-done.7) | copy-start | bytes 1179652
  135.4 2.8 %copy-start.17 = (bf16[1024,192]{1,0:T(8,128)(2,1)S(1)}, bf16[1024,192]{1,0:T(8,128)(2,1)}, u32[]{:S(2)}) copy-start(bf16[1024,192]{1,0:T(8,128)(2,1)} %copy.163) | copy-start | bytes 1179652
  143.5 6.7 %copy-start.29 = (s32[512]{0:T(512)S(1)}, s32[512]{0:T(512)}, u32[]{:S(2)}) copy-start(s32[512]{0:T(512)} %copy-done.28) | copy-start | bytes 6148
  145.4 6.4 %copy-start.1 = (bf16[1024,384]{1,0:T(8,128)(2,1)S(1)}, bf16[1024,384]{1,0:T(8,128)(2,1)}, u32[]{:S(2)}) copy-start(bf16[1024,384]{1,0:T(8,128)(2,1)} %copy-done) | copy-start | bytes 2359300
  150.9 0.9 copy-start.12
  155.1 2.8 %copy-start.6 = (bf16[1024,1,192]{0,2,1:T(8,128)(2,1)S(1)}, bf16[1024,1,192]{0,2,1:T(8,128)(2,1)}, u32[]{:S(2)}) copy-start(bf16[1024,1,192]{0,2,1:T(8,128)(2,1)} %reshape_reshape.4) | copy-start | bytes 1179652
  156.7 1.2 copy-start.13
  156.7 3.2 %copy-start.10 = (f32[192,384]{1,0:T(8,128)S(1)}, f32[192,384]{1,0:T(8,128)}, u32[]{:S(2)}) copy-start(f32[192,384]{1,0:T(8,128)} %convolution_multiply_fusion.2) | copy-start | bytes 884740
  157.8 2.1 collective-permute-start.6
  159.0 28.7 %collective-permute-start.7 = (bf16[1024,3,192]{0,2,1:T(8,128)(2,1)}, bf16[1024,3,192]{0,2,1:T(8,128)(2,1)}, u32[]{:S(2)}, u32[]{:S(2)}) collective-permute-start(bf16[1024,3,192]{0,2,1:T(8,128)(2,1)} %pad_maximum_fusion.3), channel_id=1, source_target_pairs={{0,1},{1,0},{2,3},{3,2},{4,5},{5,4},{6,7},{7,6},{8,9},{9,8},{10,11... | collective-permute-start | bytes 3538952 | tf_op jit(solution)/shard_map/ppermute | solution.py:147
  160.8 19.7 %all-to-all-start.2 = ((f32[16,24,384]{2,1,0:T(8,128)}), f32[16,24,384]{2,1,0:T(8,128)S(1)}, u32[]{:S(2)}, u32[]{:S(2)}) async-start(f32[16,24,384]{2,1,0:T(8,128)} %bitcast.106), calls=%async_computation.2 | async-start | bytes 1179648 | tf_op jit(solution)/shard_map/all_to_all | solution.py:179
  164.9 22.8 %copy-start.18 = (bf16[1024,192]{1,0:T(8,128)(2,1)S(1)}, bf16[1024,192]{1,0:T(8,128)(2,1)}, u32[]{:S(2)}) copy-start(bf16[1024,192]{1,0:T(8,128)(2,1)} %copy.163) | copy-start | bytes 1179652
  180.5 10.6 %copy-start.4 = (bf16[1024,384]{1,0:T(8,128)(2,1)S(1)}, bf16[1024,384]{1,0:T(8,128)(2,1)}, u32[]{:S(2)}) copy-start(bf16[1024,384]{1,0:T(8,128)(2,1)} %param.9) | copy-start | bytes 2359300
  191.8 1.6 collective-permute-start.8
  209.7 29.4 %copy-start.9 = (bf16[2,24,8,512]{3,2,0,1:T(8,128)(2,1)S(1)}, bf16[2,24,8,512]{3,2,0,1:T(8,128)(2,1)}, u32[]{:S(2)}) copy-start(bf16[2,24,8,512]{3,2,0,1:T(8,128)(2,1)} %copy-done.7) | copy-start | bytes 1179652
  238.3 6.0 %collective-permute-start.9 = (f32[16,36,384]{2,0,1:T(8,128)}, f32[16,36,384]{2,0,1:T(8,128)}, u32[]{:S(2)}, u32[]{:S(2)}) collective-permute-start(f32[16,36,384]{2,0,1:T(8,128)} %copy.199), channel_id=1, source_target_pairs={{0,2},{2,0},{4,6},{6,4},{8,10},{10,8},{12,14},{14,12},{16,18},{18,... | collective-permute-start | bytes 2654216 | tf_op jit(solution)/shard_map/ppermute | solution.py:165
  239.1 3.7 %copy-start.11 = (bf16[384,384]{1,0:T(8,128)(2,1)S(1)}, bf16[384,384]{1,0:T(8,128)(2,1)}, u32[]{:S(2)}) copy-start(bf16[384,384]{1,0:T(8,128)(2,1)} %param.10) | copy-start | bytes 884740

commit v7 on v3

--- a/solution.py
+++ b/solution.py
@@ -158,27 +158,55 @@
     return result
 
 
+HALVING_MASKS = (1, 2)
+
+
+def pix_swap(value, mask):
+    size = lax.axis_size("pix")
+    return lax.ppermute(value, "pix", [(i, i ^ mask) for i in range(size)])
+
+
 def pix_scatter(terms, width):
     size = lax.axis_size("pix")
+    index = lax.axis_index("pix")
+    groups = 2 ** len(HALVING_MASKS)
     flat = jnp.concatenate([term.reshape(-1, width) for term in terms], axis=0)
     rows = flat.shape[0]
-    chunk = -(-rows // size)
-    flat = jnp.pad(flat, ((0, chunk * size - rows), (0, 0)))
-    parts = lax.all_to_all(flat.reshape(size, chunk, width), "pix", 0, 0, tiled=True)
-    return jnp.sum(parts, axis=0)
+    chunk = -(-rows // (groups * size))
+    data = jnp.pad(flat, ((0, groups * size * chunk - rows), (0, 0)))
+    for mask in HALVING_MASKS:
+        high = (index // mask) % 2 == 1
+        halves = data.reshape(2, -1, width)
+        keep = jnp.where(high, halves[1], halves[0])
+        send = jnp.where(high, halves[0], halves[1])
+        data = keep + pix_swap(send, mask)
+    parts = lax.all_to_all(data.reshape(size, chunk, width), "pix", 0, 0, tiled=True)
+    return jnp.sum(parts.reshape(size // groups, groups, chunk, width), axis=0)
 
 
 def pix_gather(reduced_groups, term_groups):
     size = lax.axis_size("pix")
+    index = lax.axis_index("pix")
+    groups = 2 ** len(HALVING_MASKS)
     width = reduced_groups[0].shape[-1]
-    joined = jnp.concatenate(reduced_groups, axis=0)
-    spread = jnp.broadcast_to(joined[None], (size,) + joined.shape)
-    gathered = lax.all_to_all(spread, "pix", 0, 0, tiled=True)
+    joined = jnp.concatenate(reduced_groups, axis=1)
+    total = joined.shape[1]
+    spread = jnp.broadcast_to(joined[None], (size // groups, groups, total, width))
+    got = lax.all_to_all(spread.reshape(size, total, width), "pix", 0, 0, tiled=True)
+    blocks = got[None]
+    for mask in reversed(HALVING_MASKS):
+        high = (index // mask) % 2 == 1
+        other = pix_swap(blocks, mask)
+        blocks = jnp.where(
+            high,
+            jnp.concatenate([other, blocks], axis=0),
+            jnp.concatenate([blocks, other], axis=0),
+        )
     results = []
     offset = 0
     for reduced, terms in zip(reduced_groups, term_groups):
-        chunk = reduced.shape[0]
-        flat = gathered[:, offset : offset + chunk].reshape(size * chunk, width)
+        chunk = reduced.shape[1]
+        flat = blocks[:, :, offset : offset + chunk].reshape(groups * size * chunk, width)
         offset += chunk
         row = 0
         for term in terms:

time: 274 us -> 262 us (0.956)
  the two profiles are of different devices: /device:TPU:15 before, /device:TPU:0 now
where the time goes in v7:
time: 262 us; the launch traced here: 257 us
  matrix products  78.2 us (30%)
  waiting for transfers between devices  67 us (26%)
  blocking collectives  32.6 us (12%)
  local copies, waits for them, and re-layouts  30.7 us (12%)
  starting transfers between devices  28.1 us (11%)
  other arithmetic  17.5 us (7%)
  between operations  2.81 us (1%)
    dot_general x18, matrix products, backward_block(): jnp.einsum('bx,bc->xc', pick_table(slot_rows[:, slot], ext_rows), contrib...  37.2 us
    ppermute x6, waiting for transfers between devices, pix_swap(): return lax.ppermute(value, 'pix', [(i, i ^ mask) for i in range(size)])  26.3 us
    ppermute x6, waiting for transfers between devices, ch_exchange(): lax.ppermute(value, 'ch', [(i, (i + shift) % size) for i in range(size)])  25.9 us
    all_to_all x1, blocking collectives, pix_gather(): lax.all_to_all(spread.reshape(size, total, width), 'pix', 0, 0, tiled=True)  20.1 us
    dot_general x18, matrix products, forward_block(): jnp.dot(pick_table(slot_rows[:, slot], ext_rows), flattened, preferred_el...  18 us
    all_to_all x1, blocking collectives, pix_scatter(): lax.all_to_all(data.reshape(size, chunk, width), 'pix', 0, 0, tiled=True)  12.5 us
    all_to_all x1, waiting for transfers between devices, pix_scatter(): lax.all_to_all(data.reshape(size, chunk, width), 'pix', 0, 0, tiled=True)  8.97 us
    ppermute x6, starting transfers between devices, ch_exchange(): lax.ppermute(value, 'ch', [(i, (i + shift) % size) for i in range(size)])  8.42 us
  transfers between devices with their start and end apart: 16, of which 9 were waited for; matrix products, arithmetic and copies ran while one was open for 36% of the time, Pallas kernels for 0%

profile of v7, /device:TPU:0, one launch (start us, length us, event | category | flops | bytes accessed | tf_op | source)
XLA Modules:
  0.0 256.9 jit_solution(6562040272935997362)
XLA Ops:
  0.6 3.0 %collective-permute-start.1 = (bf16[384,384]{1,0:T(8,128)(2,1)}, bf16[384,384]{1,0:T(8,128)(2,1)S(1)}, u32[]{:S(2)}, u32[]{:S(2)}) collective-permute-start(bf16[384,384]{1,0:T(8,128)(2,1)} %param.10), channel_id=1, source_target_pairs={{0,1},{1,0},{2,3},{3,2},{4,5},{5,4},{6,7},{7,6},{8,9},{9,8},{10,11... | collective-permute-start | bytes 884744 | tf_op jit(solution)/shard_map/ppermute | solution.py:145
  5.0 1.1 reshape.185
  6.1 1.2 broadcast_select_fusion
  9.5 1.8 fusion.140
  11.7 16.0 %collective-permute-done = bf16[1024,384]{1,0:T(8,128)(2,1)S(1)} collective-permute-done((bf16[1024,384]{1,0:T(8,128)(2,1)}, bf16[1024,384]{1,0:T(8,128)(2,1)S(1)}, u32[]{:S(2)}, u32[]{:S(2)}) %collective-permute-start) | collective-permute-done | bytes 786464 | tf_op jit(solution)/shard_map/ppermute | solution.py:145
  28.4 1.0 copy.163
  29.4 1.7 collective-permute-start.2
  33.0 1.1 reshape.186
  34.1 6.1 %all-to-all-start = ((bf16[16,32,2,192]{3,2,1,0:T(2,128)(2,1)}), bf16[16,32,2,192]{3,2,1,0:T(2,128)(2,1)S(1)}, u32[]{:S(2)}, u32[]{:S(2)}) async-start(bf16[16,32,2,192]{3,2,1,0:T(2,128)(2,1)} %reshape.186), calls=%async_computation | async-start | bytes 1048576 | tf_op jit(solution)/shard_map/all_to_all | solution.py:264
  40.9 1.0 copy.164
  42.5 1.5 collective-permute-start.3
  44.9 2.3 convolution_convert_fusion.1
  47.2 9.6 %collective-permute-done.3 = bf16[3,384,192]{1,2,0:T(8,128)(2,1)S(1)} collective-permute-done((bf16[3,384,192]{1,2,0:T(8,128)(2,1)}, bf16[3,384,192]{1,2,0:T(8,128)(2,1)S(1)}, u32[]{:S(2)}, u32[]{:S(2)}) %collective-permute-start.3) | collective-permute-done | bytes 442400 | tf_op jit(solution)/shard_map/ppermute | solution.py:145
  70.3 2.1 fusion.18
  72.4 1.9 fusion.22
  74.4 1.9 fusion.26
  76.3 1.9 fusion.30
  78.2 1.9 fusion.32
  84.1 1.4 fusion.115
  93.8 1.9 fusion
  95.7 1.9 fusion.4
  97.7 1.9 fusion.8
  99.6 3.5 %fusion.12 = f32[1536,384]{1,0:T(8,128)} fusion(s32[512]{0:T(512)S(1)} %bitcast.316, bf16[512,9,384]{0,2,1:T(8,128)(2,1)S(1)} %bitcast.239), kind=kOutput, calls=%fused_computation.33 | convolution fusion | flops 604766208 | bytes 2754560 | tf_op jit(solution)/shard_map/bx,bc->xc/dot_general | solution.py:119
  104.5 2.0 fusion.37
  106.5 2.0 fusion.39
  108.6 2.0 fusion.41
  110.6 2.0 fusion.43
  112.6 2.1 fusion.14
  114.8 1.9 fusion.16
  116.8 2.2 fusion.45
  119.0 2.0 fusion.47
  121.0 2.0 fusion.49
  123.0 1.4 copy-done
  125.2 2.1 reshape.188
  127.3 6.0 %all-to-all-start.1 = ((bf16[16,32,2,192]{3,2,1,0:T(2,128)(2,1)}), bf16[16,32,2,192]{3,2,1,0:T(2,128)(2,1)}, u32[]{:S(2)}, u32[]{:S(2)}) async-start(bf16[16,32,2,192]{3,2,1,0:T(2,128)(2,1)} %reshape.188), calls=%async_computation.1 | async-start | bytes 1048576 | tf_op jit(solution)/shard_map/all_to_all | solution.py:282
  133.3 1.2 multiply_reduce_fusion.2
  134.6 1.3 multiply_reduce_fusion
  136.4 1.0 reshape_reshape.4
  137.4 2.6 %convolution_multiply_fusion.2 = f32[192,384]{1,0:T(8,128)} fusion(bf16[1024,192]{0,1:T(8,128)(2,1)S(1)} %bitcast.251, bf16[1024,192]{1,0:T(8,128)(2,1)S(1)} %copy-done.17, bf16[1024,192]{1,0:T(8,128)(2,1)} %collective-permute-done.2, pred[]{:T(512)S(6)} %eq.248), kind=kOutput, calls=%fused_computation.163 | convolution fusion | flops 154607616 | bytes 1474561 | tf_op jit(solution)/shard_map/dot_general | solution.py:272
  140.0 1.4 slice-done
  141.9 5.8 %all-to-all-done.1 = bf16[16,32,2,192]{3,2,1,0:T(2,128)(2,1)} async-done(((bf16[16,32,2,192]{3,2,1,0:T(2,128)(2,1)}), bf16[16,32,2,192]{3,2,1,0:T(2,128)(2,1)}, u32[]{:S(2)}, u32[]{:S(2)}) %all-to-all-start.1) | async-done | bytes 393248 | tf_op jit(solution)/shard_map/all_to_all | solution.py:282
  147.8 1.4 convert_element_type.211
  151.0 1.8 fusion.98
  152.8 1.4 copy.198
  154.7 1.6 reshape.189
  156.5 2.3 pad_maximum_fusion.3
  158.7 1.5 collective-permute-start.8
  160.3 1.2 select_add_fusion
  161.5 1.2 collective-permute-start.7
  162.7 8.0 %collective-permute-done.7 = f32[192,384]{1,0:T(8,128)S(1)} collective-permute-done((f32[192,384]{1,0:T(8,128)S(1)}, f32[192,384]{1,0:T(8,128)S(1)}, u32[]{:S(2)}, u32[]{:S(2)}) %collective-permute-start.7) | collective-permute-done | bytes 294944 | tf_op jit(solution)/shard_map/ppermute | solution.py:166
  171.4 4.1 %all-to-all-start.2 = ((f32[16,12,384]{2,1,0:T(8,128)}), f32[16,12,384]{2,1,0:T(8,128)S(1)}, u32[]{:S(2)}, u32[]{:S(2)}) async-start(f32[16,12,384]{2,1,0:T(8,128)} %reshape.190), calls=%async_computation.2 | async-start | bytes 786432 | tf_op jit(solution)/shard_map/all_to_all | solution.py:183
  175.6 3.2 %fusion.130 = f32[1024,384,1]{1,0,2:T(8,128)} fusion(bf16[3,384,192]{1,2,0:T(8,128)(2,1)} %param.11, bf16[1024,2,192]{0,2,1:T(8,128)(2,1)S(1)} %copy-done.14, bf16[1024,1,192]{0,2,1:T(8,128)(2,1)S(1)} %copy-done.8), kind=kOutput, calls=%fused_computation.243 | convolution fusion | flops 453574656 | bytes 3194880 | tf_op jit(solution)/shard_map/rkd,kcd->rc/dot_general | solution.py:300
  178.8 9.0 %all-to-all-done.2 = f32[16,12,384]{2,1,0:T(8,128)S(1)} async-done(((f32[16,12,384]{2,1,0:T(8,128)}), f32[16,12,384]{2,1,0:T(8,128)S(1)}, u32[]{:S(2)}, u32[]{:S(2)}) %all-to-all-start.2) | async-done | bytes 294944 | tf_op jit(solution)/shard_map/all_to_all | solution.py:183
  187.8 3.5 %fusion.58 = bf16[1024,384]{1,0:T(8,128)(2,1)S(1)} fusion(f32[1024,384,1]{1,0,2:T(8,128)} %fusion.130, bf16[1024,3,192]{0,2,1:T(8,128)(2,1)} %collective-permute-done.8, bf16[3,384,192]{1,2,0:T(8,128)(2,1)} %copy-done.49, bf16[1024,192]{1,0:T(8,128)(2,1)} %collective-permute-done.2, bf16[1024,192]{1,0:T(8,128)(2,1)S(1)} %copy-done.18, pred[]{:T(512)S(6)} %eq.248), kind=kOutput, calls=%fused_computation.92 | convolution fusion | flops 458096640 | bytes 4767745 | tf_op jit(solution)/shard_map/rkd,kcd->rc/dot_general | solution.py:304
  192.2 1.5 collective-permute-done.9
  194.4 5.3 %collective-permute-done.10 = f32[96,384]{1,0:T(8,128)S(1)} collective-permute-done((f32[96,384]{1,0:T(8,128)S(1)}, f32[96,384]{1,0:T(8,128)S(1)}, u32[]{:S(2)}, u32[]{:S(2)}) %collective-permute-start.10) | collective-permute-done | bytes 147488 | tf_op jit(solution)/shard_map/ppermute | solution.py:166
  199.7 12.5 %all_to_all.25 = f32[16,6,384]{2,1,0:T(8,128)S(1)} all-to-all(f32[16,6,384]{2,1,0:T(8,128)S(1)} %reshape.192), channel_id=1, replica_groups=mesh['pix'=16,'ch'=2] {'pix'}, dimensions={0} | all-to-all | bytes 294912 | tf_op jit(solution)/shard_map/all_to_all | solution.py:183
  212.3 20.1 %all_to_all.26 = f32[16,18,384]{2,1,0:T(8,128)S(1)} all-to-all(f32[16,18,384]{2,1,0:T(8,128)S(1)} %bitcast.247), channel_id=1, replica_groups=mesh['pix'=16,'ch'=2] {'pix'}, dimensions={0} | all-to-all | bytes 884736 | tf_op jit(solution)/shard_map/all_to_all | solution.py:195
  233.2 11.6 %collective-permute-done.11 = f32[1,16,18,384]{3,1,2,0:T(8,128)S(1)} collective-permute-done((f32[1,16,18,384]{3,1,2,0:T(8,128)S(1)}, f32[1,16,18,384]{3,1,2,0:T(8,128)S(1)}, u32[]{:S(2)}, u32[]{:S(2)}) %collective-permute-start.11) | collective-permute-done | bytes 442400 | tf_op jit(solution)/shard_map/ppermute | solution.py:166
  245.0 1.1 copy.203
  246.5 1.5 fusion.99
  248.9 2.5 convolution_convert_fusion
  251.4 1.5 copy.204
  255.1 1.3 copy.207
  (235 shorter events, 46.4 us)
Async XLA Ops:
  0.6 11.1 %collective-permute-start.1 = (bf16[384,384]{1,0:T(8,128)(2,1)}, bf16[384,384]{1,0:T(8,128)(2,1)S(1)}, u32[]{:S(2)}, u32[]{:S(2)}) collective-permute-start(bf16[384,384]{1,0:T(8,128)(2,1)} %param.10), channel_id=1, source_target_pairs={{0,1},{1,0},{2,3},{3,2},{4,5},{5,4},{6,7},{7,6},{8,9},{9,8},{10,11... | collective-permute-start | bytes 884744 | tf_op jit(solution)/shard_map/ppermute | solution.py:145
  3.6 24.1 %collective-permute-start = (bf16[1024,384]{1,0:T(8,128)(2,1)}, bf16[1024,384]{1,0:T(8,128)(2,1)S(1)}, u32[]{:S(2)}, u32[]{:S(2)}) collective-permute-start(bf16[1024,384]{1,0:T(8,128)(2,1)} %param.9), channel_id=1, source_target_pairs={{0,1},{1,0},{2,3},{3,2},{4,5},{5,4},{6,7},{7,6},{8,9},{9,8},{10,11... | collective-permute-start | bytes 2359304 | tf_op jit(solution)/shard_map/ppermute | solution.py:145
  7.4 52.8 %copy-start.29 = (s32[512,1]{0,1:T(1,128)}, s32[512,1]{0,1:T(1,128)S(1)}, u32[]{:S(2)}) copy-start(s32[512,1]{0,1:T(1,128)S(1)} %get-tuple-element.95) | copy-start | bytes 6148
  7.4 54.8 %copy-start.27 = (s32[512,1]{0,1:T(1,128)}, s32[512,1]{0,1:T(1,128)S(1)}, u32[]{:S(2)}) copy-start(s32[512,1]{0,1:T(1,128)S(1)} %get-tuple-element.93) | copy-start | bytes 6148
  7.4 56.8 %copy-start.25 = (s32[512,1]{0,1:T(1,128)}, s32[512,1]{0,1:T(1,128)S(1)}, u32[]{:S(2)}) copy-start(s32[512,1]{0,1:T(1,128)S(1)} %get-tuple-element.91) | copy-start | bytes 6148
  7.4 73.7 %copy-start.37 = (s32[512,1]{0,1:T(1,128)}, s32[512,1]{0,1:T(1,128)S(1)}, u32[]{:S(2)}) copy-start(s32[512,1]{0,1:T(1,128)S(1)} %get-tuple-element.108) | copy-start | bytes 6148
  7.4 74.7 %copy-start.39 = (s32[512,1]{0,1:T(1,128)}, s32[512,1]{0,1:T(1,128)S(1)}, u32[]{:S(2)}) copy-start(s32[512,1]{0,1:T(1,128)S(1)} %get-tuple-element.109) | copy-start | bytes 6148
  7.4 75.7 %copy-start.33 = (s32[512,1]{0,1:T(1,128)}, s32[512,1]{0,1:T(1,128)S(1)}, u32[]{:S(2)}) copy-start(s32[512,1]{0,1:T(1,128)S(1)} %get-tuple-element.110) | copy-start | bytes 6148
  7.4 76.7 %copy-start.41 = (s32[512,1]{0,1:T(1,128)}, s32[512,1]{0,1:T(1,128)S(1)}, u32[]{:S(2)}) copy-start(s32[512,1]{0,1:T(1,128)S(1)} %get-tuple-element.111) | copy-start | bytes 6148
  7.4 79.1 %copy-start.43 = (s32[512,1]{0,1:T(1,128)}, s32[512,1]{0,1:T(1,128)S(1)}, u32[]{:S(2)}) copy-start(s32[512,1]{0,1:T(1,128)S(1)} %get-tuple-element.113) | copy-start | bytes 6148
  7.4 81.0 %copy-start.45 = (s32[512,1]{0,1:T(1,128)}, s32[512,1]{0,1:T(1,128)S(1)}, u32[]{:S(2)}) copy-start(s32[512,1]{0,1:T(1,128)S(1)} %get-tuple-element.115) | copy-start | bytes 6148
  8.1 58.0 %copy-start.31 = (s32[512]{0:T(512)}, s32[512]{0:T(512)S(1)}, u32[]{:S(2)}) copy-start(s32[512]{0:T(512)S(1)} %iota_add_fusion.1) | copy-start | bytes 6148
  8.9 23.3 %copy-start.35 = (s32[512]{0:T(512)}, s32[512]{0:T(512)S(1)}, u32[]{:S(2)}) copy-start(s32[512]{0:T(512)S(1)} %eq.177) | copy-start | bytes 6148
  11.4 17.0 %copy-start.7 = (bf16[1024,192]{0,1:T(8,128)(2,1)S(1)}, bf16[1024,192]{0,1:T(8,128)(2,1)}, u32[]{:S(2)}) copy-start(bf16[1024,192]{0,1:T(8,128)(2,1)} %param.15) | copy-start | bytes 1179652
  11.4 19.8 %copy-start.19 = (bf16[3,384,192]{1,2,0:T(8,128)(2,1)S(1)}, bf16[3,384,192]{1,2,0:T(8,128)(2,1)}, u32[]{:S(2)}) copy-start(bf16[3,384,192]{1,2,0:T(8,128)(2,1)} %param.11) | copy-start | bytes 1327108
  28.3 3.8 %copy-start.1 = (bf16[1024,384]{1,0:T(8,128)(2,1)}, bf16[1024,384]{1,0:T(8,128)(2,1)S(1)}, u32[]{:S(2)}) copy-start(bf16[1024,384]{1,0:T(8,128)(2,1)S(1)} %add_convert_fusion.1) | copy-start | bytes 2359300
  29.4 15.5 %collective-permute-start.2 = (bf16[1024,192]{1,0:T(8,128)(2,1)}, bf16[1024,192]{1,0:T(8,128)(2,1)}, u32[]{:S(2)}, u32[]{:S(2)}) collective-permute-start(bf16[1024,192]{1,0:T(8,128)(2,1)} %copy.163), channel_id=1, source_target_pairs={{0,1},{1,0},{2,3},{3,2},{4,5},{5,4},{6,7},{7,6},{8,9},{9,8},{10,11... | collective-permute-start | bytes 1179656 | tf_op jit(solution)/shard_map/ppermute | solution.py:145
  33.0 11.9 %copy-start.24 = (bf16[192,384]{1,0:T(8,128)(2,1)S(1)}, bf16[192,384]{1,0:T(8,128)(2,1)}, u32[]{:S(2)}) copy-start(bf16[192,384]{1,0:T(8,128)(2,1)} %param.12) | copy-start | bytes 442372
  34.1 23.6 %all-to-all-start = ((bf16[16,32,2,192]{3,2,1,0:T(2,128)(2,1)}), bf16[16,32,2,192]{3,2,1,0:T(2,128)(2,1)S(1)}, u32[]{:S(2)}, u32[]{:S(2)}) async-start(bf16[16,32,2,192]{3,2,1,0:T(2,128)(2,1)} %reshape.186), calls=%async_computation | async-start | bytes 1048576 | tf_op jit(solution)/shard_map/all_to_all | solution.py:264
  40.8 39.3 %copy-start.47 = (s32[512]{0:T(512)}, s32[512]{0:T(512)S(1)}, u32[]{:S(2)}) copy-start(s32[512]{0:T(512)S(1)} %iota_add_fusion) | copy-start | bytes 6148
  41.9 74.8 %collective-permute-start.5 = (bf16[192,192]{1,0:T(8,128)(2,1)}, bf16[192,192]{1,0:T(8,128)(2,1)}, u32[]{:S(2)}, u32[]{:S(2)}) collective-permute-start(bf16[192,192]{1,0:T(8,128)(2,1)} %bitcast.217), channel_id=1, source_target_pairs={{0,1},{1,0},{2,3},{3,2},{4,5},{5,4},{6,7},{7,6},{8,9},{9,8},{10,11... | collective-permute-start | bytes 221192 | tf_op jit(solution)/shard_map/ppermute | solution.py:248
  42.5 14.2 %collective-permute-start.3 = (bf16[3,384,192]{1,2,0:T(8,128)(2,1)}, bf16[3,384,192]{1,2,0:T(8,128)(2,1)S(1)}, u32[]{:S(2)}, u32[]{:S(2)}) collective-permute-start(bf16[3,384,192]{1,2,0:T(8,128)(2,1)} %param.11), channel_id=1, source_target_pairs={{0,1},{1,0},{2,3},{3,2},{4,5},{5,4},{6,7},{7,6},{8,9},{9,8},{10,11... | collective-permute-start | bytes 1327112 | tf_op jit(solution)/shard_map/ppermute | solution.py:145
  56.7 0.9 copy-start.49
  58.2 8.0 %copy-start.21 = (bf16[512,384]{0,1:T(8,128)(2,1)}, bf16[512,384]{0,1:T(8,128)(2,1)S(1)}, u32[]{:S(2)}) copy-start(bf16[512,384]{0,1:T(8,128)(2,1)S(1)} %copy.161) | copy-start | bytes 1179652
  78.2 1.9 copy-start.22
  89.8 1.0 copy-start.3
  90.0 1.3 copy-start.4
  93.5 2.2 copy-start.44
  95.7 1.9 copy-start.42
  97.6 1.9 copy-start.40
  103.1 1.4 copy-start.32
  103.9 2.6 %copy-start.9 = (bf16[2,24,8,512]{3,2,0,1:T(8,128)(2,1)}, bf16[2,24,8,512]{3,2,0,1:T(8,128)(2,1)S(1)}, u32[]{:S(2)}) copy-start(bf16[2,24,8,512]{3,2,0,1:T(8,128)(2,1)S(1)} %copy.275) | copy-start | bytes 1179652
  103.9 2.6 %copy-start.30 = (s32[512,1]{0,1:T(1,128)S(1)}, s32[512,1]{0,1:T(1,128)}, u32[]{:S(2)}) copy-start(s32[512,1]{0,1:T(1,128)} %copy-done.29) | copy-start | bytes 6148
  103.9 12.8 %collective-permute-start.4 = (bf16[1024,192]{0,1:T(8,128)(2,1)S(1)}, bf16[1024,192]{0,1:T(8,128)(2,1)S(1)}, u32[]{:S(2)}, u32[]{:S(2)}) collective-permute-start(bf16[1024,192]{0,1:T(8,128)(2,1)S(1)} %bitcast.250), channel_id=1, source_target_pairs={{0,1},{1,0},{2,3},{3,2},{4,5},{5,4},{6,7},{7,6},{8,9},{9,8},{10,11... | collective-permute-start | bytes 1179656 | tf_op jit(solution)/shard_map/ppermute | solution.py:145
  106.5 2.0 copy-start.28
  108.6 2.0 copy-start.26
  110.6 2.0 copy-start.38
  112.6 2.1 copy-start.48
  114.8 2.0 copy-start.6
  114.8 2.0 copy-start.34
  116.7 2.2 copy-start.23
  123.0 1.4 copy-start
  127.3 20.5 %all-to-all-start.1 = ((bf16[16,32,2,192]{3,2,1,0:T(2,128)(2,1)}), bf16[16,32,2,192]{3,2,1,0:T(2,128)(2,1)}, u32[]{:S(2)}, u32[]{:S(2)}) async-start(bf16[16,32,2,192]{3,2,1,0:T(2,128)(2,1)} %reshape.188), calls=%async_computation.1 | async-start | bytes 1048576 | tf_op jit(solution)/shard_map/all_to_all | solution.py:282
  134.5 2.9 %copy-start.10 = (bf16[2,24,8,512]{3,2,0,1:T(8,128)(2,1)S(1)}, bf16[2,24,8,512]{3,2,0,1:T(8,128)(2,1)}, u32[]{:S(2)}) copy-start(bf16[2,24,8,512]{3,2,0,1:T(8,128)(2,1)} %copy-done.9) | copy-start | bytes 1179652
  134.6 2.8 %copy-start.17 = (bf16[1024,192]{1,0:T(8,128)(2,1)S(1)}, bf16[1024,192]{1,0:T(8,128)(2,1)}, u32[]{:S(2)}) copy-start(bf16[1024,192]{1,0:T(8,128)(2,1)} %copy.164) | copy-start | bytes 1179652
  140.0 1.4 slice-start
  141.5 7.9 %copy-start.36 = (s32[512]{0:T(512)S(1)}, s32[512]{0:T(512)}, u32[]{:S(2)}) copy-start(s32[512]{0:T(512)} %copy-done.35) | copy-start | bytes 6148
  141.9 9.1 %copy-start.2 = (bf16[1024,384]{1,0:T(8,128)(2,1)S(1)}, bf16[1024,384]{1,0:T(8,128)(2,1)}, u32[]{:S(2)}) copy-start(bf16[1024,384]{1,0:T(8,128)(2,1)} %copy-done.1) | copy-start | bytes 2359300
  150.1 0.9 copy-start.13
  154.2 2.1 copy-start.12
  154.7 1.8 copy-start.8
  156.3 3.9 %collective-permute-start.6 = (f32[384,384]{1,0:T(8,128)S(1)}, f32[384,384]{1,0:T(8,128)}, u32[]{:S(2)}, u32[]{:S(2)}) collective-permute-start(f32[384,384]{1,0:T(8,128)S(1)} %broadcast_select_fusion.2), channel_id=1, source_target_pairs={{0,2},{2,0},{4,6},{6,4},{8,10},{10,8},{12,14},{14,12},{16,18},{18,... | collective-permute-start | bytes 1769480 | tf_op jit(solution)/shard_map/ppermute | solution.py:166
  158.7 29.0 %collective-permute-start.8 = (bf16[1024,3,192]{0,2,1:T(8,128)(2,1)}, bf16[1024,3,192]{0,2,1:T(8,128)(2,1)}, u32[]{:S(2)}, u32[]{:S(2)}) collective-permute-start(bf16[1024,3,192]{0,2,1:T(8,128)(2,1)} %pad_maximum_fusion.3), channel_id=1, source_target_pairs={{0,1},{1,0},{2,3},{3,2},{4,5},{5,4},{6,7},{7,6},{8,9},{9,8},{10,11... | collective-permute-start | bytes 3538952 | tf_op jit(solution)/shard_map/ppermute | solution.py:145
  161.4 14.1 %copy-start.14 = (bf16[1024,2,192]{0,2,1:T(8,128)(2,1)S(1)}, bf16[1024,2,192]{0,2,1:T(8,128)(2,1)}, u32[]{:S(2)}) copy-start(bf16[1024,2,192]{0,2,1:T(8,128)(2,1)} %copy-done.13) | copy-start | bytes 2359300
  161.5 9.2 %collective-permute-start.7 = (f32[192,384]{1,0:T(8,128)S(1)}, f32[192,384]{1,0:T(8,128)S(1)}, u32[]{:S(2)}, u32[]{:S(2)}) collective-permute-start(f32[192,384]{1,0:T(8,128)S(1)} %slice_select_fusion.1), channel_id=1, source_target_pairs={{0,4},{2,6},{4,0},{6,2},{8,12},{10,14},{12,8},{14,10},{16,20},{18,... | collective-permute-start | bytes 884744 | tf_op jit(solution)/shard_map/ppermute | solution.py:166
  171.4 16.3 %all-to-all-start.2 = ((f32[16,12,384]{2,1,0:T(8,128)}), f32[16,12,384]{2,1,0:T(8,128)S(1)}, u32[]{:S(2)}, u32[]{:S(2)}) async-start(f32[16,12,384]{2,1,0:T(8,128)} %reshape.190), calls=%async_computation.2 | async-start | bytes 786432 | tf_op jit(solution)/shard_map/all_to_all | solution.py:183
  175.6 12.2 %copy-start.18 = (bf16[1024,192]{1,0:T(8,128)(2,1)S(1)}, bf16[1024,192]{1,0:T(8,128)(2,1)}, u32[]{:S(2)}) copy-start(bf16[1024,192]{1,0:T(8,128)(2,1)} %copy.164) | copy-start | bytes 1179652
  187.8 3.5 %copy-start.5 = (bf16[1024,384]{1,0:T(8,128)(2,1)S(1)}, bf16[1024,384]{1,0:T(8,128)(2,1)}, u32[]{:S(2)}) copy-start(bf16[1024,384]{1,0:T(8,128)(2,1)} %param.9) | copy-start | bytes 2359300
  192.0 1.6 collective-permute-start.9
  193.7 6.0 %collective-permute-start.10 = (f32[96,384]{1,0:T(8,128)S(1)}, f32[96,384]{1,0:T(8,128)S(1)}, u32[]{:S(2)}, u32[]{:S(2)}) collective-permute-start(f32[96,384]{1,0:T(8,128)S(1)} %slice_select_fusion.2), channel_id=1, source_target_pairs={{0,4},{2,6},{4,0},{6,2},{8,12},{10,14},{12,8},{14,10},{16,20},{18,... | collective-permute-start | bytes 442376 | tf_op jit(solution)/shard_map/ppermute | solution.py:166
  232.5 12.3 %collective-permute-start.11 = (f32[1,16,18,384]{3,1,2,0:T(8,128)S(1)}, f32[1,16,18,384]{3,1,2,0:T(8,128)S(1)}, u32[]{:S(2)}, u32[]{:S(2)}) collective-permute-start(f32[1,16,18,384]{3,1,2,0:T(8,128)S(1)} %copy.200), channel_id=1, source_target_pairs={{0,4},{2,6},{4,0},{6,2},{8,12},{10,14},{12,8},{14,10},{16,20},{18,... | collective-permute-start | bytes 1327112 | tf_op jit(solution)/shard_map/ppermute | solution.py:166
  244.9 1.2 copy-start.11
  244.9 1.2 copy-start.20
  246.1 5.3 %collective-permute-start.12 = (f32[2,16,18,384]{3,1,2,0:T(8,128)}, f32[2,16,18,384]{3,1,2,0:T(8,128)}, u32[]{:S(2)}, u32[]{:S(2)}) collective-permute-start(f32[2,16,18,384]{3,1,2,0:T(8,128)} %copy.203), channel_id=1, source_target_pairs={{0,2},{2,0},{4,6},{6,4},{8,10},{10,8},{12,14},{14,12},{16,18},{18,... | collective-permute-start | bytes 2654216 | tf_op jit(solution)/shard_map/ppermute | solution.py:166
  (3 other events, 2.0 us)

commit v8 on v4

--- a/solution.py
+++ b/solution.py
@@ -39,13 +39,18 @@
     def forward_block(inputs):
         query_block, neighbour_block, first_row = inputs
         slot_rows, slot_live = slot_index(neighbour_block, first_row, block_rows)
-        pieces = [
-            jnp.dot(
-                pick_table(slot_rows[:, slot], ext_rows), flattened, preferred_element_type=f32
-            ).astype(bf16)
-            for slot in range(slot_width)
-        ]
-        gathered = jnp.stack(pieces, axis=1).reshape(block_rows, slot_width, 2, span)
+        own = lax.dynamic_slice_in_dim(flattened, first_row, block_rows, axis=0)
+        picks = pick_table(slot_rows[:, 1:].T.reshape(-1), ext_rows)
+        others = (
+            jnp.dot(picks, flattened, preferred_element_type=f32)
+            .astype(bf16)
+            .reshape(slot_width - 1, block_rows, 2 * span)
+        )
+        gathered = (
+            jnp.concatenate([own[None], others], axis=0)
+            .transpose(1, 0, 2)
+            .reshape(block_rows, slot_width, 2, span)
+        )
         block_keys = gathered[:, :, 0].reshape(block_rows, slot_width, heads_here, HD)
         block_values = gathered[:, :, 1].reshape(block_rows, slot_width, heads_here, HD)
         scores = (
@@ -115,13 +120,13 @@
             .reshape(block_rows, slot_width, 2 * span)
             .astype(bf16)
         )
-        for slot in range(slot_width):
-            carried = carried + jnp.einsum(
-                "bx,bc->xc",
-                pick_table(slot_rows[:, slot], ext_rows),
-                contribution[:, slot],
-                preferred_element_type=f32,
-            )
+        picks = pick_table(slot_rows[:, 1:].T.reshape(-1), ext_rows)
+        rest = contribution[:, 1:].transpose(1, 0, 2).reshape(-1, 2 * span)
+        carried = carried + jnp.einsum("bx,bc->xc", picks, rest, preferred_element_type=f32)
+        own_rows = lax.dynamic_slice_in_dim(carried, first_row, block_rows, axis=0)
+        carried = lax.dynamic_update_slice_in_dim(
+            carried, own_rows + contribution[:, 0].astype(f32), first_row, axis=0
+        )
         return (carried, grad_query)
 
     carried = jnp.zeros((ext_rows, 2 * span), f32)

time: 252 us -> 295 us (1.17)
  local copies, waits for them, and re-layouts: 24.2 us -> 69.6 us
  matrix products: 78.7 us -> 62 us
  other arithmetic: 19.3 us -> 30.6 us
    dot_general x36 -> x4, matrix products: 55.2 us -> 37.9 us  [the longest x2 21.6 us: backward_block(): jnp.einsum('bx,bc->xc', picks, rest, preferred_element_type=f32)]
    transpose x0 -> x4, local copies, waits for them, and re-layouts: none -> 13.5 us  [backward_block(): rest = contribution[:, 1:].transpose(1, 0, 2).reshape(-1, 2 * span)]
    reshape x0 -> x2, local copies, waits for them, and re-layouts: none -> 8.02 us  [forward_block(): others = jnp.dot(picks, flattened, preferred_element_type=f32).astype(bf1...]
    unnamed x118 -> x80, local copies, waits for them, and re-layouts: 7.27 us -> 15.1 us
    dynamic_update_slice x0 -> x2, local copies, waits for them, and re-layouts: none -> 6.26 us  [backward_block(): lax.dynamic_update_slice_in_dim(carried, own_rows + contribution[:, 0].as...]
    add x2 -> x3, other arithmetic: 1.3 us -> 5.87 us  [the longest x2 3.2 us: backward_block(): own_rows + contribution[:, 0].astype(f32)]
    slice x1 -> x2, local copies, waits for them, and re-layouts: 0.02 us -> 3.53 us  [backward_block(): contribution[:, 0].astype(f32)]
    concatenate x0 -> x2, other arithmetic: none -> 3.5 us  [forward_block(): jnp.concatenate([own[None], others], axis=0).transpose(1, 0, 2)]
  transfers between devices with their start and end apart: 13 -> 13, of which waited for: 7 -> 6; matrix products, arithmetic and copies ran while one was open for 36% -> 43% of each run, Pallas kernels for 0% -> 0%
where the time goes in v8:
time: 295 us; the launch traced here: 289 us
  local copies, waits for them, and re-layouts  69.6 us (24%)
  matrix products  62 us (21%)
  waiting for transfers between devices  51.9 us (18%)
  blocking collectives  43.4 us (15%)
  other arithmetic  30.6 us (10%)
  starting transfers between devices  26.4 us (9%)
  between operations  5.67 us (2%)
    ppermute x6, waiting for transfers between devices, ch_exchange(): lax.ppermute(value, 'ch', [(i, (i + shift) % size) for i in range(size)])  33.7 us
    all_to_all x1, blocking collectives, pix_gather(): lax.all_to_all(spread.reshape(size, total, width), 'pix', 0, 0, tiled=True)  27.3 us
    dot_general x2, matrix products, backward_block(): jnp.einsum('bx,bc->xc', picks, rest, preferred_element_type=f32)  21.6 us
    dot_general x2, matrix products, forward_block(): jnp.dot(picks, flattened, preferred_element_type=f32).astype(bf16)  16.4 us
    all_to_all x1, blocking collectives, pix_scatter(): lax.all_to_all(mine.reshape(size, chunk, width), 'pix', 0, 0, tiled=True)  16.1 us
    unnamed x80, local copies, waits for them, and re-layouts  15.1 us
    transpose x4, local copies, waits for them, and re-layouts, backward_block(): rest = contribution[:, 1:].transpose(1, 0, 2).reshape(-1, 2 * span)  13.5 us
    all_to_all x1, waiting for transfers between devices, pix_scatter(): lax.all_to_all(mine.reshape(size, chunk, width), 'pix', 0, 0, tiled=True)  12.4 us
  transfers between devices with their start and end apart: 13, of which 6 were waited for; matrix products, arithmetic and copies ran while one was open for 43% of the time, Pallas kernels for 0%

profile of v8, /device:TPU:0, one launch (start us, length us, event | category | flops | bytes accessed | tf_op | source)
XLA Modules:
  0.0 289.5 jit_solution(15776491879617881513)
XLA Ops:
  0.6 3.0 %collective-permute-start = (bf16[1024,384]{1,0:T(8,128)(2,1)}, bf16[1024,384]{1,0:T(8,128)(2,1)S(1)}, u32[]{:S(2)}, u32[]{:S(2)}) collective-permute-start(bf16[1024,384]{1,0:T(8,128)(2,1)} %param.9), channel_id=1, source_target_pairs={{0,1},{1,0},{2,3},{3,2},{4,5},{5,4},{6,7},{7,6},{8,9},{9,8},{10,11... | collective-permute-start | bytes 2359304 | tf_op jit(solution)/shard_map/ppermute | solution.py:150
  3.7 1.1 reshape.159
  4.8 1.2 broadcast_select_fusion
  8.2 1.8 fusion.50
  10.0 17.7 %collective-permute-done.1 = bf16[384,384]{1,0:T(8,128)(2,1)S(1)} collective-permute-done((bf16[384,384]{1,0:T(8,128)(2,1)}, bf16[384,384]{1,0:T(8,128)(2,1)S(1)}, u32[]{:S(2)}, u32[]{:S(2)}) %collective-permute-start.1) | collective-permute-done | bytes 294944 | tf_op jit(solution)/shard_map/ppermute | solution.py:150
  29.4 1.7 collective-permute-start.2
  33.0 1.1 reshape.160
  34.1 6.2 %all-to-all-start = ((bf16[16,32,2,192]{3,2,1,0:T(2,128)(2,1)}), bf16[16,32,2,192]{3,2,1,0:T(2,128)(2,1)}, u32[]{:S(2)}, u32[]{:S(2)}) async-start(bf16[16,32,2,192]{3,2,1,0:T(2,128)(2,1)} %reshape.160), calls=%async_computation | async-start | bytes 1048576 | tf_op jit(solution)/shard_map/all_to_all | solution.py:262
  47.4 1.5 collective-permute-start.3
  49.7 2.3 convolution_convert_fusion.1
  52.0 9.7 %collective-permute-done.3 = bf16[3,384,192]{1,2,0:T(8,128)(2,1)S(1)} collective-permute-done((bf16[3,384,192]{1,2,0:T(8,128)(2,1)}, bf16[3,384,192]{1,2,0:T(8,128)(2,1)S(1)}, u32[]{:S(2)}, u32[]{:S(2)}) %collective-permute-start.3) | collective-permute-done | bytes 442400 | tf_op jit(solution)/shard_map/ppermute | solution.py:150
  63.4 1.4 concatenate.44
  64.8 1.8 fusion.30
  68.5 8.1 %fusion.8 = bf16[4096,384]{1,0:T(8,128)(2,1)} fusion(s32[4096]{0:T(1024)S(1)} %bitcast.189, bf16[512,384]{1,0:T(8,128)(2,1)S(1)} %concatenate.44, bf16[1024,384]{1,0:T(8,128)(2,1)S(1)} %copy.94), kind=kOutput, calls=%fused_computation.10 | convolution fusion | flops 4842061824 | bytes 4341760 | tf_op jit(solution)/shard_map/dot_general | solution.py:45
  76.7 3.2 %copy.96 = bf16[8,512,384]{1,2,0:T(8,128)(2,1)S(1)} copy(bf16[8,512,384]{2,1,0:T(8,128)(2,1)} %bitcast.168) | data formatting | bytes 6291456 | tf_op jit(solution)/shard_map/reshape | solution.py:47
  79.9 1.3 pad_maximum_fusion
  85.5 1.8 copy-done.2
  87.2 1.9 slice_bitcast_fusion.1
  89.1 5.0 %copy.103 = bf16[8,512,384]{2,1,0:T(8,128)(2,1)} copy(bf16[8,512,384]{1,2,0:T(8,128)(2,1)} %slice_bitcast_fusion.1) | data formatting | bytes 6291456 | tf_op jit(solution)/shard_map/transpose | solution.py:124
  94.2 10.8 %fusion.2 = f32[1536,384]{1,0:T(8,128)} fusion(bf16[4096,384]{1,0:T(8,128)(2,1)} %bitcast.165, s32[4096]{0:T(1024)S(1)} %bitcast.190), kind=kOutput, calls=%fused_computation.4 | convolution fusion | flops 4838129664 | bytes 5521408 | tf_op jit(solution)/shard_map/bx,bc->xc/dot_general | solution.py:125
  105.0 8.2 %fusion.9 = bf16[4096,384]{1,0:T(8,128)(2,1)} fusion(s32[4096]{0:T(1024)S(1)} %bitcast.187, bf16[512,384]{1,0:T(8,128)(2,1)S(1)} %copy-done.16, bf16[1024,384]{1,0:T(8,128)(2,1)S(1)} %copy-done.12), kind=kOutput, calls=%fused_computation.11 | convolution fusion | flops 4842061824 | bytes 4341760 | tf_op jit(solution)/shard_map/dot_general | solution.py:45
  113.2 4.8 %copy.98 = bf16[8,512,384]{1,2,0:T(8,128)(2,1)} copy(bf16[8,512,384]{2,1,0:T(8,128)(2,1)} %bitcast.166) | data formatting | bytes 6291456 | tf_op jit(solution)/shard_map/reshape | solution.py:47
  118.1 2.2 pad_maximum_fusion.1
  126.2 1.8 copy-done.3
  128.0 2.0 slice_bitcast_fusion
  130.0 4.6 %copy.108 = bf16[8,512,384]{2,1,0:T(8,128)(2,1)} copy(bf16[8,512,384]{1,2,0:T(8,128)(2,1)} %slice_bitcast_fusion) | data formatting | bytes 6291456 | tf_op jit(solution)/shard_map/transpose | solution.py:124
  134.6 10.8 %fusion = f32[1536,384]{1,0:T(8,128)} fusion(bf16[4096,384]{1,0:T(8,128)(2,1)} %bitcast.167, s32[4096]{0:T(1024)S(1)} %bitcast.188), kind=kOutput, calls=%fused_computation.1 | convolution fusion | flops 4838129664 | bytes 5521408 | tf_op jit(solution)/shard_map/bx,bc->xc/dot_general | solution.py:125
  145.3 1.8 slice.175
  147.1 1.9 copy.169
  149.1 2.2 convert_add_fusion.1
  151.3 1.8 slice.177
  153.0 3.1 %dynamic_update_slice.6 = f32[1536,384]{1,0:T(8,128)} dynamic-update-slice(f32[1536,384]{1,0:T(8,128)} %fusion.2, f32[512,384]{1,0:T(8,128)} %convert_add_fusion.1, s32[]{:T(128)S(6)} %select_n.102, s32[]{:T(128)} %constant.27.clone.1) | dynamic-update-slice | bytes 1572868 | tf_op jit(solution)/shard_map/dynamic_update_slice | solution.py:127
  156.2 1.9 copy.170
  158.1 2.7 add.70
  160.8 1.4 copy-done.4
  163.2 3.1 %dynamic_update_slice.7 = f32[1536,384]{1,0:T(8,128)} dynamic-update-slice(f32[1536,384]{1,0:T(8,128)} %copy-done.4, f32[512,384]{1,0:T(8,128)} %convert_add_fusion, s32[]{:T(128)S(6)} %select_n.106, s32[]{:T(128)} %constant.27.clone.1) | dynamic-update-slice | bytes 1572868 | tf_op jit(solution)/shard_map/dynamic_update_slice | solution.py:127
  166.3 1.9 slice.179
  168.2 2.1 reshape.168
  170.3 6.0 %all-to-all-start.1 = ((bf16[16,32,2,192]{3,2,1,0:T(2,128)(2,1)}), bf16[16,32,2,192]{3,2,1,0:T(2,128)(2,1)}, u32[]{:S(2)}, u32[]{:S(2)}) async-start(bf16[16,32,2,192]{3,2,1,0:T(2,128)(2,1)} %reshape.168), calls=%async_computation.1 | async-start | bytes 1048576 | tf_op jit(solution)/shard_map/all_to_all | solution.py:280
  176.3 1.2 multiply_reduce_fusion.2
  177.6 1.2 multiply_reduce_fusion
  180.3 3.1 %convolution_multiply_fusion.2 = f32[192,384]{1,0:T(8,128)} fusion(bf16[1024,192]{0,1:T(8,128)(2,1)} %bitcast.89, bf16[1024,192]{1,0:T(8,128)(2,1)} %copy.101, bf16[1024,192]{1,0:T(8,128)(2,1)} %collective-permute-done.2, pred[]{:T(512)S(6)} %eq.87), kind=kOutput, calls=%fused_computation.59 | convolution fusion | flops 154607616 | bytes 1474561 | tf_op jit(solution)/shard_map/dot_general | solution.py:270
  183.4 1.3 slice.178
  184.7 1.9 copy.111
  186.6 4.2 %all-to-all-done.1 = bf16[16,32,2,192]{3,2,1,0:T(2,128)(2,1)} async-done(((bf16[16,32,2,192]{3,2,1,0:T(2,128)(2,1)}), bf16[16,32,2,192]{3,2,1,0:T(2,128)(2,1)}, u32[]{:S(2)}, u32[]{:S(2)}) %all-to-all-start.1) | async-done | bytes 393248 | tf_op jit(solution)/shard_map/all_to_all | solution.py:280
  190.8 1.4 convert_element_type.131
  193.2 2.1 fusion.22
  196.4 1.1 broadcast_select_fusion.2
  197.7 1.1 pad_maximum_fusion.5
  198.9 1.5 collective-permute-start.7
  201.3 4.3 %all-to-all-start.2 = ((f32[16,24,384]{2,1,0:T(8,128)}), f32[16,24,384]{2,1,0:T(8,128)S(1)}, u32[]{:S(2)}, u32[]{:S(2)}) async-start(f32[16,24,384]{2,1,0:T(8,128)} %bitcast.69), calls=%async_computation.2 | async-start | bytes 1179648 | tf_op jit(solution)/shard_map/all_to_all | solution.py:182
  205.6 3.2 %fusion.42 = f32[1024,384,1]{1,0,2:T(8,128)} fusion(bf16[3,384,192]{1,2,0:T(8,128)(2,1)} %param.11, bf16[1024,2,192]{0,2,1:T(8,128)(2,1)S(1)} %copy-done.23, bf16[1024,1,192]{0,2,1:T(8,128)(2,1)S(1)} %copy-done.18), kind=kOutput, calls=%fused_computation.109 | convolution fusion | flops 453574656 | bytes 3194880 | tf_op jit(solution)/shard_map/rkd,kcd->rc/dot_general | solution.py:298
  208.7 12.4 %all-to-all-done.2 = f32[16,24,384]{2,1,0:T(8,128)S(1)} async-done(((f32[16,24,384]{2,1,0:T(8,128)}), f32[16,24,384]{2,1,0:T(8,128)S(1)}, u32[]{:S(2)}, u32[]{:S(2)}) %all-to-all-start.2) | async-done | bytes 589856 | tf_op jit(solution)/shard_map/all_to_all | solution.py:182
  221.2 6.3 %collective-permute-done.7 = bf16[1024,3,192]{0,2,1:T(8,128)(2,1)} collective-permute-done((bf16[1024,3,192]{0,2,1:T(8,128)(2,1)}, bf16[1024,3,192]{0,2,1:T(8,128)(2,1)}, u32[]{:S(2)}, u32[]{:S(2)}) %collective-permute-start.7) | collective-permute-done | bytes 1179680 | tf_op jit(solution)/shard_map/ppermute | solution.py:150
  227.5 3.7 %fusion.18 = bf16[1024,384]{1,0:T(8,128)(2,1)S(1)} fusion(f32[1024,384,1]{1,0,2:T(8,128)} %fusion.42, bf16[1024,3,192]{0,2,1:T(8,128)(2,1)} %collective-permute-done.7, bf16[3,384,192]{1,2,0:T(8,128)(2,1)} %copy-done.35, bf16[1024,192]{1,0:T(8,128)(2,1)} %collective-permute-done.2, bf16[1024,192]{1,0:T(8,128)(2,1)} %copy.101, pred[]{:T(512)S(6)} %eq.87), kind=kOutput, calls=%fused_computation.42 | convolution fusion | flops 458096640 | bytes 4767745 | tf_op jit(solution)/shard_map/rkd,kcd->rc/dot_general | solution.py:302
  232.0 1.6 collective-permute-done.8
  233.6 16.1 %all_to_all.25 = f32[16,12,384]{2,1,0:T(8,128)S(1)} all-to-all(f32[16,12,384]{2,1,0:T(8,128)S(1)} %reshape.172), channel_id=1, replica_groups=mesh['pix'=16,'ch'=2] {'pix'}, dimensions={0} | all-to-all | bytes 589824 | tf_op jit(solution)/shard_map/all_to_all | solution.py:182
  249.8 27.3 %all_to_all.26 = f32[16,36,384]{2,1,0:T(8,128)S(1)} all-to-all(f32[16,36,384]{2,1,0:T(8,128)S(1)} %bitcast.164), channel_id=1, replica_groups=mesh['pix'=16,'ch'=2] {'pix'}, dimensions={0} | all-to-all | bytes 1769472 | tf_op jit(solution)/shard_map/all_to_all | solution.py:193
  277.1 1.1 copy.115
  279.0 1.4 fusion.33
  280.4 1.5 fusion.23
  282.8 1.5 convolution_convert_fusion
  284.3 1.5 copy_select_fusion.1
  287.1 1.3 copy.119
  (162 shorter events, 33.9 us)
Async XLA Ops:
  0.6 27.1 %collective-permute-start = (bf16[1024,384]{1,0:T(8,128)(2,1)}, bf16[1024,384]{1,0:T(8,128)(2,1)S(1)}, u32[]{:S(2)}, u32[]{:S(2)}) collective-permute-start(bf16[1024,384]{1,0:T(8,128)(2,1)} %param.9), channel_id=1, source_target_pairs={{0,1},{1,0},{2,3},{3,2},{4,5},{5,4},{6,7},{7,6},{8,9},{9,8},{10,11... | collective-permute-start | bytes 2359304 | tf_op jit(solution)/shard_map/ppermute | solution.py:150
  3.6 24.1 %collective-permute-start.1 = (bf16[384,384]{1,0:T(8,128)(2,1)}, bf16[384,384]{1,0:T(8,128)(2,1)S(1)}, u32[]{:S(2)}, u32[]{:S(2)}) collective-permute-start(bf16[384,384]{1,0:T(8,128)(2,1)} %param.10), channel_id=1, source_target_pairs={{0,1},{1,0},{2,3},{3,2},{4,5},{5,4},{6,7},{7,6},{8,9},{9,8},{10,11... | collective-permute-start | bytes 884744 | tf_op jit(solution)/shard_map/ppermute | solution.py:150
  7.5 24.7 %copy-start.33 = (s32[512]{0:T(512)}, s32[512]{0:T(512)S(1)}, u32[]{:S(2)}) copy-start(s32[512]{0:T(512)S(1)} %eq.33) | copy-start | bytes 6148
  10.0 18.4 %copy-start.14 = (bf16[1024,192]{0,1:T(8,128)(2,1)S(1)}, bf16[1024,192]{0,1:T(8,128)(2,1)}, u32[]{:S(2)}) copy-start(bf16[1024,192]{0,1:T(8,128)(2,1)} %param.15) | copy-start | bytes 1179652
  10.0 21.1 %copy-start.26 = (bf16[3,384,192]{1,2,0:T(8,128)(2,1)S(1)}, bf16[3,384,192]{1,2,0:T(8,128)(2,1)}, u32[]{:S(2)}) copy-start(bf16[3,384,192]{1,2,0:T(8,128)(2,1)} %param.11) | copy-start | bytes 1327108
  28.3 3.8 %copy-start.6 = (bf16[1024,384]{1,0:T(8,128)(2,1)}, bf16[1024,384]{1,0:T(8,128)(2,1)S(1)}, u32[]{:S(2)}) copy-start(bf16[1024,384]{1,0:T(8,128)(2,1)S(1)} %add_convert_fusion.1) | copy-start | bytes 2359300
  29.4 20.3 %collective-permute-start.2 = (bf16[1024,192]{1,0:T(8,128)(2,1)}, bf16[1024,192]{1,0:T(8,128)(2,1)}, u32[]{:S(2)}, u32[]{:S(2)}) collective-permute-start(bf16[1024,192]{1,0:T(8,128)(2,1)} %copy.100), channel_id=1, source_target_pairs={{0,1},{1,0},{2,3},{3,2},{4,5},{5,4},{6,7},{7,6},{8,9},{9,8},{10,11... | collective-permute-start | bytes 1179656 | tf_op jit(solution)/shard_map/ppermute | solution.py:150
  34.1 29.4 %all-to-all-start = ((bf16[16,32,2,192]{3,2,1,0:T(2,128)(2,1)}), bf16[16,32,2,192]{3,2,1,0:T(2,128)(2,1)}, u32[]{:S(2)}, u32[]{:S(2)}) async-start(bf16[16,32,2,192]{3,2,1,0:T(2,128)(2,1)} %reshape.160), calls=%async_computation | async-start | bytes 1048576 | tf_op jit(solution)/shard_map/all_to_all | solution.py:262
  44.4 24.1 %copy-start.31 = (s32[1,4,8,128]{3,1,2,0:T(4,128)}, s32[1,4,8,128]{3,1,2,0:T(4,128)S(1)}, u32[]{:S(2)}) copy-start(s32[1,4,8,128]{3,1,2,0:T(4,128)S(1)} %copy.182) | copy-start | bytes 49156
  46.7 21.8 %copy-start.11 = (bf16[1024,384]{1,0:T(8,128)(2,1)}, bf16[1024,384]{1,0:T(8,128)(2,1)S(1)}, u32[]{:S(2)}) copy-start(bf16[1024,384]{1,0:T(8,128)(2,1)S(1)} %copy.94) | copy-start | bytes 2359300
  46.7 111.3 %collective-permute-start.5 = (bf16[192,192]{1,0:T(8,128)(2,1)}, bf16[192,192]{1,0:T(8,128)(2,1)}, u32[]{:S(2)}, u32[]{:S(2)}) collective-permute-start(bf16[192,192]{1,0:T(8,128)(2,1)} %bitcast.148), channel_id=1, source_target_pairs={{0,1},{1,0},{2,3},{3,2},{4,5},{5,4},{6,7},{7,6},{8,9},{9,8},{10,11... | collective-permute-start | bytes 221192 | tf_op jit(solution)/shard_map/ppermute | solution.py:246
  47.4 14.4 %collective-permute-start.3 = (bf16[3,384,192]{1,2,0:T(8,128)(2,1)}, bf16[3,384,192]{1,2,0:T(8,128)(2,1)S(1)}, u32[]{:S(2)}, u32[]{:S(2)}) collective-permute-start(bf16[3,384,192]{1,2,0:T(8,128)(2,1)} %param.11), channel_id=1, source_target_pairs={{0,1},{1,0},{2,3},{3,2},{4,5},{5,4},{6,7},{7,6},{8,9},{9,8},{10,11... | collective-permute-start | bytes 1327112 | tf_op jit(solution)/shard_map/ppermute | solution.py:150
  61.7 4.9 %copy-start.35 = (bf16[3,384,192]{1,2,0:T(8,128)(2,1)}, bf16[3,384,192]{1,2,0:T(8,128)(2,1)S(1)}, u32[]{:S(2)}) copy-start(bf16[3,384,192]{1,2,0:T(8,128)(2,1)S(1)} %collective-permute-done.3) | copy-start | bytes 1327108
  64.8 11.9 %copy-start.15 = (bf16[512,384]{1,0:T(8,128)(2,1)}, bf16[512,384]{1,0:T(8,128)(2,1)S(1)}, u32[]{:S(2)}) copy-start(bf16[512,384]{1,0:T(8,128)(2,1)S(1)} %concatenate.44) | copy-start | bytes 1179652
  81.2 1.0 copy-start.10
  81.4 2.0 copy-start
  84.1 1.4 copy-start.24
  85.4 1.8 copy-start.2
  89.1 5.0 %copy-start.32 = (s32[1,4,8,128]{3,1,2,0:T(4,128)S(1)}, s32[1,4,8,128]{3,1,2,0:T(4,128)}, u32[]{:S(2)}) copy-start(s32[1,4,8,128]{3,1,2,0:T(4,128)} %copy-done.31) | copy-start | bytes 49156
  94.1 10.8 %copy-start.12 = (bf16[1024,384]{1,0:T(8,128)(2,1)S(1)}, bf16[1024,384]{1,0:T(8,128)(2,1)}, u32[]{:S(2)}) copy-start(bf16[1024,384]{1,0:T(8,128)(2,1)} %copy-done.11) | copy-start | bytes 2359300
  94.1 10.8 %copy-start.16 = (bf16[512,384]{1,0:T(8,128)(2,1)S(1)}, bf16[512,384]{1,0:T(8,128)(2,1)}, u32[]{:S(2)}) copy-start(bf16[512,384]{1,0:T(8,128)(2,1)} %copy-done.15) | copy-start | bytes 1179652
  94.2 10.8 %copy-start.29 = (s32[1,4,8,128]{3,1,2,0:T(4,128)S(1)}, s32[1,4,8,128]{3,1,2,0:T(4,128)}, u32[]{:S(2)}) copy-start(s32[1,4,8,128]{3,1,2,0:T(4,128)} %copy.183) | copy-start | bytes 49156
  113.2 4.9 %copy-start.17 = (bf16[1,512,384]{1,2,0:T(8,128)(2,1)S(1)}, bf16[1,512,384]{1,2,0:T(8,128)(2,1)}, u32[]{:S(2)}) copy-start(bf16[1,512,384]{1,2,0:T(8,128)(2,1)} %copy.97) | copy-start | bytes 1179652
  120.3 1.0 copy-start.8
  120.3 1.1 copy-start.9
  120.6 2.0 copy-start.1
  120.6 2.0 copy-start.28
  123.1 2.3 copy-start.25
  124.3 33.8 %collective-permute-start.4 = (bf16[1024,192]{0,1:T(8,128)(2,1)}, bf16[1024,192]{0,1:T(8,128)(2,1)}, u32[]{:S(2)}, u32[]{:S(2)}) collective-permute-start(bf16[1024,192]{0,1:T(8,128)(2,1)} %bitcast.89), channel_id=1, source_target_pairs={{0,1},{1,0},{2,3},{3,2},{4,5},{5,4},{6,7},{7,6},{8,9},{9,8},{10,11... | collective-permute-start | bytes 1179656 | tf_op jit(solution)/shard_map/ppermute | solution.py:150
  126.2 1.8 copy-start.3
  130.0 4.6 %copy-start.30 = (s32[1,4,8,128]{3,1,2,0:T(4,128)S(1)}, s32[1,4,8,128]{3,1,2,0:T(4,128)}, u32[]{:S(2)}) copy-start(s32[1,4,8,128]{3,1,2,0:T(4,128)} %copy.183) | copy-start | bytes 49156
  158.1 4.1 %copy-start.19 = (bf16[512,1,384]{2,0,1:T(8,128)(2,1)S(1)}, bf16[512,1,384]{2,0,1:T(8,128)(2,1)}, u32[]{:S(2)}) copy-start(bf16[512,1,384]{2,0,1:T(8,128)(2,1)} %copy.170) | copy-start | bytes 1179652
  160.8 1.4 copy-start.4
  170.3 20.5 %all-to-all-start.1 = ((bf16[16,32,2,192]{3,2,1,0:T(2,128)(2,1)}), bf16[16,32,2,192]{3,2,1,0:T(2,128)(2,1)}, u32[]{:S(2)}, u32[]{:S(2)}) async-start(bf16[16,32,2,192]{3,2,1,0:T(2,128)(2,1)} %reshape.168), calls=%async_computation.1 | async-start | bytes 1048576 | tf_op jit(solution)/shard_map/all_to_all | solution.py:280
  179.3 4.1 %copy-start.5 = (f32[1536,384]{1,0:T(8,128)S(1)}, f32[1536,384]{1,0:T(8,128)}, u32[]{:S(2)}) copy-start(f32[1536,384]{1,0:T(8,128)} %dynamic_update_slice.7) | copy-start | bytes 7077892
  184.7 7.7 %copy-start.34 = (s32[512]{0:T(512)S(1)}, s32[512]{0:T(512)}, u32[]{:S(2)}) copy-start(s32[512]{0:T(512)} %copy-done.33) | copy-start | bytes 6148
  186.6 6.6 %copy-start.7 = (bf16[1024,384]{1,0:T(8,128)(2,1)S(1)}, bf16[1024,384]{1,0:T(8,128)(2,1)}, u32[]{:S(2)}) copy-start(bf16[1024,384]{1,0:T(8,128)(2,1)} %copy-done.6) | copy-start | bytes 2359300
  193.2 2.1 copy-start.22
  196.4 1.3 copy-start.18
  196.4 1.3 copy-start.23
  196.4 4.0 %copy-start.20 = (f32[192,384]{1,0:T(8,128)S(1)}, f32[192,384]{1,0:T(8,128)}, u32[]{:S(2)}) copy-start(f32[192,384]{1,0:T(8,128)} %convolution_multiply_fusion.2) | copy-start | bytes 884740
  197.6 2.8 collective-permute-start.6
  198.9 28.6 %collective-permute-start.7 = (bf16[1024,3,192]{0,2,1:T(8,128)(2,1)}, bf16[1024,3,192]{0,2,1:T(8,128)(2,1)}, u32[]{:S(2)}, u32[]{:S(2)}) collective-permute-start(bf16[1024,3,192]{0,2,1:T(8,128)(2,1)} %pad_maximum_fusion.5), channel_id=1, source_target_pairs={{0,1},{1,0},{2,3},{3,2},{4,5},{5,4},{6,7},{7,6},{8,9},{9,8},{10,11... | collective-permute-start | bytes 3538952 | tf_op jit(solution)/shard_map/ppermute | solution.py:150
  201.3 19.9 %all-to-all-start.2 = ((f32[16,24,384]{2,1,0:T(8,128)}), f32[16,24,384]{2,1,0:T(8,128)S(1)}, u32[]{:S(2)}, u32[]{:S(2)}) async-start(f32[16,24,384]{2,1,0:T(8,128)} %bitcast.69), calls=%async_computation.2 | async-start | bytes 1179648 | tf_op jit(solution)/shard_map/all_to_all | solution.py:182
  221.2 10.0 %copy-start.13 = (bf16[1024,384]{1,0:T(8,128)(2,1)S(1)}, bf16[1024,384]{1,0:T(8,128)(2,1)}, u32[]{:S(2)}) copy-start(bf16[1024,384]{1,0:T(8,128)(2,1)} %param.9) | copy-start | bytes 2359300
  231.9 1.6 collective-permute-start.8
  249.8 29.2 %copy-start.27 = (bf16[192,1,192]{2,1,0:T(2,128)(2,1)S(1)}, bf16[192,1,192]{2,1,0:T(2,128)(2,1)}, u32[]{:S(2)}) copy-start(bf16[192,1,192]{2,1,0:T(2,128)(2,1)} %get-tuple-element.88) | copy-start | bytes 221188
  278.2 6.1 %collective-permute-start.9 = (f32[16,36,384]{2,0,1:T(8,128)}, f32[16,36,384]{2,0,1:T(8,128)}, u32[]{:S(2)}, u32[]{:S(2)}) collective-permute-start(f32[16,36,384]{2,0,1:T(8,128)} %copy.115), channel_id=1, source_target_pairs={{0,2},{2,0},{4,6},{6,4},{8,10},{10,8},{12,14},{14,12},{16,18},{18,... | collective-permute-start | bytes 2654216 | tf_op jit(solution)/shard_map/ppermute | solution.py:168
  279.0 3.8 %copy-start.21 = (bf16[384,384]{1,0:T(8,128)(2,1)S(1)}, bf16[384,384]{1,0:T(8,128)(2,1)}, u32[]{:S(2)}) copy-start(bf16[384,384]{1,0:T(8,128)(2,1)} %param.10) | copy-start | bytes 884740

commit v9 on v8

--- a/solution.py
+++ b/solution.py
@@ -39,23 +39,17 @@
     def forward_block(inputs):
         query_block, neighbour_block, first_row = inputs
         slot_rows, slot_live = slot_index(neighbour_block, first_row, block_rows)
-        own = lax.dynamic_slice_in_dim(flattened, first_row, block_rows, axis=0)
-        picks = pick_table(slot_rows[:, 1:].T.reshape(-1), ext_rows)
-        others = (
+        picks = pick_table(slot_rows.T.reshape(-1), ext_rows)
+        gathered = (
             jnp.dot(picks, flattened, preferred_element_type=f32)
             .astype(bf16)
-            .reshape(slot_width - 1, block_rows, 2 * span)
-        )
-        gathered = (
-            jnp.concatenate([own[None], others], axis=0)
-            .transpose(1, 0, 2)
-            .reshape(block_rows, slot_width, 2, span)
-        )
-        block_keys = gathered[:, :, 0].reshape(block_rows, slot_width, heads_here, HD)
-        block_values = gathered[:, :, 1].reshape(block_rows, slot_width, heads_here, HD)
+            .reshape(slot_width, block_rows, 2, span)
+        )
+        block_keys = gathered[:, :, 0].reshape(slot_width, block_rows, heads_here, HD)
+        block_values = gathered[:, :, 1].reshape(slot_width, block_rows, heads_here, HD)
         scores = (
             jnp.einsum(
-                "bhd,bmhd->bhm",
+                "bhd,mbhd->bhm",
                 query_block.reshape(block_rows, heads_here, HD),
                 block_keys,
                 preferred_element_type=f32,
@@ -68,7 +62,7 @@
         raised = jnp.where(shut, jnp.exp(masked - largest), 0.0)
         probabilities = raised / jnp.sum(raised, axis=2, keepdims=True)
         weights = probabilities.astype(bf16)
-        mixture = jnp.einsum("bhm,bmhd->bhd", weights, block_values, preferred_element_type=f32)
+        mixture = jnp.einsum("bhm,mbhd->bhd", weights, block_values, preferred_element_type=f32)
         return (mixture.reshape(block_rows, span).astype(bf16), probabilities, gathered)
 
     outputs = [
@@ -101,31 +95,28 @@
     def backward_block(carried, inputs):
         query_block, neighbour_block, first_row, grad_block, probabilities, gathered = inputs
         slot_rows, slot_live = slot_index(neighbour_block, first_row, block_rows)
-        block_keys = gathered[:, :, 0].reshape(block_rows, slot_width, heads_here, HD).astype(f32)
-        block_values = gathered[:, :, 1].reshape(block_rows, slot_width, heads_here, HD).astype(f32)
+        block_keys = gathered[:, :, 0].reshape(slot_width, block_rows, heads_here, HD).astype(f32)
+        block_values = gathered[:, :, 1].reshape(slot_width, block_rows, heads_here, HD).astype(f32)
         grad_mix = grad_block.reshape(block_rows, heads_here, HD).astype(f32)
-        grad_weights = jnp.einsum("bhd,bmhd->bhm", grad_mix, block_values)
+        grad_weights = jnp.einsum("bhd,mbhd->bhm", grad_mix, block_values)
         grad_scores = (
             probabilities
             * (grad_weights - jnp.sum(probabilities * grad_weights, axis=2, keepdims=True))
             * score_scale
         )
-        grad_query = jnp.einsum("bhm,bmhd->bhd", grad_scores, block_keys).reshape(block_rows, span)
+        grad_query = jnp.einsum("bhm,mbhd->bhd", grad_scores, block_keys).reshape(block_rows, span)
         query_wide = query_block.reshape(block_rows, heads_here, HD).astype(f32)
-        grad_keys = jnp.einsum("bhm,bhd->bmhd", grad_scores, query_wide)
+        grad_keys = jnp.einsum("bhm,bhd->mbhd", grad_scores, query_wide)
         rounded = lax.optimization_barrier(probabilities.astype(bf16))
-        grad_values = jnp.einsum("bhm,bhd->bmhd", rounded.astype(f32), grad_mix)
+        grad_values = jnp.einsum("bhm,bhd->mbhd", rounded.astype(f32), grad_mix)
         contribution = (
             jnp.stack([grad_keys, grad_values], axis=2)
-            .reshape(block_rows, slot_width, 2 * span)
+            .reshape(slot_width * block_rows, 2 * span)
             .astype(bf16)
         )
-        picks = pick_table(slot_rows[:, 1:].T.reshape(-1), ext_rows)
-        rest = contribution[:, 1:].transpose(1, 0, 2).reshape(-1, 2 * span)
-        carried = carried + jnp.einsum("bx,bc->xc", picks, rest, preferred_element_type=f32)
-        own_rows = lax.dynamic_slice_in_dim(carried, first_row, block_rows, axis=0)
-        carried = lax.dynamic_update_slice_in_dim(
-            carried, own_rows + contribution[:, 0].astype(f32), first_row, axis=0
+        picks = pick_table(slot_rows.T.reshape(-1), ext_rows)
+        carried = carried + jnp.einsum(
+            "bx,bc->xc", picks, contribution, preferred_element_type=f32
         )
         return (carried, grad_query)
 

time: 295 us -> 348 us (1.18)
  local copies, waits for them, and re-layouts: 69.6 us -> 124 us
  between operations: 5.67 us -> 2.07 us
    unnamed x80 -> x88, local copies, waits for them, and re-layouts: 15.1 us -> 64.3 us
    slice x4 -> x2, local copies, waits for them, and re-layouts: 3.99 us -> 22 us  [forward_block(): gathered[:, :, 0].reshape(slot_width, block_rows, heads_here, HD)]
    reshape x2, local copies, waits for them, and re-layouts: 8.02 us -> 22.4 us  [forward_block(): gathered = jnp.dot(picks, flattened, preferred_element_type=f32).astype(b...]
    transpose x4 -> x0, local copies, waits for them, and re-layouts: 13.5 us -> none  [backward_block(): rest = contribution[:, 1:].transpose(1, 0, 2).reshape(-1, 2 * span)]
    dynamic_update_slice x2 -> x0, local copies, waits for them, and re-layouts: 6.26 us -> none  [backward_block(): lax.dynamic_update_slice_in_dim(carried, own_rows + contribution[:, 0].as...]
    another operation x6, other arithmetic: 2.66 us -> 7.09 us  [backward_block(): jnp.stack([grad_keys, grad_values], axis=2)]
    add x3, other arithmetic: 5.87 us -> 1.61 us  [the longest x2 1.3 us: slot_index(): own_rows = first_row + jnp.arange(block_rows, dtype=jnp.int32)]
    unnamed x8 -> x9, other arithmetic: 4.01 us -> 7.56 us
  transfers between devices with their start and end apart: 13 -> 13, of which waited for: 6 -> 7; matrix products, arithmetic and copies ran while one was open for 43% -> 56% of each run, Pallas kernels for 0% -> 0%
where the time goes in v9:
time: 348 us; the launch traced here: 342 us
  local copies, waits for them, and re-layouts  124 us (36%)
  matrix products  61.5 us (18%)
  waiting for transfers between devices  51.4 us (15%)
  blocking collectives  43.3 us (12%)
  other arithmetic  32.4 us (9%)
  starting transfers between devices  27.1 us (8%)
    unnamed x88, local copies, waits for them, and re-layouts  64.3 us
    ppermute x6, waiting for transfers between devices, ch_exchange(): lax.ppermute(value, 'ch', [(i, (i + shift) % size) for i in range(size)])  30.9 us
    all_to_all x1, blocking collectives, pix_gather(): lax.all_to_all(spread.reshape(size, total, width), 'pix', 0, 0, tiled=True)  27 us
    reshape x2, local copies, waits for them, and re-layouts, forward_block(): gathered = jnp.dot(picks, flattened, preferred_element_type=f32).astype(b...  22.4 us
    slice x2, local copies, waits for them, and re-layouts, forward_block(): gathered[:, :, 0].reshape(slot_width, block_rows, heads_here, HD)  22 us
    dot_general x2, matrix products, forward_block(): jnp.dot(picks, flattened, preferred_element_type=f32).astype(bf16)  19.7 us
    dot_general x2, matrix products, backward_block(): jnp.einsum('bx,bc->xc', picks, contribution, preferred_element_type=f32)  18.5 us
    all_to_all x1, blocking collectives, pix_scatter(): lax.all_to_all(mine.reshape(size, chunk, width), 'pix', 0, 0, tiled=True)  16.2 us
  transfers between devices with their start and end apart: 13, of which 7 were waited for; matrix products, arithmetic and copies ran while one was open for 56% of the time, Pallas kernels for 0%

profile of v9, /device:TPU:0, one launch (start us, length us, event | category | flops | bytes accessed | tf_op | source)
XLA Modules:
  0.0 341.8 jit_solution(10703003110413272552)
XLA Ops:
  0.6 3.0 collective-permute-start
  5.0 1.1 reshape.157
  6.1 1.2 broadcast_select_fusion
  10.1 1.8 fusion.104
  12.0 15.8 %collective-permute-done.1 = bf16[384,384]{1,0:T(8,128)(2,1)S(1)} collective-permute-done((bf16[384,384]{1,0:T(8,128)(2,1)}, bf16[384,384]{1,0:T(8,128)(2,1)S(1)}, u32[]{:S(2)}, u32[]{:S(2)}) %collective-permute-start.1) | collective-permute-done | bytes 294944 | tf_op jit(solution)/shard_map/ppermute | solution.py:141
  31.0 1.0 copy.92
  32.0 1.7 collective-permute-start.2
  34.5 1.1 reshape.158
  35.6 6.2 %all-to-all-start = ((bf16[16,32,2,192]{3,2,1,0:T(2,128)(2,1)}), bf16[16,32,2,192]{3,2,1,0:T(2,128)(2,1)S(1)}, u32[]{:S(2)}, u32[]{:S(2)}) async-start(bf16[16,32,2,192]{3,2,1,0:T(2,128)(2,1)} %reshape.158), calls=%async_computation | async-start | bytes 1048576 | tf_op jit(solution)/shard_map/all_to_all | solution.py:253
  43.6 1.6 collective-permute-start.5
  45.5 2.0 convolution_convert_fusion.1
  47.5 7.8 %collective-permute-done.3 = bf16[3,384,192]{1,2,0:T(8,128)(2,1)S(1)} collective-permute-done((bf16[3,384,192]{1,2,0:T(8,128)(2,1)}, bf16[3,384,192]{1,2,0:T(8,128)(2,1)S(1)}, u32[]{:S(2)}, u32[]{:S(2)}) %collective-permute-start.3) | collective-permute-done | bytes 442400 | tf_op jit(solution)/shard_map/ppermute | solution.py:141
  57.5 9.7 %fusion.18 = bf16[4608,384]{1,0:T(8,128)(2,1)} fusion(s32[4608]{0:T(1024)S(1)} %eq.33, bf16[512,384]{0,1:T(8,128)(2,1)S(1)} %copy.86, bf16[1024,384]{0,1:T(8,128)(2,1)S(1)} %bitcast.160), kind=kOutput, calls=%fused_computation.18 | convolution fusion | flops 5447024640 | bytes 4737024 | tf_op jit(solution)/shard_map/dot_general | solution.py:44
  67.3 11.2 %reshape.159 = bf16[9,512,2,192]{3,2,1,0:T(2,128)(2,1)} reshape(bf16[4608,384]{1,0:T(8,128)(2,1)} %fusion.18) | data formatting | bytes 7077888 | tf_op jit(solution)/shard_map/reshape | solution.py:46
  78.5 11.0 %fusion.93 = (bf16[9,512,1,192]{3,2,1,0:T(2,128)(2,1)}, bf16[9,512,1,192]{3,2,1,0:T(2,128)(2,1)}) fusion(bf16[9,512,2,192]{3,2,1,0:T(2,128)(2,1)} %reshape.159), kind=kLoop, calls=%fused_computation.136 | loop fusion | bytes 7077888 | tf_op jit(solution)/shard_map/slice | solution.py:48
  89.4 10.9 %copy.163 = bf16[9,512,1,192]{1,3,0,2:T(8,128)(2,1)S(1)} copy(bf16[9,512,1,192]{3,2,1,0:T(2,128)(2,1)} %get-tuple-element.68) | data formatting | bytes 3538944
  102.2 10.0 %fusion.19 = bf16[4608,384]{1,0:T(8,128)(2,1)} fusion(s32[4608]{0:T(1024)S(1)} %eq.41, bf16[512,384]{0,1:T(8,128)(2,1)S(1)} %copy.86, bf16[1024,384]{0,1:T(8,128)(2,1)S(1)} %bitcast.161), kind=kOutput, calls=%fused_computation.19 | convolution fusion | flops 5447024640 | bytes 4737024 | tf_op jit(solution)/shard_map/dot_general | solution.py:44
  112.2 11.2 %reshape.160 = bf16[9,512,2,192]{3,2,1,0:T(2,128)(2,1)} reshape(bf16[4608,384]{1,0:T(8,128)(2,1)} %fusion.19) | data formatting | bytes 7077888 | tf_op jit(solution)/shard_map/reshape | solution.py:46
  123.4 11.1 %fusion.94 = (bf16[9,512,1,192]{3,2,1,0:T(2,128)(2,1)}, bf16[9,512,1,192]{3,2,1,0:T(2,128)(2,1)}) fusion(bf16[9,512,2,192]{3,2,1,0:T(2,128)(2,1)} %reshape.160), kind=kLoop, calls=%fused_computation.137 | loop fusion | bytes 7077888 | tf_op jit(solution)/shard_map/slice | solution.py:48
  134.4 10.9 %copy.165 = bf16[9,512,1,192]{1,3,0,2:T(8,128)(2,1)S(1)} copy(bf16[9,512,1,192]{3,2,1,0:T(2,128)(2,1)} %get-tuple-element.70) | data formatting | bytes 3538944
  145.4 2.1 multiply_reduce_fusion.5
  147.5 1.7 fusion.98
  149.2 1.4 copy.176
  150.6 10.8 %copy.166 = bf16[9,512,1,192]{1,3,0,2:T(8,128)(2,1)} copy(bf16[9,512,1,192]{3,2,1,0:T(2,128)(2,1)} %get-tuple-element.71) | data formatting | bytes 3538944
  161.5 11.3 %copy.164 = bf16[9,512,1,192]{1,3,0,2:T(8,128)(2,1)} copy(bf16[9,512,1,192]{3,2,1,0:T(2,128)(2,1)} %get-tuple-element.69) | data formatting | bytes 3538944
  172.8 2.0 multiply_reduce_fusion.1
  174.9 1.0 fusion.48
  175.9 2.0 fusion.22
  177.9 1.2 fusion.23
  179.9 4.1 %copy.187 = bf16[48,8,9,512]{3,1,2,0:T(8,128)(2,1)S(1)} copy(bf16[48,8,9,512]{3,2,1,0:T(8,128)(2,1)S(1)} %bitcast.137) | data formatting | bytes 7077888
  184.1 9.9 %fusion.12 = f32[1536,384]{1,0:T(8,128)} fusion(bf16[4608,384]{0,1:T(8,128)(2,1)S(1)} %bitcast.150, s32[4608]{0:T(1024)S(1)} %copy-done.35), kind=kOutput, calls=%fused_computation.13 | convolution fusion | flops 5449973760 | bytes 5916672 | tf_op jit(solution)/shard_map/bx,bc->xc/dot_general | solution.py:118
  194.9 1.2 fusion.20
  196.1 1.2 fusion.21
  198.1 4.1 %copy.186 = bf16[48,8,9,512]{3,1,2,0:T(8,128)(2,1)S(1)} copy(bf16[48,8,9,512]{3,2,1,0:T(8,128)(2,1)S(1)} %bitcast.138) | data formatting | bytes 7077888
  202.6 1.1 copy-done
  204.2 1.7 collective-permute-start.4
  205.9 8.5 %fusion.10 = f32[1536,384]{1,0:T(8,128)S(1)} fusion(bf16[4608,384]{0,1:T(8,128)(2,1)S(1)} %bitcast.149, s32[4608]{0:T(1024)S(1)} %copy-done.33), kind=kOutput, calls=%fused_computation.12 | convolution fusion | flops 5449973760 | bytes 5916672 | tf_op jit(solution)/shard_map/bx,bc->xc/dot_general | solution.py:118
  216.5 1.4 copy-done.2
  218.7 2.1 reshape.162
  220.8 6.2 %all-to-all-start.1 = ((bf16[16,32,2,192]{3,2,1,0:T(2,128)(2,1)}), bf16[16,32,2,192]{3,2,1,0:T(2,128)(2,1)}, u32[]{:S(2)}, u32[]{:S(2)}) async-start(bf16[16,32,2,192]{3,2,1,0:T(2,128)(2,1)} %reshape.162), calls=%async_computation.1 | async-start | bytes 1048576 | tf_op jit(solution)/shard_map/all_to_all | solution.py:271
  227.0 1.2 multiply_reduce_fusion
  228.3 1.3 multiply_reduce_fusion.2
  230.4 2.8 convolution_multiply_fusion.2
  233.2 1.6 copy.99
  234.8 6.7 %all-to-all-done.1 = bf16[16,32,2,192]{3,2,1,0:T(2,128)(2,1)} async-done(((bf16[16,32,2,192]{3,2,1,0:T(2,128)(2,1)}), bf16[16,32,2,192]{3,2,1,0:T(2,128)(2,1)}, u32[]{:S(2)}, u32[]{:S(2)}) %all-to-all-start.1) | async-done | bytes 393248 | tf_op jit(solution)/shard_map/all_to_all | solution.py:271
  241.5 1.4 convert_element_type.115
  243.1 2.1 add_convert_fusion
  248.1 1.1 broadcast_select_fusion.2
  249.3 2.3 pad_maximum_fusion.3
  252.9 4.7 %all-to-all-start.2 = ((f32[16,24,384]{2,1,0:T(8,128)}), f32[16,24,384]{2,1,0:T(8,128)S(1)}, u32[]{:S(2)}, u32[]{:S(2)}) async-start(f32[16,24,384]{2,1,0:T(8,128)} %bitcast.59), calls=%async_computation.2 | async-start | bytes 1179648 | tf_op jit(solution)/shard_map/all_to_all | solution.py:173
  257.7 3.3 fusion.92
  260.9 12.2 %all-to-all-done.2 = f32[16,24,384]{2,1,0:T(8,128)S(1)} async-done(((f32[16,24,384]{2,1,0:T(8,128)}), f32[16,24,384]{2,1,0:T(8,128)S(1)}, u32[]{:S(2)}, u32[]{:S(2)}) %all-to-all-start.2) | async-done | bytes 589856 | tf_op jit(solution)/shard_map/all_to_all | solution.py:173
  273.2 7.0 %collective-permute-done.7 = bf16[1024,3,192]{0,2,1:T(8,128)(2,1)} collective-permute-done((bf16[1024,3,192]{0,2,1:T(8,128)(2,1)}, bf16[1024,3,192]{0,2,1:T(8,128)(2,1)}, u32[]{:S(2)}, u32[]{:S(2)}) %collective-permute-start.7) | collective-permute-done | bytes 1179680 | tf_op jit(solution)/shard_map/ppermute | solution.py:141
  280.2 3.4 fusion.28
  284.4 1.6 collective-permute-done.8
  286.1 16.2 %all_to_all.25 = f32[16,12,384]{2,1,0:T(8,128)S(1)} all-to-all(f32[16,12,384]{2,1,0:T(8,128)S(1)} %reshape.166), channel_id=1, replica_groups=mesh['pix'=16,'ch'=2] {'pix'}, dimensions={0} | all-to-all | bytes 589824 | tf_op jit(solution)/shard_map/all_to_all | solution.py:173
  302.4 27.0 %all_to_all.26 = f32[16,36,384]{2,1,0:T(8,128)S(1)} all-to-all(f32[16,36,384]{2,1,0:T(8,128)S(1)} %bitcast.148), channel_id=1, replica_groups=mesh['pix'=16,'ch'=2] {'pix'}, dimensions={0} | all-to-all | bytes 1769472 | tf_op jit(solution)/shard_map/all_to_all | solution.py:184
  329.4 1.1 copy.103
  331.3 1.3 fusion.55
  332.6 1.5 fusion.33
  334.0 0.9 copy.106
  335.0 1.5 convolution_convert_fusion
  336.5 1.5 copy_select_fusion.1
  339.2 1.3 copy.107
  (159 shorter events, 29.4 us)
Async XLA Ops:
  0.6 27.1 %collective-permute-start = (bf16[1024,384]{1,0:T(8,128)(2,1)}, bf16[1024,384]{1,0:T(8,128)(2,1)S(1)}, u32[]{:S(2)}, u32[]{:S(2)}) collective-permute-start(bf16[1024,384]{1,0:T(8,128)(2,1)} %param.9), channel_id=1, source_target_pairs={{0,1},{1,0},{2,3},{3,2},{4,5},{5,4},{6,7},{7,6},{8,9},{9,8},{10,11... | collective-permute-start | bytes 2359304 | tf_op jit(solution)/shard_map/ppermute | solution.py:141
  3.6 24.1 %collective-permute-start.1 = (bf16[384,384]{1,0:T(8,128)(2,1)}, bf16[384,384]{1,0:T(8,128)(2,1)S(1)}, u32[]{:S(2)}, u32[]{:S(2)}) collective-permute-start(bf16[384,384]{1,0:T(8,128)(2,1)} %param.10), channel_id=1, source_target_pairs={{0,1},{1,0},{2,3},{3,2},{4,5},{5,4},{6,7},{7,6},{8,9},{9,8},{10,11... | collective-permute-start | bytes 884744 | tf_op jit(solution)/shard_map/ppermute | solution.py:141
  8.7 20.5 %copy-start.23 = (bf16[3,384,192]{1,2,0:T(8,128)(2,1)S(1)}, bf16[3,384,192]{1,2,0:T(8,128)(2,1)}, u32[]{:S(2)}) copy-start(bf16[3,384,192]{1,2,0:T(8,128)(2,1)} %param.11) | copy-start | bytes 1327108
  28.3 0.9 copy-start.3
  30.0 1.0 copy-start.11
  32.0 13.4 %collective-permute-start.2 = (bf16[1024,192]{1,0:T(8,128)(2,1)}, bf16[1024,192]{1,0:T(8,128)(2,1)}, u32[]{:S(2)}, u32[]{:S(2)}) collective-permute-start(bf16[1024,192]{1,0:T(8,128)(2,1)} %copy.92), channel_id=1, source_target_pairs={{0,1},{1,0},{2,3},{3,2},{4,5},{5,4},{6,7},{7,6},{8,9},{9,8},{10,11... | collective-permute-start | bytes 1179656 | tf_op jit(solution)/shard_map/ppermute | solution.py:141
  35.6 21.4 %all-to-all-start = ((bf16[16,32,2,192]{3,2,1,0:T(2,128)(2,1)}), bf16[16,32,2,192]{3,2,1,0:T(2,128)(2,1)S(1)}, u32[]{:S(2)}, u32[]{:S(2)}) async-start(bf16[16,32,2,192]{3,2,1,0:T(2,128)(2,1)} %reshape.158), calls=%async_computation | async-start | bytes 1048576 | tf_op jit(solution)/shard_map/all_to_all | solution.py:253
  42.0 13.4 %copy-start.20 = (bf16[1024,192]{1,0:T(8,128)(2,1)}, bf16[1024,192]{1,0:T(8,128)(2,1)S(1)}, u32[]{:S(2)}) copy-start(bf16[1024,192]{1,0:T(8,128)(2,1)S(1)} %copy.93) | copy-start | bytes 1179652
  42.0 60.2 %copy-start.34 = (s32[4608]{0:T(1024)}, s32[4608]{0:T(1024)S(1)}, u32[]{:S(2)}) copy-start(s32[4608]{0:T(1024)S(1)} %eq.41) | copy-start | bytes 55300
  42.1 15.5 %copy-start.32 = (s32[4608]{0:T(1024)}, s32[4608]{0:T(1024)S(1)}, u32[]{:S(2)}) copy-start(s32[4608]{0:T(1024)S(1)} %eq.33) | copy-start | bytes 55300
  42.1 13.2 %collective-permute-start.3 = (bf16[3,384,192]{1,2,0:T(8,128)(2,1)}, bf16[3,384,192]{1,2,0:T(8,128)(2,1)S(1)}, u32[]{:S(2)}, u32[]{:S(2)}) collective-permute-start(bf16[3,384,192]{1,2,0:T(8,128)(2,1)} %param.11), channel_id=1, source_target_pairs={{0,1},{1,0},{2,3},{3,2},{4,5},{5,4},{6,7},{7,6},{8,9},{9,8},{10,11... | collective-permute-start | bytes 1327112 | tf_op jit(solution)/shard_map/ppermute | solution.py:141
  43.6 56.8 %copy-start.5 = (f32[512,3,64]{0,2,1:T(8,128)}, f32[512,3,64]{0,2,1:T(8,128)S(1)}, u32[]{:S(2)}) copy-start(f32[512,3,64]{0,2,1:T(8,128)S(1)} %convert.64) | copy-start | bytes 1179652
  43.6 172.2 %collective-permute-start.5 = (bf16[192,192]{1,0:T(8,128)(2,1)}, bf16[192,192]{1,0:T(8,128)(2,1)}, u32[]{:S(2)}, u32[]{:S(2)}) collective-permute-start(bf16[192,192]{1,0:T(8,128)(2,1)} %bitcast.173), channel_id=1, source_target_pairs={{0,1},{1,0},{2,3},{3,2},{4,5},{5,4},{6,7},{7,6},{8,9},{9,8},{10,11... | collective-permute-start | bytes 221192 | tf_op jit(solution)/shard_map/ppermute | solution.py:237
  55.3 0.9 copy-start.36
  101.6 10.6 %copy-start.28 = (bf16[512,3,9]{0,2,1:T(8,128)(2,1)}, bf16[512,3,9]{0,2,1:T(8,128)(2,1)S(1)}, u32[]{:S(2)}) copy-start(bf16[512,3,9]{0,2,1:T(8,128)(2,1)S(1)} %get-tuple-element.86) | copy-start | bytes 82948
  172.8 5.1 %copy-start.30 = (bf16[512,3,9]{0,2,1:T(8,128)(2,1)S(1)}, bf16[512,3,9]{0,2,1:T(8,128)(2,1)}, u32[]{:S(2)}) copy-start(bf16[512,3,9]{0,2,1:T(8,128)(2,1)} %get-tuple-element.84) | copy-start | bytes 82948
  172.8 5.1 %copy-start.8 = (f32[512,3,64]{0,2,1:T(8,128)S(1)}, f32[512,3,64]{0,2,1:T(8,128)}, u32[]{:S(2)}) copy-start(f32[512,3,64]{0,2,1:T(8,128)} %convert.75) | copy-start | bytes 1179652
  179.9 4.1 %copy-start.35 = (s32[4608]{0:T(1024)S(1)}, s32[4608]{0:T(1024)}, u32[]{:S(2)}) copy-start(s32[4608]{0:T(1024)} %copy-done.34) | copy-start | bytes 55300
  184.0 10.0 %copy-start.1 = (bf16[9,512,1,192]{1,3,0,2:T(8,128)(2,1)S(1)}, bf16[9,512,1,192]{1,3,0,2:T(8,128)(2,1)}, u32[]{:S(2)}) copy-start(bf16[9,512,1,192]{1,3,0,2:T(8,128)(2,1)} %copy.164) | copy-start | bytes 5308420
  184.0 10.0 %copy-start.7 = (f32[512,3,64]{0,2,1:T(8,128)S(1)}, f32[512,3,64]{0,2,1:T(8,128)}, u32[]{:S(2)}) copy-start(f32[512,3,64]{0,2,1:T(8,128)} %convert.72) | copy-start | bytes 1179652
  184.1 10.4 %copy-start.31 = (f32[512,3,9]{0,2,1:T(8,128)S(1)}, f32[512,3,9]{0,2,1:T(8,128)}, u32[]{:S(2)}) copy-start(f32[512,3,9]{0,2,1:T(8,128)} %get-tuple-element.87) | copy-start | bytes 165892
  184.1 10.8 %copy-start.6 = (f32[512,3,64]{0,2,1:T(8,128)S(1)}, f32[512,3,64]{0,2,1:T(8,128)}, u32[]{:S(2)}) copy-start(f32[512,3,64]{0,2,1:T(8,128)} %copy-done.5) | copy-start | bytes 1179652
  194.0 2.1 copy-start.29
  198.1 4.2 %copy-start.26 = (f32[512,3,9]{0,1,2:T(4,128)S(1)}, f32[512,3,9]{0,1,2:T(4,128)}, u32[]{:S(2)}) copy-start(f32[512,3,9]{0,1,2:T(4,128)} %copy.174) | copy-start | bytes 165892
  198.1 4.5 %copy-start.27 = (f32[512,3,9]{0,1,2:T(4,128)S(1)}, f32[512,3,9]{0,1,2:T(4,128)}, u32[]{:S(2)}) copy-start(f32[512,3,9]{0,1,2:T(4,128)} %copy.176) | copy-start | bytes 165892
  202.2 1.5 copy-start
  202.2 3.6 %copy-start.33 = (s32[4608]{0:T(1024)S(1)}, s32[4608]{0:T(1024)}, u32[]{:S(2)}) copy-start(s32[4608]{0:T(1024)} %copy-done.32) | copy-start | bytes 55300
  204.2 10.2 %copy-start.14 = (bf16[2,24,8,512]{3,2,0,1:T(8,128)(2,1)}, bf16[2,24,8,512]{3,2,0,1:T(8,128)(2,1)S(1)}, u32[]{:S(2)}) copy-start(bf16[2,24,8,512]{3,2,0,1:T(8,128)(2,1)S(1)} %copy.185) | copy-start | bytes 1179652
  204.2 11.6 %collective-permute-start.4 = (bf16[1024,192]{0,1:T(8,128)(2,1)S(1)}, bf16[1024,192]{0,1:T(8,128)(2,1)S(1)}, u32[]{:S(2)}, u32[]{:S(2)}) collective-permute-start(bf16[1024,192]{0,1:T(8,128)(2,1)S(1)} %bitcast.156), channel_id=1, source_target_pairs={{0,1},{1,0},{2,3},{3,2},{4,5},{5,4},{6,7},{7,6},{8,9},{9,8},{10,11... | collective-permute-start | bytes 1179656 | tf_op jit(solution)/shard_map/ppermute | solution.py:141
  205.9 9.9 %copy-start.10 = (f32[1536,384]{1,0:T(8,128)S(1)}, f32[1536,384]{1,0:T(8,128)}, u32[]{:S(2)}) copy-start(f32[1536,384]{1,0:T(8,128)} %fusion.12) | copy-start | bytes 7077892
  215.7 0.7 copy-start.25
  216.5 1.4 copy-start.2
  220.8 20.7 %all-to-all-start.1 = ((bf16[16,32,2,192]{3,2,1,0:T(2,128)(2,1)}), bf16[16,32,2,192]{3,2,1,0:T(2,128)(2,1)}, u32[]{:S(2)}, u32[]{:S(2)}) async-start(bf16[16,32,2,192]{3,2,1,0:T(2,128)(2,1)} %reshape.162), calls=%async_computation.1 | async-start | bytes 1048576 | tf_op jit(solution)/shard_map/all_to_all | solution.py:271
  228.2 2.1 copy-start.15
  228.2 2.1 copy-start.21
  230.3 14.9 %copy-start.12 = (bf16[1024,1,192]{0,2,1:T(8,128)(2,1)}, bf16[1024,1,192]{0,2,1:T(8,128)(2,1)S(1)}, u32[]{:S(2)}) copy-start(bf16[1024,1,192]{0,2,1:T(8,128)(2,1)S(1)} %reshape_reshape.4) | copy-start | bytes 1179652
  230.3 2.8 slice-start
  233.2 12.9 %copy-start.4 = (bf16[1024,384]{1,0:T(8,128)(2,1)S(1)}, bf16[1024,384]{1,0:T(8,128)(2,1)}, u32[]{:S(2)}) copy-start(bf16[1024,384]{1,0:T(8,128)(2,1)} %copy-done.3) | copy-start | bytes 2359300
  245.2 0.9 copy-start.19
  247.6 1.7 copy-start.13
  248.1 4.0 %copy-start.17 = (f32[192,384]{1,0:T(8,128)S(1)}, f32[192,384]{1,0:T(8,128)}, u32[]{:S(2)}) copy-start(f32[192,384]{1,0:T(8,128)} %convolution_multiply_fusion.2) | copy-start | bytes 884740
  249.2 8.5 %copy-start.24 = (bf16[3,384,192]{1,2,0:T(8,128)(2,1)S(1)}, bf16[3,384,192]{1,2,0:T(8,128)(2,1)}, u32[]{:S(2)}) copy-start(bf16[3,384,192]{1,2,0:T(8,128)(2,1)} %param.11) | copy-start | bytes 1327108
  249.2 2.8 collective-permute-start.6
  251.6 28.6 %collective-permute-start.7 = (bf16[1024,3,192]{0,2,1:T(8,128)(2,1)}, bf16[1024,3,192]{0,2,1:T(8,128)(2,1)}, u32[]{:S(2)}, u32[]{:S(2)}) collective-permute-start(bf16[1024,3,192]{0,2,1:T(8,128)(2,1)} %pad_maximum_fusion.3), channel_id=1, source_target_pairs={{0,1},{1,0},{2,3},{3,2},{4,5},{5,4},{6,7},{7,6},{8,9},{9,8},{10,11... | collective-permute-start | bytes 3538952 | tf_op jit(solution)/shard_map/ppermute | solution.py:141
  252.9 27.3 %copy-start.22 = (bf16[1024,192]{1,0:T(8,128)(2,1)S(1)}, bf16[1024,192]{1,0:T(8,128)(2,1)}, u32[]{:S(2)}) copy-start(bf16[1024,192]{1,0:T(8,128)(2,1)} %copy-done.20) | copy-start | bytes 1179652
  252.9 20.3 %all-to-all-start.2 = ((f32[16,24,384]{2,1,0:T(8,128)}), f32[16,24,384]{2,1,0:T(8,128)S(1)}, u32[]{:S(2)}, u32[]{:S(2)}) async-start(f32[16,24,384]{2,1,0:T(8,128)} %bitcast.59), calls=%async_computation.2 | async-start | bytes 1179648 | tf_op jit(solution)/shard_map/all_to_all | solution.py:173
  273.2 10.4 %copy-start.9 = (bf16[1024,384]{1,0:T(8,128)(2,1)S(1)}, bf16[1024,384]{1,0:T(8,128)(2,1)}, u32[]{:S(2)}) copy-start(bf16[1024,384]{1,0:T(8,128)(2,1)} %param.9) | copy-start | bytes 2359300
  284.3 1.6 collective-permute-start.8
  286.0 45.2 %copy-start.16 = (bf16[2,24,8,512]{3,2,0,1:T(8,128)(2,1)S(1)}, bf16[2,24,8,512]{3,2,0,1:T(8,128)(2,1)}, u32[]{:S(2)}) copy-start(bf16[2,24,8,512]{3,2,0,1:T(8,128)(2,1)} %copy-done.14) | copy-start | bytes 1179652
  329.4 5.5 %copy-start.18 = (bf16[384,384]{1,0:T(8,128)(2,1)S(1)}, bf16[384,384]{1,0:T(8,128)(2,1)}, u32[]{:S(2)}) copy-start(bf16[384,384]{1,0:T(8,128)(2,1)} %param.10) | copy-start | bytes 884740
  330.5 6.0 %collective-permute-start.9 = (f32[16,36,384]{2,0,1:T(8,128)}, f32[16,36,384]{2,0,1:T(8,128)}, u32[]{:S(2)}, u32[]{:S(2)}) collective-permute-start(f32[16,36,384]{2,0,1:T(8,128)} %copy.103), channel_id=1, source_target_pairs={{0,2},{2,0},{4,6},{6,4},{8,10},{10,8},{12,14},{14,12},{16,18},{18,... | collective-permute-start | bytes 2654216 | tf_op jit(solution)/shard_map/ppermute | solution.py:159

commit v10 on v8

--- a/solution.py
+++ b/solution.py
@@ -39,16 +39,11 @@
     def forward_block(inputs):
         query_block, neighbour_block, first_row = inputs
         slot_rows, slot_live = slot_index(neighbour_block, first_row, block_rows)
-        own = lax.dynamic_slice_in_dim(flattened, first_row, block_rows, axis=0)
-        picks = pick_table(slot_rows[:, 1:].T.reshape(-1), ext_rows)
-        others = (
-            jnp.dot(picks, flattened, preferred_element_type=f32)
+        gathered = (
+            jnp.dot(
+                pick_table(slot_rows.reshape(-1), ext_rows), flattened, preferred_element_type=f32
+            )
             .astype(bf16)
-            .reshape(slot_width - 1, block_rows, 2 * span)
-        )
-        gathered = (
-            jnp.concatenate([own[None], others], axis=0)
-            .transpose(1, 0, 2)
             .reshape(block_rows, slot_width, 2, span)
         )
         block_keys = gathered[:, :, 0].reshape(block_rows, slot_width, heads_here, HD)
@@ -120,12 +115,11 @@
             .reshape(block_rows, slot_width, 2 * span)
             .astype(bf16)
         )
-        picks = pick_table(slot_rows[:, 1:].T.reshape(-1), ext_rows)
-        rest = contribution[:, 1:].transpose(1, 0, 2).reshape(-1, 2 * span)
-        carried = carried + jnp.einsum("bx,bc->xc", picks, rest, preferred_element_type=f32)
-        own_rows = lax.dynamic_slice_in_dim(carried, first_row, block_rows, axis=0)
-        carried = lax.dynamic_update_slice_in_dim(
-            carried, own_rows + contribution[:, 0].astype(f32), first_row, axis=0
+        carried = carried + jnp.einsum(
+            "bx,bc->xc",
+            pick_table(slot_rows.reshape(-1), ext_rows),
+            contribution.reshape(block_rows * slot_width, 2 * span),
+            preferred_element_type=f32,
         )
         return (carried, grad_query)
 

time: 295 us -> 397 us (1.35)
  local copies, waits for them, and re-layouts: 69.6 us -> 172 us
    unnamed x80 -> x98, local copies, waits for them, and re-layouts: 15.1 us -> 52.8 us
    convert_element_type x0 -> x2, local copies, waits for them, and re-layouts: none -> 34.9 us  [backward_block(): contribution = jnp.stack([grad_keys, grad_values], axis=2).reshape(block_...]
    another operation x0 -> x2, local copies, waits for them, and re-layouts: none -> 26.6 us  [backward_block(): jnp.stack([grad_keys, grad_values], axis=2)]
    slice x2, local copies, waits for them, and re-layouts: 0.46 us -> 21.7 us  [forward_block(): gathered[:, :, 0].reshape(block_rows, slot_width, heads_here, HD)]
    transpose x4 -> x0, local copies, waits for them, and re-layouts: 13.5 us -> none  [backward_block(): rest = contribution[:, 1:].transpose(1, 0, 2).reshape(-1, 2 * span)]
    reshape x2, local copies, waits for them, and re-layouts: 8.02 us -> 15.7 us  [forward_block(): gathered = jnp.dot(pick_table(slot_rows.reshape(-1), ext_rows), flattened...]
    dynamic_update_slice x2 -> x0, local copies, waits for them, and re-layouts: 6.26 us -> none  [backward_block(): lax.dynamic_update_slice_in_dim(carried, own_rows + contribution[:, 0].as...]
    add x3, other arithmetic: 5.87 us -> 1.54 us  [the longest x2 1.3 us: slot_index(): own_rows = first_row + jnp.arange(block_rows, dtype=jnp.int32)]
  transfers between devices with their start and end apart: 13 -> 13, of which waited for: 6 -> 7; matrix products, arithmetic and copies ran while one was open for 43% -> 61% of each run, Pallas kernels for 0% -> 0%
where the time goes in v10:
time: 397 us; the launch traced here: 390 us
  local copies, waits for them, and re-layouts  172 us (43%)
  matrix products  62.7 us (16%)
  waiting for transfers between devices  50.7 us (13%)
  blocking collectives  43.5 us (11%)
  other arithmetic  33.3 us (8%)
  starting transfers between devices  25.9 us (7%)
    unnamed x98, local copies, waits for them, and re-layouts  52.8 us
    convert_element_type x2, local copies, waits for them, and re-layouts, backward_block(): contribution = jnp.stack([grad_keys, grad_values], axis=2).reshape(block_...  34.9 us
    ppermute x6, waiting for transfers between devices, ch_exchange(): lax.ppermute(value, 'ch', [(i, (i + shift) % size) for i in range(size)])  31.3 us
    all_to_all x1, blocking collectives, pix_gather(): lax.all_to_all(spread.reshape(size, total, width), 'pix', 0, 0, tiled=True)  27.4 us
    another operation x2, local copies, waits for them, and re-layouts, backward_block(): jnp.stack([grad_keys, grad_values], axis=2)  26.6 us
    slice x2, local copies, waits for them, and re-layouts, forward_block(): gathered[:, :, 0].reshape(block_rows, slot_width, heads_here, HD)  21.7 us
    dot_general x2, matrix products, backward_block(): jnp.einsum('bx,bc->xc', pick_table(slot_rows.reshape(-1), ext_rows), cont...  20.3 us
    dot_general x2, matrix products, forward_block(): jnp.dot(pick_table(slot_rows.reshape(-1), ext_rows), flattened, preferred...  19.3 us
  transfers between devices with their start and end apart: 13, of which 7 were waited for; matrix products, arithmetic and copies ran while one was open for 61% of the time, Pallas kernels for 0%

profile of v10, /device:TPU:0, one launch (start us, length us, event | category | flops | bytes accessed | tf_op | source)
XLA Modules:
  0.0 389.7 jit_solution(13126066127678901900)
XLA Ops:
  0.6 3.0 collective-permute-start
  5.0 1.1 reshape.161
  6.1 1.2 broadcast_select_fusion
  10.1 1.8 fusion.46
  12.0 15.8 %collective-permute-done.1 = bf16[384,384]{1,0:T(8,128)(2,1)S(1)} collective-permute-done((bf16[384,384]{1,0:T(8,128)(2,1)}, bf16[384,384]{1,0:T(8,128)(2,1)S(1)}, u32[]{:S(2)}, u32[]{:S(2)}) %collective-permute-start.1) | collective-permute-done | bytes 294944 | tf_op jit(solution)/shard_map/ppermute | solution.py:144
  31.2 1.8 collective-permute-start.2
  33.8 1.1 reshape.162
  34.9 6.5 %all-to-all-start = ((bf16[16,32,2,192]{3,2,1,0:T(2,128)(2,1)}), bf16[16,32,2,192]{3,2,1,0:T(2,128)(2,1)S(1)}, u32[]{:S(2)}, u32[]{:S(2)}) async-start(bf16[16,32,2,192]{3,2,1,0:T(2,128)(2,1)} %reshape.162), calls=%async_computation | async-start | bytes 1048576 | tf_op jit(solution)/shard_map/all_to_all | solution.py:256
  45.8 1.5 collective-permute-start.5
  47.3 2.0 convolution_convert_fusion.1
  49.4 7.4 %collective-permute-done.3 = bf16[3,384,192]{1,2,0:T(8,128)(2,1)S(1)} collective-permute-done((bf16[3,384,192]{1,2,0:T(8,128)(2,1)}, bf16[3,384,192]{1,2,0:T(8,128)(2,1)S(1)}, u32[]{:S(2)}, u32[]{:S(2)}) %collective-permute-start.3) | collective-permute-done | bytes 442400 | tf_op jit(solution)/shard_map/ppermute | solution.py:144
  59.7 9.4 %fusion.8 = bf16[4608,384]{1,0:T(8,128)(2,1)S(1)} fusion(s32[4608]{0:T(1024)} %eq.33, bf16[512,384]{0,1:T(8,128)(2,1)} %copy.107, bf16[1024,384]{0,1:T(8,128)(2,1)} %bitcast.142), kind=kOutput, calls=%fused_computation.10 | convolution fusion | flops 5447024640 | bytes 4737024 | tf_op jit(solution)/shard_map/dot_general | solution.py:43
  69.2 4.6 %reshape.163 = bf16[512,9,2,192]{3,2,1,0:T(2,128)(2,1)} reshape(bf16[4608,384]{1,0:T(8,128)(2,1)S(1)} %fusion.8) | data formatting | bytes 7077888 | tf_op jit(solution)/shard_map/reshape | solution.py:47
  73.7 10.9 %fusion.41 = (bf16[512,9,1,192]{3,2,1,0:T(2,128)(2,1)}, bf16[512,9,1,192]{3,2,1,0:T(2,128)(2,1)}) fusion(bf16[512,9,2,192]{3,2,1,0:T(2,128)(2,1)} %reshape.163), kind=kLoop, calls=%fused_computation.102 | loop fusion | bytes 7077888 | tf_op jit(solution)/shard_map/slice | solution.py:49
  84.6 11.0 %copy.179 = bf16[512,9,1,192]{0,3,1,2:T(8,128)(2,1)S(1)} copy(bf16[512,9,1,192]{3,2,1,0:T(2,128)(2,1)} %get-tuple-element.76) | data formatting | bytes 3538944
  97.4 11.0 %copy.180 = bf16[512,9,1,192]{0,3,1,2:T(8,128)(2,1)} copy(bf16[512,9,1,192]{3,2,1,0:T(2,128)(2,1)} %get-tuple-element.77) | data formatting | bytes 3538944
  108.4 9.9 %fusion.9 = bf16[4608,384]{1,0:T(8,128)(2,1)} fusion(s32[4608]{0:T(1024)S(1)} %copy-done.41, bf16[512,384]{0,1:T(8,128)(2,1)S(1)} %copy-done.33, bf16[1024,384]{0,1:T(8,128)(2,1)S(1)} %bitcast.143), kind=kOutput, calls=%fused_computation.11 | convolution fusion | flops 5447024640 | bytes 4737024 | tf_op jit(solution)/shard_map/dot_general | solution.py:43
  118.3 11.2 %reshape.164 = bf16[512,9,2,192]{3,2,1,0:T(2,128)(2,1)} reshape(bf16[4608,384]{1,0:T(8,128)(2,1)} %fusion.9) | data formatting | bytes 7077888 | tf_op jit(solution)/shard_map/reshape | solution.py:47
  129.4 10.9 %fusion.42 = (bf16[512,9,1,192]{3,2,1,0:T(2,128)(2,1)}, bf16[512,9,1,192]{3,2,1,0:T(2,128)(2,1)}) fusion(bf16[512,9,2,192]{3,2,1,0:T(2,128)(2,1)} %reshape.164), kind=kLoop, calls=%fused_computation.103 | loop fusion | bytes 7077888 | tf_op jit(solution)/shard_map/slice | solution.py:49
  140.3 10.9 %copy.181 = bf16[512,9,1,192]{0,3,1,2:T(8,128)(2,1)S(1)} copy(bf16[512,9,1,192]{3,2,1,0:T(2,128)(2,1)} %get-tuple-element.78) | data formatting | bytes 3538944
  151.2 1.5 multiply_reduce_fusion.5
  154.0 10.9 %copy.182 = bf16[512,9,1,192]{0,3,1,2:T(8,128)(2,1)} copy(bf16[512,9,1,192]{3,2,1,0:T(2,128)(2,1)} %get-tuple-element.79) | data formatting | bytes 3538944
  164.9 2.1 multiply_reduce_fusion.1
  166.9 1.0 multiply_reduce_fusion.8
  169.7 2.2 pad_maximum_fusion.1
  171.9 13.3 %copy.121 = bf16[512,9,2,3,64]{4,3,2,1,0:T(4,128)(2,1)} copy(bf16[512,9,2,3,64]{0,4,3,2,1:T(8,128)(2,1)} %pad_maximum_fusion.1) | data formatting | bytes 7077888 | tf_op jit(solution)/shard_map/stack | solution.py:114
  185.2 17.3 %convert_element_type.115 = bf16[4608,384]{1,0:T(8,128)(2,1)} reshape(bf16[512,9,2,3,64]{4,3,2,1,0:T(4,128)(2,1)} %copy.121) | data formatting | bytes 7077888 | tf_op jit(solution)/shard_map/convert_element_type | solution.py:116
  202.6 11.9 %fusion = f32[1536,384]{1,0:T(8,128)} fusion(bf16[4608,384]{1,0:T(8,128)(2,1)} %convert_element_type.115, s32[4608]{0:T(1024)} %eq.41), kind=kOutput, calls=%fused_computation.1 | convolution fusion | flops 5442895872 | bytes 5916672 | tf_op jit(solution)/shard_map/bx,bc->xc/dot_general | solution.py:118
  216.9 2.2 pad_maximum_fusion
  219.1 13.3 %copy.117 = bf16[512,9,2,3,64]{4,3,2,1,0:T(4,128)(2,1)} copy(bf16[512,9,2,3,64]{0,4,3,2,1:T(8,128)(2,1)} %pad_maximum_fusion) | data formatting | bytes 7077888 | tf_op jit(solution)/shard_map/stack | solution.py:114
  232.3 17.5 %convert_element_type.112 = bf16[4608,384]{1,0:T(8,128)(2,1)} reshape(bf16[512,9,2,3,64]{4,3,2,1,0:T(4,128)(2,1)} %copy.117) | data formatting | bytes 7077888 | tf_op jit(solution)/shard_map/convert_element_type | solution.py:116
  249.9 2.0 multiply_reduce_fusion.6
  251.9 1.4 multiply_reduce_fusion.4
  254.0 8.5 %fusion.2 = f32[1536,384]{1,0:T(8,128)S(1)} fusion(bf16[4608,384]{1,0:T(8,128)(2,1)S(1)} %copy-done.5, s32[4608]{0:T(1024)S(1)} %copy-done.40), kind=kOutput, calls=%fused_computation.4 | convolution fusion | flops 5442895872 | bytes 5916672 | tf_op jit(solution)/shard_map/bx,bc->xc/dot_general | solution.py:118
  262.5 1.3 collective-permute-done.4
  264.6 1.4 copy-done.2
  266.8 2.1 reshape.166
  268.9 5.6 %all-to-all-start.1 = ((bf16[16,32,2,192]{3,2,1,0:T(2,128)(2,1)}), bf16[16,32,2,192]{3,2,1,0:T(2,128)(2,1)}, u32[]{:S(2)}, u32[]{:S(2)}) async-start(bf16[16,32,2,192]{3,2,1,0:T(2,128)(2,1)} %reshape.166), calls=%async_computation.1 | async-start | bytes 1048576 | tf_op jit(solution)/shard_map/all_to_all | solution.py:274
  274.5 1.2 multiply_reduce_fusion.2
  275.8 1.3 multiply_reduce_fusion
  277.5 1.0 reshape_reshape.4
  278.6 2.8 convolution_multiply_fusion.2
  281.3 1.4 slice-done
  283.2 5.8 %all-to-all-done.1 = bf16[16,32,2,192]{3,2,1,0:T(2,128)(2,1)} async-done(((bf16[16,32,2,192]{3,2,1,0:T(2,128)(2,1)}), bf16[16,32,2,192]{3,2,1,0:T(2,128)(2,1)}, u32[]{:S(2)}, u32[]{:S(2)}) %all-to-all-start.1) | async-done | bytes 393248 | tf_op jit(solution)/shard_map/all_to_all | solution.py:274
  289.0 1.4 convert_element_type.117
  292.2 1.8 fusion.22
  295.5 1.4 copy.125
  297.0 1.1 broadcast_select_fusion.2
  298.3 1.1 pad_maximum_fusion.3
  299.4 1.0 collective-permute-start.7
  301.3 4.4 %all-to-all-start.2 = ((f32[16,24,384]{2,1,0:T(8,128)}), f32[16,24,384]{2,1,0:T(8,128)S(1)}, u32[]{:S(2)}, u32[]{:S(2)}) async-start(f32[16,24,384]{2,1,0:T(8,128)} %bitcast.57), calls=%async_computation.2 | async-start | bytes 1179648 | tf_op jit(solution)/shard_map/all_to_all | solution.py:176
  305.7 3.4 fusion.38
  309.2 12.1 %all-to-all-done.2 = f32[16,24,384]{2,1,0:T(8,128)S(1)} async-done(((f32[16,24,384]{2,1,0:T(8,128)}), f32[16,24,384]{2,1,0:T(8,128)S(1)}, u32[]{:S(2)}, u32[]{:S(2)}) %all-to-all-start.2) | async-done | bytes 589856 | tf_op jit(solution)/shard_map/all_to_all | solution.py:176
  321.3 6.8 %collective-permute-done.7 = bf16[1024,3,192]{0,2,1:T(8,128)(2,1)} collective-permute-done((bf16[1024,3,192]{0,2,1:T(8,128)(2,1)}, bf16[1024,3,192]{0,2,1:T(8,128)(2,1)}, u32[]{:S(2)}, u32[]{:S(2)}) %collective-permute-start.7) | collective-permute-done | bytes 1179680 | tf_op jit(solution)/shard_map/ppermute | solution.py:144
  328.1 3.4 fusion.18
  332.3 1.6 collective-permute-done.8
  333.9 16.1 %all_to_all.25 = f32[16,12,384]{2,1,0:T(8,128)S(1)} all-to-all(f32[16,12,384]{2,1,0:T(8,128)S(1)} %reshape.170), channel_id=1, replica_groups=mesh['pix'=16,'ch'=2] {'pix'}, dimensions={0} | all-to-all | bytes 589824 | tf_op jit(solution)/shard_map/all_to_all | solution.py:176
  350.1 27.4 %all_to_all.26 = f32[16,36,384]{2,1,0:T(8,128)S(1)} all-to-all(f32[16,36,384]{2,1,0:T(8,128)S(1)} %bitcast.132), channel_id=1, replica_groups=mesh['pix'=16,'ch'=2] {'pix'}, dimensions={0} | all-to-all | bytes 1769472 | tf_op jit(solution)/shard_map/all_to_all | solution.py:187
  377.5 1.1 copy.127
  379.4 1.3 fusion.29
  380.7 1.5 fusion.23
  383.1 1.5 convolution_convert_fusion
  384.6 1.5 copy_select_fusion.1
  387.3 1.3 copy.131
  (179 shorter events, 35.4 us)
Async XLA Ops:
  0.6 27.1 %collective-permute-start = (bf16[1024,384]{1,0:T(8,128)(2,1)}, bf16[1024,384]{1,0:T(8,128)(2,1)S(1)}, u32[]{:S(2)}, u32[]{:S(2)}) collective-permute-start(bf16[1024,384]{1,0:T(8,128)(2,1)} %param.9), channel_id=1, source_target_pairs={{0,1},{1,0},{2,3},{3,2},{4,5},{5,4},{6,7},{7,6},{8,9},{9,8},{10,11... | collective-permute-start | bytes 2359304 | tf_op jit(solution)/shard_map/ppermute | solution.py:144
  3.6 24.1 %collective-permute-start.1 = (bf16[384,384]{1,0:T(8,128)(2,1)}, bf16[384,384]{1,0:T(8,128)(2,1)S(1)}, u32[]{:S(2)}, u32[]{:S(2)}) collective-permute-start(bf16[384,384]{1,0:T(8,128)(2,1)} %param.10), channel_id=1, source_target_pairs={{0,1},{1,0},{2,3},{3,2},{4,5},{5,4},{6,7},{7,6},{8,9},{9,8},{10,11... | collective-permute-start | bytes 884744 | tf_op jit(solution)/shard_map/ppermute | solution.py:144
  10.1 23.0 %copy-start.42 = (s32[512]{0:T(512)}, s32[512]{0:T(512)S(1)}, u32[]{:S(2)}) copy-start(s32[512]{0:T(512)S(1)} %eq.37) | copy-start | bytes 6148
  11.9 17.3 %copy-start.32 = (bf16[3,384,192]{1,2,0:T(8,128)(2,1)S(1)}, bf16[3,384,192]{1,2,0:T(8,128)(2,1)}, u32[]{:S(2)}) copy-start(bf16[3,384,192]{1,2,0:T(8,128)(2,1)} %param.11) | copy-start | bytes 1327108
  28.3 0.9 copy-start.3
  30.0 1.0 copy-start.13
  31.0 3.9 copy-start.23
  31.2 16.1 %collective-permute-start.2 = (bf16[1024,192]{1,0:T(8,128)(2,1)S(1)}, bf16[1024,192]{1,0:T(8,128)(2,1)}, u32[]{:S(2)}, u32[]{:S(2)}) collective-permute-start(bf16[1024,192]{1,0:T(8,128)(2,1)S(1)} %copy.114), channel_id=1, source_target_pairs={{0,1},{1,0},{2,3},{3,2},{4,5},{5,4},{6,7},{7,6},{8,9},{9,8},{10,11... | collective-permute-start | bytes 1179656 | tf_op jit(solution)/shard_map/ppermute | solution.py:144
  34.9 23.6 %all-to-all-start = ((bf16[16,32,2,192]{3,2,1,0:T(2,128)(2,1)}), bf16[16,32,2,192]{3,2,1,0:T(2,128)(2,1)S(1)}, u32[]{:S(2)}, u32[]{:S(2)}) async-start(bf16[16,32,2,192]{3,2,1,0:T(2,128)(2,1)} %reshape.162), calls=%async_computation | async-start | bytes 1048576 | tf_op jit(solution)/shard_map/all_to_all | solution.py:256
  41.4 6.0 %copy-start.35 = (bf16[192,384]{1,0:T(8,128)(2,1)S(1)}, bf16[192,384]{1,0:T(8,128)(2,1)}, u32[]{:S(2)}) copy-start(bf16[192,384]{1,0:T(8,128)(2,1)} %param.12) | copy-start | bytes 442372
  41.6 7.8 %copy-start.29 = (bf16[1024,192]{1,0:T(8,128)(2,1)}, bf16[1024,192]{1,0:T(8,128)(2,1)S(1)}, u32[]{:S(2)}) copy-start(bf16[1024,192]{1,0:T(8,128)(2,1)S(1)} %copy.115) | copy-start | bytes 1179652
  43.6 13.2 %collective-permute-start.3 = (bf16[3,384,192]{1,2,0:T(8,128)(2,1)}, bf16[3,384,192]{1,2,0:T(8,128)(2,1)S(1)}, u32[]{:S(2)}, u32[]{:S(2)}) collective-permute-start(bf16[3,384,192]{1,2,0:T(8,128)(2,1)} %param.11), channel_id=1, source_target_pairs={{0,1},{1,0},{2,3},{3,2},{4,5},{5,4},{6,7},{7,6},{8,9},{9,8},{10,11... | collective-permute-start | bytes 1327112 | tf_op jit(solution)/shard_map/ppermute | solution.py:144
  45.8 216.7 %collective-permute-start.5 = (bf16[192,192]{1,0:T(8,128)(2,1)}, bf16[192,192]{1,0:T(8,128)(2,1)}, u32[]{:S(2)}, u32[]{:S(2)}) collective-permute-start(bf16[192,192]{1,0:T(8,128)(2,1)} %bitcast.122), channel_id=1, source_target_pairs={{0,1},{1,0},{2,3},{3,2},{4,5},{5,4},{6,7},{7,6},{8,9},{9,8},{10,11... | collective-permute-start | bytes 221192 | tf_op jit(solution)/shard_map/ppermute | solution.py:240
  56.8 0.9 copy-start.44
  84.6 11.0 %copy-start.6 = (f32[512,3,64]{0,2,1:T(8,128)S(1)}, f32[512,3,64]{0,2,1:T(8,128)}, u32[]{:S(2)}) copy-start(f32[512,3,64]{0,2,1:T(8,128)} %convert.64) | copy-start | bytes 1179652
  96.1 0.6 copy-start.19
  96.7 0.7 copy-start.36
  97.4 11.0 %copy-start.24 = (bf16[1024,2,192]{0,2,1:T(8,128)(2,1)S(1)}, bf16[1024,2,192]{0,2,1:T(8,128)(2,1)}, u32[]{:S(2)}) copy-start(bf16[1024,2,192]{0,2,1:T(8,128)(2,1)} %copy-done.23) | copy-start | bytes 2359300
  97.4 11.0 %copy-start.33 = (bf16[512,384]{0,1:T(8,128)(2,1)S(1)}, bf16[512,384]{0,1:T(8,128)(2,1)}, u32[]{:S(2)}) copy-start(bf16[512,384]{0,1:T(8,128)(2,1)} %copy.107) | copy-start | bytes 1179652
  97.4 11.0 %copy-start.41 = (s32[4608]{0:T(1024)S(1)}, s32[4608]{0:T(1024)}, u32[]{:S(2)}) copy-start(s32[4608]{0:T(1024)} %eq.41) | copy-start | bytes 55300
  152.7 0.6 copy-start.21
  153.3 0.7 copy-start.38
  164.9 3.8 copy-start.10
  164.9 4.4 %copy-start.9 = (f32[512,3,64]{0,2,1:T(8,128)S(1)}, f32[512,3,64]{0,2,1:T(8,128)}, u32[]{:S(2)}) copy-start(f32[512,3,64]{0,2,1:T(8,128)} %convert.68) | copy-start | bytes 1179652
  168.6 0.6 copy-start.27
  202.5 11.9 %copy-start = (bf16[512,9,1,192]{0,3,1,2:T(8,128)(2,1)S(1)}, bf16[512,9,1,192]{0,3,1,2:T(8,128)(2,1)}, u32[]{:S(2)}) copy-start(bf16[512,9,1,192]{0,3,1,2:T(8,128)(2,1)} %copy.180) | copy-start | bytes 5308420
  202.6 11.9 %copy-start.8 = (f32[512,3,64]{0,2,1:T(8,128)S(1)}, f32[512,3,64]{0,2,1:T(8,128)}, u32[]{:S(2)}) copy-start(f32[512,3,64]{0,2,1:T(8,128)} %convert.72) | copy-start | bytes 1179652
  202.6 12.4 %copy-start.20 = (f32[512,3,9]{0,1,2:T(4,128)S(1)}, f32[512,3,9]{0,1,2:T(4,128)}, u32[]{:S(2)}) copy-start(f32[512,3,9]{0,1,2:T(4,128)} %copy-done.19) | copy-start | bytes 165892
  202.6 12.4 %copy-start.37 = (f32[512,3]{0,1:T(4,128)S(1)}, f32[512,3]{0,1:T(4,128)}, u32[]{:S(2)}) copy-start(f32[512,3]{0,1:T(4,128)} %copy-done.36) | copy-start | bytes 18436
  202.6 12.4 %copy-start.39 = (f32[512,3]{0,1:T(4,128)S(1)}, f32[512,3]{0,1:T(4,128)}, u32[]{:S(2)}) copy-start(f32[512,3]{0,1:T(4,128)} %fusion.34) | copy-start | bytes 18436
  214.5 1.3 copy-start.7
  215.7 0.6 copy-start.28
  249.9 2.0 copy-start.1
  249.9 4.1 %copy-start.5 = (bf16[4608,384]{1,0:T(8,128)(2,1)S(1)}, bf16[4608,384]{1,0:T(8,128)(2,1)}, u32[]{:S(2)}) copy-start(bf16[4608,384]{1,0:T(8,128)(2,1)} %convert_element_type.112) | copy-start | bytes 10616836
  249.9 4.1 %copy-start.40 = (s32[4608]{0:T(1024)S(1)}, s32[4608]{0:T(1024)}, u32[]{:S(2)}) copy-start(s32[4608]{0:T(1024)} %eq.33) | copy-start | bytes 55300
  253.4 9.1 %copy-start.15 = (bf16[2,24,8,512]{3,2,0,1:T(8,128)(2,1)}, bf16[2,24,8,512]{3,2,0,1:T(8,128)(2,1)S(1)}, u32[]{:S(2)}) copy-start(bf16[2,24,8,512]{3,2,0,1:T(8,128)(2,1)S(1)} %copy.199) | copy-start | bytes 1179652
  253.4 10.4 %copy-start.12 = (f32[1536,384]{1,0:T(8,128)S(1)}, f32[1536,384]{1,0:T(8,128)}, u32[]{:S(2)}) copy-start(f32[1536,384]{1,0:T(8,128)} %fusion) | copy-start | bytes 7077892
  253.4 10.4 %collective-permute-start.4 = (bf16[1024,192]{0,1:T(8,128)(2,1)S(1)}, bf16[1024,192]{0,1:T(8,128)(2,1)S(1)}, u32[]{:S(2)}, u32[]{:S(2)}) collective-permute-start(bf16[1024,192]{0,1:T(8,128)(2,1)S(1)} %bitcast.138), channel_id=1, source_target_pairs={{0,1},{1,0},{2,3},{3,2},{4,5},{5,4},{6,7},{7,6},{8,9},{9,8},{10,11... | collective-permute-start | bytes 1179656 | tf_op jit(solution)/shard_map/ppermute | solution.py:144
  263.8 0.8 copy-start.34
  264.6 1.4 copy-start.2
  268.9 20.1 %all-to-all-start.1 = ((bf16[16,32,2,192]{3,2,1,0:T(2,128)(2,1)}), bf16[16,32,2,192]{3,2,1,0:T(2,128)(2,1)}, u32[]{:S(2)}, u32[]{:S(2)}) async-start(bf16[16,32,2,192]{3,2,1,0:T(2,128)(2,1)} %reshape.166), calls=%async_computation.1 | async-start | bytes 1048576 | tf_op jit(solution)/shard_map/all_to_all | solution.py:274
  275.7 2.8 copy-start.16
  275.7 2.8 copy-start.30
  281.3 1.4 slice-start
  282.7 7.8 %copy-start.43 = (s32[512]{0:T(512)S(1)}, s32[512]{0:T(512)}, u32[]{:S(2)}) copy-start(s32[512]{0:T(512)} %copy-done.42) | copy-start | bytes 6148
  283.2 9.0 %copy-start.4 = (bf16[1024,384]{1,0:T(8,128)(2,1)S(1)}, bf16[1024,384]{1,0:T(8,128)(2,1)}, u32[]{:S(2)}) copy-start(bf16[1024,384]{1,0:T(8,128)(2,1)} %copy-done.3) | copy-start | bytes 2359300
  291.3 0.9 copy-start.25
  295.4 2.8 copy-start.14
  297.0 1.2 copy-start.26
  297.0 3.4 copy-start.18
  298.2 2.2 collective-permute-start.6
  299.4 28.7 %collective-permute-start.7 = (bf16[1024,3,192]{0,2,1:T(8,128)(2,1)}, bf16[1024,3,192]{0,2,1:T(8,128)(2,1)}, u32[]{:S(2)}, u32[]{:S(2)}) collective-permute-start(bf16[1024,3,192]{0,2,1:T(8,128)(2,1)} %pad_maximum_fusion.3), channel_id=1, source_target_pairs={{0,1},{1,0},{2,3},{3,2},{4,5},{5,4},{6,7},{7,6},{8,9},{9,8},{10,11... | collective-permute-start | bytes 3538952 | tf_op jit(solution)/shard_map/ppermute | solution.py:144
  301.3 19.9 %all-to-all-start.2 = ((f32[16,24,384]{2,1,0:T(8,128)}), f32[16,24,384]{2,1,0:T(8,128)S(1)}, u32[]{:S(2)}, u32[]{:S(2)}) async-start(f32[16,24,384]{2,1,0:T(8,128)} %bitcast.57), calls=%async_computation.2 | async-start | bytes 1179648 | tf_op jit(solution)/shard_map/all_to_all | solution.py:176
  305.7 22.4 %copy-start.31 = (bf16[1024,192]{1,0:T(8,128)(2,1)S(1)}, bf16[1024,192]{1,0:T(8,128)(2,1)}, u32[]{:S(2)}) copy-start(bf16[1024,192]{1,0:T(8,128)(2,1)} %copy-done.29) | copy-start | bytes 1179652
  321.3 10.2 %copy-start.11 = (bf16[1024,384]{1,0:T(8,128)(2,1)S(1)}, bf16[1024,384]{1,0:T(8,128)(2,1)}, u32[]{:S(2)}) copy-start(bf16[1024,384]{1,0:T(8,128)(2,1)} %param.9) | copy-start | bytes 2359300
  332.2 1.6 collective-permute-start.8
  350.1 29.3 %copy-start.17 = (bf16[2,24,8,512]{3,2,0,1:T(8,128)(2,1)S(1)}, bf16[2,24,8,512]{3,2,0,1:T(8,128)(2,1)}, u32[]{:S(2)}) copy-start(bf16[2,24,8,512]{3,2,0,1:T(8,128)(2,1)} %copy-done.15) | copy-start | bytes 1179652
  378.6 6.0 %collective-permute-start.9 = (f32[16,36,384]{2,0,1:T(8,128)}, f32[16,36,384]{2,0,1:T(8,128)}, u32[]{:S(2)}, u32[]{:S(2)}) collective-permute-start(f32[16,36,384]{2,0,1:T(8,128)} %copy.127), channel_id=1, source_target_pairs={{0,2},{2,0},{4,6},{6,4},{8,10},{10,8},{12,14},{14,12},{16,18},{18,... | collective-permute-start | bytes 2654216 | tf_op jit(solution)/shard_map/ppermute | solution.py:162
  379.4 3.7 copy-start.22

commit v11 on v4

--- a/solution.py
+++ b/solution.py
@@ -31,7 +31,6 @@
     score_scale = 1.0 / math.sqrt(HD)
     block_rows = math.gcd(row_count, 512)
     block_count = row_count // block_rows
-    block_starts = row_offset + jnp.arange(block_count, dtype=jnp.int32) * block_rows
     query_blocks = queries.reshape(block_count, block_rows, span)
     neighbour_blocks = neighbours.reshape(block_count, block_rows, slot_width - 1)
     flattened = extended.reshape(ext_rows, 2 * span)
@@ -39,11 +38,11 @@
     def forward_block(inputs):
         query_block, neighbour_block, first_row = inputs
         slot_rows, slot_live = slot_index(neighbour_block, first_row, block_rows)
-        pieces = [
+        pieces = [flattened[first_row : first_row + block_rows]] + [
             jnp.dot(
                 pick_table(slot_rows[:, slot], ext_rows), flattened, preferred_element_type=f32
             ).astype(bf16)
-            for slot in range(slot_width)
+            for slot in range(1, slot_width)
         ]
         gathered = jnp.stack(pieces, axis=1).reshape(block_rows, slot_width, 2, span)
         block_keys = gathered[:, :, 0].reshape(block_rows, slot_width, heads_here, HD)
@@ -67,7 +66,7 @@
         return (mixture.reshape(block_rows, span).astype(bf16), probabilities, gathered)
 
     outputs = [
-        forward_block((query_blocks[b], neighbour_blocks[b], block_starts[b]))
+        forward_block((query_blocks[b], neighbour_blocks[b], row_offset + b * block_rows))
         for b in range(block_count)
     ]
     attn_blocks = jnp.stack([out[0] for out in outputs])
@@ -88,7 +87,6 @@
     score_scale = 1.0 / math.sqrt(HD)
     block_rows = math.gcd(row_count, 512)
     block_count = row_count // block_rows
-    block_starts = row_offset + jnp.arange(block_count, dtype=jnp.int32) * block_rows
     query_blocks = queries.reshape(block_count, block_rows, span)
     neighbour_blocks = neighbours.reshape(block_count, block_rows, slot_width - 1)
     grad_blocks = grad_attended.reshape(block_count, block_rows, span)
@@ -115,27 +113,29 @@
             .reshape(block_rows, slot_width, 2 * span)
             .astype(bf16)
         )
-        for slot in range(slot_width):
+        for slot in range(1, slot_width):
             carried = carried + jnp.einsum(
                 "bx,bc->xc",
                 pick_table(slot_rows[:, slot], ext_rows),
                 contribution[:, slot],
                 preferred_element_type=f32,
             )
-        return (carried, grad_query)
+        return (carried, (grad_query, contribution[:, 0]))
 
     carried = jnp.zeros((ext_rows, 2 * span), f32)
     query_grads = []
     for b in range(block_count):
         carried, grad_query = backward_block(
             carried,
-            (query_blocks[b], neighbour_blocks[b], block_starts[b], grad_blocks[b],
+            (query_blocks[b], neighbour_blocks[b], row_offset + b * block_rows, grad_blocks[b],
              prob_blocks[b], kv_blocks[b]),
         )
         query_grads.append(grad_query)
         if b == 0:
             carried, riders = lax.optimization_barrier((carried, riders))
-    query_grads = jnp.stack(query_grads)
+    own_grads = jnp.concatenate([pair[1] for pair in query_grads], axis=0)
+    query_grads = jnp.stack([pair[0] for pair in query_grads])
+    carried = carried.at[:row_count].add(own_grads.astype(f32))
     return (carried.reshape(ext_rows, 2, span), query_grads.reshape(row_count, span), riders)
 
 

time: 252 us -> 252 us (level)
  matrix products: 78.7 us -> 59.1 us
  waiting for transfers between devices: 52 us -> 63.8 us
  local copies, waits for them, and re-layouts: 24.2 us -> 34.8 us
  other arithmetic: 19.3 us -> 15.8 us
    dot_general x18 -> x16, matrix products: 37.2 us -> 20.2 us  [backward_block(): jnp.einsum('bx,bc->xc', pick_table(slot_rows[:, slot], ext_rows), contrib...]
    ppermute x6, waiting for transfers between devices: 32.2 us -> 48.6 us  [ch_exchange(): lax.ppermute(value, 'ch', [(i, (i + shift) % size) for i in range(size)])]
    all_to_all x1, waiting for transfers between devices: 5.87 us -> 1.17 us  [per_device(): lax.all_to_all(remote_grads, 'pix', split_axis=0, concat_axis=0, tiled=True)]
    unnamed x118 -> x80, local copies, waits for them, and re-layouts: 7.27 us -> 11.9 us
    dot_general x18 -> x16, matrix products: 18 us -> 16.9 us  [forward_block(): jnp.dot(pick_table(slot_rows[:, slot], ext_rows), flattened, preferred_el...]
  transfers between devices with their start and end apart: 13 -> 13, of which waited for: 7 -> 8; matrix products, arithmetic and copies ran while one was open for 36% -> 30% of each run, Pallas kernels for 0% -> 0%
where the time goes in v11:
time: 252 us; the launch traced here: 247 us
  waiting for transfers between devices  63.8 us (25%)
  matrix products  59.1 us (23%)
  blocking collectives  43.9 us (17%)
  local copies, waits for them, and re-layouts  34.8 us (14%)
  starting transfers between devices  28.1 us (11%)
  other arithmetic  15.8 us (6%)
    ppermute x6, waiting for transfers between devices, ch_exchange(): lax.ppermute(value, 'ch', [(i, (i + shift) % size) for i in range(size)])  48.6 us
    all_to_all x1, blocking collectives, pix_gather(): lax.all_to_all(spread.reshape(size, total, width), 'pix', 0, 0, tiled=True)  27.2 us
    dot_general x16, matrix products, backward_block(): jnp.einsum('bx,bc->xc', pick_table(slot_rows[:, slot], ext_rows), contrib...  20.2 us
    dot_general x16, matrix products, forward_block(): jnp.dot(pick_table(slot_rows[:, slot], ext_rows), flattened, preferred_el...  16.9 us
    all_to_all x1, blocking collectives, pix_scatter(): lax.all_to_all(mine.reshape(size, chunk, width), 'pix', 0, 0, tiled=True)  16.8 us
    all_to_all x1, waiting for transfers between devices, pix_scatter(): lax.all_to_all(mine.reshape(size, chunk, width), 'pix', 0, 0, tiled=True)  12.4 us
    unnamed x80, local copies, waits for them, and re-layouts  11.9 us
    ppermute x6, starting transfers between devices, ch_exchange(): lax.ppermute(value, 'ch', [(i, (i + shift) % size) for i in range(size)])  8.22 us
  transfers between devices with their start and end apart: 13, of which 8 were waited for; matrix products, arithmetic and copies ran while one was open for 30% of the time, Pallas kernels for 0%

profile of v11, /device:TPU:0, one launch (start us, length us, event | category | flops | bytes accessed | tf_op | source)
XLA Modules:
  0.0 247.4 jit_solution(13452404353455707526)
XLA Ops:
  0.7 3.0 %collective-permute-start = (bf16[1024,384]{1,0:T(8,128)(2,1)}, bf16[1024,384]{1,0:T(8,128)(2,1)S(1)}, u32[]{:S(2)}, u32[]{:S(2)}) collective-permute-start(bf16[1024,384]{1,0:T(8,128)(2,1)} %param.11), channel_id=1, source_target_pairs={{0,1},{1,0},{2,3},{3,2},{4,5},{5,4},{6,7},{7,6},{8,9},{9,8},{10,11... | collective-permute-start | bytes 2359304 | tf_op jit(solution)/shard_map/ppermute | solution.py:145
  3.7 1.1 reshape.203
  6.2 1.2 broadcast_select_fusion
  8.8 1.2 copy.109
  10.7 17.1 %collective-permute-done.1 = bf16[384,384]{1,0:T(8,128)(2,1)} collective-permute-done((bf16[384,384]{1,0:T(8,128)(2,1)}, bf16[384,384]{1,0:T(8,128)(2,1)}, u32[]{:S(2)}, u32[]{:S(2)}) %collective-permute-start.1) | collective-permute-done | bytes 294944 | tf_op jit(solution)/shard_map/ppermute | solution.py:145
  27.8 1.6 add_convert_fusion.1
  32.1 1.1 reshape.204
  33.2 6.8 %all-to-all-start = ((bf16[16,32,2,192]{3,2,1,0:T(2,128)(2,1)}), bf16[16,32,2,192]{3,2,1,0:T(2,128)(2,1)}, u32[]{:S(2)}, u32[]{:S(2)}) async-start(bf16[16,32,2,192]{3,2,1,0:T(2,128)(2,1)} %reshape.204), calls=%async_computation | async-start | bytes 1048576 | tf_op jit(solution)/shard_map/all_to_all | solution.py:257
  41.0 1.5 collective-permute-start.2
  43.2 1.6 collective-permute-start.5
  45.7 10.2 %collective-permute-done.2 = bf16[1024,192]{1,0:T(8,128)(2,1)S(1)} collective-permute-done((bf16[1024,192]{1,0:T(8,128)(2,1)}, bf16[1024,192]{1,0:T(8,128)(2,1)S(1)}, u32[]{:S(2)}, u32[]{:S(2)}) %collective-permute-start.2) | collective-permute-done | bytes 393248 | tf_op jit(solution)/shard_map/ppermute | solution.py:145
  56.7 8.7 %collective-permute-done.3 = bf16[3,384,192]{1,2,0:T(8,128)(2,1)S(1)} collective-permute-done((bf16[3,384,192]{1,2,0:T(8,128)(2,1)}, bf16[3,384,192]{1,2,0:T(8,128)(2,1)S(1)}, u32[]{:S(2)}, u32[]{:S(2)}) %collective-permute-start.3) | collective-permute-done | bytes 442400 | tf_op jit(solution)/shard_map/ppermute | solution.py:145
  66.3 1.4 concatenate.45
  68.6 2.3 fusion.100
  78.8 1.3 copy-done.4
  83.3 1.3 fusion.53
  84.6 1.2 fusion.51
  96.5 1.2 fusion.40
  97.7 1.4 convolution_add_fusion.11
  99.1 1.2 convolution_add_fusion.10
  100.3 1.2 convolution_add_fusion.9
  101.5 1.2 convolution_add_fusion.8
  102.7 1.2 convolution_add_fusion.7
  103.9 1.2 convolution_add_fusion.6
  105.2 1.2 convolution_add_fusion.5
  106.4 1.6 collective-permute-start.4
  107.9 1.2 fusion.49
  109.5 7.0 %collective-permute-done.4 = bf16[1024,192]{0,1:T(8,128)(2,1)S(1)} collective-permute-done((bf16[1024,192]{0,1:T(8,128)(2,1)S(1)}, bf16[1024,192]{0,1:T(8,128)(2,1)S(1)}, u32[]{:S(2)}, u32[]{:S(2)}) %collective-permute-start.4) | collective-permute-done | bytes 393248 | tf_op jit(solution)/shard_map/ppermute | solution.py:145
  116.4 1.6 convolution_add_fusion.4
  118.0 1.2 convolution_add_fusion.3
  119.2 1.6 convolution_add_fusion.2
  120.8 1.2 convolution_add_fusion.1
  122.0 1.2 convolution_add_fusion
  123.2 1.5 copy-done.2
  124.8 1.1 reshape.206
  125.8 5.6 %all-to-all-start.1 = ((bf16[16,32,2,192]{3,2,1,0:T(2,128)(2,1)}), bf16[16,32,2,192]{3,2,1,0:T(2,128)(2,1)}, u32[]{:S(2)}, u32[]{:S(2)}) async-start(bf16[16,32,2,192]{3,2,1,0:T(2,128)(2,1)} %reshape.206), calls=%async_computation.1 | async-start | bytes 1048576 | tf_op jit(solution)/shard_map/all_to_all | solution.py:275
  131.8 1.0 slice.367
  132.8 1.0 slice.366
  135.7 1.2 copy.113
  136.9 1.4 reshape_reshape.4
  138.3 3.2 %convolution_multiply_fusion.2 = f32[192,384]{1,0:T(8,128)} fusion(bf16[1024,192]{0,1:T(8,128)(2,1)} %bitcast.237, bf16[1024,192]{1,0:T(8,128)(2,1)} %copy-done.22, bf16[1024,192]{1,0:T(8,128)(2,1)} %copy-done.28, pred[]{:T(512)S(6)} %eq.213), kind=kOutput, calls=%fused_computation.152 | convolution fusion | flops 154607616 | bytes 1474561 | tf_op jit(solution)/shard_map/dot_general | solution.py:265
  141.6 1.3 slice_add_fusion
  142.9 1.9 copy.124
  144.8 1.2 all-to-all-done.1
  145.9 1.4 convert_element_type.203
  148.2 1.7 add_convert_fusion
  152.1 1.3 copy.126
  153.9 1.1 broadcast_select_fusion.2
  155.2 1.1 pad_maximum_fusion.3
  156.4 1.5 collective-permute-start.7
  158.8 5.0 %all-to-all-start.2 = ((f32[16,24,384]{2,1,0:T(8,128)}), f32[16,24,384]{2,1,0:T(8,128)S(1)}, u32[]{:S(2)}, u32[]{:S(2)}) async-start(f32[16,24,384]{2,1,0:T(8,128)} %bitcast.101), calls=%async_computation.2 | async-start | bytes 1179648 | tf_op jit(solution)/shard_map/all_to_all | solution.py:177
  163.8 3.1 %fusion.128 = f32[1024,384,1]{1,0,2:T(8,128)} fusion(bf16[3,384,192]{1,2,0:T(8,128)(2,1)} %param.13, bf16[1024,2,192]{0,2,1:T(8,128)(2,1)S(1)} %copy-done.21, bf16[1024,1,192]{0,2,1:T(8,128)(2,1)S(1)} %copy-done.10), kind=kOutput, calls=%fused_computation.229 | convolution fusion | flops 453574656 | bytes 3194880 | tf_op jit(solution)/shard_map/rkd,kcd->rc/dot_general | solution.py:293
  166.9 12.4 %all-to-all-done.2 = f32[16,24,384]{2,1,0:T(8,128)S(1)} async-done(((f32[16,24,384]{2,1,0:T(8,128)}), f32[16,24,384]{2,1,0:T(8,128)S(1)}, u32[]{:S(2)}, u32[]{:S(2)}) %all-to-all-start.2) | async-done | bytes 589856 | tf_op jit(solution)/shard_map/all_to_all | solution.py:177
  179.4 5.6 %collective-permute-done.7 = bf16[1024,3,192]{0,2,1:T(8,128)(2,1)} collective-permute-done((bf16[1024,3,192]{0,2,1:T(8,128)(2,1)}, bf16[1024,3,192]{0,2,1:T(8,128)(2,1)}, u32[]{:S(2)}, u32[]{:S(2)}) %collective-permute-start.7) | collective-permute-done | bytes 1179680 | tf_op jit(solution)/shard_map/ppermute | solution.py:145
  185.0 3.7 %fusion.60 = bf16[1024,384]{1,0:T(8,128)(2,1)S(1)} fusion(f32[1024,384,1]{1,0,2:T(8,128)} %fusion.128, bf16[1024,3,192]{0,2,1:T(8,128)(2,1)} %collective-permute-done.7, bf16[3,384,192]{1,2,0:T(8,128)(2,1)} %copy-done.29, bf16[1024,192]{1,0:T(8,128)(2,1)} %copy-done.28, bf16[1024,192]{1,0:T(8,128)(2,1)} %copy-done.22, pred[]{:T(512)S(6)} %eq.213), kind=kOutput, calls=%fused_computation.88 | convolution fusion | flops 458096640 | bytes 4767745 | tf_op jit(solution)/shard_map/rkd,kcd->rc/dot_general | solution.py:297
  189.5 1.6 collective-permute-done.8
  191.1 16.8 %all_to_all.25 = f32[16,12,384]{2,1,0:T(8,128)S(1)} all-to-all(f32[16,12,384]{2,1,0:T(8,128)S(1)} %reshape.210), channel_id=1, replica_groups=mesh['pix'=16,'ch'=2] {'pix'}, dimensions={0} | all-to-all | bytes 589824 | tf_op jit(solution)/shard_map/all_to_all | solution.py:177
  208.0 27.2 %all_to_all.26 = f32[16,36,384]{2,1,0:T(8,128)S(1)} all-to-all(f32[16,36,384]{2,1,0:T(8,128)S(1)} %bitcast.230), channel_id=1, replica_groups=mesh['pix'=16,'ch'=2] {'pix'}, dimensions={0} | all-to-all | bytes 1769472 | tf_op jit(solution)/shard_map/all_to_all | solution.py:188
  235.2 1.1 copy.128
  237.0 1.3 fusion.121
  238.4 1.5 fusion.97
  240.8 1.5 convolution_convert_fusion
  242.3 1.5 copy_select_fusion.1
  245.1 1.3 copy.132
  (178 shorter events, 44.7 us)
Async XLA Ops:
  0.6 9.4 %copy-start.6 = (bf16[1024,384]{1,0:T(8,128)(2,1)S(1)}, bf16[1024,384]{1,0:T(8,128)(2,1)}, u32[]{:S(2)}) copy-start(bf16[1024,384]{1,0:T(8,128)(2,1)} %param.11) | copy-start | bytes 2359300
  0.6 9.4 %copy-start.16 = (bf16[384,384]{1,0:T(8,128)(2,1)S(1)}, bf16[384,384]{1,0:T(8,128)(2,1)}, u32[]{:S(2)}) copy-start(bf16[384,384]{1,0:T(8,128)(2,1)} %param.12) | copy-start | bytes 884740
  0.7 27.2 %collective-permute-start = (bf16[1024,384]{1,0:T(8,128)(2,1)}, bf16[1024,384]{1,0:T(8,128)(2,1)S(1)}, u32[]{:S(2)}, u32[]{:S(2)}) collective-permute-start(bf16[1024,384]{1,0:T(8,128)(2,1)} %param.11), channel_id=1, source_target_pairs={{0,1},{1,0},{2,3},{3,2},{4,5},{5,4},{6,7},{7,6},{8,9},{9,8},{10,11... | collective-permute-start | bytes 2359304 | tf_op jit(solution)/shard_map/ppermute | solution.py:145
  3.7 24.2 %collective-permute-start.1 = (bf16[384,384]{1,0:T(8,128)(2,1)}, bf16[384,384]{1,0:T(8,128)(2,1)}, u32[]{:S(2)}, u32[]{:S(2)}) collective-permute-start(bf16[384,384]{1,0:T(8,128)(2,1)} %param.12), channel_id=1, source_target_pairs={{0,1},{1,0},{2,3},{3,2},{4,5},{5,4},{6,7},{7,6},{8,9},{9,8},{10,11... | collective-permute-start | bytes 884744 | tf_op jit(solution)/shard_map/ppermute | solution.py:145
  10.0 46.0 %copy-start.22 = (bf16[1024,192]{1,0:T(8,128)(2,1)}, bf16[1024,192]{1,0:T(8,128)(2,1)S(1)}, u32[]{:S(2)}) copy-start(bf16[1024,192]{1,0:T(8,128)(2,1)S(1)} %copy.109) | copy-start | bytes 1179652
  10.7 18.7 %copy-start.23 = (bf16[3,384,192]{1,2,0:T(8,128)(2,1)S(1)}, bf16[3,384,192]{1,2,0:T(8,128)(2,1)}, u32[]{:S(2)}) copy-start(bf16[3,384,192]{1,2,0:T(8,128)(2,1)} %param.13) | copy-start | bytes 1327108
  30.5 0.9 copy-start.18
  30.5 9.5 %copy-start.8 = (bf16[1024,192]{0,1:T(8,128)(2,1)S(1)}, bf16[1024,192]{0,1:T(8,128)(2,1)}, u32[]{:S(2)}) copy-start(bf16[1024,192]{0,1:T(8,128)(2,1)} %param.17) | copy-start | bytes 1179652
  33.2 33.1 %all-to-all-start = ((bf16[16,32,2,192]{3,2,1,0:T(2,128)(2,1)}), bf16[16,32,2,192]{3,2,1,0:T(2,128)(2,1)}, u32[]{:S(2)}, u32[]{:S(2)}) async-start(bf16[16,32,2,192]{3,2,1,0:T(2,128)(2,1)} %reshape.204), calls=%async_computation | async-start | bytes 1048576 | tf_op jit(solution)/shard_map/all_to_all | solution.py:257
  41.0 15.0 %copy-start.26 = (bf16[192,384]{1,0:T(8,128)(2,1)S(1)}, bf16[192,384]{1,0:T(8,128)(2,1)}, u32[]{:S(2)}) copy-start(bf16[192,384]{1,0:T(8,128)(2,1)} %param.14) | copy-start | bytes 442372
  41.0 15.0 %collective-permute-start.2 = (bf16[1024,192]{1,0:T(8,128)(2,1)}, bf16[1024,192]{1,0:T(8,128)(2,1)S(1)}, u32[]{:S(2)}, u32[]{:S(2)}) collective-permute-start(bf16[1024,192]{1,0:T(8,128)(2,1)} %copy.108), channel_id=1, source_target_pairs={{0,1},{1,0},{2,3},{3,2},{4,5},{5,4},{6,7},{7,6},{8,9},{9,8},{10,11... | collective-permute-start | bytes 1179656 | tf_op jit(solution)/shard_map/ppermute | solution.py:145
  42.5 22.9 %collective-permute-start.3 = (bf16[3,384,192]{1,2,0:T(8,128)(2,1)}, bf16[3,384,192]{1,2,0:T(8,128)(2,1)S(1)}, u32[]{:S(2)}, u32[]{:S(2)}) collective-permute-start(bf16[3,384,192]{1,2,0:T(8,128)(2,1)} %param.13), channel_id=1, source_target_pairs={{0,1},{1,0},{2,3},{3,2},{4,5},{5,4},{6,7},{7,6},{8,9},{9,8},{10,11... | collective-permute-start | bytes 1327112 | tf_op jit(solution)/shard_map/ppermute | solution.py:145
  43.2 66.2 %collective-permute-start.5 = (bf16[192,192]{1,0:T(8,128)(2,1)}, bf16[192,192]{1,0:T(8,128)(2,1)}, u32[]{:S(2)}, u32[]{:S(2)}) collective-permute-start(bf16[192,192]{1,0:T(8,128)(2,1)} %bitcast.285), channel_id=1, source_target_pairs={{0,1},{1,0},{2,3},{3,2},{4,5},{5,4},{6,7},{7,6},{8,9},{9,8},{10,11... | collective-permute-start | bytes 221192 | tf_op jit(solution)/shard_map/ppermute | solution.py:241
  56.0 9.6 %copy-start.28 = (bf16[1024,192]{1,0:T(8,128)(2,1)}, bf16[1024,192]{1,0:T(8,128)(2,1)S(1)}, u32[]{:S(2)}) copy-start(bf16[1024,192]{1,0:T(8,128)(2,1)S(1)} %collective-permute-done.2) | copy-start | bytes 1179652
  65.4 0.8 copy-start.29
  68.6 2.3 copy-start.19
  68.6 2.3 copy-start.24
  71.9 1.0 copy-start.27
  76.8 2.0 copy-start.5
  77.8 2.3 copy-start.4
  83.3 38.8 %copy-start.1 = (bf16[512,9,2,3,64]{0,4,3,2,1:T(8,128)(2,1)}, bf16[512,9,2,3,64]{0,4,3,2,1:T(8,128)(2,1)S(1)}, u32[]{:S(2)}) copy-start(bf16[512,9,2,3,64]{0,4,3,2,1:T(8,128)(2,1)S(1)} %pad_maximum_fusion.1) | copy-start | bytes 10616836
  95.1 11.2 %copy-start.11 = (bf16[2,24,8,512]{3,2,0,1:T(8,128)(2,1)}, bf16[2,24,8,512]{3,2,0,1:T(8,128)(2,1)S(1)}, u32[]{:S(2)}) copy-start(bf16[2,24,8,512]{3,2,0,1:T(8,128)(2,1)S(1)} %copy.201) | copy-start | bytes 1179652
  96.5 8.6 %copy-start = (bf16[512,9,2,3,64]{0,4,3,2,1:T(8,128)(2,1)}, bf16[512,9,2,3,64]{0,4,3,2,1:T(8,128)(2,1)S(1)}, u32[]{:S(2)}) copy-start(bf16[512,9,2,3,64]{0,4,3,2,1:T(8,128)(2,1)S(1)} %pad_maximum_fusion) | copy-start | bytes 10616836
  106.4 10.1 %collective-permute-start.4 = (bf16[1024,192]{0,1:T(8,128)(2,1)S(1)}, bf16[1024,192]{0,1:T(8,128)(2,1)S(1)}, u32[]{:S(2)}, u32[]{:S(2)}) collective-permute-start(bf16[1024,192]{0,1:T(8,128)(2,1)S(1)} %bitcast.236), channel_id=1, source_target_pairs={{0,1},{1,0},{2,3},{3,2},{4,5},{5,4},{6,7},{7,6},{8,9},{9,8},{10,11... | collective-permute-start | bytes 1179656 | tf_op jit(solution)/shard_map/ppermute | solution.py:145
  116.4 1.6 copy-start.25
  123.2 1.5 copy-start.2
  125.8 20.1 %all-to-all-start.1 = ((bf16[16,32,2,192]{3,2,1,0:T(2,128)(2,1)}), bf16[16,32,2,192]{3,2,1,0:T(2,128)(2,1)}, u32[]{:S(2)}, u32[]{:S(2)}) async-start(bf16[16,32,2,192]{3,2,1,0:T(2,128)(2,1)} %reshape.206), calls=%async_computation.1 | async-start | bytes 1048576 | tf_op jit(solution)/shard_map/all_to_all | solution.py:275
  136.9 4.7 %copy-start.3 = (f32[1536,384]{1,0:T(8,128)S(1)}, f32[1536,384]{1,0:T(8,128)}, u32[]{:S(2)}) copy-start(f32[1536,384]{1,0:T(8,128)} %copy-done.2) | copy-start | bytes 7077892
  138.3 11.7 %copy-start.9 = (bf16[1024,1,192]{0,2,1:T(8,128)(2,1)}, bf16[1024,1,192]{0,2,1:T(8,128)(2,1)S(1)}, u32[]{:S(2)}) copy-start(bf16[1024,1,192]{0,2,1:T(8,128)(2,1)S(1)} %reshape_reshape.4) | copy-start | bytes 1179652
  138.3 3.3 %copy-start.13 = (bf16[512,1,384]{2,0,1:T(8,128)(2,1)S(1)}, bf16[512,1,384]{2,0,1:T(8,128)(2,1)}, u32[]{:S(2)}) copy-start(bf16[512,1,384]{2,0,1:T(8,128)(2,1)} %copy.190) | copy-start | bytes 1179652
  138.3 3.3 %copy-start.14 = (bf16[512,1,384]{2,0,1:T(8,128)(2,1)S(1)}, bf16[512,1,384]{2,0,1:T(8,128)(2,1)}, u32[]{:S(2)}) copy-start(bf16[512,1,384]{2,0,1:T(8,128)(2,1)} %copy.189) | copy-start | bytes 1179652
  150.0 0.9 copy-start.20
  153.9 1.3 copy-start.10
  153.9 1.3 copy-start.21
  153.9 3.9 %copy-start.15 = (f32[192,384]{1,0:T(8,128)S(1)}, f32[192,384]{1,0:T(8,128)}, u32[]{:S(2)}) copy-start(f32[192,384]{1,0:T(8,128)} %convolution_multiply_fusion.2) | copy-start | bytes 884740
  155.1 2.8 %collective-permute-start.6 = (f32[384,384]{1,0:T(8,128)S(1)}, f32[384,384]{1,0:T(8,128)S(1)}, u32[]{:S(2)}, u32[]{:S(2)}) collective-permute-start(f32[384,384]{1,0:T(8,128)S(1)} %broadcast_select_fusion.2), channel_id=1, source_target_pairs={{0,2},{2,0},{4,6},{6,4},{8,10},{10,8},{12,14},{14,12},{16,18},{18,... | collective-permute-start | bytes 1769480 | tf_op jit(solution)/shard_map/ppermute | solution.py:163
  156.4 28.6 %collective-permute-start.7 = (bf16[1024,3,192]{0,2,1:T(8,128)(2,1)}, bf16[1024,3,192]{0,2,1:T(8,128)(2,1)}, u32[]{:S(2)}, u32[]{:S(2)}) collective-permute-start(bf16[1024,3,192]{0,2,1:T(8,128)(2,1)} %pad_maximum_fusion.3), channel_id=1, source_target_pairs={{0,1},{1,0},{2,3},{3,2},{4,5},{5,4},{6,7},{7,6},{8,9},{9,8},{10,11... | collective-permute-start | bytes 3538952 | tf_op jit(solution)/shard_map/ppermute | solution.py:145
  158.8 20.6 %all-to-all-start.2 = ((f32[16,24,384]{2,1,0:T(8,128)}), f32[16,24,384]{2,1,0:T(8,128)S(1)}, u32[]{:S(2)}, u32[]{:S(2)}) async-start(f32[16,24,384]{2,1,0:T(8,128)} %bitcast.101), calls=%async_computation.2 | async-start | bytes 1179648 | tf_op jit(solution)/shard_map/all_to_all | solution.py:177
  179.4 9.3 %copy-start.7 = (bf16[1024,384]{1,0:T(8,128)(2,1)S(1)}, bf16[1024,384]{1,0:T(8,128)(2,1)}, u32[]{:S(2)}) copy-start(bf16[1024,384]{1,0:T(8,128)(2,1)} %param.11) | copy-start | bytes 2359300
  189.4 1.6 collective-permute-start.8
  208.0 29.1 %copy-start.12 = (bf16[2,24,8,512]{3,2,0,1:T(8,128)(2,1)S(1)}, bf16[2,24,8,512]{3,2,0,1:T(8,128)(2,1)}, u32[]{:S(2)}) copy-start(bf16[2,24,8,512]{3,2,0,1:T(8,128)(2,1)} %copy-done.11) | copy-start | bytes 1179652
  236.3 6.0 %collective-permute-start.9 = (f32[16,36,384]{2,0,1:T(8,128)}, f32[16,36,384]{2,0,1:T(8,128)}, u32[]{:S(2)}, u32[]{:S(2)}) collective-permute-start(f32[16,36,384]{2,0,1:T(8,128)} %copy.128), channel_id=1, source_target_pairs={{0,2},{2,0},{4,6},{6,4},{8,10},{10,8},{12,14},{14,12},{16,18},{18,... | collective-permute-start | bytes 2654216 | tf_op jit(solution)/shard_map/ppermute | solution.py:163
  237.0 3.7 %copy-start.17 = (bf16[384,384]{1,0:T(8,128)(2,1)S(1)}, bf16[384,384]{1,0:T(8,128)(2,1)}, u32[]{:S(2)}) copy-start(bf16[384,384]{1,0:T(8,128)(2,1)} %param.12) | copy-start | bytes 884740

commit v12 on v11

--- a/solution.py
+++ b/solution.py
@@ -173,9 +173,9 @@
     halves = flat.reshape(2, size * chunk, width)
     keep = jnp.where(core == 0, halves[0], halves[1])
     send = jnp.where(core == 0, halves[1], halves[0])
-    mine = keep + core_swap(send)
+    mine = (keep + core_swap(send)).astype(jnp.bfloat16)
     parts = lax.all_to_all(mine.reshape(size, chunk, width), "pix", 0, 0, tiled=True)
-    return jnp.sum(parts.reshape(size // 2, 2, chunk, width), axis=0)
+    return jnp.sum(parts.reshape(size // 2, 2, chunk, width).astype(jnp.float32), axis=0)
 
 
 def pix_gather(reduced_groups, term_groups):

time: 252 us -> 248 us (0.984)
  blocking collectives: 43.9 us -> 40 us
    ppermute x6, waiting for transfers between devices: 48.6 us -> 53.7 us  [ch_exchange(): lax.ppermute(value, 'ch', [(i, (i + shift) % size) for i in range(size)])]
    all_to_all x1, waiting for transfers between devices: 12.4 us -> 7.34 us  [pix_scatter(): lax.all_to_all(mine.reshape(size, chunk, width), 'pix', 0, 0, tiled=True)]
    all_to_all x1, blocking collectives: 16.8 us -> 13.6 us  [pix_scatter(): lax.all_to_all(mine.reshape(size, chunk, width), 'pix', 0, 0, tiled=True)]
    unnamed x80 -> x82, local copies, waits for them, and re-layouts: 11.9 us -> 11.9 us
where the time goes in v12:
time: 248 us; the launch traced here: 243 us
  waiting for transfers between devices  63.8 us (26%)
  matrix products  58.8 us (24%)
  blocking collectives  40 us (16%)
  local copies, waits for them, and re-layouts  34.7 us (14%)
  starting transfers between devices  28.1 us (11%)
  other arithmetic  15.7 us (6%)
    ppermute x6, waiting for transfers between devices, ch_exchange(): lax.ppermute(value, 'ch', [(i, (i + shift) % size) for i in range(size)])  53.7 us
    all_to_all x1, blocking collectives, pix_gather(): lax.all_to_all(spread.reshape(size, total, width), 'pix', 0, 0, tiled=True)  26.4 us
    dot_general x16, matrix products, backward_block(): jnp.einsum('bx,bc->xc', pick_table(slot_rows[:, slot], ext_rows), contrib...  20.2 us
    dot_general x16, matrix products, forward_block(): jnp.dot(pick_table(slot_rows[:, slot], ext_rows), flattened, preferred_el...  16.9 us
    all_to_all x1, blocking collectives, pix_scatter(): lax.all_to_all(mine.reshape(size, chunk, width), 'pix', 0, 0, tiled=True)  13.6 us
    unnamed x82, local copies, waits for them, and re-layouts  11.9 us
    ppermute x6, starting transfers between devices, ch_exchange(): lax.ppermute(value, 'ch', [(i, (i + shift) % size) for i in range(size)])  8.22 us
    all_to_all x1, waiting for transfers between devices, pix_scatter(): lax.all_to_all(mine.reshape(size, chunk, width), 'pix', 0, 0, tiled=True)  7.34 us
  transfers between devices with their start and end apart: 13, of which 8 were waited for; matrix products, arithmetic and copies ran while one was open for 30% of the time, Pallas kernels for 0%

profile of v12, /device:TPU:0, one launch (start us, length us, event | category | flops | bytes accessed | tf_op | source)
XLA Modules:
  0.0 243.1 jit_solution(9856294566314396425)
XLA Ops:
  0.7 3.0 %collective-permute-start = (bf16[1024,384]{1,0:T(8,128)(2,1)}, bf16[1024,384]{1,0:T(8,128)(2,1)S(1)}, u32[]{:S(2)}, u32[]{:S(2)}) collective-permute-start(bf16[1024,384]{1,0:T(8,128)(2,1)} %param.11), channel_id=1, source_target_pairs={{0,1},{1,0},{2,3},{3,2},{4,5},{5,4},{6,7},{7,6},{8,9},{9,8},{10,11... | collective-permute-start | bytes 2359304 | tf_op jit(solution)/shard_map/ppermute | solution.py:145
  3.7 1.1 reshape.203
  6.1 1.2 broadcast_select_fusion
  8.7 1.2 copy.109
  10.7 17.2 %collective-permute-done.1 = bf16[384,384]{1,0:T(8,128)(2,1)} collective-permute-done((bf16[384,384]{1,0:T(8,128)(2,1)}, bf16[384,384]{1,0:T(8,128)(2,1)}, u32[]{:S(2)}, u32[]{:S(2)}) %collective-permute-start.1) | collective-permute-done | bytes 294944 | tf_op jit(solution)/shard_map/ppermute | solution.py:145
  27.8 1.6 add_convert_fusion.1
  32.1 1.1 reshape.204
  33.2 6.8 %all-to-all-start = ((bf16[16,32,2,192]{3,2,1,0:T(2,128)(2,1)}), bf16[16,32,2,192]{3,2,1,0:T(2,128)(2,1)}, u32[]{:S(2)}, u32[]{:S(2)}) async-start(bf16[16,32,2,192]{3,2,1,0:T(2,128)(2,1)} %reshape.204), calls=%async_computation | async-start | bytes 1048576 | tf_op jit(solution)/shard_map/all_to_all | solution.py:257
  41.0 1.5 collective-permute-start.2
  43.2 1.6 collective-permute-start.5
  45.7 10.2 %collective-permute-done.2 = bf16[1024,192]{1,0:T(8,128)(2,1)S(1)} collective-permute-done((bf16[1024,192]{1,0:T(8,128)(2,1)}, bf16[1024,192]{1,0:T(8,128)(2,1)S(1)}, u32[]{:S(2)}, u32[]{:S(2)}) %collective-permute-start.2) | collective-permute-done | bytes 393248 | tf_op jit(solution)/shard_map/ppermute | solution.py:145
  56.7 8.7 %collective-permute-done.3 = bf16[3,384,192]{1,2,0:T(8,128)(2,1)S(1)} collective-permute-done((bf16[3,384,192]{1,2,0:T(8,128)(2,1)}, bf16[3,384,192]{1,2,0:T(8,128)(2,1)S(1)}, u32[]{:S(2)}, u32[]{:S(2)}) %collective-permute-start.3) | collective-permute-done | bytes 442400 | tf_op jit(solution)/shard_map/ppermute | solution.py:145
  66.3 1.4 concatenate.45
  68.6 2.3 fusion.100
  78.8 1.3 copy-done.4
  83.3 1.3 fusion.53
  84.6 1.2 fusion.51
  96.5 1.2 fusion.40
  97.7 1.4 convolution_add_fusion.11
  99.1 1.2 convolution_add_fusion.10
  100.3 1.2 convolution_add_fusion.9
  101.5 1.2 convolution_add_fusion.8
  102.7 1.2 convolution_add_fusion.7
  103.9 1.2 convolution_add_fusion.6
  105.2 1.2 convolution_add_fusion.5
  106.4 1.6 collective-permute-start.4
  107.9 1.2 fusion.49
  109.5 7.0 %collective-permute-done.4 = bf16[1024,192]{0,1:T(8,128)(2,1)S(1)} collective-permute-done((bf16[1024,192]{0,1:T(8,128)(2,1)S(1)}, bf16[1024,192]{0,1:T(8,128)(2,1)S(1)}, u32[]{:S(2)}, u32[]{:S(2)}) %collective-permute-start.4) | collective-permute-done | bytes 393248 | tf_op jit(solution)/shard_map/ppermute | solution.py:145
  116.4 1.6 convolution_add_fusion.4
  118.0 1.2 convolution_add_fusion.3
  119.2 1.6 convolution_add_fusion.2
  120.8 1.2 convolution_add_fusion.1
  122.0 1.2 convolution_add_fusion
  123.2 1.5 copy-done.2
  124.8 1.1 reshape.206
  125.8 5.6 %all-to-all-start.1 = ((bf16[16,32,2,192]{3,2,1,0:T(2,128)(2,1)}), bf16[16,32,2,192]{3,2,1,0:T(2,128)(2,1)}, u32[]{:S(2)}, u32[]{:S(2)}) async-start(bf16[16,32,2,192]{3,2,1,0:T(2,128)(2,1)} %reshape.206), calls=%async_computation.1 | async-start | bytes 1048576 | tf_op jit(solution)/shard_map/all_to_all | solution.py:275
  131.8 1.0 slice.367
  132.8 1.0 slice.366
  135.7 1.2 copy.113
  136.9 1.4 reshape_reshape.4
  138.3 3.2 %convolution_multiply_fusion.2 = f32[192,384]{1,0:T(8,128)} fusion(bf16[1024,192]{0,1:T(8,128)(2,1)} %bitcast.237, bf16[1024,192]{1,0:T(8,128)(2,1)} %copy-done.22, bf16[1024,192]{1,0:T(8,128)(2,1)} %copy-done.29, pred[]{:T(512)S(6)} %eq.213), kind=kOutput, calls=%fused_computation.152 | convolution fusion | flops 154607616 | bytes 1474561 | tf_op jit(solution)/shard_map/dot_general | solution.py:265
  141.6 1.3 slice_add_fusion
  142.9 1.9 copy.124
  144.8 1.1 all-to-all-done.1
  145.9 1.4 convert_element_type.221
  148.2 1.7 add_convert_fusion
  152.1 1.3 copy.126
  153.9 1.1 broadcast_select_fusion.2
  155.2 1.1 pad_maximum_fusion.3
  156.3 1.5 collective-permute-start.7
  158.7 5.1 %all-to-all-start.2 = ((bf16[16,24,384]{2,1,0:T(8,128)(2,1)}), bf16[16,24,384]{2,1,0:T(8,128)(2,1)S(1)}, u32[]{:S(2)}, u32[]{:S(2)}) async-start(bf16[16,24,384]{2,1,0:T(8,128)(2,1)} %bitcast.101), calls=%async_computation.2 | async-start | bytes 589824 | tf_op jit(solution)/shard_map/all_to_all | solution.py:177
  163.8 3.2 %fusion.128 = f32[1024,384,1]{1,0,2:T(8,128)} fusion(bf16[3,384,192]{1,2,0:T(8,128)(2,1)} %param.13, bf16[1024,2,192]{0,2,1:T(8,128)(2,1)S(1)} %copy-done.21, bf16[1024,1,192]{0,2,1:T(8,128)(2,1)S(1)} %copy-done.10), kind=kOutput, calls=%fused_computation.231 | convolution fusion | flops 453574656 | bytes 3194880 | tf_op jit(solution)/shard_map/rkd,kcd->rc/dot_general | solution.py:293
  167.0 7.3 %all-to-all-done.2 = bf16[16,24,384]{2,1,0:T(8,128)(2,1)S(1)} async-done(((bf16[16,24,384]{2,1,0:T(8,128)(2,1)}), bf16[16,24,384]{2,1,0:T(8,128)(2,1)S(1)}, u32[]{:S(2)}, u32[]{:S(2)}) %all-to-all-start.2) | async-done | bytes 294944 | tf_op jit(solution)/shard_map/all_to_all | solution.py:177
  174.4 10.6 %collective-permute-done.7 = bf16[1024,3,192]{0,2,1:T(8,128)(2,1)} collective-permute-done((bf16[1024,3,192]{0,2,1:T(8,128)(2,1)}, bf16[1024,3,192]{0,2,1:T(8,128)(2,1)}, u32[]{:S(2)}, u32[]{:S(2)}) %collective-permute-start.7) | collective-permute-done | bytes 1179680 | tf_op jit(solution)/shard_map/ppermute | solution.py:145
  185.0 3.4 %fusion.60 = bf16[1024,384]{1,0:T(8,128)(2,1)S(1)} fusion(f32[1024,384,1]{1,0,2:T(8,128)} %fusion.128, bf16[1024,3,192]{0,2,1:T(8,128)(2,1)} %collective-permute-done.7, bf16[3,384,192]{1,2,0:T(8,128)(2,1)} %copy-done.30, bf16[1024,192]{1,0:T(8,128)(2,1)} %copy-done.29, bf16[1024,192]{1,0:T(8,128)(2,1)S(1)} %copy-done.23, pred[]{:T(512)S(6)} %eq.213), kind=kOutput, calls=%fused_computation.88 | convolution fusion | flops 458096640 | bytes 4767745 | tf_op jit(solution)/shard_map/rkd,kcd->rc/dot_general | solution.py:297
  189.1 1.6 collective-permute-done.8
  190.8 13.6 %all_to_all.25 = bf16[16,12,384]{2,1,0:T(8,128)(2,1)S(1)} all-to-all(bf16[16,12,384]{2,1,0:T(8,128)(2,1)S(1)} %reshape.209), channel_id=1, replica_groups=mesh['pix'=16,'ch'=2] {'pix'}, dimensions={0} | all-to-all | bytes 294912 | tf_op jit(solution)/shard_map/all_to_all | solution.py:177
  204.5 26.4 %all_to_all.26 = f32[16,36,384]{2,1,0:T(8,128)S(1)} all-to-all(f32[16,36,384]{2,1,0:T(8,128)S(1)} %bitcast.232), channel_id=1, replica_groups=mesh['pix'=16,'ch'=2] {'pix'}, dimensions={0} | all-to-all | bytes 1769472 | tf_op jit(solution)/shard_map/all_to_all | solution.py:188
  231.0 1.1 copy.128
  232.8 1.3 fusion.121
  234.1 1.5 fusion.97
  236.5 1.5 convolution_convert_fusion
  238.1 1.5 copy_select_fusion.1
  240.8 1.3 copy.132
  (180 shorter events, 44.6 us)
Async XLA Ops:
  0.6 9.4 %copy-start.6 = (bf16[1024,384]{1,0:T(8,128)(2,1)S(1)}, bf16[1024,384]{1,0:T(8,128)(2,1)}, u32[]{:S(2)}) copy-start(bf16[1024,384]{1,0:T(8,128)(2,1)} %param.11) | copy-start | bytes 2359300
  0.6 9.4 %copy-start.16 = (bf16[384,384]{1,0:T(8,128)(2,1)S(1)}, bf16[384,384]{1,0:T(8,128)(2,1)}, u32[]{:S(2)}) copy-start(bf16[384,384]{1,0:T(8,128)(2,1)} %param.12) | copy-start | bytes 884740
  0.7 27.2 %collective-permute-start = (bf16[1024,384]{1,0:T(8,128)(2,1)}, bf16[1024,384]{1,0:T(8,128)(2,1)S(1)}, u32[]{:S(2)}, u32[]{:S(2)}) collective-permute-start(bf16[1024,384]{1,0:T(8,128)(2,1)} %param.11), channel_id=1, source_target_pairs={{0,1},{1,0},{2,3},{3,2},{4,5},{5,4},{6,7},{7,6},{8,9},{9,8},{10,11... | collective-permute-start | bytes 2359304 | tf_op jit(solution)/shard_map/ppermute | solution.py:145
  3.7 24.2 %collective-permute-start.1 = (bf16[384,384]{1,0:T(8,128)(2,1)}, bf16[384,384]{1,0:T(8,128)(2,1)}, u32[]{:S(2)}, u32[]{:S(2)}) collective-permute-start(bf16[384,384]{1,0:T(8,128)(2,1)} %param.12), channel_id=1, source_target_pairs={{0,1},{1,0},{2,3},{3,2},{4,5},{5,4},{6,7},{7,6},{8,9},{9,8},{10,11... | collective-permute-start | bytes 884744 | tf_op jit(solution)/shard_map/ppermute | solution.py:145
  9.9 46.0 %copy-start.22 = (bf16[1024,192]{1,0:T(8,128)(2,1)}, bf16[1024,192]{1,0:T(8,128)(2,1)S(1)}, u32[]{:S(2)}) copy-start(bf16[1024,192]{1,0:T(8,128)(2,1)S(1)} %copy.109) | copy-start | bytes 1179652
  10.6 18.8 %copy-start.24 = (bf16[3,384,192]{1,2,0:T(8,128)(2,1)S(1)}, bf16[3,384,192]{1,2,0:T(8,128)(2,1)}, u32[]{:S(2)}) copy-start(bf16[3,384,192]{1,2,0:T(8,128)(2,1)} %param.13) | copy-start | bytes 1327108
  30.5 0.9 copy-start.18
  30.5 9.5 %copy-start.8 = (bf16[1024,192]{0,1:T(8,128)(2,1)S(1)}, bf16[1024,192]{0,1:T(8,128)(2,1)}, u32[]{:S(2)}) copy-start(bf16[1024,192]{0,1:T(8,128)(2,1)} %param.17) | copy-start | bytes 1179652
  33.2 33.0 %all-to-all-start = ((bf16[16,32,2,192]{3,2,1,0:T(2,128)(2,1)}), bf16[16,32,2,192]{3,2,1,0:T(2,128)(2,1)}, u32[]{:S(2)}, u32[]{:S(2)}) async-start(bf16[16,32,2,192]{3,2,1,0:T(2,128)(2,1)} %reshape.204), calls=%async_computation | async-start | bytes 1048576 | tf_op jit(solution)/shard_map/all_to_all | solution.py:257
  41.0 15.0 %copy-start.27 = (bf16[192,384]{1,0:T(8,128)(2,1)S(1)}, bf16[192,384]{1,0:T(8,128)(2,1)}, u32[]{:S(2)}) copy-start(bf16[192,384]{1,0:T(8,128)(2,1)} %param.14) | copy-start | bytes 442372
  41.0 15.0 %collective-permute-start.2 = (bf16[1024,192]{1,0:T(8,128)(2,1)}, bf16[1024,192]{1,0:T(8,128)(2,1)S(1)}, u32[]{:S(2)}, u32[]{:S(2)}) collective-permute-start(bf16[1024,192]{1,0:T(8,128)(2,1)} %copy.108), channel_id=1, source_target_pairs={{0,1},{1,0},{2,3},{3,2},{4,5},{5,4},{6,7},{7,6},{8,9},{9,8},{10,11... | collective-permute-start | bytes 1179656 | tf_op jit(solution)/shard_map/ppermute | solution.py:145
  42.5 22.9 %collective-permute-start.3 = (bf16[3,384,192]{1,2,0:T(8,128)(2,1)}, bf16[3,384,192]{1,2,0:T(8,128)(2,1)S(1)}, u32[]{:S(2)}, u32[]{:S(2)}) collective-permute-start(bf16[3,384,192]{1,2,0:T(8,128)(2,1)} %param.13), channel_id=1, source_target_pairs={{0,1},{1,0},{2,3},{3,2},{4,5},{5,4},{6,7},{7,6},{8,9},{9,8},{10,11... | collective-permute-start | bytes 1327112 | tf_op jit(solution)/shard_map/ppermute | solution.py:145
  43.2 66.2 %collective-permute-start.5 = (bf16[192,192]{1,0:T(8,128)(2,1)}, bf16[192,192]{1,0:T(8,128)(2,1)}, u32[]{:S(2)}, u32[]{:S(2)}) collective-permute-start(bf16[192,192]{1,0:T(8,128)(2,1)} %bitcast.287), channel_id=1, source_target_pairs={{0,1},{1,0},{2,3},{3,2},{4,5},{5,4},{6,7},{7,6},{8,9},{9,8},{10,11... | collective-permute-start | bytes 221192 | tf_op jit(solution)/shard_map/ppermute | solution.py:241
  56.0 9.6 %copy-start.29 = (bf16[1024,192]{1,0:T(8,128)(2,1)}, bf16[1024,192]{1,0:T(8,128)(2,1)S(1)}, u32[]{:S(2)}) copy-start(bf16[1024,192]{1,0:T(8,128)(2,1)S(1)} %collective-permute-done.2) | copy-start | bytes 1179652
  65.4 0.8 copy-start.30
  68.6 2.3 copy-start.19
  68.6 2.3 copy-start.25
  71.9 1.0 copy-start.28
  76.8 2.0 copy-start.5
  77.8 2.3 copy-start.4
  83.3 38.8 %copy-start.1 = (bf16[512,9,2,3,64]{0,4,3,2,1:T(8,128)(2,1)}, bf16[512,9,2,3,64]{0,4,3,2,1:T(8,128)(2,1)S(1)}, u32[]{:S(2)}) copy-start(bf16[512,9,2,3,64]{0,4,3,2,1:T(8,128)(2,1)S(1)} %pad_maximum_fusion.1) | copy-start | bytes 10616836
  95.1 11.2 %copy-start.11 = (bf16[2,24,8,512]{3,2,0,1:T(8,128)(2,1)}, bf16[2,24,8,512]{3,2,0,1:T(8,128)(2,1)S(1)}, u32[]{:S(2)}) copy-start(bf16[2,24,8,512]{3,2,0,1:T(8,128)(2,1)S(1)} %copy.201) | copy-start | bytes 1179652
  96.5 8.6 %copy-start = (bf16[512,9,2,3,64]{0,4,3,2,1:T(8,128)(2,1)}, bf16[512,9,2,3,64]{0,4,3,2,1:T(8,128)(2,1)S(1)}, u32[]{:S(2)}) copy-start(bf16[512,9,2,3,64]{0,4,3,2,1:T(8,128)(2,1)S(1)} %pad_maximum_fusion) | copy-start | bytes 10616836
  106.4 10.1 %collective-permute-start.4 = (bf16[1024,192]{0,1:T(8,128)(2,1)S(1)}, bf16[1024,192]{0,1:T(8,128)(2,1)S(1)}, u32[]{:S(2)}, u32[]{:S(2)}) collective-permute-start(bf16[1024,192]{0,1:T(8,128)(2,1)S(1)} %bitcast.236), channel_id=1, source_target_pairs={{0,1},{1,0},{2,3},{3,2},{4,5},{5,4},{6,7},{7,6},{8,9},{9,8},{10,11... | collective-permute-start | bytes 1179656 | tf_op jit(solution)/shard_map/ppermute | solution.py:145
  116.4 1.6 copy-start.26
  123.2 1.5 copy-start.2
  125.8 20.1 %all-to-all-start.1 = ((bf16[16,32,2,192]{3,2,1,0:T(2,128)(2,1)}), bf16[16,32,2,192]{3,2,1,0:T(2,128)(2,1)}, u32[]{:S(2)}, u32[]{:S(2)}) async-start(bf16[16,32,2,192]{3,2,1,0:T(2,128)(2,1)} %reshape.206), calls=%async_computation.1 | async-start | bytes 1048576 | tf_op jit(solution)/shard_map/all_to_all | solution.py:275
  136.9 4.7 %copy-start.3 = (f32[1536,384]{1,0:T(8,128)S(1)}, f32[1536,384]{1,0:T(8,128)}, u32[]{:S(2)}) copy-start(f32[1536,384]{1,0:T(8,128)} %copy-done.2) | copy-start | bytes 7077892
  138.3 11.7 %copy-start.9 = (bf16[1024,1,192]{0,2,1:T(8,128)(2,1)}, bf16[1024,1,192]{0,2,1:T(8,128)(2,1)S(1)}, u32[]{:S(2)}) copy-start(bf16[1024,1,192]{0,2,1:T(8,128)(2,1)S(1)} %reshape_reshape.4) | copy-start | bytes 1179652
  138.3 3.3 %copy-start.13 = (bf16[512,1,384]{2,0,1:T(8,128)(2,1)S(1)}, bf16[512,1,384]{2,0,1:T(8,128)(2,1)}, u32[]{:S(2)}) copy-start(bf16[512,1,384]{2,0,1:T(8,128)(2,1)} %copy.190) | copy-start | bytes 1179652
  138.3 3.3 %copy-start.14 = (bf16[512,1,384]{2,0,1:T(8,128)(2,1)S(1)}, bf16[512,1,384]{2,0,1:T(8,128)(2,1)}, u32[]{:S(2)}) copy-start(bf16[512,1,384]{2,0,1:T(8,128)(2,1)} %copy.189) | copy-start | bytes 1179652
  150.0 0.9 copy-start.20
  153.9 1.3 copy-start.10
  153.9 1.3 copy-start.21
  153.9 3.9 %copy-start.15 = (f32[192,384]{1,0:T(8,128)S(1)}, f32[192,384]{1,0:T(8,128)}, u32[]{:S(2)}) copy-start(f32[192,384]{1,0:T(8,128)} %convolution_multiply_fusion.2) | copy-start | bytes 884740
  155.1 2.8 %collective-permute-start.6 = (f32[384,384]{1,0:T(8,128)S(1)}, f32[384,384]{1,0:T(8,128)S(1)}, u32[]{:S(2)}, u32[]{:S(2)}) collective-permute-start(f32[384,384]{1,0:T(8,128)S(1)} %broadcast_select_fusion.2), channel_id=1, source_target_pairs={{0,2},{2,0},{4,6},{6,4},{8,10},{10,8},{12,14},{14,12},{16,18},{18,... | collective-permute-start | bytes 1769480 | tf_op jit(solution)/shard_map/ppermute | solution.py:163
  156.3 28.6 %collective-permute-start.7 = (bf16[1024,3,192]{0,2,1:T(8,128)(2,1)}, bf16[1024,3,192]{0,2,1:T(8,128)(2,1)}, u32[]{:S(2)}, u32[]{:S(2)}) collective-permute-start(bf16[1024,3,192]{0,2,1:T(8,128)(2,1)} %pad_maximum_fusion.3), channel_id=1, source_target_pairs={{0,1},{1,0},{2,3},{3,2},{4,5},{5,4},{6,7},{7,6},{8,9},{9,8},{10,11... | collective-permute-start | bytes 3538952 | tf_op jit(solution)/shard_map/ppermute | solution.py:145
  158.7 15.6 %all-to-all-start.2 = ((bf16[16,24,384]{2,1,0:T(8,128)(2,1)}), bf16[16,24,384]{2,1,0:T(8,128)(2,1)S(1)}, u32[]{:S(2)}, u32[]{:S(2)}) async-start(bf16[16,24,384]{2,1,0:T(8,128)(2,1)} %bitcast.101), calls=%async_computation.2 | async-start | bytes 589824 | tf_op jit(solution)/shard_map/all_to_all | solution.py:177
  163.7 21.2 %copy-start.23 = (bf16[1024,192]{1,0:T(8,128)(2,1)S(1)}, bf16[1024,192]{1,0:T(8,128)(2,1)}, u32[]{:S(2)}) copy-start(bf16[1024,192]{1,0:T(8,128)(2,1)} %copy-done.22) | copy-start | bytes 1179652
  174.3 14.0 %copy-start.7 = (bf16[1024,384]{1,0:T(8,128)(2,1)S(1)}, bf16[1024,384]{1,0:T(8,128)(2,1)}, u32[]{:S(2)}) copy-start(bf16[1024,384]{1,0:T(8,128)(2,1)} %param.11) | copy-start | bytes 2359300
  189.1 1.6 collective-permute-start.8
  204.5 28.3 %copy-start.12 = (bf16[2,24,8,512]{3,2,0,1:T(8,128)(2,1)S(1)}, bf16[2,24,8,512]{3,2,0,1:T(8,128)(2,1)}, u32[]{:S(2)}) copy-start(bf16[2,24,8,512]{3,2,0,1:T(8,128)(2,1)} %copy-done.11) | copy-start | bytes 1179652
  232.0 6.0 %collective-permute-start.9 = (f32[16,36,384]{2,0,1:T(8,128)}, f32[16,36,384]{2,0,1:T(8,128)}, u32[]{:S(2)}, u32[]{:S(2)}) collective-permute-start(f32[16,36,384]{2,0,1:T(8,128)} %copy.128), channel_id=1, source_target_pairs={{0,2},{2,0},{4,6},{6,4},{8,10},{10,8},{12,14},{14,12},{16,18},{18,... | collective-permute-start | bytes 2654216 | tf_op jit(solution)/shard_map/ppermute | solution.py:163
  232.8 3.7 %copy-start.17 = (bf16[384,384]{1,0:T(8,128)(2,1)S(1)}, bf16[384,384]{1,0:T(8,128)(2,1)}, u32[]{:S(2)}) copy-start(bf16[384,384]{1,0:T(8,128)(2,1)} %param.12) | copy-start | bytes 884740

commit v13 on v11

--- a/solution.py
+++ b/solution.py
@@ -20,12 +20,12 @@
     return (slot_rows, slot_live)
 
 
-def attention_forward(queries, extended, neighbours, row_offset):
+def attention_forward(queries, key_value, halo, neighbours, row_offset):
     f32 = jnp.float32
     bf16 = jnp.bfloat16
     row_count = queries.shape[0]
     span = queries.shape[1]
-    ext_rows = extended.shape[0]
+    halo_rows = halo.shape[0]
     heads_here = span // HD
     slot_width = neighbours.shape[1] + 1
     score_scale = 1.0 / math.sqrt(HD)
@@ -33,16 +33,33 @@
     block_count = row_count // block_rows
     query_blocks = queries.reshape(block_count, block_rows, span)
     neighbour_blocks = neighbours.reshape(block_count, block_rows, slot_width - 1)
-    flattened = extended.reshape(ext_rows, 2 * span)
+    local_flat = key_value.reshape(row_count, 2 * span)
+    halo_flat = halo.reshape(halo_rows, 2 * span)
+
+    block_parts = []
+    for b in range(block_count):
+        slot_rows, _ = slot_index(neighbour_blocks[b], row_offset + b * block_rows, block_rows)
+        block_parts.append([
+            jnp.dot(
+                pick_table(slot_rows[:, slot], row_count), local_flat, preferred_element_type=f32
+            )
+            for slot in range(1, slot_width)
+        ])
+    block_parts, halo_flat = lax.optimization_barrier((block_parts, halo_flat))
 
     def forward_block(inputs):
-        query_block, neighbour_block, first_row = inputs
+        query_block, neighbour_block, first_row, local_parts = inputs
         slot_rows, slot_live = slot_index(neighbour_block, first_row, block_rows)
-        pieces = [flattened[first_row : first_row + block_rows]] + [
-            jnp.dot(
-                pick_table(slot_rows[:, slot], ext_rows), flattened, preferred_element_type=f32
+        pieces = [local_flat[first_row : first_row + block_rows]] + [
+            (
+                local_part
+                + jnp.dot(
+                    pick_table(slot_rows[:, slot] - row_count, halo_rows),
+                    halo_flat,
+                    preferred_element_type=f32,
+                )
             ).astype(bf16)
-            for slot in range(1, slot_width)
+            for slot, local_part in zip(range(1, slot_width), local_parts)
         ]
         gathered = jnp.stack(pieces, axis=1).reshape(block_rows, slot_width, 2, span)
         block_keys = gathered[:, :, 0].reshape(block_rows, slot_width, heads_here, HD)
@@ -66,7 +83,9 @@
         return (mixture.reshape(block_rows, span).astype(bf16), probabilities, gathered)
 
     outputs = [
-        forward_block((query_blocks[b], neighbour_blocks[b], row_offset + b * block_rows))
+        forward_block(
+            (query_blocks[b], neighbour_blocks[b], row_offset + b * block_rows, block_parts[b])
+        )
         for b in range(block_count)
     ]
     attn_blocks = jnp.stack([out[0] for out in outputs])
@@ -255,16 +274,14 @@
         .reshape(peer_count, slot_count, 2, half_width)
     )
     incoming = lax.all_to_all(outgoing, "pix", split_axis=0, concat_axis=0, tiled=True)
-    extended = jnp.concatenate(
-        [key_value, incoming.reshape(peer_count * slot_count, 2, half_width)], axis=0
-    )
-    attended, prob_blocks, kv_blocks = attention_forward(queries, extended, neighbours, 0)
+    halo = incoming.reshape(peer_count * slot_count, 2, half_width)
+    attended, prob_blocks, kv_blocks = attention_forward(queries, key_value, halo, neighbours, 0)
     attended_others = ch_exchange(attended)
     grad_attended = jnp.dot(upstream, mixing_weight.T, preferred_element_type=f32).astype(bf16)
     grad_attended, proj_others = lax.optimization_barrier((grad_attended, proj_others))
     mixing_term = jnp.dot(attended.T, upstream, preferred_element_type=f32) * grad_scale
     carried, query_grads, (attended_others, mix_others) = attention_backward(
-        queries, extended.shape[0], neighbours, 0, grad_attended, prob_blocks, kv_blocks,
+        queries, row_count + halo.shape[0], neighbours, 0, grad_attended, prob_blocks, kv_blocks,
         (attended_others, mix_others),
     )
     branch = jnp.dot(attended, mix_own, preferred_element_type=f32)

time: 252 us -> 323 us (1.28)
  matrix products: 59.1 us -> 104 us
  local copies, waits for them, and re-layouts: 34.8 us -> 74.6 us
  waiting for transfers between devices: 63.8 us -> 46.5 us
    dot_general x16 -> x32, matrix products: 16.9 us -> 58.6 us  [the longest x16 32.1 us: forward_block(): jnp.dot(pick_table(slot_rows[:, slot] - row_count, halo_rows), halo_flat,...]
    convert_element_type x0 -> x16, local copies, waits for them, and re-layouts: none -> 22.9 us  [forward_block(): pieces = [local_flat[first_row:first_row + block_rows]] + [(local_part +...]
    ppermute x6, waiting for transfers between devices: 48.6 us -> 31.1 us  [ch_exchange(): lax.ppermute(value, 'ch', [(i, (i + shift) % size) for i in range(size)])]
    unnamed x80 -> x120, local copies, waits for them, and re-layouts: 11.9 us -> 26.7 us
    slice x2, local copies, waits for them, and re-layouts: 0.53 us -> 4.62 us  [forward_block(): gathered[:, :, 0].reshape(block_rows, slot_width, heads_here, HD)]
  transfers between devices with their start and end apart: 13 -> 13, of which waited for: 8 -> 8; matrix products, arithmetic and copies ran while one was open for 30% -> 52% of each run, Pallas kernels for 0% -> 0%
where the time goes in v13:
time: 323 us; the launch traced here: 317 us
  matrix products  104 us (32%)
  local copies, waits for them, and re-layouts  74.6 us (23%)
  waiting for transfers between devices  46.5 us (14%)
  blocking collectives  44.4 us (14%)
  starting transfers between devices  26.2 us (8%)
  other arithmetic  18.8 us (6%)
    dot_general x16, matrix products, forward_block(): jnp.dot(pick_table(slot_rows[:, slot] - row_count, halo_rows), halo_flat,...  32.1 us
    ppermute x6, waiting for transfers between devices, ch_exchange(): lax.ppermute(value, 'ch', [(i, (i + shift) % size) for i in range(size)])  31.1 us
    all_to_all x1, blocking collectives, pix_gather(): lax.all_to_all(spread.reshape(size, total, width), 'pix', 0, 0, tiled=True)  27.4 us
    unnamed x120, local copies, waits for them, and re-layouts  26.7 us
    dot_general x16, matrix products, attention_forward(): jnp.dot(pick_table(slot_rows[:, slot], row_count), local_flat, preferred_...  26.5 us
    convert_element_type x16, local copies, waits for them, and re-layouts, forward_block(): pieces = [local_flat[first_row:first_row + block_rows]] + [(local_part +...  22.9 us
    dot_general x16, matrix products, backward_block(): jnp.einsum('bx,bc->xc', pick_table(slot_rows[:, slot], ext_rows), contrib...  22.3 us
    all_to_all x1, blocking collectives, pix_scatter(): lax.all_to_all(mine.reshape(size, chunk, width), 'pix', 0, 0, tiled=True)  16.9 us
  transfers between devices with their start and end apart: 13, of which 8 were waited for; matrix products, arithmetic and copies ran while one was open for 52% of the time, Pallas kernels for 0%

profile of v13, /device:TPU:0, one launch (start us, length us, event | category | flops | bytes accessed | tf_op | source)
XLA Modules:
  0.0 316.7 jit_solution(5036859402002276985)
XLA Ops:
  0.7 3.0 collective-permute-start.1
  8.9 2.0 copy.264
  11.7 16.0 %collective-permute-done = bf16[1024,384]{1,0:T(8,128)(2,1)S(1)} collective-permute-done((bf16[1024,384]{1,0:T(8,128)(2,1)}, bf16[1024,384]{1,0:T(8,128)(2,1)S(1)}, u32[]{:S(2)}, u32[]{:S(2)}) %collective-permute-start) | collective-permute-done | bytes 786464 | tf_op jit(solution)/shard_map/ppermute | solution.py:164
  28.4 1.8 collective-permute-start.5
  31.5 1.7 collective-permute-start.2
  33.2 1.8 fusion.152
  37.1 6.2 %all-to-all-start = ((bf16[16,32,2,192]{3,2,1,0:T(2,128)(2,1)}), bf16[16,32,2,192]{3,2,1,0:T(2,128)(2,1)S(1)}, u32[]{:S(2)}, u32[]{:S(2)}) async-start(bf16[16,32,2,192]{3,2,1,0:T(2,128)(2,1)} %reshape.203), calls=%async_computation | async-start | bytes 1048576 | tf_op jit(solution)/shard_map/all_to_all | solution.py:276
  43.3 1.7 fusion.33
  45.0 1.7 fusion.32
  46.6 1.6 fusion.31
  48.3 1.7 fusion.30
  50.0 1.6 fusion.29
  51.6 1.6 fusion.28
  53.2 1.7 fusion.27
  54.9 1.6 fusion.26
  58.2 1.6 fusion.24
  59.8 1.7 fusion.23
  61.5 1.7 fusion.22
  63.2 1.6 fusion.21
  64.8 1.7 fusion.20
  66.5 1.7 fusion.19
  71.7 1.9 convolution_convert_fusion.1
  75.9 1.7 fusion.83
  85.4 2.4 fusion.95
  89.0 2.4 fusion.96
  91.3 1.9 copy.257
  93.3 2.4 fusion.98
  95.6 2.0 copy.261
  97.6 2.4 fusion.97
  100.0 1.9 copy.259
  101.9 2.1 constant_dynamic-update-slice_fusion.7
  109.4 2.4 fusion.148
  115.4 2.7 fusion.45
  118.1 2.6 fusion.47
  121.9 1.9 copy.233
  123.8 2.4 fusion.85
  126.2 1.9 copy.235
  128.1 2.5 fusion.86
  130.7 1.9 copy.237
  132.6 2.4 fusion.87
  134.9 1.9 copy.239
  136.9 2.4 fusion.88
  139.2 1.9 copy.241
  141.2 2.4 fusion.89
  143.5 1.9 copy.243
  145.5 2.4 fusion.90
  147.8 2.0 copy.245
  149.8 1.9 constant_dynamic-update-slice_fusion.6
  151.7 1.8 constant_dynamic-update-slice_fusion.5
  157.4 2.2 fusion.147
  176.5 8.6 %collective-permute-done.4 = bf16[1024,192]{0,1:T(8,128)(2,1)S(1)} collective-permute-done((bf16[1024,192]{0,1:T(8,128)(2,1)S(1)}, bf16[1024,192]{0,1:T(8,128)(2,1)S(1)}, u32[]{:S(2)}, u32[]{:S(2)}) %collective-permute-start.4) | collective-permute-done | bytes 393248 | tf_op jit(solution)/shard_map/ppermute | solution.py:164
  194.0 6.1 %all-to-all-start.1 = ((bf16[16,32,2,192]{3,2,1,0:T(2,128)(2,1)}), bf16[16,32,2,192]{3,2,1,0:T(2,128)(2,1)}, u32[]{:S(2)}, u32[]{:S(2)}) async-start(bf16[16,32,2,192]{3,2,1,0:T(2,128)(2,1)} %reshape.205), calls=%async_computation.1 | async-start | bytes 1048576 | tf_op jit(solution)/shard_map/all_to_all | solution.py:292
  201.4 1.8 slice.383
  204.8 2.1 copy.361
  206.9 3.2 convolution_multiply_fusion.2
  211.5 1.9 copy.279
  216.8 1.7 add_convert_fusion
  226.6 4.9 %all-to-all-start.2 = ((f32[16,24,384]{2,1,0:T(8,128)}), f32[16,24,384]{2,1,0:T(8,128)S(1)}, u32[]{:S(2)}, u32[]{:S(2)}) async-start(f32[16,24,384]{2,1,0:T(8,128)} %bitcast.117), calls=%async_computation.2 | async-start | bytes 1179648 | tf_op jit(solution)/shard_map/all_to_all | solution.py:196
  231.6 3.2 fusion.144
  234.7 12.4 %all-to-all-done.2 = f32[16,24,384]{2,1,0:T(8,128)S(1)} async-done(((f32[16,24,384]{2,1,0:T(8,128)}), f32[16,24,384]{2,1,0:T(8,128)S(1)}, u32[]{:S(2)}, u32[]{:S(2)}) %all-to-all-start.2) | async-done | bytes 589856 | tf_op jit(solution)/shard_map/all_to_all | solution.py:196
  247.2 6.4 %collective-permute-done.7 = bf16[1024,3,192]{0,2,1:T(8,128)(2,1)} collective-permute-done((bf16[1024,3,192]{0,2,1:T(8,128)(2,1)}, bf16[1024,3,192]{0,2,1:T(8,128)(2,1)}, u32[]{:S(2)}, u32[]{:S(2)}) %collective-permute-start.7) | collective-permute-done | bytes 1179680 | tf_op jit(solution)/shard_map/ppermute | solution.py:164
  253.6 3.7 %fusion.60 = bf16[1024,384]{1,0:T(8,128)(2,1)S(1)} fusion(f32[1024,384,1]{1,0,2:T(8,128)} %fusion.144, bf16[1024,3,192]{0,2,1:T(8,128)(2,1)} %collective-permute-done.7, bf16[3,384,192]{1,2,0:T(8,128)(2,1)} %collective-permute-done.3, bf16[1024,192]{1,0:T(8,128)(2,1)} %collective-permute-done.2, bf16[1024,192]{1,0:T(8,128)(2,1)} %copy.264, pred[]{:T(512)S(6)} %eq.854), kind=kOutput, calls=%fused_computation.104 | convolution fusion | flops 458096640 | bytes 4767745 | tf_op jit(solution)/shard_map/rkd,kcd->rc/dot_general | solution.py:314
  259.7 16.9 %all_to_all.25 = f32[16,12,384]{2,1,0:T(8,128)S(1)} all-to-all(f32[16,12,384]{2,1,0:T(8,128)S(1)} %reshape.209), channel_id=1, replica_groups=mesh['pix'=16,'ch'=2] {'pix'}, dimensions={0} | all-to-all | bytes 589824 | tf_op jit(solution)/shard_map/all_to_all | solution.py:196
  276.8 27.4 %all_to_all.26 = f32[16,36,384]{2,1,0:T(8,128)S(1)} all-to-all(f32[16,36,384]{2,1,0:T(8,128)S(1)} %bitcast.278), channel_id=1, replica_groups=mesh['pix'=16,'ch'=2] {'pix'}, dimensions={0} | all-to-all | bytes 1769472 | tf_op jit(solution)/shard_map/all_to_all | solution.py:207
  (249 shorter events, 96.2 us)
Async XLA Ops:
  0.6 10.3 %copy-start.30 = (bf16[384,384]{1,0:T(8,128)(2,1)S(1)}, bf16[384,384]{1,0:T(8,128)(2,1)}, u32[]{:S(2)}) copy-start(bf16[384,384]{1,0:T(8,128)(2,1)} %param.12) | copy-start | bytes 884740
  0.6 10.3 %copy-start.10 = (bf16[1024,384]{1,0:T(8,128)(2,1)S(1)}, bf16[1024,384]{1,0:T(8,128)(2,1)}, u32[]{:S(2)}) copy-start(bf16[1024,384]{1,0:T(8,128)(2,1)} %param.11) | copy-start | bytes 2359300
  0.7 11.1 %collective-permute-start.1 = (bf16[384,384]{1,0:T(8,128)(2,1)}, bf16[384,384]{1,0:T(8,128)(2,1)S(1)}, u32[]{:S(2)}, u32[]{:S(2)}) collective-permute-start(bf16[384,384]{1,0:T(8,128)(2,1)} %param.12), channel_id=1, source_target_pairs={{0,1},{1,0},{2,3},{3,2},{4,5},{5,4},{6,7},{7,6},{8,9},{9,8},{10,11... | collective-permute-start | bytes 884744 | tf_op jit(solution)/shard_map/ppermute | solution.py:164
  3.7 24.1 %collective-permute-start = (bf16[1024,384]{1,0:T(8,128)(2,1)}, bf16[1024,384]{1,0:T(8,128)(2,1)S(1)}, u32[]{:S(2)}, u32[]{:S(2)}) collective-permute-start(bf16[1024,384]{1,0:T(8,128)(2,1)} %param.11), channel_id=1, source_target_pairs={{0,1},{1,0},{2,3},{3,2},{4,5},{5,4},{6,7},{7,6},{8,9},{9,8},{10,11... | collective-permute-start | bytes 2359304 | tf_op jit(solution)/shard_map/ppermute | solution.py:164
  5.6 46.0 %copy-start.48 = (s32[512,1]{0,1:T(1,128)}, s32[512,1]{0,1:T(1,128)S(1)}, u32[]{:S(2)}) copy-start(s32[512,1]{0,1:T(1,128)S(1)} %get-tuple-element.169) | copy-start | bytes 6148
  5.6 47.6 %copy-start.46 = (s32[512,1]{0,1:T(1,128)}, s32[512,1]{0,1:T(1,128)S(1)}, u32[]{:S(2)}) copy-start(s32[512,1]{0,1:T(1,128)S(1)} %get-tuple-element.170) | copy-start | bytes 6148
  5.6 49.3 %copy-start.42 = (s32[512,1]{0,1:T(1,128)}, s32[512,1]{0,1:T(1,128)S(1)}, u32[]{:S(2)}) copy-start(s32[512,1]{0,1:T(1,128)S(1)} %get-tuple-element.171) | copy-start | bytes 6148
  6.2 61.9 %copy-start.44 = (s32[512,1]{0,1:T(1,128)}, s32[512,1]{0,1:T(1,128)S(1)}, u32[]{:S(2)}) copy-start(s32[512,1]{0,1:T(1,128)S(1)} %get-tuple-element.155) | copy-start | bytes 6148
  8.2 27.1 %copy-start.40 = (s32[512]{0:T(512)}, s32[512]{0:T(512)S(1)}, u32[]{:S(2)}) copy-start(s32[512]{0:T(512)S(1)} %eq.783) | copy-start | bytes 6148
  11.6 18.9 %copy-start.14 = (bf16[1024,192]{0,1:T(8,128)(2,1)S(1)}, bf16[1024,192]{0,1:T(8,128)(2,1)}, u32[]{:S(2)}) copy-start(bf16[1024,192]{0,1:T(8,128)(2,1)} %param.17) | copy-start | bytes 1179652
  28.4 148.1 %collective-permute-start.5 = (bf16[192,192]{1,0:T(8,128)(2,1)}, bf16[192,192]{1,0:T(8,128)(2,1)}, u32[]{:S(2)}, u32[]{:S(2)}) collective-permute-start(bf16[192,192]{1,0:T(8,128)(2,1)} %bitcast.250), channel_id=1, source_target_pairs={{0,1},{1,0},{2,3},{3,2},{4,5},{5,4},{6,7},{7,6},{8,9},{9,8},{10,11... | collective-permute-start | bytes 221192 | tf_op jit(solution)/shard_map/ppermute | solution.py:260
  30.2 43.4 %collective-permute-start.3 = (bf16[3,384,192]{1,2,0:T(8,128)(2,1)}, bf16[3,384,192]{1,2,0:T(8,128)(2,1)}, u32[]{:S(2)}, u32[]{:S(2)}) collective-permute-start(bf16[3,384,192]{1,2,0:T(8,128)(2,1)} %param.13), channel_id=1, source_target_pairs={{0,1},{1,0},{2,3},{3,2},{4,5},{5,4},{6,7},{7,6},{8,9},{9,8},{10,11... | collective-permute-start | bytes 1327112 | tf_op jit(solution)/shard_map/ppermute | solution.py:164
  31.5 40.2 %collective-permute-start.2 = (bf16[1024,192]{1,0:T(8,128)(2,1)}, bf16[1024,192]{1,0:T(8,128)(2,1)}, u32[]{:S(2)}, u32[]{:S(2)}) collective-permute-start(bf16[1024,192]{1,0:T(8,128)(2,1)} %copy.263), channel_id=1, source_target_pairs={{0,1},{1,0},{2,3},{3,2},{4,5},{5,4},{6,7},{7,6},{8,9},{9,8},{10,11... | collective-permute-start | bytes 1179656 | tf_op jit(solution)/shard_map/ppermute | solution.py:164
  37.1 38.1 %all-to-all-start = ((bf16[16,32,2,192]{3,2,1,0:T(2,128)(2,1)}), bf16[16,32,2,192]{3,2,1,0:T(2,128)(2,1)S(1)}, u32[]{:S(2)}, u32[]{:S(2)}) async-start(bf16[16,32,2,192]{3,2,1,0:T(2,128)(2,1)} %reshape.203), calls=%async_computation | async-start | bytes 1048576 | tf_op jit(solution)/shard_map/all_to_all | solution.py:276
  69.8 1.9 copy-start.36
  69.8 1.9 copy-start.38
  75.9 5.2 %copy-start.33 = (f32[512,384]{1,0:T(8,128)S(1)}, f32[512,384]{1,0:T(8,128)}, u32[]{:S(2)}) copy-start(f32[512,384]{1,0:T(8,128)} %fusion.27) | copy-start | bytes 2359300
  101.9 5.2 %copy-start.18 = (bf16[512,384]{0,1:T(8,128)(2,1)S(1)}, bf16[512,384]{0,1:T(8,128)(2,1)}, u32[]{:S(2)}) copy-start(bf16[512,384]{0,1:T(8,128)(2,1)} %copy.257) | copy-start | bytes 1179652
  104.0 3.9 %copy-start.22 = (bf16[512,384]{0,1:T(8,128)(2,1)S(1)}, bf16[512,384]{0,1:T(8,128)(2,1)}, u32[]{:S(2)}) copy-start(bf16[512,384]{0,1:T(8,128)(2,1)} %copy.259) | copy-start | bytes 1179652
  104.0 4.7 %copy-start.17 = (bf16[512,384]{0,1:T(8,128)(2,1)S(1)}, bf16[512,384]{0,1:T(8,128)(2,1)}, u32[]{:S(2)}) copy-start(bf16[512,384]{0,1:T(8,128)(2,1)} %copy.261) | copy-start | bytes 1179652
  109.4 2.4 copy-start.8
  111.8 1.8 copy-start
  111.8 1.3 copy-start.9
  114.7 0.7 copy-start.49
  115.1 3.0 copy-start.3
  115.4 2.7 copy-start.47
  118.1 2.6 copy-start.32
  118.1 2.6 copy-start.39
  147.8 5.7 %copy-start.19 = (bf16[512,384]{0,1:T(8,128)(2,1)S(1)}, bf16[512,384]{0,1:T(8,128)(2,1)}, u32[]{:S(2)}) copy-start(bf16[512,384]{0,1:T(8,128)(2,1)} %copy.237) | copy-start | bytes 1179652
  149.8 4.5 %copy-start.20 = (bf16[512,384]{0,1:T(8,128)(2,1)S(1)}, bf16[512,384]{0,1:T(8,128)(2,1)}, u32[]{:S(2)}) copy-start(bf16[512,384]{0,1:T(8,128)(2,1)} %copy.239) | copy-start | bytes 1179652
  149.8 5.3 %copy-start.21 = (bf16[512,384]{0,1:T(8,128)(2,1)S(1)}, bf16[512,384]{0,1:T(8,128)(2,1)}, u32[]{:S(2)}) copy-start(bf16[512,384]{0,1:T(8,128)(2,1)} %copy.241) | copy-start | bytes 1179652
  149.8 6.0 %copy-start.23 = (bf16[512,384]{0,1:T(8,128)(2,1)S(1)}, bf16[512,384]{0,1:T(8,128)(2,1)}, u32[]{:S(2)}) copy-start(bf16[512,384]{0,1:T(8,128)(2,1)} %copy.243) | copy-start | bytes 1179652
  149.8 6.8 %copy-start.24 = (bf16[512,384]{0,1:T(8,128)(2,1)S(1)}, bf16[512,384]{0,1:T(8,128)(2,1)}, u32[]{:S(2)}) copy-start(bf16[512,384]{0,1:T(8,128)(2,1)} %copy.245) | copy-start | bytes 1179652
  159.6 1.0 copy-start.7
  162.3 0.7 copy-start.45
  162.6 8.9 %copy-start.2 = (bf16[512,9,2,3,64]{0,4,3,2,1:T(8,128)(2,1)}, bf16[512,9,2,3,64]{0,4,3,2,1:T(8,128)(2,1)S(1)}, u32[]{:S(2)}) copy-start(bf16[512,9,2,3,64]{0,4,3,2,1:T(8,128)(2,1)S(1)} %pad_maximum_fusion) | copy-start | bytes 10616836
  171.5 1.6 copy-start.1
  172.8 2.2 copy-start.4
  172.8 2.2 copy-start.43
  173.6 2.5 copy-start.25
  173.6 11.5 %collective-permute-start.4 = (bf16[1024,192]{0,1:T(8,128)(2,1)S(1)}, bf16[1024,192]{0,1:T(8,128)(2,1)S(1)}, u32[]{:S(2)}, u32[]{:S(2)}) collective-permute-start(bf16[1024,192]{0,1:T(8,128)(2,1)S(1)} %bitcast.298), channel_id=1, source_target_pairs={{0,1},{1,0},{2,3},{3,2},{4,5},{5,4},{6,7},{7,6},{8,9},{9,8},{10,11... | collective-permute-start | bytes 1179656 | tf_op jit(solution)/shard_map/ppermute | solution.py:164
  175.0 10.1 %copy-start.12 = (f32[1536,384]{1,0:T(8,128)S(1)}, f32[1536,384]{1,0:T(8,128)}, u32[]{:S(2)}) copy-start(f32[1536,384]{1,0:T(8,128)} %fusion.45) | copy-start | bytes 7077892
  175.0 10.1 %copy-start.13 = (f32[1536,384]{1,0:T(8,128)S(1)}, f32[1536,384]{1,0:T(8,128)}, u32[]{:S(2)}) copy-start(f32[1536,384]{1,0:T(8,128)} %fusion.47) | copy-start | bytes 7077892
  185.1 1.4 copy-start.37
  191.3 1.5 copy-start.5
  194.0 20.6 %all-to-all-start.1 = ((bf16[16,32,2,192]{3,2,1,0:T(2,128)(2,1)}), bf16[16,32,2,192]{3,2,1,0:T(2,128)(2,1)}, u32[]{:S(2)}, u32[]{:S(2)}) async-start(bf16[16,32,2,192]{3,2,1,0:T(2,128)(2,1)} %reshape.205), calls=%async_computation.1 | async-start | bytes 1048576 | tf_op jit(solution)/shard_map/all_to_all | solution.py:292
  204.8 13.7 %copy-start.15 = (bf16[1024,1,192]{0,2,1:T(8,128)(2,1)}, bf16[1024,1,192]{0,2,1:T(8,128)(2,1)S(1)}, u32[]{:S(2)}) copy-start(bf16[1024,1,192]{0,2,1:T(8,128)(2,1)S(1)} %reshape_reshape.8) | copy-start | bytes 1179652
  204.8 5.3 %copy-start.6 = (f32[1536,384]{1,0:T(8,128)S(1)}, f32[1536,384]{1,0:T(8,128)}, u32[]{:S(2)}) copy-start(f32[1536,384]{1,0:T(8,128)} %copy-done.5) | copy-start | bytes 7077892
  206.9 3.2 copy-start.27
  206.9 3.2 copy-start.28
  211.5 5.4 %copy-start.41 = (s32[512]{0:T(512)S(1)}, s32[512]{0:T(512)}, u32[]{:S(2)}) copy-start(s32[512]{0:T(512)} %copy-done.40) | copy-start | bytes 6148
  218.6 0.9 copy-start.34
  222.5 1.3 copy-start.16
  222.5 1.3 copy-start.35
  222.5 3.2 %copy-start.29 = (f32[192,384]{1,0:T(8,128)S(1)}, f32[192,384]{1,0:T(8,128)}, u32[]{:S(2)}) copy-start(f32[192,384]{1,0:T(8,128)} %convolution_multiply_fusion.2) | copy-start | bytes 884740
  223.6 2.1 collective-permute-start.6
  225.0 28.6 %collective-permute-start.7 = (bf16[1024,3,192]{0,2,1:T(8,128)(2,1)}, bf16[1024,3,192]{0,2,1:T(8,128)(2,1)}, u32[]{:S(2)}, u32[]{:S(2)}) collective-permute-start(bf16[1024,3,192]{0,2,1:T(8,128)(2,1)} %pad_maximum_fusion.2), channel_id=1, source_target_pairs={{0,1},{1,0},{2,3},{3,2},{4,5},{5,4},{6,7},{7,6},{8,9},{9,8},{10,11... | collective-permute-start | bytes 3538952 | tf_op jit(solution)/shard_map/ppermute | solution.py:164
  226.6 20.5 %all-to-all-start.2 = ((f32[16,24,384]{2,1,0:T(8,128)}), f32[16,24,384]{2,1,0:T(8,128)S(1)}, u32[]{:S(2)}, u32[]{:S(2)}) async-start(f32[16,24,384]{2,1,0:T(8,128)} %bitcast.117), calls=%async_computation.2 | async-start | bytes 1179648 | tf_op jit(solution)/shard_map/all_to_all | solution.py:196
  247.2 10.1 %copy-start.11 = (bf16[1024,384]{1,0:T(8,128)(2,1)S(1)}, bf16[1024,384]{1,0:T(8,128)(2,1)}, u32[]{:S(2)}) copy-start(bf16[1024,384]{1,0:T(8,128)(2,1)} %param.11) | copy-start | bytes 2359300
  258.0 1.6 collective-permute-start.8
  276.7 29.4 %copy-start.26 = (bf16[2,24,8,512]{3,2,0,1:T(8,128)(2,1)S(1)}, bf16[2,24,8,512]{3,2,0,1:T(8,128)(2,1)}, u32[]{:S(2)}) copy-start(bf16[2,24,8,512]{3,2,0,1:T(8,128)(2,1)} %copy-done.25) | copy-start | bytes 1179652
  305.3 6.0 %collective-permute-start.9 = (f32[16,36,384]{2,0,1:T(8,128)}, f32[16,36,384]{2,0,1:T(8,128)}, u32[]{:S(2)}, u32[]{:S(2)}) collective-permute-start(f32[16,36,384]{2,0,1:T(8,128)} %copy.283), channel_id=1, source_target_pairs={{0,2},{2,0},{4,6},{6,4},{8,10},{10,8},{12,14},{14,12},{16,18},{18,... | collective-permute-start | bytes 2654216 | tf_op jit(solution)/shard_map/ppermute | solution.py:182
  306.1 3.7 %copy-start.31 = (bf16[384,384]{1,0:T(8,128)(2,1)S(1)}, bf16[384,384]{1,0:T(8,128)(2,1)}, u32[]{:S(2)}) copy-start(bf16[384,384]{1,0:T(8,128)(2,1)} %param.12) | copy-start | bytes 884740

commit v14 on v11

--- a/solution.py
+++ b/solution.py
@@ -261,11 +261,10 @@
     attended, prob_blocks, kv_blocks = attention_forward(queries, extended, neighbours, 0)
     attended_others = ch_exchange(attended)
     grad_attended = jnp.dot(upstream, mixing_weight.T, preferred_element_type=f32).astype(bf16)
-    grad_attended, proj_others = lax.optimization_barrier((grad_attended, proj_others))
     mixing_term = jnp.dot(attended.T, upstream, preferred_element_type=f32) * grad_scale
-    carried, query_grads, (attended_others, mix_others) = attention_backward(
+    carried, query_grads, (attended_others, mix_others, proj_others) = attention_backward(
         queries, extended.shape[0], neighbours, 0, grad_attended, prob_blocks, kv_blocks,
-        (attended_others, mix_others),
+        (attended_others, mix_others, proj_others),
     )
     branch = jnp.dot(attended, mix_own, preferred_element_type=f32)
     for attended_other, mix_other in zip(attended_others, mix_others):

time: 252 us -> 241 us (0.956)
  waiting for transfers between devices: 63.8 us -> 55 us
    ppermute x6, waiting for transfers between devices: 48.6 us -> 39.9 us  [ch_exchange(): lax.ppermute(value, 'ch', [(i, (i + shift) % size) for i in range(size)])]
    unnamed x80 -> x78, local copies, waits for them, and re-layouts: 11.9 us -> 11.2 us
  transfers between devices with their start and end apart: 13 -> 13, of which waited for: 8 -> 7; matrix products, arithmetic and copies ran while one was open for 30% -> 31% of each run, Pallas kernels for 0% -> 0%
where the time goes in v14:
time: 241 us; the launch traced here: 237 us
  matrix products  58.1 us (24%)
  waiting for transfers between devices  55 us (23%)
  blocking collectives  43.9 us (18%)
  local copies, waits for them, and re-layouts  34 us (14%)
  starting transfers between devices  28 us (12%)
  other arithmetic  15.8 us (7%)
    ppermute x6, waiting for transfers between devices, ch_exchange(): lax.ppermute(value, 'ch', [(i, (i + shift) % size) for i in range(size)])  39.9 us
    all_to_all x1, blocking collectives, pix_gather(): lax.all_to_all(spread.reshape(size, total, width), 'pix', 0, 0, tiled=True)  27.2 us
    dot_general x16, matrix products, backward_block(): jnp.einsum('bx,bc->xc', pick_table(slot_rows[:, slot], ext_rows), contrib...  20.2 us
    dot_general x16, matrix products, forward_block(): jnp.dot(pick_table(slot_rows[:, slot], ext_rows), flattened, preferred_el...  16.8 us
    all_to_all x1, blocking collectives, pix_scatter(): lax.all_to_all(mine.reshape(size, chunk, width), 'pix', 0, 0, tiled=True)  16.8 us
    all_to_all x1, waiting for transfers between devices, pix_scatter(): lax.all_to_all(mine.reshape(size, chunk, width), 'pix', 0, 0, tiled=True)  12.4 us
    unnamed x78, local copies, waits for them, and re-layouts  11.2 us
    ppermute x6, starting transfers between devices, ch_exchange(): lax.ppermute(value, 'ch', [(i, (i + shift) % size) for i in range(size)])  9.07 us
  transfers between devices with their start and end apart: 13, of which 7 were waited for; matrix products, arithmetic and copies ran while one was open for 31% of the time, Pallas kernels for 0%

profile of v14, /device:TPU:0, one launch (start us, length us, event | category | flops | bytes accessed | tf_op | source)
XLA Modules:
  0.0 236.8 jit_solution(14471658344324330094)
XLA Ops:
  0.7 3.0 %collective-permute-start = (bf16[1024,384]{1,0:T(8,128)(2,1)}, bf16[1024,384]{1,0:T(8,128)(2,1)S(1)}, u32[]{:S(2)}, u32[]{:S(2)}) collective-permute-start(bf16[1024,384]{1,0:T(8,128)(2,1)} %param.11), channel_id=1, source_target_pairs={{0,1},{1,0},{2,3},{3,2},{4,5},{5,4},{6,7},{7,6},{8,9},{9,8},{10,11... | collective-permute-start | bytes 2359304 | tf_op jit(solution)/shard_map/ppermute | solution.py:145
  3.7 1.1 reshape.203
  6.2 1.2 broadcast_select_fusion
  8.8 1.2 copy.109
  10.7 17.0 %collective-permute-done.1 = bf16[384,384]{1,0:T(8,128)(2,1)S(1)} collective-permute-done((bf16[384,384]{1,0:T(8,128)(2,1)}, bf16[384,384]{1,0:T(8,128)(2,1)S(1)}, u32[]{:S(2)}, u32[]{:S(2)}) %collective-permute-start.1) | collective-permute-done | bytes 294944 | tf_op jit(solution)/shard_map/ppermute | solution.py:145
  31.1 1.1 reshape.204
  32.2 6.8 %all-to-all-start = ((bf16[16,32,2,192]{3,2,1,0:T(2,128)(2,1)}), bf16[16,32,2,192]{3,2,1,0:T(2,128)(2,1)}, u32[]{:S(2)}, u32[]{:S(2)}) async-start(bf16[16,32,2,192]{3,2,1,0:T(2,128)(2,1)} %reshape.204), calls=%async_computation | async-start | bytes 1048576 | tf_op jit(solution)/shard_map/all_to_all | solution.py:257
  38.9 1.0 copy.108
  39.9 1.5 collective-permute-start.2
  42.1 1.5 collective-permute-start.5
  44.6 10.3 %collective-permute-done.2 = bf16[1024,192]{1,0:T(8,128)(2,1)S(1)} collective-permute-done((bf16[1024,192]{1,0:T(8,128)(2,1)}, bf16[1024,192]{1,0:T(8,128)(2,1)S(1)}, u32[]{:S(2)}, u32[]{:S(2)}) %collective-permute-start.2) | collective-permute-done | bytes 393248 | tf_op jit(solution)/shard_map/ppermute | solution.py:145
  55.8 1.4 concatenate.45
  58.1 2.3 fusion.100
  60.4 1.0 fusion.108
  68.3 1.3 copy-done.4
  72.8 1.3 fusion.53
  74.2 1.2 fusion.51
  86.0 1.2 fusion.40
  87.2 1.4 convolution_add_fusion.11
  88.6 1.2 convolution_add_fusion.10
  89.8 1.2 convolution_add_fusion.9
  91.0 1.2 convolution_add_fusion.8
  92.2 1.2 convolution_add_fusion.7
  93.4 1.2 convolution_add_fusion.6
  94.6 1.2 convolution_add_fusion.5
  95.8 1.5 collective-permute-start.3
  97.4 1.2 fusion.49
  98.9 7.0 %collective-permute-done.3 = bf16[1024,192]{0,1:T(8,128)(2,1)S(1)} collective-permute-done((bf16[1024,192]{0,1:T(8,128)(2,1)S(1)}, bf16[1024,192]{0,1:T(8,128)(2,1)S(1)}, u32[]{:S(2)}, u32[]{:S(2)}) %collective-permute-start.3) | collective-permute-done | bytes 393248 | tf_op jit(solution)/shard_map/ppermute | solution.py:145
  105.9 1.6 convolution_add_fusion.4
  107.5 1.2 convolution_add_fusion.3
  108.7 1.6 convolution_add_fusion.2
  110.3 1.2 convolution_add_fusion.1
  111.5 1.2 convolution_add_fusion
  112.7 1.5 copy-done.2
  114.2 1.1 reshape.206
  115.3 5.6 %all-to-all-start.1 = ((bf16[16,32,2,192]{3,2,1,0:T(2,128)(2,1)}), bf16[16,32,2,192]{3,2,1,0:T(2,128)(2,1)}, u32[]{:S(2)}, u32[]{:S(2)}) async-start(bf16[16,32,2,192]{3,2,1,0:T(2,128)(2,1)} %reshape.206), calls=%async_computation.1 | async-start | bytes 1048576 | tf_op jit(solution)/shard_map/all_to_all | solution.py:274
  121.2 1.0 slice.369
  122.3 1.0 slice.368
  125.2 1.1 copy.113
  126.3 1.4 reshape_reshape.4
  127.8 3.2 %convolution_multiply_fusion.2 = f32[192,384]{1,0:T(8,128)} fusion(bf16[1024,192]{0,1:T(8,128)(2,1)} %bitcast.237, bf16[1024,192]{1,0:T(8,128)(2,1)} %copy-done.22, bf16[1024,192]{1,0:T(8,128)(2,1)} %copy-done.28, pred[]{:T(512)S(6)} %eq.213), kind=kOutput, calls=%fused_computation.152 | convolution fusion | flops 154607616 | bytes 1474561 | tf_op jit(solution)/shard_map/dot_general | solution.py:264
  131.0 1.3 slice_add_fusion
  132.4 1.9 copy.124
  134.2 1.2 all-to-all-done.1
  135.4 1.4 convert_element_type.203
  137.7 1.7 add_convert_fusion
  141.6 1.3 copy.126
  143.4 1.1 broadcast_select_fusion.2
  144.7 1.1 pad_maximum_fusion.3
  145.8 1.5 collective-permute-start.7
  148.2 5.0 %all-to-all-start.2 = ((f32[16,24,384]{2,1,0:T(8,128)}), f32[16,24,384]{2,1,0:T(8,128)S(1)}, u32[]{:S(2)}, u32[]{:S(2)}) async-start(f32[16,24,384]{2,1,0:T(8,128)} %bitcast.101), calls=%async_computation.2 | async-start | bytes 1179648 | tf_op jit(solution)/shard_map/all_to_all | solution.py:177
  153.3 3.1 %fusion.128 = f32[1024,384,1]{1,0,2:T(8,128)} fusion(bf16[3,384,192]{1,2,0:T(8,128)(2,1)} %param.13, bf16[1024,2,192]{0,2,1:T(8,128)(2,1)S(1)} %copy-done.21, bf16[1024,1,192]{0,2,1:T(8,128)(2,1)S(1)} %copy-done.10), kind=kOutput, calls=%fused_computation.229 | convolution fusion | flops 453574656 | bytes 3194880 | tf_op jit(solution)/shard_map/rkd,kcd->rc/dot_general | solution.py:292
  156.4 12.4 %all-to-all-done.2 = f32[16,24,384]{2,1,0:T(8,128)S(1)} async-done(((f32[16,24,384]{2,1,0:T(8,128)}), f32[16,24,384]{2,1,0:T(8,128)S(1)}, u32[]{:S(2)}, u32[]{:S(2)}) %all-to-all-start.2) | async-done | bytes 589856 | tf_op jit(solution)/shard_map/all_to_all | solution.py:177
  168.8 5.6 %collective-permute-done.7 = bf16[1024,3,192]{0,2,1:T(8,128)(2,1)} collective-permute-done((bf16[1024,3,192]{0,2,1:T(8,128)(2,1)}, bf16[1024,3,192]{0,2,1:T(8,128)(2,1)}, u32[]{:S(2)}, u32[]{:S(2)}) %collective-permute-start.7) | collective-permute-done | bytes 1179680 | tf_op jit(solution)/shard_map/ppermute | solution.py:145
  174.4 3.7 %fusion.60 = bf16[1024,384]{1,0:T(8,128)(2,1)S(1)} fusion(f32[1024,384,1]{1,0,2:T(8,128)} %fusion.128, bf16[1024,3,192]{0,2,1:T(8,128)(2,1)} %collective-permute-done.7, bf16[3,384,192]{1,2,0:T(8,128)(2,1)} %collective-permute-done.5, bf16[1024,192]{1,0:T(8,128)(2,1)} %copy-done.28, bf16[1024,192]{1,0:T(8,128)(2,1)} %copy-done.22, pred[]{:T(512)S(6)} %eq.213), kind=kOutput, calls=%fused_computation.88 | convolution fusion | flops 458096640 | bytes 4767745 | tf_op jit(solution)/shard_map/rkd,kcd->rc/dot_general | solution.py:296
  178.9 1.6 collective-permute-done.8
  180.6 16.8 %all_to_all.25 = f32[16,12,384]{2,1,0:T(8,128)S(1)} all-to-all(f32[16,12,384]{2,1,0:T(8,128)S(1)} %reshape.210), channel_id=1, replica_groups=mesh['pix'=16,'ch'=2] {'pix'}, dimensions={0} | all-to-all | bytes 589824 | tf_op jit(solution)/shard_map/all_to_all | solution.py:177
  197.5 27.2 %all_to_all.26 = f32[16,36,384]{2,1,0:T(8,128)S(1)} all-to-all(f32[16,36,384]{2,1,0:T(8,128)S(1)} %bitcast.230), channel_id=1, replica_groups=mesh['pix'=16,'ch'=2] {'pix'}, dimensions={0} | all-to-all | bytes 1769472 | tf_op jit(solution)/shard_map/all_to_all | solution.py:188
  224.6 1.1 copy.128
  226.5 1.3 fusion.121
  227.8 1.5 fusion.97
  230.2 1.5 convolution_convert_fusion
  231.7 1.5 copy_select_fusion.1
  234.5 1.3 copy.132
  (176 shorter events, 42.7 us)
Async XLA Ops:
  0.6 9.4 %copy-start.6 = (bf16[1024,384]{1,0:T(8,128)(2,1)S(1)}, bf16[1024,384]{1,0:T(8,128)(2,1)}, u32[]{:S(2)}) copy-start(bf16[1024,384]{1,0:T(8,128)(2,1)} %param.11) | copy-start | bytes 2359300
  0.6 9.4 %copy-start.16 = (bf16[384,384]{1,0:T(8,128)(2,1)S(1)}, bf16[384,384]{1,0:T(8,128)(2,1)}, u32[]{:S(2)}) copy-start(bf16[384,384]{1,0:T(8,128)(2,1)} %param.12) | copy-start | bytes 884740
  0.7 27.1 %collective-permute-start = (bf16[1024,384]{1,0:T(8,128)(2,1)}, bf16[1024,384]{1,0:T(8,128)(2,1)S(1)}, u32[]{:S(2)}, u32[]{:S(2)}) collective-permute-start(bf16[1024,384]{1,0:T(8,128)(2,1)} %param.11), channel_id=1, source_target_pairs={{0,1},{1,0},{2,3},{3,2},{4,5},{5,4},{6,7},{7,6},{8,9},{9,8},{10,11... | collective-permute-start | bytes 2359304 | tf_op jit(solution)/shard_map/ppermute | solution.py:145
  3.7 24.1 %collective-permute-start.1 = (bf16[384,384]{1,0:T(8,128)(2,1)}, bf16[384,384]{1,0:T(8,128)(2,1)S(1)}, u32[]{:S(2)}, u32[]{:S(2)}) collective-permute-start(bf16[384,384]{1,0:T(8,128)(2,1)} %param.12), channel_id=1, source_target_pairs={{0,1},{1,0},{2,3},{3,2},{4,5},{5,4},{6,7},{7,6},{8,9},{9,8},{10,11... | collective-permute-start | bytes 884744 | tf_op jit(solution)/shard_map/ppermute | solution.py:145
  10.0 44.9 %copy-start.22 = (bf16[1024,192]{1,0:T(8,128)(2,1)}, bf16[1024,192]{1,0:T(8,128)(2,1)S(1)}, u32[]{:S(2)}) copy-start(bf16[1024,192]{1,0:T(8,128)(2,1)S(1)} %copy.109) | copy-start | bytes 1179652
  10.7 17.7 %copy-start.23 = (bf16[3,384,192]{1,2,0:T(8,128)(2,1)S(1)}, bf16[3,384,192]{1,2,0:T(8,128)(2,1)}, u32[]{:S(2)}) copy-start(bf16[3,384,192]{1,2,0:T(8,128)(2,1)} %param.13) | copy-start | bytes 1327108
  29.4 0.9 copy-start.18
  29.4 9.5 %copy-start.8 = (bf16[1024,192]{0,1:T(8,128)(2,1)S(1)}, bf16[1024,192]{0,1:T(8,128)(2,1)}, u32[]{:S(2)}) copy-start(bf16[1024,192]{0,1:T(8,128)(2,1)} %param.17) | copy-start | bytes 1179652
  32.2 23.6 %all-to-all-start = ((bf16[16,32,2,192]{3,2,1,0:T(2,128)(2,1)}), bf16[16,32,2,192]{3,2,1,0:T(2,128)(2,1)}, u32[]{:S(2)}, u32[]{:S(2)}) async-start(bf16[16,32,2,192]{3,2,1,0:T(2,128)(2,1)} %reshape.204), calls=%async_computation | async-start | bytes 1048576 | tf_op jit(solution)/shard_map/all_to_all | solution.py:257
  39.9 15.0 %copy-start.26 = (bf16[192,384]{1,0:T(8,128)(2,1)S(1)}, bf16[192,384]{1,0:T(8,128)(2,1)}, u32[]{:S(2)}) copy-start(bf16[192,384]{1,0:T(8,128)(2,1)} %param.14) | copy-start | bytes 442372
  39.9 15.0 %collective-permute-start.2 = (bf16[1024,192]{1,0:T(8,128)(2,1)}, bf16[1024,192]{1,0:T(8,128)(2,1)S(1)}, u32[]{:S(2)}, u32[]{:S(2)}) collective-permute-start(bf16[1024,192]{1,0:T(8,128)(2,1)} %copy.108), channel_id=1, source_target_pairs={{0,1},{1,0},{2,3},{3,2},{4,5},{5,4},{6,7},{7,6},{8,9},{9,8},{10,11... | collective-permute-start | bytes 1179656 | tf_op jit(solution)/shard_map/ppermute | solution.py:145
  41.5 57.4 %collective-permute-start.4 = (bf16[192,192]{1,0:T(8,128)(2,1)}, bf16[192,192]{1,0:T(8,128)(2,1)}, u32[]{:S(2)}, u32[]{:S(2)}) collective-permute-start(bf16[192,192]{1,0:T(8,128)(2,1)} %bitcast.285), channel_id=1, source_target_pairs={{0,1},{1,0},{2,3},{3,2},{4,5},{5,4},{6,7},{7,6},{8,9},{9,8},{10,11... | collective-permute-start | bytes 221192 | tf_op jit(solution)/shard_map/ppermute | solution.py:241
  42.1 56.8 %collective-permute-start.5 = (bf16[3,384,192]{1,2,0:T(8,128)(2,1)}, bf16[3,384,192]{1,2,0:T(8,128)(2,1)}, u32[]{:S(2)}, u32[]{:S(2)}) collective-permute-start(bf16[3,384,192]{1,2,0:T(8,128)(2,1)} %param.13), channel_id=1, source_target_pairs={{0,1},{1,0},{2,3},{3,2},{4,5},{5,4},{6,7},{7,6},{8,9},{9,8},{10,11... | collective-permute-start | bytes 1327112 | tf_op jit(solution)/shard_map/ppermute | solution.py:145
  54.9 0.8 copy-start.28
  58.1 2.3 copy-start.19
  58.1 2.3 copy-start.24
  61.4 1.0 copy-start.27
  66.3 2.0 copy-start.5
  67.3 2.3 copy-start.4
  72.8 38.7 %copy-start.1 = (bf16[512,9,2,3,64]{0,4,3,2,1:T(8,128)(2,1)}, bf16[512,9,2,3,64]{0,4,3,2,1:T(8,128)(2,1)S(1)}, u32[]{:S(2)}) copy-start(bf16[512,9,2,3,64]{0,4,3,2,1:T(8,128)(2,1)S(1)} %pad_maximum_fusion.1) | copy-start | bytes 10616836
  84.6 11.2 %copy-start.11 = (bf16[2,24,8,512]{3,2,0,1:T(8,128)(2,1)}, bf16[2,24,8,512]{3,2,0,1:T(8,128)(2,1)S(1)}, u32[]{:S(2)}) copy-start(bf16[2,24,8,512]{3,2,0,1:T(8,128)(2,1)S(1)} %copy.201) | copy-start | bytes 1179652
  86.0 8.6 %copy-start = (bf16[512,9,2,3,64]{0,4,3,2,1:T(8,128)(2,1)}, bf16[512,9,2,3,64]{0,4,3,2,1:T(8,128)(2,1)S(1)}, u32[]{:S(2)}) copy-start(bf16[512,9,2,3,64]{0,4,3,2,1:T(8,128)(2,1)S(1)} %pad_maximum_fusion) | copy-start | bytes 10616836
  95.8 10.1 %collective-permute-start.3 = (bf16[1024,192]{0,1:T(8,128)(2,1)S(1)}, bf16[1024,192]{0,1:T(8,128)(2,1)S(1)}, u32[]{:S(2)}, u32[]{:S(2)}) collective-permute-start(bf16[1024,192]{0,1:T(8,128)(2,1)S(1)} %bitcast.236), channel_id=1, source_target_pairs={{0,1},{1,0},{2,3},{3,2},{4,5},{5,4},{6,7},{7,6},{8,9},{9,8},{10,11... | collective-permute-start | bytes 1179656 | tf_op jit(solution)/shard_map/ppermute | solution.py:145
  105.9 1.6 copy-start.25
  112.7 1.5 copy-start.2
  115.3 20.1 %all-to-all-start.1 = ((bf16[16,32,2,192]{3,2,1,0:T(2,128)(2,1)}), bf16[16,32,2,192]{3,2,1,0:T(2,128)(2,1)}, u32[]{:S(2)}, u32[]{:S(2)}) async-start(bf16[16,32,2,192]{3,2,1,0:T(2,128)(2,1)} %reshape.206), calls=%async_computation.1 | async-start | bytes 1048576 | tf_op jit(solution)/shard_map/all_to_all | solution.py:274
  126.3 4.7 %copy-start.3 = (f32[1536,384]{1,0:T(8,128)S(1)}, f32[1536,384]{1,0:T(8,128)}, u32[]{:S(2)}) copy-start(f32[1536,384]{1,0:T(8,128)} %copy-done.2) | copy-start | bytes 7077892
  127.7 11.7 %copy-start.9 = (bf16[1024,1,192]{0,2,1:T(8,128)(2,1)}, bf16[1024,1,192]{0,2,1:T(8,128)(2,1)S(1)}, u32[]{:S(2)}) copy-start(bf16[1024,1,192]{0,2,1:T(8,128)(2,1)S(1)} %reshape_reshape.4) | copy-start | bytes 1179652
  127.7 3.3 %copy-start.13 = (bf16[512,1,384]{2,0,1:T(8,128)(2,1)S(1)}, bf16[512,1,384]{2,0,1:T(8,128)(2,1)}, u32[]{:S(2)}) copy-start(bf16[512,1,384]{2,0,1:T(8,128)(2,1)} %copy.190) | copy-start | bytes 1179652
  127.7 3.3 %copy-start.14 = (bf16[512,1,384]{2,0,1:T(8,128)(2,1)S(1)}, bf16[512,1,384]{2,0,1:T(8,128)(2,1)}, u32[]{:S(2)}) copy-start(bf16[512,1,384]{2,0,1:T(8,128)(2,1)} %copy.189) | copy-start | bytes 1179652
  139.4 0.9 copy-start.20
  143.3 1.3 copy-start.10
  143.4 1.3 copy-start.21
  143.4 3.9 %copy-start.15 = (f32[192,384]{1,0:T(8,128)S(1)}, f32[192,384]{1,0:T(8,128)}, u32[]{:S(2)}) copy-start(f32[192,384]{1,0:T(8,128)} %convolution_multiply_fusion.2) | copy-start | bytes 884740
  144.5 2.8 %collective-permute-start.6 = (f32[384,384]{1,0:T(8,128)S(1)}, f32[384,384]{1,0:T(8,128)S(1)}, u32[]{:S(2)}, u32[]{:S(2)}) collective-permute-start(f32[384,384]{1,0:T(8,128)S(1)} %broadcast_select_fusion.2), channel_id=1, source_target_pairs={{0,2},{2,0},{4,6},{6,4},{8,10},{10,8},{12,14},{14,12},{16,18},{18,... | collective-permute-start | bytes 1769480 | tf_op jit(solution)/shard_map/ppermute | solution.py:163
  145.8 28.6 %collective-permute-start.7 = (bf16[1024,3,192]{0,2,1:T(8,128)(2,1)}, bf16[1024,3,192]{0,2,1:T(8,128)(2,1)}, u32[]{:S(2)}, u32[]{:S(2)}) collective-permute-start(bf16[1024,3,192]{0,2,1:T(8,128)(2,1)} %pad_maximum_fusion.3), channel_id=1, source_target_pairs={{0,1},{1,0},{2,3},{3,2},{4,5},{5,4},{6,7},{7,6},{8,9},{9,8},{10,11... | collective-permute-start | bytes 3538952 | tf_op jit(solution)/shard_map/ppermute | solution.py:145
  148.2 20.6 %all-to-all-start.2 = ((f32[16,24,384]{2,1,0:T(8,128)}), f32[16,24,384]{2,1,0:T(8,128)S(1)}, u32[]{:S(2)}, u32[]{:S(2)}) async-start(f32[16,24,384]{2,1,0:T(8,128)} %bitcast.101), calls=%async_computation.2 | async-start | bytes 1179648 | tf_op jit(solution)/shard_map/all_to_all | solution.py:177
  168.8 9.3 %copy-start.7 = (bf16[1024,384]{1,0:T(8,128)(2,1)S(1)}, bf16[1024,384]{1,0:T(8,128)(2,1)}, u32[]{:S(2)}) copy-start(bf16[1024,384]{1,0:T(8,128)(2,1)} %param.11) | copy-start | bytes 2359300
  178.8 1.6 collective-permute-start.8
  197.4 29.1 %copy-start.12 = (bf16[2,24,8,512]{3,2,0,1:T(8,128)(2,1)S(1)}, bf16[2,24,8,512]{3,2,0,1:T(8,128)(2,1)}, u32[]{:S(2)}) copy-start(bf16[2,24,8,512]{3,2,0,1:T(8,128)(2,1)} %copy-done.11) | copy-start | bytes 1179652
  225.7 6.0 %collective-permute-start.9 = (f32[16,36,384]{2,0,1:T(8,128)}, f32[16,36,384]{2,0,1:T(8,128)}, u32[]{:S(2)}, u32[]{:S(2)}) collective-permute-start(f32[16,36,384]{2,0,1:T(8,128)} %copy.128), channel_id=1, source_target_pairs={{0,2},{2,0},{4,6},{6,4},{8,10},{10,8},{12,14},{14,12},{16,18},{18,... | collective-permute-start | bytes 2654216 | tf_op jit(solution)/shard_map/ppermute | solution.py:163
  226.5 3.7 %copy-start.17 = (bf16[384,384]{1,0:T(8,128)(2,1)S(1)}, bf16[384,384]{1,0:T(8,128)(2,1)}, u32[]{:S(2)}) copy-start(bf16[384,384]{1,0:T(8,128)(2,1)} %param.12) | copy-start | bytes 884740

commit v15 on v14

--- a/solution.py
+++ b/solution.py
@@ -20,7 +20,7 @@
     return (slot_rows, slot_live)
 
 
-def attention_forward(queries, extended, neighbours, row_offset):
+def attention_forward(queries, extended, neighbours, row_offset, riders):
     f32 = jnp.float32
     bf16 = jnp.bfloat16
     row_count = queries.shape[0]
@@ -65,14 +65,16 @@
         mixture = jnp.einsum("bhm,bmhd->bhd", weights, block_values, preferred_element_type=f32)
         return (mixture.reshape(block_rows, span).astype(bf16), probabilities, gathered)
 
-    outputs = [
-        forward_block((query_blocks[b], neighbour_blocks[b], row_offset + b * block_rows))
-        for b in range(block_count)
-    ]
+    outputs = []
+    for b in range(block_count):
+        out = forward_block((query_blocks[b], neighbour_blocks[b], row_offset + b * block_rows))
+        if b == 0:
+            out, riders = lax.optimization_barrier((out, riders))
+        outputs.append(out)
     attn_blocks = jnp.stack([out[0] for out in outputs])
     prob_blocks = [out[1] for out in outputs]
     kv_blocks = [out[2] for out in outputs]
-    return (attn_blocks.reshape(row_count, span), prob_blocks, kv_blocks)
+    return (attn_blocks.reshape(row_count, span), prob_blocks, kv_blocks, riders)
 
 
 def attention_backward(
@@ -243,7 +245,6 @@
     ]
     mix_own = jnp.take(mix_pieces, ch_index, axis=1)
     pooled = lax.dynamic_slice_in_dim(pooled_all, ch_index * half_width, half_width, axis=1)
-    upstream = ch_assemble(cotangent, cot_others, axis=1)
     projected = jnp.einsum(
         "rc,kcd->rkd", pooled_all, projections, preferred_element_type=f32
     ).astype(bf16)
@@ -258,7 +259,10 @@
     extended = jnp.concatenate(
         [key_value, incoming.reshape(peer_count * slot_count, 2, half_width)], axis=0
     )
-    attended, prob_blocks, kv_blocks = attention_forward(queries, extended, neighbours, 0)
+    attended, prob_blocks, kv_blocks, cot_others = attention_forward(
+        queries, extended, neighbours, 0, cot_others
+    )
+    upstream = ch_assemble(cotangent, cot_others, axis=1)
     attended_others = ch_exchange(attended)
     grad_attended = jnp.dot(upstream, mixing_weight.T, preferred_element_type=f32).astype(bf16)
     mixing_term = jnp.dot(attended.T, upstream, preferred_element_type=f32) * grad_scale

time: 241 us -> 248 us (1.029)
  waiting for transfers between devices: 55 us -> 47.3 us
  local copies, waits for them, and re-layouts: 34 us -> 40.6 us
  matrix products: 58.1 us -> 62.4 us
    ppermute x6, waiting for transfers between devices: 39.9 us -> 30 us  [ch_exchange(): lax.ppermute(value, 'ch', [(i, (i + shift) % size) for i in range(size)])]
    unnamed x78 -> x114, local copies, waits for them, and re-layouts: 11.2 us -> 16.9 us
    all_to_all x1, waiting for transfers between devices: 0.01 us -> 3.58 us  [per_device(): lax.all_to_all(outgoing, 'pix', split_axis=0, concat_axis=0, tiled=True)]
  transfers between devices with their start and end apart: 13 -> 13, of which waited for: 7 -> 6; matrix products, arithmetic and copies ran while one was open for 31% -> 34% of each run, Pallas kernels for 0% -> 0%
where the time goes in v15:
time: 248 us; the launch traced here: 243 us
  matrix products  62.4 us (25%)
  waiting for transfers between devices  47.3 us (19%)
  blocking collectives  45.1 us (18%)
  local copies, waits for them, and re-layouts  40.6 us (16%)
  starting transfers between devices  28.1 us (11%)
  other arithmetic  17.2 us (7%)
    ppermute x6, waiting for transfers between devices, ch_exchange(): lax.ppermute(value, 'ch', [(i, (i + shift) % size) for i in range(size)])  30 us
    all_to_all x1, blocking collectives, pix_gather(): lax.all_to_all(spread.reshape(size, total, width), 'pix', 0, 0, tiled=True)  27.2 us
    dot_general x16, matrix products, backward_block(): jnp.einsum('bx,bc->xc', pick_table(slot_rows[:, slot], ext_rows), contrib...  20 us
    all_to_all x1, blocking collectives, pix_scatter(): lax.all_to_all(mine.reshape(size, chunk, width), 'pix', 0, 0, tiled=True)  18 us
    dot_general x16, matrix products, forward_block(): jnp.dot(pick_table(slot_rows[:, slot], ext_rows), flattened, preferred_el...  17.2 us
    unnamed x114, local copies, waits for them, and re-layouts  16.9 us
    all_to_all x1, waiting for transfers between devices, pix_scatter(): lax.all_to_all(mine.reshape(size, chunk, width), 'pix', 0, 0, tiled=True)  12 us
    ppermute x6, starting transfers between devices, ch_exchange(): lax.ppermute(value, 'ch', [(i, (i + shift) % size) for i in range(size)])  8.19 us
  transfers between devices with their start and end apart: 13, of which 6 were waited for; matrix products, arithmetic and copies ran while one was open for 34% of the time, Pallas kernels for 0%

profile of v15, /device:TPU:0, one launch (start us, length us, event | category | flops | bytes accessed | tf_op | source)
XLA Modules:
  0.0 242.9 jit_solution(13452186045123247145)
XLA Ops:
  0.6 3.0 %collective-permute-start = (bf16[1024,384]{1,0:T(8,128)(2,1)}, bf16[1024,384]{1,0:T(8,128)(2,1)S(1)}, u32[]{:S(2)}, u32[]{:S(2)}) collective-permute-start(bf16[1024,384]{1,0:T(8,128)(2,1)} %param.11), channel_id=1, source_target_pairs={{0,1},{1,0},{2,3},{3,2},{4,5},{5,4},{6,7},{7,6},{8,9},{9,8},{10,11... | collective-permute-start | bytes 2359304 | tf_op jit(solution)/shard_map/ppermute | solution.py:147
  3.7 1.1 reshape.193
  5.5 1.2 broadcast_select_fusion
  8.2 1.8 fusion.137
  10.0 17.7 %collective-permute-done.1 = bf16[384,384]{1,0:T(8,128)(2,1)S(1)} collective-permute-done((bf16[384,384]{1,0:T(8,128)(2,1)}, bf16[384,384]{1,0:T(8,128)(2,1)S(1)}, u32[]{:S(2)}, u32[]{:S(2)}) %collective-permute-start.1) | collective-permute-done | bytes 294944 | tf_op jit(solution)/shard_map/ppermute | solution.py:147
  28.4 2.1 fusion.138
  32.4 1.1 reshape.194
  33.5 6.8 %all-to-all-start = ((bf16[16,32,2,192]{3,2,1,0:T(2,128)(2,1)}), bf16[16,32,2,192]{3,2,1,0:T(2,128)(2,1)}, u32[]{:S(2)}, u32[]{:S(2)}) async-start(bf16[16,32,2,192]{3,2,1,0:T(2,128)(2,1)} %reshape.194), calls=%async_computation | async-start | bytes 1048576 | tf_op jit(solution)/shard_map/all_to_all | solution.py:258
  44.4 1.5 collective-permute-start.2
  47.3 1.5 collective-permute-start.4
  48.8 1.9 fusion.120
  50.7 3.6 %all-to-all-done = bf16[16,32,2,192]{3,2,1,0:T(2,128)(2,1)} async-done(((bf16[16,32,2,192]{3,2,1,0:T(2,128)(2,1)}), bf16[16,32,2,192]{3,2,1,0:T(2,128)(2,1)}, u32[]{:S(2)}, u32[]{:S(2)}) %all-to-all-start) | async-done | bytes 393248 | tf_op jit(solution)/shard_map/all_to_all | solution.py:258
  54.3 2.1 concatenate.45
  56.4 1.9 copy.106
  58.3 2.3 fusion.108
  70.4 1.4 copy-done
  72.8 2.0 convolution_convert_fusion.1
  75.9 1.2 fusion.110
  86.3 1.2 fusion.49
  87.5 1.2 fusion.51
  91.5 1.2 fusion.40
  92.7 1.4 convolution_add_fusion.11
  94.1 1.2 convolution_add_fusion.10
  95.3 1.2 convolution_add_fusion.9
  96.5 1.2 convolution_add_fusion.8
  97.7 1.2 convolution_add_fusion.7
  98.9 1.2 convolution_add_fusion.6
  100.2 1.2 convolution_add_fusion.5
  101.8 1.6 collective-permute-start.3
  103.4 1.2 fusion.53
  105.0 8.0 %collective-permute-done.3 = bf16[1024,192]{0,1:T(8,128)(2,1)S(1)} collective-permute-done((bf16[1024,192]{0,1:T(8,128)(2,1)S(1)}, bf16[1024,192]{0,1:T(8,128)(2,1)S(1)}, u32[]{:S(2)}, u32[]{:S(2)}) %collective-permute-start.3) | collective-permute-done | bytes 393248 | tf_op jit(solution)/shard_map/ppermute | solution.py:147
  112.9 1.6 convolution_add_fusion.4
  114.5 1.2 convolution_add_fusion.3
  115.7 1.6 convolution_add_fusion.2
  117.3 1.2 convolution_add_fusion.1
  118.5 1.2 convolution_add_fusion
  119.7 1.5 copy-done.5
  121.2 1.1 reshape.196
  122.3 4.4 %all-to-all-start.1 = ((bf16[16,32,2,192]{3,2,1,0:T(2,128)(2,1)}), bf16[16,32,2,192]{3,2,1,0:T(2,128)(2,1)S(1)}, u32[]{:S(2)}, u32[]{:S(2)}) async-start(bf16[16,32,2,192]{3,2,1,0:T(2,128)(2,1)} %reshape.196), calls=%async_computation.1 | async-start | bytes 1048576 | tf_op jit(solution)/shard_map/all_to_all | solution.py:278
  127.1 1.0 slice.375
  128.1 1.8 slice.374
  131.5 2.1 copy.189
  133.6 3.2 %convolution_multiply_fusion.2 = f32[192,384]{1,0:T(8,128)} fusion(bf16[1024,192]{0,1:T(8,128)(2,1)} %bitcast.240, bf16[1024,192]{1,0:T(8,128)(2,1)} %copy.109, bf16[1024,192]{1,0:T(8,128)(2,1)} %collective-permute-done.2, pred[]{:T(512)S(6)} %eq.213), kind=kOutput, calls=%fused_computation.152 | convolution fusion | flops 154607616 | bytes 1474561 | tf_op jit(solution)/shard_map/dot_general | solution.py:268
  136.8 1.3 slice_add_fusion
  138.1 3.1 %copy.124 = f32[1024,384]{0,1:T(8,128)} copy(f32[1024,384]{1,0:T(8,128)} %slice_add_fusion) | data formatting | bytes 3145728 | tf_op jit(solution)/shard_map/add | solution.py:140
  141.7 2.1 add_convert_fusion
  147.0 1.3 copy.126
  148.5 1.1 broadcast_select_fusion.2
  150.1 1.1 pad_maximum_fusion.3
  151.2 1.5 collective-permute-start.7
  153.7 5.9 %all-to-all-start.2 = ((f32[16,24,384]{2,1,0:T(8,128)}), f32[16,24,384]{2,1,0:T(8,128)S(1)}, u32[]{:S(2)}, u32[]{:S(2)}) async-start(f32[16,24,384]{2,1,0:T(8,128)} %bitcast.104), calls=%async_computation.2 | async-start | bytes 1179648 | tf_op jit(solution)/shard_map/all_to_all | solution.py:179
  159.6 3.5 %fusion.128 = f32[1024,384,1]{1,0,2:T(8,128)} fusion(bf16[3,384,192]{1,2,0:T(8,128)(2,1)} %param.13, bf16[1024,2,192]{0,2,1:T(8,128)(2,1)} %copy-done.22, bf16[1024,1,192]{0,2,1:T(8,128)(2,1)S(1)} %reshape_reshape.4), kind=kOutput, calls=%fused_computation.230 | convolution fusion | flops 453574656 | bytes 3194880 | tf_op jit(solution)/shard_map/rkd,kcd->rc/dot_general | solution.py:296
  163.1 12.0 %all-to-all-done.2 = f32[16,24,384]{2,1,0:T(8,128)S(1)} async-done(((f32[16,24,384]{2,1,0:T(8,128)}), f32[16,24,384]{2,1,0:T(8,128)S(1)}, u32[]{:S(2)}, u32[]{:S(2)}) %all-to-all-start.2) | async-done | bytes 589856 | tf_op jit(solution)/shard_map/all_to_all | solution.py:179
  175.2 4.4 %collective-permute-done.7 = bf16[1024,3,192]{0,2,1:T(8,128)(2,1)} collective-permute-done((bf16[1024,3,192]{0,2,1:T(8,128)(2,1)}, bf16[1024,3,192]{0,2,1:T(8,128)(2,1)}, u32[]{:S(2)}, u32[]{:S(2)}) %collective-permute-start.7) | collective-permute-done | bytes 1179680 | tf_op jit(solution)/shard_map/ppermute | solution.py:147
  179.6 3.4 %fusion.60 = bf16[1024,384]{1,0:T(8,128)(2,1)S(1)} fusion(f32[1024,384,1]{1,0,2:T(8,128)} %fusion.128, bf16[1024,3,192]{0,2,1:T(8,128)(2,1)} %collective-permute-done.7, bf16[3,384,192]{1,2,0:T(8,128)(2,1)} %collective-permute-done.5, bf16[1024,192]{1,0:T(8,128)(2,1)} %collective-permute-done.2, bf16[1024,192]{1,0:T(8,128)(2,1)S(1)} %copy-done.25, pred[]{:T(512)S(6)} %eq.213), kind=kOutput, calls=%fused_computation.88 | convolution fusion | flops 458096640 | bytes 4767745 | tf_op jit(solution)/shard_map/rkd,kcd->rc/dot_general | solution.py:300
  183.7 1.6 collective-permute-done.8
  185.4 18.0 %all_to_all.25 = f32[16,12,384]{2,1,0:T(8,128)S(1)} all-to-all(f32[16,12,384]{2,1,0:T(8,128)S(1)} %reshape.200), channel_id=1, replica_groups=mesh['pix'=16,'ch'=2] {'pix'}, dimensions={0} | all-to-all | bytes 589824 | tf_op jit(solution)/shard_map/all_to_all | solution.py:179
  203.5 27.2 %all_to_all.26 = f32[16,36,384]{2,1,0:T(8,128)S(1)} all-to-all(f32[16,36,384]{2,1,0:T(8,128)S(1)} %bitcast.233), channel_id=1, replica_groups=mesh['pix'=16,'ch'=2] {'pix'}, dimensions={0} | all-to-all | bytes 1769472 | tf_op jit(solution)/shard_map/all_to_all | solution.py:190
  230.7 1.1 copy.128
  232.5 1.3 fusion.121
  233.8 1.5 fusion.97
  236.2 1.5 convolution_convert_fusion
  237.8 1.5 copy_select_fusion.1
  240.5 1.3 copy.132
  (214 shorter events, 46.4 us)
Async XLA Ops:
  0.6 27.1 %collective-permute-start = (bf16[1024,384]{1,0:T(8,128)(2,1)}, bf16[1024,384]{1,0:T(8,128)(2,1)S(1)}, u32[]{:S(2)}, u32[]{:S(2)}) collective-permute-start(bf16[1024,384]{1,0:T(8,128)(2,1)} %param.11), channel_id=1, source_target_pairs={{0,1},{1,0},{2,3},{3,2},{4,5},{5,4},{6,7},{7,6},{8,9},{9,8},{10,11... | collective-permute-start | bytes 2359304 | tf_op jit(solution)/shard_map/ppermute | solution.py:147
  3.6 24.1 %collective-permute-start.1 = (bf16[384,384]{1,0:T(8,128)(2,1)}, bf16[384,384]{1,0:T(8,128)(2,1)S(1)}, u32[]{:S(2)}, u32[]{:S(2)}) collective-permute-start(bf16[384,384]{1,0:T(8,128)(2,1)} %param.12), channel_id=1, source_target_pairs={{0,1},{1,0},{2,3},{3,2},{4,5},{5,4},{6,7},{7,6},{8,9},{9,8},{10,11... | collective-permute-start | bytes 884744 | tf_op jit(solution)/shard_map/ppermute | solution.py:147
  8.2 22.6 %copy-start.41 = (s32[512]{0:T(512)}, s32[512]{0:T(512)S(1)}, u32[]{:S(2)}) copy-start(s32[512]{0:T(512)S(1)} %eq.149) | copy-start | bytes 6148
  28.3 2.1 copy-start.7
  30.7 11.9 %copy-start.4 = (bf16[1024,3,192]{0,2,1:T(8,128)(2,1)}, bf16[1024,3,192]{0,2,1:T(8,128)(2,1)S(1)}, u32[]{:S(2)}) copy-start(bf16[1024,3,192]{0,2,1:T(8,128)(2,1)S(1)} %convert_element_type.167) | copy-start | bytes 3538948
  30.7 0.9 copy-start.20
  30.7 10.2 %copy-start.13 = (bf16[1024,192]{0,1:T(8,128)(2,1)S(1)}, bf16[1024,192]{0,1:T(8,128)(2,1)}, u32[]{:S(2)}) copy-start(bf16[1024,192]{0,1:T(8,128)(2,1)} %param.17) | copy-start | bytes 1179652
  33.5 20.8 %all-to-all-start = ((bf16[16,32,2,192]{3,2,1,0:T(2,128)(2,1)}), bf16[16,32,2,192]{3,2,1,0:T(2,128)(2,1)}, u32[]{:S(2)}, u32[]{:S(2)}) async-start(bf16[16,32,2,192]{3,2,1,0:T(2,128)(2,1)} %reshape.194), calls=%async_computation | async-start | bytes 1048576 | tf_op jit(solution)/shard_map/all_to_all | solution.py:258
  44.4 28.4 %collective-permute-start.2 = (bf16[1024,192]{1,0:T(8,128)(2,1)}, bf16[1024,192]{1,0:T(8,128)(2,1)}, u32[]{:S(2)}, u32[]{:S(2)}) collective-permute-start(bf16[1024,192]{1,0:T(8,128)(2,1)} %copy.107), channel_id=1, source_target_pairs={{0,1},{1,0},{2,3},{3,2},{4,5},{5,4},{6,7},{7,6},{8,9},{9,8},{10,11... | collective-permute-start | bytes 1179656 | tf_op jit(solution)/shard_map/ppermute | solution.py:147
  46.7 58.2 %collective-permute-start.5 = (bf16[3,384,192]{1,2,0:T(8,128)(2,1)}, bf16[3,384,192]{1,2,0:T(8,128)(2,1)}, u32[]{:S(2)}, u32[]{:S(2)}) collective-permute-start(bf16[3,384,192]{1,2,0:T(8,128)(2,1)} %param.13), channel_id=1, source_target_pairs={{0,1},{1,0},{2,3},{3,2},{4,5},{5,4},{6,7},{7,6},{8,9},{9,8},{10,11... | collective-permute-start | bytes 1327112 | tf_op jit(solution)/shard_map/ppermute | solution.py:147
  47.3 57.7 %collective-permute-start.4 = (bf16[192,192]{1,0:T(8,128)(2,1)}, bf16[192,192]{1,0:T(8,128)(2,1)}, u32[]{:S(2)}, u32[]{:S(2)}) collective-permute-start(bf16[192,192]{1,0:T(8,128)(2,1)} %bitcast.205), channel_id=1, source_target_pairs={{0,1},{1,0},{2,3},{3,2},{4,5},{5,4},{6,7},{7,6},{8,9},{9,8},{10,11... | collective-permute-start | bytes 221192 | tf_op jit(solution)/shard_map/ppermute | solution.py:243
  58.3 2.3 copy-start.21
  58.3 2.3 copy-start.26
  58.3 2.3 copy-start.46
  60.6 1.0 copy-start.40
  61.7 1.0 copy-start.39
  62.7 1.0 copy-start.38
  63.7 1.0 copy-start.37
  64.7 1.0 copy-start.36
  65.7 1.0 copy-start.35
  66.7 1.0 copy-start.34
  67.7 2.0 copy-start.9
  70.0 1.8 copy-start
  70.0 1.7 copy-start.10
  71.8 1.0 copy-start.24
  71.8 1.1 copy-start.28
  72.8 2.1 copy-start.44
  74.9 1.0 copy-start.43
  75.9 1.2 copy-start.33
  77.1 1.0 copy-start.32
  78.1 1.0 copy-start.31
  79.1 1.0 copy-start.30
  80.1 1.0 copy-start.29
  82.4 1.0 copy-start.11
  85.6 0.7 copy-start.45
  86.0 32.6 %copy-start.3 = (bf16[512,9,2,3,64]{0,4,3,2,1:T(8,128)(2,1)}, bf16[512,9,2,3,64]{0,4,3,2,1:T(8,128)(2,1)S(1)}, u32[]{:S(2)}) copy-start(bf16[512,9,2,3,64]{0,4,3,2,1:T(8,128)(2,1)S(1)} %pad_maximum_fusion.1) | copy-start | bytes 10616836
  87.5 2.0 copy-start.1
  91.5 8.6 %copy-start.2 = (bf16[512,9,2,3,64]{0,4,3,2,1:T(8,128)(2,1)}, bf16[512,9,2,3,64]{0,4,3,2,1:T(8,128)(2,1)S(1)}, u32[]{:S(2)}) copy-start(bf16[512,9,2,3,64]{0,4,3,2,1:T(8,128)(2,1)S(1)} %pad_maximum_fusion) | copy-start | bytes 10616836
  101.8 2.8 %copy-start.14 = (bf16[2,24,8,512]{3,2,0,1:T(8,128)(2,1)}, bf16[2,24,8,512]{3,2,0,1:T(8,128)(2,1)S(1)}, u32[]{:S(2)}) copy-start(bf16[2,24,8,512]{3,2,0,1:T(8,128)(2,1)S(1)} %copy.201) | copy-start | bytes 1179652
  101.8 11.1 %collective-permute-start.3 = (bf16[1024,192]{0,1:T(8,128)(2,1)S(1)}, bf16[1024,192]{0,1:T(8,128)(2,1)S(1)}, u32[]{:S(2)}, u32[]{:S(2)}) collective-permute-start(bf16[1024,192]{0,1:T(8,128)(2,1)S(1)} %bitcast.239), channel_id=1, source_target_pairs={{0,1},{1,0},{2,3},{3,2},{4,5},{5,4},{6,7},{7,6},{8,9},{9,8},{10,11... | collective-permute-start | bytes 1179656 | tf_op jit(solution)/shard_map/ppermute | solution.py:147
  112.9 1.6 copy-start.27
  119.7 1.5 copy-start.5
  122.3 18.9 %all-to-all-start.1 = ((bf16[16,32,2,192]{3,2,1,0:T(2,128)(2,1)}), bf16[16,32,2,192]{3,2,1,0:T(2,128)(2,1)S(1)}, u32[]{:S(2)}, u32[]{:S(2)}) async-start(bf16[16,32,2,192]{3,2,1,0:T(2,128)(2,1)} %reshape.196), calls=%async_computation.1 | async-start | bytes 1048576 | tf_op jit(solution)/shard_map/all_to_all | solution.py:278
  131.5 5.2 %copy-start.6 = (f32[1536,384]{1,0:T(8,128)S(1)}, f32[1536,384]{1,0:T(8,128)}, u32[]{:S(2)}) copy-start(f32[1536,384]{1,0:T(8,128)} %copy-done.5) | copy-start | bytes 7077892
  133.6 3.2 %copy-start.16 = (bf16[512,1,384]{2,0,1:T(8,128)(2,1)S(1)}, bf16[512,1,384]{2,0,1:T(8,128)(2,1)}, u32[]{:S(2)}) copy-start(bf16[512,1,384]{2,0,1:T(8,128)(2,1)} %copy.190) | copy-start | bytes 1179652
  133.6 3.2 %copy-start.17 = (bf16[512,1,384]{2,0,1:T(8,128)(2,1)S(1)}, bf16[512,1,384]{2,0,1:T(8,128)(2,1)}, u32[]{:S(2)}) copy-start(bf16[512,1,384]{2,0,1:T(8,128)(2,1)} %copy.189) | copy-start | bytes 1179652
  138.1 3.6 %copy-start.42 = (s32[512]{0:T(512)S(1)}, s32[512]{0:T(512)}, u32[]{:S(2)}) copy-start(s32[512]{0:T(512)} %copy-done.41) | copy-start | bytes 6148
  141.2 3.5 %copy-start.8 = (bf16[1024,384]{1,0:T(8,128)(2,1)S(1)}, bf16[1024,384]{1,0:T(8,128)(2,1)}, u32[]{:S(2)}) copy-start(bf16[1024,384]{1,0:T(8,128)(2,1)} %copy-done.7) | copy-start | bytes 2359300
  143.8 0.9 copy-start.22
  148.5 1.6 copy-start.23
  148.5 4.2 %copy-start.18 = (f32[192,384]{1,0:T(8,128)S(1)}, f32[192,384]{1,0:T(8,128)}, u32[]{:S(2)}) copy-start(f32[192,384]{1,0:T(8,128)} %convolution_multiply_fusion.2) | copy-start | bytes 884740
  149.6 3.1 %collective-permute-start.6 = (f32[384,384]{1,0:T(8,128)S(1)}, f32[384,384]{1,0:T(8,128)S(1)}, u32[]{:S(2)}, u32[]{:S(2)}) collective-permute-start(f32[384,384]{1,0:T(8,128)S(1)} %broadcast_select_fusion.2), channel_id=1, source_target_pairs={{0,2},{2,0},{4,6},{6,4},{8,10},{10,8},{12,14},{14,12},{16,18},{18,... | collective-permute-start | bytes 1769480 | tf_op jit(solution)/shard_map/ppermute | solution.py:165
  151.2 28.3 %collective-permute-start.7 = (bf16[1024,3,192]{0,2,1:T(8,128)(2,1)}, bf16[1024,3,192]{0,2,1:T(8,128)(2,1)}, u32[]{:S(2)}, u32[]{:S(2)}) collective-permute-start(bf16[1024,3,192]{0,2,1:T(8,128)(2,1)} %pad_maximum_fusion.3), channel_id=1, source_target_pairs={{0,1},{1,0},{2,3},{3,2},{4,5},{5,4},{6,7},{7,6},{8,9},{9,8},{10,11... | collective-permute-start | bytes 3538952 | tf_op jit(solution)/shard_map/ppermute | solution.py:147
  153.7 21.5 %all-to-all-start.2 = ((f32[16,24,384]{2,1,0:T(8,128)}), f32[16,24,384]{2,1,0:T(8,128)S(1)}, u32[]{:S(2)}, u32[]{:S(2)}) async-start(f32[16,24,384]{2,1,0:T(8,128)} %bitcast.104), calls=%async_computation.2 | async-start | bytes 1179648 | tf_op jit(solution)/shard_map/all_to_all | solution.py:179
  159.6 19.9 %copy-start.25 = (bf16[1024,192]{1,0:T(8,128)(2,1)S(1)}, bf16[1024,192]{1,0:T(8,128)(2,1)}, u32[]{:S(2)}) copy-start(bf16[1024,192]{1,0:T(8,128)(2,1)} %copy.109) | copy-start | bytes 1179652
  175.2 7.8 %copy-start.12 = (bf16[1024,384]{1,0:T(8,128)(2,1)S(1)}, bf16[1024,384]{1,0:T(8,128)(2,1)}, u32[]{:S(2)}) copy-start(bf16[1024,384]{1,0:T(8,128)(2,1)} %param.11) | copy-start | bytes 2359300
  183.7 1.6 collective-permute-start.8
  203.4 29.1 %copy-start.15 = (bf16[2,24,8,512]{3,2,0,1:T(8,128)(2,1)S(1)}, bf16[2,24,8,512]{3,2,0,1:T(8,128)(2,1)}, u32[]{:S(2)}) copy-start(bf16[2,24,8,512]{3,2,0,1:T(8,128)(2,1)} %copy-done.14) | copy-start | bytes 1179652
  231.7 6.0 %collective-permute-start.9 = (f32[16,36,384]{2,0,1:T(8,128)}, f32[16,36,384]{2,0,1:T(8,128)}, u32[]{:S(2)}, u32[]{:S(2)}) collective-permute-start(f32[16,36,384]{2,0,1:T(8,128)} %copy.128), channel_id=1, source_target_pairs={{0,2},{2,0},{4,6},{6,4},{8,10},{10,8},{12,14},{14,12},{16,18},{18,... | collective-permute-start | bytes 2654216 | tf_op jit(solution)/shard_map/ppermute | solution.py:165
  232.5 3.7 %copy-start.19 = (bf16[384,384]{1,0:T(8,128)(2,1)S(1)}, bf16[384,384]{1,0:T(8,128)(2,1)}, u32[]{:S(2)}) copy-start(bf16[384,384]{1,0:T(8,128)(2,1)} %param.12) | copy-start | bytes 884740

commit v16 on v14

--- a/solution.py
+++ b/solution.py
@@ -131,7 +131,7 @@
              prob_blocks[b], kv_blocks[b]),
         )
         query_grads.append(grad_query)
-        if b == 0:
+        if b == block_count - 1:
             carried, riders = lax.optimization_barrier((carried, riders))
     own_grads = jnp.concatenate([pair[1] for pair in query_grads], axis=0)
     query_grads = jnp.stack([pair[0] for pair in query_grads])

time: 241 us -> 242 us (level)
  waiting for transfers between devices: 55 us -> 50.6 us
  other arithmetic: 15.8 us -> 18.3 us
    ppermute x6, waiting for transfers between devices: 39.9 us -> 36.7 us  [ch_exchange(): lax.ppermute(value, 'ch', [(i, (i + shift) % size) for i in range(size)])]
    unnamed x78 -> x116, local copies, waits for them, and re-layouts: 11.2 us -> 12.5 us
  transfers between devices with their start and end apart: 13 -> 13, of which waited for: 7 -> 7; matrix products, arithmetic and copies ran while one was open for 31% -> 35% of each run, Pallas kernels for 0% -> 0%
where the time goes in v16:
time: 242 us; the launch traced here: 238 us
  matrix products  58.8 us (24%)
  waiting for transfers between devices  50.6 us (21%)
  blocking collectives  44.8 us (19%)
  local copies, waits for them, and re-layouts  34.2 us (14%)
  starting transfers between devices  28.8 us (12%)
  other arithmetic  18.3 us (8%)
    ppermute x6, waiting for transfers between devices, ch_exchange(): lax.ppermute(value, 'ch', [(i, (i + shift) % size) for i in range(size)])  36.7 us
    all_to_all x1, blocking collectives, pix_gather(): lax.all_to_all(spread.reshape(size, total, width), 'pix', 0, 0, tiled=True)  27.2 us
    dot_general x16, matrix products, backward_block(): jnp.einsum('bx,bc->xc', pick_table(slot_rows[:, slot], ext_rows), contrib...  19.7 us
    all_to_all x1, blocking collectives, pix_scatter(): lax.all_to_all(mine.reshape(size, chunk, width), 'pix', 0, 0, tiled=True)  17.6 us
    dot_general x16, matrix products, forward_block(): jnp.dot(pick_table(slot_rows[:, slot], ext_rows), flattened, preferred_el...  17.2 us
    unnamed x116, local copies, waits for them, and re-layouts  12.5 us
    all_to_all x1, waiting for transfers between devices, pix_scatter(): lax.all_to_all(mine.reshape(size, chunk, width), 'pix', 0, 0, tiled=True)  12 us
    ppermute x6, starting transfers between devices, ch_exchange(): lax.ppermute(value, 'ch', [(i, (i + shift) % size) for i in range(size)])  8.18 us
  transfers between devices with their start and end apart: 13, of which 7 were waited for; matrix products, arithmetic and copies ran while one was open for 35% of the time, Pallas kernels for 0%

profile of v16, /device:TPU:0, one launch (start us, length us, event | category | flops | bytes accessed | tf_op | source)
XLA Modules:
  0.0 237.8 jit_solution(17777227186441427318)
XLA Ops:
  0.7 3.0 %collective-permute-start = (bf16[1024,384]{1,0:T(8,128)(2,1)}, bf16[1024,384]{1,0:T(8,128)(2,1)S(1)}, u32[]{:S(2)}, u32[]{:S(2)}) collective-permute-start(bf16[1024,384]{1,0:T(8,128)(2,1)} %param.11), channel_id=1, source_target_pairs={{0,1},{1,0},{2,3},{3,2},{4,5},{5,4},{6,7},{7,6},{8,9},{9,8},{10,11... | collective-permute-start | bytes 2359304 | tf_op jit(solution)/shard_map/ppermute | solution.py:145
  3.7 1.1 reshape.203
  6.8 1.2 broadcast_select_fusion
  9.4 1.2 copy.77
  12.6 15.3 %collective-permute-done.1 = bf16[384,384]{1,0:T(8,128)(2,1)} collective-permute-done((bf16[384,384]{1,0:T(8,128)(2,1)}, bf16[384,384]{1,0:T(8,128)(2,1)}, u32[]{:S(2)}, u32[]{:S(2)}) %collective-permute-start.1) | collective-permute-done | bytes 294944 | tf_op jit(solution)/shard_map/ppermute | solution.py:145
  27.8 1.6 add_convert_fusion.1
  32.1 1.1 reshape.204
  33.2 6.7 %all-to-all-start = ((bf16[16,32,2,192]{3,2,1,0:T(2,128)(2,1)}), bf16[16,32,2,192]{3,2,1,0:T(2,128)(2,1)S(1)}, u32[]{:S(2)}, u32[]{:S(2)}) async-start(bf16[16,32,2,192]{3,2,1,0:T(2,128)(2,1)} %reshape.204), calls=%async_computation | async-start | bytes 1048576 | tf_op jit(solution)/shard_map/all_to_all | solution.py:257
  40.0 1.0 copy.76
  41.0 1.5 collective-permute-start.2
  43.9 1.5 collective-permute-start.4
  46.4 9.6 %collective-permute-done.2 = bf16[1024,192]{1,0:T(8,128)(2,1)S(1)} collective-permute-done((bf16[1024,192]{1,0:T(8,128)(2,1)}, bf16[1024,192]{1,0:T(8,128)(2,1)S(1)}, u32[]{:S(2)}, u32[]{:S(2)}) %collective-permute-start.2) | collective-permute-done | bytes 393248 | tf_op jit(solution)/shard_map/ppermute | solution.py:145
  58.1 2.2 fusion.105
  62.3 1.0 fusion.99
  67.4 1.0 fusion.104
  68.4 1.3 copy-done.4
  73.0 1.2 fusion.108
  83.8 1.2 fusion.40
  85.0 1.2 convolution_add_fusion.14
  86.2 1.2 convolution_add_fusion.13
  87.4 1.2 convolution_add_fusion.12
  88.6 1.4 convolution_add_fusion.11
  90.0 1.2 convolution_add_fusion.10
  91.2 1.2 convolution_add_fusion.9
  92.4 1.2 convolution_add_fusion.8
  94.0 1.2 convolution_add_fusion.7
  95.2 1.2 convolution_add_fusion.6
  96.4 1.2 convolution_add_fusion.5
  97.6 1.2 convolution_add_fusion.4
  98.8 1.2 convolution_add_fusion.3
  100.0 1.2 convolution_add_fusion.2
  101.2 1.6 convolution_add_fusion.1
  103.6 1.6 collective-permute-start.3
  105.2 1.2 convolution_add_fusion
  106.8 7.1 %collective-permute-done.3 = bf16[1024,192]{0,1:T(8,128)(2,1)} collective-permute-done((bf16[1024,192]{0,1:T(8,128)(2,1)S(1)}, bf16[1024,192]{0,1:T(8,128)(2,1)}, u32[]{:S(2)}, u32[]{:S(2)}) %collective-permute-start.3) | collective-permute-done | bytes 393248 | tf_op jit(solution)/shard_map/ppermute | solution.py:145
  113.9 1.1 reshape.206
  115.0 5.5 %all-to-all-start.1 = ((bf16[16,32,2,192]{3,2,1,0:T(2,128)(2,1)}), bf16[16,32,2,192]{3,2,1,0:T(2,128)(2,1)}, u32[]{:S(2)}, u32[]{:S(2)}) async-start(bf16[16,32,2,192]{3,2,1,0:T(2,128)(2,1)} %reshape.206), calls=%async_computation.1 | async-start | bytes 1048576 | tf_op jit(solution)/shard_map/all_to_all | solution.py:274
  120.5 1.2 multiply_reduce_fusion
  121.8 1.0 slice.368
  122.8 1.8 slice.367
  126.2 2.1 copy.141
  128.3 3.2 %convolution_multiply_fusion.2 = f32[192,384]{1,0:T(8,128)} fusion(bf16[1024,192]{0,1:T(8,128)(2,1)} %bitcast.237, bf16[1024,192]{1,0:T(8,128)(2,1)} %copy-done.23, bf16[1024,192]{1,0:T(8,128)(2,1)} %copy-done.47, pred[]{:T(512)S(6)} %eq.213), kind=kOutput, calls=%fused_computation.152 | convolution fusion | flops 154607616 | bytes 1474561 | tf_op jit(solution)/shard_map/dot_general | solution.py:264
  131.5 1.4 convert_add_fusion
  132.8 1.9 copy.84
  135.1 1.4 convert_element_type.203
  137.4 1.7 add_convert_fusion
  142.3 1.3 copy.86
  143.8 1.1 broadcast_select_fusion.2
  145.0 1.1 pad_maximum_fusion.3
  146.2 1.5 collective-permute-start.7
  148.6 5.9 %all-to-all-start.2 = ((f32[16,24,384]{2,1,0:T(8,128)}), f32[16,24,384]{2,1,0:T(8,128)S(1)}, u32[]{:S(2)}, u32[]{:S(2)}) async-start(f32[16,24,384]{2,1,0:T(8,128)} %bitcast.101), calls=%async_computation.2 | async-start | bytes 1179648 | tf_op jit(solution)/shard_map/all_to_all | solution.py:177
  154.5 3.5 %fusion.125 = f32[1024,384,1]{1,0,2:T(8,128)} fusion(bf16[3,384,192]{1,2,0:T(8,128)(2,1)} %param.13, bf16[1024,2,192]{0,2,1:T(8,128)(2,1)} %copy-done.20, bf16[1024,1,192]{0,2,1:T(8,128)(2,1)S(1)} %reshape_reshape.4), kind=kOutput, calls=%fused_computation.229 | convolution fusion | flops 453574656 | bytes 3194880 | tf_op jit(solution)/shard_map/rkd,kcd->rc/dot_general | solution.py:292
  158.0 12.0 %all-to-all-done.2 = f32[16,24,384]{2,1,0:T(8,128)S(1)} async-done(((f32[16,24,384]{2,1,0:T(8,128)}), f32[16,24,384]{2,1,0:T(8,128)S(1)}, u32[]{:S(2)}, u32[]{:S(2)}) %all-to-all-start.2) | async-done | bytes 589856 | tf_op jit(solution)/shard_map/all_to_all | solution.py:177
  170.1 4.7 %collective-permute-done.7 = bf16[1024,3,192]{0,2,1:T(8,128)(2,1)} collective-permute-done((bf16[1024,3,192]{0,2,1:T(8,128)(2,1)}, bf16[1024,3,192]{0,2,1:T(8,128)(2,1)}, u32[]{:S(2)}, u32[]{:S(2)}) %collective-permute-start.7) | collective-permute-done | bytes 1179680 | tf_op jit(solution)/shard_map/ppermute | solution.py:145
  174.8 3.4 %fusion.57 = bf16[1024,384]{1,0:T(8,128)(2,1)S(1)} fusion(f32[1024,384,1]{1,0,2:T(8,128)} %fusion.125, bf16[1024,3,192]{0,2,1:T(8,128)(2,1)} %collective-permute-done.7, bf16[3,384,192]{1,2,0:T(8,128)(2,1)} %collective-permute-done.5, bf16[1024,192]{1,0:T(8,128)(2,1)} %copy-done.47, bf16[1024,192]{1,0:T(8,128)(2,1)S(1)} %copy-done.24, pred[]{:T(512)S(6)} %eq.213), kind=kOutput, calls=%fused_computation.87 | convolution fusion | flops 458096640 | bytes 4767745 | tf_op jit(solution)/shard_map/rkd,kcd->rc/dot_general | solution.py:296
  179.0 1.6 collective-permute-done.8
  180.7 17.6 %all_to_all.25 = f32[16,12,384]{2,1,0:T(8,128)S(1)} all-to-all(f32[16,12,384]{2,1,0:T(8,128)S(1)} %reshape.210), channel_id=1, replica_groups=mesh['pix'=16,'ch'=2] {'pix'}, dimensions={0} | all-to-all | bytes 589824 | tf_op jit(solution)/shard_map/all_to_all | solution.py:177
  198.4 27.2 %all_to_all.26 = f32[16,36,384]{2,1,0:T(8,128)S(1)} all-to-all(f32[16,36,384]{2,1,0:T(8,128)S(1)} %bitcast.230), channel_id=1, replica_groups=mesh['pix'=16,'ch'=2] {'pix'}, dimensions={0} | all-to-all | bytes 1769472 | tf_op jit(solution)/shard_map/all_to_all | solution.py:188
  225.6 1.1 copy.88
  227.4 1.3 fusion.118
  228.7 1.5 fusion.94
  231.2 1.5 convolution_convert_fusion
  232.7 1.5 copy_select_fusion.1
  235.4 1.3 copy.92
  (214 shorter events, 44.6 us)
Async XLA Ops:
  0.6 11.3 %copy-start.8 = (bf16[1024,384]{1,0:T(8,128)(2,1)S(1)}, bf16[1024,384]{1,0:T(8,128)(2,1)}, u32[]{:S(2)}) copy-start(bf16[1024,384]{1,0:T(8,128)(2,1)} %param.11) | copy-start | bytes 2359300
  0.6 11.3 %copy-start.16 = (bf16[384,384]{1,0:T(8,128)(2,1)S(1)}, bf16[384,384]{1,0:T(8,128)(2,1)}, u32[]{:S(2)}) copy-start(bf16[384,384]{1,0:T(8,128)(2,1)} %param.12) | copy-start | bytes 884740
  0.7 27.2 %collective-permute-start = (bf16[1024,384]{1,0:T(8,128)(2,1)}, bf16[1024,384]{1,0:T(8,128)(2,1)S(1)}, u32[]{:S(2)}, u32[]{:S(2)}) collective-permute-start(bf16[1024,384]{1,0:T(8,128)(2,1)} %param.11), channel_id=1, source_target_pairs={{0,1},{1,0},{2,3},{3,2},{4,5},{5,4},{6,7},{7,6},{8,9},{9,8},{10,11... | collective-permute-start | bytes 2359304 | tf_op jit(solution)/shard_map/ppermute | solution.py:145
  3.7 24.2 %collective-permute-start.1 = (bf16[384,384]{1,0:T(8,128)(2,1)}, bf16[384,384]{1,0:T(8,128)(2,1)}, u32[]{:S(2)}, u32[]{:S(2)}) collective-permute-start(bf16[384,384]{1,0:T(8,128)(2,1)} %param.12), channel_id=1, source_target_pairs={{0,1},{1,0},{2,3},{3,2},{4,5},{5,4},{6,7},{7,6},{8,9},{9,8},{10,11... | collective-permute-start | bytes 884744 | tf_op jit(solution)/shard_map/ppermute | solution.py:145
  9.4 21.1 %copy-start.44 = (s32[512]{0:T(512)}, s32[512]{0:T(512)S(1)}, u32[]{:S(2)}) copy-start(s32[512]{0:T(512)S(1)} %eq.149) | copy-start | bytes 6148
  10.6 45.3 %copy-start.23 = (bf16[1024,192]{1,0:T(8,128)(2,1)}, bf16[1024,192]{1,0:T(8,128)(2,1)S(1)}, u32[]{:S(2)}) copy-start(bf16[1024,192]{1,0:T(8,128)(2,1)S(1)} %copy.77) | copy-start | bytes 1179652
  12.6 16.9 %copy-start.25 = (bf16[3,384,192]{1,2,0:T(8,128)(2,1)S(1)}, bf16[3,384,192]{1,2,0:T(8,128)(2,1)}, u32[]{:S(2)}) copy-start(bf16[3,384,192]{1,2,0:T(8,128)(2,1)} %param.13) | copy-start | bytes 1327108
  30.5 0.9 copy-start.18
  30.5 9.4 %copy-start.10 = (bf16[1024,192]{0,1:T(8,128)(2,1)S(1)}, bf16[1024,192]{0,1:T(8,128)(2,1)}, u32[]{:S(2)}) copy-start(bf16[1024,192]{0,1:T(8,128)(2,1)} %param.17) | copy-start | bytes 1179652
  33.2 24.4 %all-to-all-start = ((bf16[16,32,2,192]{3,2,1,0:T(2,128)(2,1)}), bf16[16,32,2,192]{3,2,1,0:T(2,128)(2,1)S(1)}, u32[]{:S(2)}, u32[]{:S(2)}) async-start(bf16[16,32,2,192]{3,2,1,0:T(2,128)(2,1)} %reshape.204), calls=%async_computation | async-start | bytes 1048576 | tf_op jit(solution)/shard_map/all_to_all | solution.py:257
  39.9 16.0 %copy-start.26 = (bf16[192,384]{1,0:T(8,128)(2,1)S(1)}, bf16[192,384]{1,0:T(8,128)(2,1)}, u32[]{:S(2)}) copy-start(bf16[192,384]{1,0:T(8,128)(2,1)} %param.14) | copy-start | bytes 442372
  41.0 15.0 %collective-permute-start.2 = (bf16[1024,192]{1,0:T(8,128)(2,1)}, bf16[1024,192]{1,0:T(8,128)(2,1)S(1)}, u32[]{:S(2)}, u32[]{:S(2)}) collective-permute-start(bf16[1024,192]{1,0:T(8,128)(2,1)} %copy.76), channel_id=1, source_target_pairs={{0,1},{1,0},{2,3},{3,2},{4,5},{5,4},{6,7},{7,6},{8,9},{9,8},{10,11... | collective-permute-start | bytes 1179656 | tf_op jit(solution)/shard_map/ppermute | solution.py:145
  43.4 63.4 %collective-permute-start.5 = (bf16[3,384,192]{1,2,0:T(8,128)(2,1)}, bf16[3,384,192]{1,2,0:T(8,128)(2,1)}, u32[]{:S(2)}, u32[]{:S(2)}) collective-permute-start(bf16[3,384,192]{1,2,0:T(8,128)(2,1)} %param.13), channel_id=1, source_target_pairs={{0,1},{1,0},{2,3},{3,2},{4,5},{5,4},{6,7},{7,6},{8,9},{9,8},{10,11... | collective-permute-start | bytes 1327112 | tf_op jit(solution)/shard_map/ppermute | solution.py:145
  43.9 62.9 %collective-permute-start.4 = (bf16[192,192]{1,0:T(8,128)(2,1)}, bf16[192,192]{1,0:T(8,128)(2,1)}, u32[]{:S(2)}, u32[]{:S(2)}) collective-permute-start(bf16[192,192]{1,0:T(8,128)(2,1)} %bitcast.285), channel_id=1, source_target_pairs={{0,1},{1,0},{2,3},{3,2},{4,5},{5,4},{6,7},{7,6},{8,9},{9,8},{10,11... | collective-permute-start | bytes 221192 | tf_op jit(solution)/shard_map/ppermute | solution.py:241
  55.9 0.8 copy-start.47
  56.7 1.4 copy-start.36
  58.1 2.2 copy-start.19
  58.1 2.2 copy-start.46
  60.3 1.0 copy-start.43
  61.3 1.0 copy-start.42
  62.3 1.0 copy-start.41
  63.3 1.0 copy-start.40
  64.3 1.0 copy-start.39
  65.3 1.0 copy-start.38
  66.4 1.0 copy-start.37
  66.4 2.0 copy-start.5
  67.4 2.3 copy-start.4
  70.0 0.8 copy-start.27
  70.3 0.7 copy-start.35
  71.0 1.0 copy-start.34
  72.0 1.0 copy-start.33
  73.0 1.2 copy-start.32
  74.2 1.0 copy-start.31
  75.2 1.0 copy-start.30
  76.2 1.0 copy-start.29
  78.5 1.0 copy-start.6
  78.5 1.4 copy-start.28
  78.8 1.3 copy-start.7
  80.7 0.6 copy-start.22
  83.8 8.6 %copy-start.1 = (bf16[512,9,2,3,64]{0,4,3,2,1:T(8,128)(2,1)}, bf16[512,9,2,3,64]{0,4,3,2,1:T(8,128)(2,1)S(1)}, u32[]{:S(2)}) copy-start(bf16[512,9,2,3,64]{0,4,3,2,1:T(8,128)(2,1)S(1)} %pad_maximum_fusion) | copy-start | bytes 10616836
  94.0 11.2 %copy-start = (bf16[512,9,2,3,64]{0,4,3,2,1:T(8,128)(2,1)}, bf16[512,9,2,3,64]{0,4,3,2,1:T(8,128)(2,1)S(1)}, u32[]{:S(2)}) copy-start(bf16[512,9,2,3,64]{0,4,3,2,1:T(8,128)(2,1)S(1)} %pad_maximum_fusion.1) | copy-start | bytes 10616836
  103.6 2.8 %copy-start.11 = (bf16[2,24,8,512]{3,2,0,1:T(8,128)(2,1)}, bf16[2,24,8,512]{3,2,0,1:T(8,128)(2,1)S(1)}, u32[]{:S(2)}) copy-start(bf16[2,24,8,512]{3,2,0,1:T(8,128)(2,1)S(1)} %copy.153) | copy-start | bytes 1179652
  103.6 10.2 %collective-permute-start.3 = (bf16[1024,192]{0,1:T(8,128)(2,1)S(1)}, bf16[1024,192]{0,1:T(8,128)(2,1)}, u32[]{:S(2)}, u32[]{:S(2)}) collective-permute-start(bf16[1024,192]{0,1:T(8,128)(2,1)S(1)} %bitcast.236), channel_id=1, source_target_pairs={{0,1},{1,0},{2,3},{3,2},{4,5},{5,4},{6,7},{7,6},{8,9},{9,8},{10,11... | collective-permute-start | bytes 1179656 | tf_op jit(solution)/shard_map/ppermute | solution.py:145
  106.4 7.5 %copy-start.2 = (f32[1536,384]{1,0:T(8,128)}, f32[1536,384]{1,0:T(8,128)S(1)}, u32[]{:S(2)}) copy-start(f32[1536,384]{1,0:T(8,128)S(1)} %convolution_add_fusion) | copy-start | bytes 7077892
  115.0 20.1 %all-to-all-start.1 = ((bf16[16,32,2,192]{3,2,1,0:T(2,128)(2,1)}), bf16[16,32,2,192]{3,2,1,0:T(2,128)(2,1)}, u32[]{:S(2)}, u32[]{:S(2)}) async-start(bf16[16,32,2,192]{3,2,1,0:T(2,128)(2,1)} %reshape.206), calls=%async_computation.1 | async-start | bytes 1048576 | tf_op jit(solution)/shard_map/all_to_all | solution.py:274
  126.2 5.2 %copy-start.3 = (f32[1536,384]{1,0:T(8,128)S(1)}, f32[1536,384]{1,0:T(8,128)}, u32[]{:S(2)}) copy-start(f32[1536,384]{1,0:T(8,128)} %copy-done.2) | copy-start | bytes 7077892
  128.3 3.2 %copy-start.13 = (bf16[512,1,384]{2,0,1:T(8,128)(2,1)S(1)}, bf16[512,1,384]{2,0,1:T(8,128)(2,1)}, u32[]{:S(2)}) copy-start(bf16[512,1,384]{2,0,1:T(8,128)(2,1)} %copy.142) | copy-start | bytes 1179652
  128.3 3.2 %copy-start.14 = (bf16[512,1,384]{2,0,1:T(8,128)(2,1)S(1)}, bf16[512,1,384]{2,0,1:T(8,128)(2,1)}, u32[]{:S(2)}) copy-start(bf16[512,1,384]{2,0,1:T(8,128)(2,1)} %copy.141) | copy-start | bytes 1179652
  132.8 4.5 %copy-start.45 = (s32[512]{0:T(512)S(1)}, s32[512]{0:T(512)}, u32[]{:S(2)}) copy-start(s32[512]{0:T(512)} %copy-done.44) | copy-start | bytes 6148
  139.1 0.9 copy-start.20
  143.8 1.2 copy-start.21
  143.8 3.9 %copy-start.15 = (f32[192,384]{1,0:T(8,128)S(1)}, f32[192,384]{1,0:T(8,128)}, u32[]{:S(2)}) copy-start(f32[192,384]{1,0:T(8,128)} %convolution_multiply_fusion.2) | copy-start | bytes 884740
  144.9 2.7 %collective-permute-start.6 = (f32[384,384]{1,0:T(8,128)S(1)}, f32[384,384]{1,0:T(8,128)S(1)}, u32[]{:S(2)}, u32[]{:S(2)}) collective-permute-start(f32[384,384]{1,0:T(8,128)S(1)} %broadcast_select_fusion.2), channel_id=1, source_target_pairs={{0,2},{2,0},{4,6},{6,4},{8,10},{10,8},{12,14},{14,12},{16,18},{18,... | collective-permute-start | bytes 1769480 | tf_op jit(solution)/shard_map/ppermute | solution.py:163
  146.2 28.7 %collective-permute-start.7 = (bf16[1024,3,192]{0,2,1:T(8,128)(2,1)}, bf16[1024,3,192]{0,2,1:T(8,128)(2,1)}, u32[]{:S(2)}, u32[]{:S(2)}) collective-permute-start(bf16[1024,3,192]{0,2,1:T(8,128)(2,1)} %pad_maximum_fusion.3), channel_id=1, source_target_pairs={{0,1},{1,0},{2,3},{3,2},{4,5},{5,4},{6,7},{7,6},{8,9},{9,8},{10,11... | collective-permute-start | bytes 3538952 | tf_op jit(solution)/shard_map/ppermute | solution.py:145
  148.6 21.5 %all-to-all-start.2 = ((f32[16,24,384]{2,1,0:T(8,128)}), f32[16,24,384]{2,1,0:T(8,128)S(1)}, u32[]{:S(2)}, u32[]{:S(2)}) async-start(f32[16,24,384]{2,1,0:T(8,128)} %bitcast.101), calls=%async_computation.2 | async-start | bytes 1179648 | tf_op jit(solution)/shard_map/all_to_all | solution.py:177
  154.5 20.3 %copy-start.24 = (bf16[1024,192]{1,0:T(8,128)(2,1)S(1)}, bf16[1024,192]{1,0:T(8,128)(2,1)}, u32[]{:S(2)}) copy-start(bf16[1024,192]{1,0:T(8,128)(2,1)} %copy-done.23) | copy-start | bytes 1179652
  170.1 8.2 %copy-start.9 = (bf16[1024,384]{1,0:T(8,128)(2,1)S(1)}, bf16[1024,384]{1,0:T(8,128)(2,1)}, u32[]{:S(2)}) copy-start(bf16[1024,384]{1,0:T(8,128)(2,1)} %param.11) | copy-start | bytes 2359300
  178.9 1.6 collective-permute-start.8
  198.3 29.1 %copy-start.12 = (bf16[2,24,8,512]{3,2,0,1:T(8,128)(2,1)S(1)}, bf16[2,24,8,512]{3,2,0,1:T(8,128)(2,1)}, u32[]{:S(2)}) copy-start(bf16[2,24,8,512]{3,2,0,1:T(8,128)(2,1)} %copy-done.11) | copy-start | bytes 1179652
  226.7 6.0 %collective-permute-start.9 = (f32[16,36,384]{2,0,1:T(8,128)}, f32[16,36,384]{2,0,1:T(8,128)}, u32[]{:S(2)}, u32[]{:S(2)}) collective-permute-start(f32[16,36,384]{2,0,1:T(8,128)} %copy.88), channel_id=1, source_target_pairs={{0,2},{2,0},{4,6},{6,4},{8,10},{10,8},{12,14},{14,12},{16,18},{18,... | collective-permute-start | bytes 2654216 | tf_op jit(solution)/shard_map/ppermute | solution.py:163
  227.4 3.7 %copy-start.17 = (bf16[384,384]{1,0:T(8,128)(2,1)S(1)}, bf16[384,384]{1,0:T(8,128)(2,1)}, u32[]{:S(2)}) copy-start(bf16[384,384]{1,0:T(8,128)(2,1)} %param.12) | copy-start | bytes 884740

commit v17 on v14

--- a/solution.py
+++ b/solution.py
@@ -222,11 +222,18 @@
     slot_count = send_list.shape[1]
     grad_scale = 1.0 / math.sqrt(row_count * peer_count)
     send_pick = pick_table(send_list.reshape(-1), row_count)
-    fine_others = ch_exchange(fine_pixels)
+    half_rows = row_count // 2
+    fine_tops = ch_exchange(fine_pixels[:half_rows])
+    fine_bottoms = ch_exchange(fine_pixels[half_rows:])
     kernel_others = ch_exchange(pool_kernel)
-    pooled_sum = jnp.dot(fine_pixels, pool_kernel, preferred_element_type=f32)
-    for fine_other, kernel_other in zip(fine_others, kernel_others):
-        pooled_sum = pooled_sum + jnp.dot(fine_other, kernel_other, preferred_element_type=f32)
+    pooled_top = jnp.dot(fine_pixels[:half_rows], pool_kernel, preferred_element_type=f32)
+    pooled_bottom = jnp.dot(fine_pixels[half_rows:], pool_kernel, preferred_element_type=f32)
+    for fine_top, fine_bottom, kernel_other in zip(fine_tops, fine_bottoms, kernel_others):
+        pooled_top = pooled_top + jnp.dot(fine_top, kernel_other, preferred_element_type=f32)
+        pooled_bottom = pooled_bottom + jnp.dot(
+            fine_bottom, kernel_other, preferred_element_type=f32
+        )
+    pooled_sum = jnp.concatenate([pooled_top, pooled_bottom], axis=0)
     pooled_all = pooled_sum.astype(bf16)
     mix_pieces = mixing_weight.reshape(mixing_weight.shape[0], ch_size, half_width)
     mix_sends = [

time: 241 us -> 249 us (1.033)
  matrix products: 58.1 us -> 62.8 us
  local copies, waits for them, and re-layouts: 34 us -> 38.1 us
  waiting for transfers between devices: 55 us -> 52.2 us
    dot_general x2 -> x4, matrix products: 1.25 us -> 4.63 us  [the longest x1 1.47 us: per_device(): jnp.dot(fine_pixels[half_rows:], pool_kernel, preferred_element_type=f32)]
    ppermute x6 -> x7, waiting for transfers between devices: 39.9 us -> 37.3 us  [ch_exchange(): lax.ppermute(value, 'ch', [(i, (i + shift) % size) for i in range(size)])]
    ppermute x6 -> x7, starting transfers between devices: 9.07 us -> 11 us  [ch_exchange(): lax.ppermute(value, 'ch', [(i, (i + shift) % size) for i in range(size)])]
    unnamed x78 -> x94, local copies, waits for them, and re-layouts: 11.2 us -> 12 us
  transfers between devices with their start and end apart: 13 -> 14, of which waited for: 7 -> 8; matrix products, arithmetic and copies ran while one was open for 31% -> 31% of each run, Pallas kernels for 0% -> 0%
where the time goes in v17:
time: 249 us; the launch traced here: 245 us
  matrix products  62.8 us (25%)
  waiting for transfers between devices  52.2 us (21%)
  blocking collectives  44.1 us (18%)
  local copies, waits for them, and re-layouts  38.1 us (15%)
  starting transfers between devices  30.1 us (12%)
  other arithmetic  15.1 us (6%)
    ppermute x7, waiting for transfers between devices, ch_exchange(): lax.ppermute(value, 'ch', [(i, (i + shift) % size) for i in range(size)])  37.3 us
    all_to_all x1, blocking collectives, pix_gather(): lax.all_to_all(spread.reshape(size, total, width), 'pix', 0, 0, tiled=True)  27.2 us
    dot_general x16, matrix products, backward_block(): jnp.einsum('bx,bc->xc', pick_table(slot_rows[:, slot], ext_rows), contrib...  20.2 us
    all_to_all x1, blocking collectives, pix_scatter(): lax.all_to_all(mine.reshape(size, chunk, width), 'pix', 0, 0, tiled=True)  16.9 us
    dot_general x16, matrix products, forward_block(): jnp.dot(pick_table(slot_rows[:, slot], ext_rows), flattened, preferred_el...  16.8 us
    all_to_all x1, waiting for transfers between devices, pix_scatter(): lax.all_to_all(mine.reshape(size, chunk, width), 'pix', 0, 0, tiled=True)  12.1 us
    unnamed x94, local copies, waits for them, and re-layouts  12 us
    ppermute x7, starting transfers between devices, ch_exchange(): lax.ppermute(value, 'ch', [(i, (i + shift) % size) for i in range(size)])  11 us
  transfers between devices with their start and end apart: 14, of which 8 were waited for; matrix products, arithmetic and copies ran while one was open for 31% of the time, Pallas kernels for 0%

profile of v17, /device:TPU:0, one launch (start us, length us, event | category | flops | bytes accessed | tf_op | source)
XLA Modules:
  0.0 244.6 jit_solution(7325701019550826117)
XLA Ops:
  0.7 2.2 fusion.140
  2.8 2.9 %collective-permute-start.2 = (bf16[512,384]{1,0:T(8,128)(2,1)}, bf16[512,384]{1,0:T(8,128)(2,1)}, u32[]{:S(2)}, u32[]{:S(2)}) collective-permute-start(bf16[512,384]{1,0:T(8,128)(2,1)} %get-tuple-element.97), channel_id=1, source_target_pairs={{0,1},{1,0},{2,3},{3,2},{4,5},{5,4},{6,7},{7,6},{8,9},{9,8},{10,11... | collective-permute-start | bytes 1179656 | tf_op jit(solution)/shard_map/ppermute | solution.py:145
  5.9 2.0 collective-permute-start
  7.8 1.5 fusion.130
  10.4 1.2 broadcast_select_fusion
  14.0 8.3 %collective-permute-done.1 = bf16[384,384]{1,0:T(8,128)(2,1)S(1)} collective-permute-done((bf16[384,384]{1,0:T(8,128)(2,1)}, bf16[384,384]{1,0:T(8,128)(2,1)S(1)}, u32[]{:S(2)}, u32[]{:S(2)}) %collective-permute-start.1) | collective-permute-done | bytes 294944 | tf_op jit(solution)/shard_map/ppermute | solution.py:145
  22.3 1.4 fusion.100
  23.6 6.3 %collective-permute-done = bf16[512,384]{1,0:T(8,128)(2,1)} collective-permute-done((bf16[512,384]{1,0:T(8,128)(2,1)}, bf16[512,384]{1,0:T(8,128)(2,1)}, u32[]{:S(2)}, u32[]{:S(2)}) %collective-permute-start) | collective-permute-done | bytes 393248 | tf_op jit(solution)/shard_map/ppermute | solution.py:145
  30.0 1.4 fusion.99
  31.4 2.1 fusion.144
  36.5 6.8 %all-to-all-start = ((bf16[16,32,2,192]{3,2,1,0:T(2,128)(2,1)}), bf16[16,32,2,192]{3,2,1,0:T(2,128)(2,1)}, u32[]{:S(2)}, u32[]{:S(2)}) async-start(bf16[16,32,2,192]{3,2,1,0:T(2,128)(2,1)} %reshape.204), calls=%async_computation | async-start | bytes 1048576 | tf_op jit(solution)/shard_map/all_to_all | solution.py:264
  44.4 1.5 collective-permute-start.3
  46.6 1.5 collective-permute-start.6
  49.0 10.3 %collective-permute-done.3 = bf16[1024,192]{1,0:T(8,128)(2,1)S(1)} collective-permute-done((bf16[1024,192]{1,0:T(8,128)(2,1)}, bf16[1024,192]{1,0:T(8,128)(2,1)S(1)}, u32[]{:S(2)}, u32[]{:S(2)}) %collective-permute-start.3) | collective-permute-done | bytes 393248 | tf_op jit(solution)/shard_map/ppermute | solution.py:145
  60.2 1.4 concatenate.50
  62.5 2.3 fusion.102
  72.7 1.3 copy-done.7
  77.2 1.3 fusion.53
  78.6 1.2 fusion.51
  90.5 1.2 fusion.40
  91.6 1.4 convolution_add_fusion.11
  93.1 1.2 convolution_add_fusion.10
  94.3 1.2 convolution_add_fusion.9
  95.5 1.2 convolution_add_fusion.8
  96.7 1.2 convolution_add_fusion.7
  97.9 1.2 convolution_add_fusion.6
  99.1 1.2 convolution_add_fusion.5
  100.3 1.6 collective-permute-start.4
  101.9 1.2 fusion.49
  103.4 6.9 %collective-permute-done.4 = bf16[1024,192]{0,1:T(8,128)(2,1)S(1)} collective-permute-done((bf16[1024,192]{0,1:T(8,128)(2,1)S(1)}, bf16[1024,192]{0,1:T(8,128)(2,1)S(1)}, u32[]{:S(2)}, u32[]{:S(2)}) %collective-permute-start.4) | collective-permute-done | bytes 393248 | tf_op jit(solution)/shard_map/ppermute | solution.py:145
  110.4 1.6 convolution_add_fusion.4
  111.9 1.2 convolution_add_fusion.3
  113.1 1.6 convolution_add_fusion.2
  114.8 1.2 convolution_add_fusion.1
  116.0 1.2 convolution_add_fusion
  117.2 1.5 copy-done.2
  119.8 5.6 %all-to-all-start.1 = ((bf16[16,32,2,192]{3,2,1,0:T(2,128)(2,1)}), bf16[16,32,2,192]{3,2,1,0:T(2,128)(2,1)}, u32[]{:S(2)}, u32[]{:S(2)}) async-start(bf16[16,32,2,192]{3,2,1,0:T(2,128)(2,1)} %reshape.206), calls=%async_computation.1 | async-start | bytes 1048576 | tf_op jit(solution)/shard_map/all_to_all | solution.py:281
  129.7 1.2 copy.113
  130.9 1.4 reshape_reshape.4
  132.3 3.2 %convolution_multiply_fusion.2 = f32[192,384]{1,0:T(8,128)} fusion(bf16[1024,192]{0,1:T(8,128)(2,1)} %bitcast.240, bf16[1024,192]{1,0:T(8,128)(2,1)} %copy.109, bf16[1024,192]{1,0:T(8,128)(2,1)} %copy-done.36, pred[]{:T(512)S(6)} %eq.213), kind=kOutput, calls=%fused_computation.155 | convolution fusion | flops 154607616 | bytes 1474561 | tf_op jit(solution)/shard_map/dot_general | solution.py:271
  135.6 1.3 slice_add_fusion
  136.9 1.9 copy.124
  138.8 1.1 all-to-all-done.1
  139.9 2.1 convert_element_type.200
  142.1 1.9 copy.125
  144.0 1.7 add_convert_fusion
  146.7 1.4 copy.127
  148.5 1.6 reshape.207
  150.1 1.1 broadcast_select_fusion.2
  151.4 1.1 pad_maximum_fusion.3
  152.5 1.5 collective-permute-start.8
  154.9 5.2 %all-to-all-start.2 = ((f32[16,24,384]{2,1,0:T(8,128)}), f32[16,24,384]{2,1,0:T(8,128)S(1)}, u32[]{:S(2)}, u32[]{:S(2)}) async-start(f32[16,24,384]{2,1,0:T(8,128)} %bitcast.234), calls=%async_computation.2 | async-start | bytes 1179648 | tf_op jit(solution)/shard_map/all_to_all | solution.py:177
  160.1 3.4 %fusion.134 = f32[1024,384,1]{1,0,2:T(8,128)} fusion(bf16[3,384,192]{1,2,0:T(8,128)(2,1)} %param.13, bf16[1024,2,192]{0,2,1:T(8,128)(2,1)} %copy-done.21, bf16[1024,1,192]{0,2,1:T(8,128)(2,1)S(1)} %copy-done.13), kind=kOutput, calls=%fused_computation.237 | convolution fusion | flops 453574656 | bytes 3194880 | tf_op jit(solution)/shard_map/rkd,kcd->rc/dot_general | solution.py:299
  163.5 12.1 %all-to-all-done.2 = f32[16,24,384]{2,1,0:T(8,128)S(1)} async-done(((f32[16,24,384]{2,1,0:T(8,128)}), f32[16,24,384]{2,1,0:T(8,128)S(1)}, u32[]{:S(2)}, u32[]{:S(2)}) %all-to-all-start.2) | async-done | bytes 589856 | tf_op jit(solution)/shard_map/all_to_all | solution.py:177
  175.7 5.5 %collective-permute-done.8 = bf16[1024,3,192]{0,2,1:T(8,128)(2,1)} collective-permute-done((bf16[1024,3,192]{0,2,1:T(8,128)(2,1)}, bf16[1024,3,192]{0,2,1:T(8,128)(2,1)}, u32[]{:S(2)}, u32[]{:S(2)}) %collective-permute-start.8) | collective-permute-done | bytes 1179680 | tf_op jit(solution)/shard_map/ppermute | solution.py:145
  181.2 3.7 %fusion.60 = bf16[1024,384]{1,0:T(8,128)(2,1)S(1)} fusion(f32[1024,384,1]{1,0,2:T(8,128)} %fusion.134, bf16[1024,3,192]{0,2,1:T(8,128)(2,1)} %collective-permute-done.8, bf16[3,384,192]{1,2,0:T(8,128)(2,1)} %collective-permute-done.6, bf16[1024,192]{1,0:T(8,128)(2,1)} %copy-done.36, bf16[1024,192]{1,0:T(8,128)(2,1)} %copy.109, pred[]{:T(512)S(6)} %eq.213), kind=kOutput, calls=%fused_computation.88 | convolution fusion | flops 458096640 | bytes 4767745 | tf_op jit(solution)/shard_map/rkd,kcd->rc/dot_general | solution.py:303
  185.7 1.6 collective-permute-done.9
  187.3 16.9 %all_to_all.25 = f32[16,12,384]{2,1,0:T(8,128)S(1)} all-to-all(f32[16,12,384]{2,1,0:T(8,128)S(1)} %reshape.210), channel_id=1, replica_groups=mesh['pix'=16,'ch'=2] {'pix'}, dimensions={0} | all-to-all | bytes 589824 | tf_op jit(solution)/shard_map/all_to_all | solution.py:177
  204.4 27.2 %all_to_all.26 = f32[16,36,384]{2,1,0:T(8,128)S(1)} all-to-all(f32[16,36,384]{2,1,0:T(8,128)S(1)} %bitcast.232), channel_id=1, replica_groups=mesh['pix'=16,'ch'=2] {'pix'}, dimensions={0} | all-to-all | bytes 1769472 | tf_op jit(solution)/shard_map/all_to_all | solution.py:188
  233.7 2.3 fusion.97
  236.0 2.0 copy.131
  238.0 1.5 convolution_convert_fusion
  239.5 1.5 copy_select_fusion.1
  242.3 1.3 copy.132
  (198 shorter events, 45.8 us)
Async XLA Ops:
  0.6 8.7 %copy-start.4 = (bf16[1024,384]{1,0:T(8,128)(2,1)S(1)}, bf16[1024,384]{1,0:T(8,128)(2,1)}, u32[]{:S(2)}) copy-start(bf16[1024,384]{1,0:T(8,128)(2,1)} %param.11) | copy-start | bytes 2359300
  0.6 8.7 %copy-start.9 = (bf16[384,384]{1,0:T(8,128)(2,1)S(1)}, bf16[384,384]{1,0:T(8,128)(2,1)}, u32[]{:S(2)}) copy-start(bf16[384,384]{1,0:T(8,128)(2,1)} %param.12) | copy-start | bytes 884740
  0.7 9.0 %copy-start.28 = (s32[1024,8]{0,1:T(8,128)S(1)}, s32[1024,8]{0,1:T(8,128)}, u32[]{:S(2)}) copy-start(s32[1024,8]{0,1:T(8,128)} %param.16) | copy-start | bytes 98308
  0.7 9.6 %copy-start.27 = (bf16[192,384]{1,0:T(8,128)(2,1)S(1)}, bf16[192,384]{1,0:T(8,128)(2,1)}, u32[]{:S(2)}) copy-start(bf16[192,384]{1,0:T(8,128)(2,1)} %param.14) | copy-start | bytes 442372
  2.8 9.4 %copy-start.29 = (s32[16,32]{1,0:T(8,128)S(1)}, s32[16,32]{1,0:T(8,128)}, u32[]{:S(2)}) copy-start(s32[16,32]{1,0:T(8,128)} %param.15) | copy-start | bytes 6148
  2.8 9.5 %copy-start.11 = (bf16[1024,192]{0,1:T(8,128)(2,1)S(1)}, bf16[1024,192]{0,1:T(8,128)(2,1)}, u32[]{:S(2)}) copy-start(bf16[1024,192]{0,1:T(8,128)(2,1)} %param.17) | copy-start | bytes 1179652
  2.8 19.4 %collective-permute-start.2 = (bf16[512,384]{1,0:T(8,128)(2,1)}, bf16[512,384]{1,0:T(8,128)(2,1)}, u32[]{:S(2)}, u32[]{:S(2)}) collective-permute-start(bf16[512,384]{1,0:T(8,128)(2,1)} %get-tuple-element.97), channel_id=1, source_target_pairs={{0,1},{1,0},{2,3},{3,2},{4,5},{5,4},{6,7},{7,6},{8,9},{9,8},{10,11... | collective-permute-start | bytes 1179656 | tf_op jit(solution)/shard_map/ppermute | solution.py:145
  5.8 16.5 %collective-permute-start.1 = (bf16[384,384]{1,0:T(8,128)(2,1)}, bf16[384,384]{1,0:T(8,128)(2,1)S(1)}, u32[]{:S(2)}, u32[]{:S(2)}) collective-permute-start(bf16[384,384]{1,0:T(8,128)(2,1)} %param.12), channel_id=1, source_target_pairs={{0,1},{1,0},{2,3},{3,2},{4,5},{5,4},{6,7},{7,6},{8,9},{9,8},{10,11... | collective-permute-start | bytes 884744 | tf_op jit(solution)/shard_map/ppermute | solution.py:145
  5.9 24.1 %collective-permute-start = (bf16[512,384]{1,0:T(8,128)(2,1)}, bf16[512,384]{1,0:T(8,128)(2,1)}, u32[]{:S(2)}, u32[]{:S(2)}) collective-permute-start(bf16[512,384]{1,0:T(8,128)(2,1)} %get-tuple-element.96), channel_id=1, source_target_pairs={{0,1},{1,0},{2,3},{3,2},{4,5},{5,4},{6,7},{7,6},{8,9},{9,8},{10,11... | collective-permute-start | bytes 1179656 | tf_op jit(solution)/shard_map/ppermute | solution.py:145
  12.4 21.5 %copy-start.30 = (s32[512]{0:T(512)}, s32[512]{0:T(512)S(1)}, u32[]{:S(2)}) copy-start(s32[512]{0:T(512)S(1)} %eq.149) | copy-start | bytes 6148
  31.4 2.1 copy-start.5
  33.8 0.9 copy-start.19
  36.5 23.7 %all-to-all-start = ((bf16[16,32,2,192]{3,2,1,0:T(2,128)(2,1)}), bf16[16,32,2,192]{3,2,1,0:T(2,128)(2,1)}, u32[]{:S(2)}, u32[]{:S(2)}) async-start(bf16[16,32,2,192]{3,2,1,0:T(2,128)(2,1)} %reshape.204), calls=%async_computation | async-start | bytes 1048576 | tf_op jit(solution)/shard_map/all_to_all | solution.py:264
  44.3 15.0 %copy-start.23 = (bf16[1024,192]{1,0:T(8,128)(2,1)S(1)}, bf16[1024,192]{1,0:T(8,128)(2,1)}, u32[]{:S(2)}) copy-start(bf16[1024,192]{1,0:T(8,128)(2,1)} %copy.109) | copy-start | bytes 1179652
  44.4 15.0 %collective-permute-start.3 = (bf16[1024,192]{1,0:T(8,128)(2,1)}, bf16[1024,192]{1,0:T(8,128)(2,1)S(1)}, u32[]{:S(2)}, u32[]{:S(2)}) collective-permute-start(bf16[1024,192]{1,0:T(8,128)(2,1)} %copy.108), channel_id=1, source_target_pairs={{0,1},{1,0},{2,3},{3,2},{4,5},{5,4},{6,7},{7,6},{8,9},{9,8},{10,11... | collective-permute-start | bytes 1179656 | tf_op jit(solution)/shard_map/ppermute | solution.py:145
  46.0 57.4 %collective-permute-start.5 = (bf16[192,192]{1,0:T(8,128)(2,1)}, bf16[192,192]{1,0:T(8,128)(2,1)}, u32[]{:S(2)}, u32[]{:S(2)}) collective-permute-start(bf16[192,192]{1,0:T(8,128)(2,1)} %bitcast.204), channel_id=1, source_target_pairs={{0,1},{1,0},{2,3},{3,2},{4,5},{5,4},{6,7},{7,6},{8,9},{9,8},{10,11... | collective-permute-start | bytes 221192 | tf_op jit(solution)/shard_map/ppermute | solution.py:248
  46.6 56.8 %collective-permute-start.6 = (bf16[3,384,192]{1,2,0:T(8,128)(2,1)}, bf16[3,384,192]{1,2,0:T(8,128)(2,1)}, u32[]{:S(2)}, u32[]{:S(2)}) collective-permute-start(bf16[3,384,192]{1,2,0:T(8,128)(2,1)} %param.13), channel_id=1, source_target_pairs={{0,1},{1,0},{2,3},{3,2},{4,5},{5,4},{6,7},{7,6},{8,9},{9,8},{10,11... | collective-permute-start | bytes 1327112 | tf_op jit(solution)/shard_map/ppermute | solution.py:145
  59.3 0.8 copy-start.36
  60.1 2.5 %copy-start.32 = (s32[512,1]{0,1:T(1,128)S(1)}, s32[512,1]{0,1:T(1,128)}, u32[]{:S(2)}) copy-start(s32[512,1]{0,1:T(1,128)} %get-tuple-element.113) | copy-start | bytes 6148
  62.5 2.3 copy-start.20
  62.5 2.3 copy-start.25
  62.5 2.3 copy-start.33
  64.9 1.0 copy-start.34
  65.9 1.0 copy-start.35
  70.7 2.0 copy-start.8
  71.7 2.3 copy-start.7
  77.2 38.8 %copy-start.1 = (bf16[512,9,2,3,64]{0,4,3,2,1:T(8,128)(2,1)}, bf16[512,9,2,3,64]{0,4,3,2,1:T(8,128)(2,1)S(1)}, u32[]{:S(2)}) copy-start(bf16[512,9,2,3,64]{0,4,3,2,1:T(8,128)(2,1)S(1)} %pad_maximum_fusion.1) | copy-start | bytes 10616836
  89.1 11.2 %copy-start.14 = (bf16[2,24,8,512]{3,2,0,1:T(8,128)(2,1)}, bf16[2,24,8,512]{3,2,0,1:T(8,128)(2,1)S(1)}, u32[]{:S(2)}) copy-start(bf16[2,24,8,512]{3,2,0,1:T(8,128)(2,1)S(1)} %copy.201) | copy-start | bytes 1179652
  90.5 8.6 %copy-start = (bf16[512,9,2,3,64]{0,4,3,2,1:T(8,128)(2,1)}, bf16[512,9,2,3,64]{0,4,3,2,1:T(8,128)(2,1)S(1)}, u32[]{:S(2)}) copy-start(bf16[512,9,2,3,64]{0,4,3,2,1:T(8,128)(2,1)S(1)} %pad_maximum_fusion) | copy-start | bytes 10616836
  100.3 10.1 %collective-permute-start.4 = (bf16[1024,192]{0,1:T(8,128)(2,1)S(1)}, bf16[1024,192]{0,1:T(8,128)(2,1)S(1)}, u32[]{:S(2)}, u32[]{:S(2)}) collective-permute-start(bf16[1024,192]{0,1:T(8,128)(2,1)S(1)} %bitcast.239), channel_id=1, source_target_pairs={{0,1},{1,0},{2,3},{3,2},{4,5},{5,4},{6,7},{7,6},{8,9},{9,8},{10,11... | collective-permute-start | bytes 1179656 | tf_op jit(solution)/shard_map/ppermute | solution.py:145
  110.4 1.6 copy-start.26
  117.2 1.5 copy-start.2
  119.8 20.2 %all-to-all-start.1 = ((bf16[16,32,2,192]{3,2,1,0:T(2,128)(2,1)}), bf16[16,32,2,192]{3,2,1,0:T(2,128)(2,1)}, u32[]{:S(2)}, u32[]{:S(2)}) async-start(bf16[16,32,2,192]{3,2,1,0:T(2,128)(2,1)} %reshape.206), calls=%async_computation.1 | async-start | bytes 1048576 | tf_op jit(solution)/shard_map/all_to_all | solution.py:281
  130.9 4.7 %copy-start.3 = (f32[1536,384]{1,0:T(8,128)S(1)}, f32[1536,384]{1,0:T(8,128)}, u32[]{:S(2)}) copy-start(f32[1536,384]{1,0:T(8,128)} %copy-done.2) | copy-start | bytes 7077892
  132.3 13.4 %copy-start.12 = (bf16[1024,1,192]{0,2,1:T(8,128)(2,1)}, bf16[1024,1,192]{0,2,1:T(8,128)(2,1)S(1)}, u32[]{:S(2)}) copy-start(bf16[1024,1,192]{0,2,1:T(8,128)(2,1)S(1)} %reshape_reshape.4) | copy-start | bytes 1179652
  132.3 3.3 %copy-start.16 = (bf16[512,1,384]{2,0,1:T(8,128)(2,1)S(1)}, bf16[512,1,384]{2,0,1:T(8,128)(2,1)}, u32[]{:S(2)}) copy-start(bf16[512,1,384]{2,0,1:T(8,128)(2,1)} %copy.190) | copy-start | bytes 1179652
  132.3 3.3 %copy-start.17 = (bf16[512,1,384]{2,0,1:T(8,128)(2,1)S(1)}, bf16[512,1,384]{2,0,1:T(8,128)(2,1)}, u32[]{:S(2)}) copy-start(bf16[512,1,384]{2,0,1:T(8,128)(2,1)} %copy.189) | copy-start | bytes 1179652
  136.9 7.1 %copy-start.31 = (s32[512]{0:T(512)S(1)}, s32[512]{0:T(512)}, u32[]{:S(2)}) copy-start(s32[512]{0:T(512)} %copy-done.30) | copy-start | bytes 6148
  138.8 6.9 %copy-start.6 = (bf16[1024,384]{1,0:T(8,128)(2,1)S(1)}, bf16[1024,384]{1,0:T(8,128)(2,1)}, u32[]{:S(2)}) copy-start(bf16[1024,384]{1,0:T(8,128)(2,1)} %copy-done.5) | copy-start | bytes 2359300
  145.7 0.9 copy-start.21
  148.5 2.8 %copy-start.13 = (bf16[1024,1,192]{0,2,1:T(8,128)(2,1)S(1)}, bf16[1024,1,192]{0,2,1:T(8,128)(2,1)}, u32[]{:S(2)}) copy-start(bf16[1024,1,192]{0,2,1:T(8,128)(2,1)} %copy-done.12) | copy-start | bytes 1179652
  150.1 1.2 copy-start.22
  150.1 3.9 %copy-start.18 = (f32[192,384]{1,0:T(8,128)S(1)}, f32[192,384]{1,0:T(8,128)}, u32[]{:S(2)}) copy-start(f32[192,384]{1,0:T(8,128)} %convolution_multiply_fusion.2) | copy-start | bytes 884740
  151.3 2.7 %collective-permute-start.7 = (f32[384,384]{1,0:T(8,128)S(1)}, f32[384,384]{1,0:T(8,128)S(1)}, u32[]{:S(2)}, u32[]{:S(2)}) collective-permute-start(f32[384,384]{1,0:T(8,128)S(1)} %broadcast_select_fusion.2), channel_id=1, source_target_pairs={{0,2},{2,0},{4,6},{6,4},{8,10},{10,8},{12,14},{14,12},{16,18},{18,... | collective-permute-start | bytes 1769480 | tf_op jit(solution)/shard_map/ppermute | solution.py:163
  152.5 28.7 %collective-permute-start.8 = (bf16[1024,3,192]{0,2,1:T(8,128)(2,1)}, bf16[1024,3,192]{0,2,1:T(8,128)(2,1)}, u32[]{:S(2)}, u32[]{:S(2)}) collective-permute-start(bf16[1024,3,192]{0,2,1:T(8,128)(2,1)} %pad_maximum_fusion.3), channel_id=1, source_target_pairs={{0,1},{1,0},{2,3},{3,2},{4,5},{5,4},{6,7},{7,6},{8,9},{9,8},{10,11... | collective-permute-start | bytes 3538952 | tf_op jit(solution)/shard_map/ppermute | solution.py:145
  154.9 20.7 %all-to-all-start.2 = ((f32[16,24,384]{2,1,0:T(8,128)}), f32[16,24,384]{2,1,0:T(8,128)S(1)}, u32[]{:S(2)}, u32[]{:S(2)}) async-start(f32[16,24,384]{2,1,0:T(8,128)} %bitcast.234), calls=%async_computation.2 | async-start | bytes 1179648 | tf_op jit(solution)/shard_map/all_to_all | solution.py:177
  185.6 1.6 collective-permute-start.9
  204.3 29.1 %copy-start.15 = (bf16[2,24,8,512]{3,2,0,1:T(8,128)(2,1)S(1)}, bf16[2,24,8,512]{3,2,0,1:T(8,128)(2,1)}, u32[]{:S(2)}) copy-start(bf16[2,24,8,512]{3,2,0,1:T(8,128)(2,1)} %copy-done.14) | copy-start | bytes 1179652
  204.3 29.1 %copy-start.24 = (bf16[192,1,192]{2,1,0:T(2,128)(2,1)S(1)}, bf16[192,1,192]{2,1,0:T(2,128)(2,1)}, u32[]{:S(2)}) copy-start(bf16[192,1,192]{2,1,0:T(2,128)(2,1)} %get-tuple-element.100) | copy-start | bytes 221188
  232.6 6.9 %collective-permute-start.10 = (f32[16,36,384]{2,0,1:T(8,128)}, f32[16,36,384]{2,0,1:T(8,128)}, u32[]{:S(2)}, u32[]{:S(2)}) collective-permute-start(f32[16,36,384]{2,0,1:T(8,128)} %copy.128), channel_id=1, source_target_pairs={{0,2},{2,0},{4,6},{6,4},{8,10},{10,8},{12,14},{14,12},{16,18},{18,... | collective-permute-start | bytes 2654216 | tf_op jit(solution)/shard_map/ppermute | solution.py:163
  233.4 4.6 %copy-start.10 = (bf16[384,384]{1,0:T(8,128)(2,1)S(1)}, bf16[384,384]{1,0:T(8,128)(2,1)}, u32[]{:S(2)}) copy-start(bf16[384,384]{1,0:T(8,128)(2,1)} %param.12) | copy-start | bytes 884740

commit v18 on v14

--- a/solution.py
+++ b/solution.py
@@ -288,7 +288,6 @@
         * grad_scale
     )
     early_reduced = pix_scatter((projection_term, mixing_term), mixing_weight.shape[1])
-    early_reduced, grad_others = lax.optimization_barrier((early_reduced, grad_others))
     pooled_sum = upstream.astype(f32) + jnp.einsum(
         "rkd,kcd->rc", grad_projected, projections, preferred_element_type=f32
     )

time: 241 us -> 238 us (0.988)
  blocking collectives: 43.9 us -> 27.2 us
  waiting for transfers between devices: 55 us -> 62.7 us
  starting transfers between devices: 28 us -> 32.9 us
    all_to_all x1 -> x0, blocking collectives: 16.8 us -> none  [pix_scatter(): lax.all_to_all(mine.reshape(size, chunk, width), 'pix', 0, 0, tiled=True)]
    ppermute x6, waiting for transfers between devices: 39.9 us -> 47.8 us  [ch_exchange(): lax.ppermute(value, 'ch', [(i, (i + shift) % size) for i in range(size)])]
    all_to_all x1 -> x2, starting transfers between devices: 5.03 us -> 9.94 us  [pix_scatter(): lax.all_to_all(mine.reshape(size, chunk, width), 'pix', 0, 0, tiled=True)]
    all_to_all x1 -> x2, waiting for transfers between devices: 12.4 us -> 12.2 us  [pix_scatter(): lax.all_to_all(mine.reshape(size, chunk, width), 'pix', 0, 0, tiled=True)]
    unnamed x78 -> x82, local copies, waits for them, and re-layouts: 11.2 us -> 11.3 us
  transfers between devices with their start and end apart: 13 -> 14, of which waited for: 7 -> 7; matrix products, arithmetic and copies ran while one was open for 31% -> 35% of each run, Pallas kernels for 0% -> 0%
where the time goes in v18:
time: 238 us; the launch traced here: 233 us
  waiting for transfers between devices  62.7 us (26%)
  matrix products  57.7 us (24%)
  local copies, waits for them, and re-layouts  34.8 us (15%)
  starting transfers between devices  32.9 us (14%)
  blocking collectives  27.2 us (11%)
  other arithmetic  15.9 us (7%)
    ppermute x6, waiting for transfers between devices, ch_exchange(): lax.ppermute(value, 'ch', [(i, (i + shift) % size) for i in range(size)])  47.8 us
    all_to_all x1, blocking collectives, pix_gather(): lax.all_to_all(spread.reshape(size, total, width), 'pix', 0, 0, tiled=True)  27.2 us
    dot_general x16, matrix products, backward_block(): jnp.einsum('bx,bc->xc', pick_table(slot_rows[:, slot], ext_rows), contrib...  20.2 us
    dot_general x16, matrix products, forward_block(): jnp.dot(pick_table(slot_rows[:, slot], ext_rows), flattened, preferred_el...  16.8 us
    all_to_all x2, waiting for transfers between devices, pix_scatter(): lax.all_to_all(mine.reshape(size, chunk, width), 'pix', 0, 0, tiled=True)  12.2 us
    unnamed x82, local copies, waits for them, and re-layouts  11.3 us
    all_to_all x2, starting transfers between devices, pix_scatter(): lax.all_to_all(mine.reshape(size, chunk, width), 'pix', 0, 0, tiled=True)  9.94 us
    ppermute x6, starting transfers between devices, ch_exchange(): lax.ppermute(value, 'ch', [(i, (i + shift) % size) for i in range(size)])  9.1 us
  transfers between devices with their start and end apart: 14, of which 7 were waited for; matrix products, arithmetic and copies ran while one was open for 35% of the time, Pallas kernels for 0%

profile of v18, /device:TPU:0, one launch (start us, length us, event | category | flops | bytes accessed | tf_op | source)
XLA Modules:
  0.0 233.2 jit_solution(11697823739588177800)
XLA Ops:
  0.7 3.0 %collective-permute-start = (bf16[1024,384]{1,0:T(8,128)(2,1)}, bf16[1024,384]{1,0:T(8,128)(2,1)S(1)}, u32[]{:S(2)}, u32[]{:S(2)}) collective-permute-start(bf16[1024,384]{1,0:T(8,128)(2,1)} %param.11), channel_id=1, source_target_pairs={{0,1},{1,0},{2,3},{3,2},{4,5},{5,4},{6,7},{7,6},{8,9},{9,8},{10,11... | collective-permute-start | bytes 2359304 | tf_op jit(solution)/shard_map/ppermute | solution.py:145
  3.7 1.1 reshape.203
  6.1 1.2 broadcast_select_fusion
  8.7 1.2 copy.109
  10.7 17.2 %collective-permute-done.1 = bf16[384,384]{1,0:T(8,128)(2,1)} collective-permute-done((bf16[384,384]{1,0:T(8,128)(2,1)}, bf16[384,384]{1,0:T(8,128)(2,1)}, u32[]{:S(2)}, u32[]{:S(2)}) %collective-permute-start.1) | collective-permute-done | bytes 294944 | tf_op jit(solution)/shard_map/ppermute | solution.py:145
  27.8 1.6 add_convert_fusion.1
  32.1 1.1 reshape.204
  33.2 6.8 %all-to-all-start = ((bf16[16,32,2,192]{3,2,1,0:T(2,128)(2,1)}), bf16[16,32,2,192]{3,2,1,0:T(2,128)(2,1)}, u32[]{:S(2)}, u32[]{:S(2)}) async-start(bf16[16,32,2,192]{3,2,1,0:T(2,128)(2,1)} %reshape.204), calls=%async_computation | async-start | bytes 1048576 | tf_op jit(solution)/shard_map/all_to_all | solution.py:257
  40.0 1.0 copy.108
  41.0 1.5 collective-permute-start.2
  43.2 1.5 collective-permute-start.5
  45.7 10.3 %collective-permute-done.2 = bf16[1024,192]{1,0:T(8,128)(2,1)S(1)} collective-permute-done((bf16[1024,192]{1,0:T(8,128)(2,1)}, bf16[1024,192]{1,0:T(8,128)(2,1)S(1)}, u32[]{:S(2)}, u32[]{:S(2)}) %collective-permute-start.2) | collective-permute-done | bytes 393248 | tf_op jit(solution)/shard_map/ppermute | solution.py:145
  56.9 1.4 concatenate.45
  59.2 2.3 fusion.100
  69.4 1.3 copy-done.4
  73.9 1.3 fusion.53
  75.2 1.2 fusion.51
  87.1 1.2 fusion.40
  88.2 1.4 convolution_add_fusion.11
  89.7 1.2 convolution_add_fusion.10
  90.9 1.2 convolution_add_fusion.9
  92.0 1.2 convolution_add_fusion.8
  93.3 1.2 convolution_add_fusion.7
  94.5 1.2 convolution_add_fusion.6
  95.7 1.2 convolution_add_fusion.5
  96.9 1.6 collective-permute-start.3
  98.4 1.2 fusion.49
  100.0 6.9 %collective-permute-done.3 = bf16[1024,192]{0,1:T(8,128)(2,1)S(1)} collective-permute-done((bf16[1024,192]{0,1:T(8,128)(2,1)S(1)}, bf16[1024,192]{0,1:T(8,128)(2,1)S(1)}, u32[]{:S(2)}, u32[]{:S(2)}) %collective-permute-start.3) | collective-permute-done | bytes 393248 | tf_op jit(solution)/shard_map/ppermute | solution.py:145
  106.9 1.6 convolution_add_fusion.4
  108.5 1.2 convolution_add_fusion.3
  109.7 1.6 convolution_add_fusion.2
  111.4 1.2 convolution_add_fusion.1
  112.6 1.2 convolution_add_fusion
  113.8 1.5 copy-done.2
  115.3 1.1 reshape.206
  116.4 5.6 %all-to-all-start.1 = ((bf16[16,32,2,192]{3,2,1,0:T(2,128)(2,1)}), bf16[16,32,2,192]{3,2,1,0:T(2,128)(2,1)}, u32[]{:S(2)}, u32[]{:S(2)}) async-start(bf16[16,32,2,192]{3,2,1,0:T(2,128)(2,1)} %reshape.206), calls=%async_computation.1 | async-start | bytes 1048576 | tf_op jit(solution)/shard_map/all_to_all | solution.py:274
  122.3 1.0 slice.369
  123.3 1.0 slice.368
  126.3 1.1 copy.113
  127.4 1.4 reshape_reshape.4
  128.9 3.2 %convolution_multiply_fusion.2 = f32[192,384]{1,0:T(8,128)} fusion(bf16[1024,192]{0,1:T(8,128)(2,1)} %bitcast.237, bf16[1024,192]{1,0:T(8,128)(2,1)} %copy-done.22, bf16[1024,192]{1,0:T(8,128)(2,1)} %copy-done.30, pred[]{:T(512)S(6)} %eq.213), kind=kOutput, calls=%fused_computation.152 | convolution fusion | flops 154607616 | bytes 1474561 | tf_op jit(solution)/shard_map/dot_general | solution.py:264
  132.1 1.4 slice_add_fusion
  133.5 1.9 copy.124
  135.3 1.1 all-to-all-done.1
  136.5 1.4 convert_element_type.203
  138.8 1.7 add_convert_fusion
  140.5 1.2 pad_maximum_fusion.3
  141.8 1.5 collective-permute-start.6
  145.3 1.3 copy.126
  147.1 1.1 broadcast_select_fusion.2
  148.5 2.1 fusion.128
  151.6 5.0 %all-to-all-start.2 = ((f32[16,24,384]{2,1,0:T(8,128)}), f32[16,24,384]{2,1,0:T(8,128)S(1)}, u32[]{:S(2)}, u32[]{:S(2)}) async-start(f32[16,24,384]{2,1,0:T(8,128)} %bitcast.102), calls=%async_computation.2 | async-start | bytes 1179648 | tf_op jit(solution)/shard_map/all_to_all | solution.py:177
  156.6 13.4 %collective-permute-done.6 = bf16[1024,3,192]{0,2,1:T(8,128)(2,1)} collective-permute-done((bf16[1024,3,192]{0,2,1:T(8,128)(2,1)}, bf16[1024,3,192]{0,2,1:T(8,128)(2,1)}, u32[]{:S(2)}, u32[]{:S(2)}) %collective-permute-start.6) | collective-permute-done | bytes 1179680 | tf_op jit(solution)/shard_map/ppermute | solution.py:145
  170.0 3.4 %fusion.60 = bf16[1024,384]{1,0:T(8,128)(2,1)S(1)} fusion(f32[1024,384,1]{1,0,2:T(8,128)} %fusion.128, bf16[1024,3,192]{0,2,1:T(8,128)(2,1)} %collective-permute-done.6, bf16[3,384,192]{1,2,0:T(8,128)(2,1)} %collective-permute-done.5, bf16[1024,192]{1,0:T(8,128)(2,1)} %copy-done.30, bf16[1024,192]{1,0:T(8,128)(2,1)S(1)} %copy-done.23, pred[]{:T(512)S(6)} %eq.213), kind=kOutput, calls=%fused_computation.88 | convolution fusion | flops 458096640 | bytes 4767745 | tf_op jit(solution)/shard_map/rkd,kcd->rc/dot_general | solution.py:295
  174.1 1.6 collective-permute-done.8
  176.5 4.9 %all-to-all-start.3 = ((f32[16,12,384]{2,1,0:T(8,128)}), f32[16,12,384]{2,1,0:T(8,128)S(1)}, u32[]{:S(2)}, u32[]{:S(2)}) async-start(f32[16,12,384]{2,1,0:T(8,128)} %reshape.210), calls=%async_computation.3 | async-start | bytes 786432 | tf_op jit(solution)/shard_map/all_to_all | solution.py:177
  181.5 12.2 %all-to-all-done.3 = f32[16,12,384]{2,1,0:T(8,128)S(1)} async-done(((f32[16,12,384]{2,1,0:T(8,128)}), f32[16,12,384]{2,1,0:T(8,128)S(1)}, u32[]{:S(2)}, u32[]{:S(2)}) %all-to-all-start.3) | async-done | bytes 294944 | tf_op jit(solution)/shard_map/all_to_all | solution.py:177
  193.8 27.2 %all_to_all.25 = f32[16,36,384]{2,1,0:T(8,128)S(1)} all-to-all(f32[16,36,384]{2,1,0:T(8,128)S(1)} %bitcast.230), channel_id=1, replica_groups=mesh['pix'=16,'ch'=2] {'pix'}, dimensions={0} | all-to-all | bytes 1769472 | tf_op jit(solution)/shard_map/all_to_all | solution.py:188
  221.0 1.1 copy.128
  222.8 1.3 fusion.121
  224.2 1.5 fusion.97
  226.6 1.5 convolution_convert_fusion
  228.1 1.5 copy_select_fusion.1
  230.9 1.3 copy.132
  (181 shorter events, 43.7 us)
Async XLA Ops:
  0.6 9.4 %copy-start.6 = (bf16[1024,384]{1,0:T(8,128)(2,1)S(1)}, bf16[1024,384]{1,0:T(8,128)(2,1)}, u32[]{:S(2)}) copy-start(bf16[1024,384]{1,0:T(8,128)(2,1)} %param.11) | copy-start | bytes 2359300
  0.6 9.4 %copy-start.16 = (bf16[384,384]{1,0:T(8,128)(2,1)S(1)}, bf16[384,384]{1,0:T(8,128)(2,1)}, u32[]{:S(2)}) copy-start(bf16[384,384]{1,0:T(8,128)(2,1)} %param.12) | copy-start | bytes 884740
  0.7 27.2 %collective-permute-start = (bf16[1024,384]{1,0:T(8,128)(2,1)}, bf16[1024,384]{1,0:T(8,128)(2,1)S(1)}, u32[]{:S(2)}, u32[]{:S(2)}) collective-permute-start(bf16[1024,384]{1,0:T(8,128)(2,1)} %param.11), channel_id=1, source_target_pairs={{0,1},{1,0},{2,3},{3,2},{4,5},{5,4},{6,7},{7,6},{8,9},{9,8},{10,11... | collective-permute-start | bytes 2359304 | tf_op jit(solution)/shard_map/ppermute | solution.py:145
  3.7 24.2 %collective-permute-start.1 = (bf16[384,384]{1,0:T(8,128)(2,1)}, bf16[384,384]{1,0:T(8,128)(2,1)}, u32[]{:S(2)}, u32[]{:S(2)}) collective-permute-start(bf16[384,384]{1,0:T(8,128)(2,1)} %param.12), channel_id=1, source_target_pairs={{0,1},{1,0},{2,3},{3,2},{4,5},{5,4},{6,7},{7,6},{8,9},{9,8},{10,11... | collective-permute-start | bytes 884744 | tf_op jit(solution)/shard_map/ppermute | solution.py:145
  9.9 46.0 %copy-start.22 = (bf16[1024,192]{1,0:T(8,128)(2,1)}, bf16[1024,192]{1,0:T(8,128)(2,1)S(1)}, u32[]{:S(2)}) copy-start(bf16[1024,192]{1,0:T(8,128)(2,1)S(1)} %copy.109) | copy-start | bytes 1179652
  10.6 18.8 %copy-start.24 = (bf16[3,384,192]{1,2,0:T(8,128)(2,1)S(1)}, bf16[3,384,192]{1,2,0:T(8,128)(2,1)}, u32[]{:S(2)}) copy-start(bf16[3,384,192]{1,2,0:T(8,128)(2,1)} %param.13) | copy-start | bytes 1327108
  30.5 0.9 copy-start.18
  30.5 9.5 %copy-start.8 = (bf16[1024,192]{0,1:T(8,128)(2,1)S(1)}, bf16[1024,192]{0,1:T(8,128)(2,1)}, u32[]{:S(2)}) copy-start(bf16[1024,192]{0,1:T(8,128)(2,1)} %param.17) | copy-start | bytes 1179652
  33.2 23.6 %all-to-all-start = ((bf16[16,32,2,192]{3,2,1,0:T(2,128)(2,1)}), bf16[16,32,2,192]{3,2,1,0:T(2,128)(2,1)}, u32[]{:S(2)}, u32[]{:S(2)}) async-start(bf16[16,32,2,192]{3,2,1,0:T(2,128)(2,1)} %reshape.204), calls=%async_computation | async-start | bytes 1048576 | tf_op jit(solution)/shard_map/all_to_all | solution.py:257
  41.0 15.0 %copy-start.28 = (bf16[192,384]{1,0:T(8,128)(2,1)S(1)}, bf16[192,384]{1,0:T(8,128)(2,1)}, u32[]{:S(2)}) copy-start(bf16[192,384]{1,0:T(8,128)(2,1)} %param.14) | copy-start | bytes 442372
  41.0 15.0 %collective-permute-start.2 = (bf16[1024,192]{1,0:T(8,128)(2,1)}, bf16[1024,192]{1,0:T(8,128)(2,1)S(1)}, u32[]{:S(2)}, u32[]{:S(2)}) collective-permute-start(bf16[1024,192]{1,0:T(8,128)(2,1)} %copy.108), channel_id=1, source_target_pairs={{0,1},{1,0},{2,3},{3,2},{4,5},{5,4},{6,7},{7,6},{8,9},{9,8},{10,11... | collective-permute-start | bytes 1179656 | tf_op jit(solution)/shard_map/ppermute | solution.py:145
  42.6 57.4 %collective-permute-start.4 = (bf16[192,192]{1,0:T(8,128)(2,1)}, bf16[192,192]{1,0:T(8,128)(2,1)}, u32[]{:S(2)}, u32[]{:S(2)}) collective-permute-start(bf16[192,192]{1,0:T(8,128)(2,1)} %bitcast.285), channel_id=1, source_target_pairs={{0,1},{1,0},{2,3},{3,2},{4,5},{5,4},{6,7},{7,6},{8,9},{9,8},{10,11... | collective-permute-start | bytes 221192 | tf_op jit(solution)/shard_map/ppermute | solution.py:241
  43.2 56.8 %collective-permute-start.5 = (bf16[3,384,192]{1,2,0:T(8,128)(2,1)}, bf16[3,384,192]{1,2,0:T(8,128)(2,1)}, u32[]{:S(2)}, u32[]{:S(2)}) collective-permute-start(bf16[3,384,192]{1,2,0:T(8,128)(2,1)} %param.13), channel_id=1, source_target_pairs={{0,1},{1,0},{2,3},{3,2},{4,5},{5,4},{6,7},{7,6},{8,9},{9,8},{10,11... | collective-permute-start | bytes 1327112 | tf_op jit(solution)/shard_map/ppermute | solution.py:145
  56.0 0.8 copy-start.30
  59.2 2.3 copy-start.19
  59.2 2.3 %copy-start.26 = (bf16[512,384]{0,1:T(8,128)(2,1)S(1)}, bf16[512,384]{0,1:T(8,128)(2,1)}, u32[]{:S(2)}) copy-start(bf16[512,384]{0,1:T(8,128)(2,1)} %copy.106) | copy-start | bytes 1179652
  62.5 1.0 copy-start.29
  67.4 2.0 copy-start.5
  68.3 2.3 %copy-start.4 = (bf16[512,9,2,192]{0,3,2,1:T(8,128)(2,1)S(1)}, bf16[512,9,2,192]{0,3,2,1:T(8,128)(2,1)}, u32[]{:S(2)}) copy-start(bf16[512,9,2,192]{0,3,2,1:T(8,128)(2,1)} %get-tuple-element.90) | copy-start | bytes 10616836
  73.8 38.7 %copy-start.1 = (bf16[512,9,2,3,64]{0,4,3,2,1:T(8,128)(2,1)}, bf16[512,9,2,3,64]{0,4,3,2,1:T(8,128)(2,1)S(1)}, u32[]{:S(2)}) copy-start(bf16[512,9,2,3,64]{0,4,3,2,1:T(8,128)(2,1)S(1)} %pad_maximum_fusion.1) | copy-start | bytes 10616836
  85.7 11.2 %copy-start.11 = (bf16[2,24,8,512]{3,2,0,1:T(8,128)(2,1)}, bf16[2,24,8,512]{3,2,0,1:T(8,128)(2,1)S(1)}, u32[]{:S(2)}) copy-start(bf16[2,24,8,512]{3,2,0,1:T(8,128)(2,1)S(1)} %copy.201) | copy-start | bytes 1179652
  87.1 8.6 %copy-start = (bf16[512,9,2,3,64]{0,4,3,2,1:T(8,128)(2,1)}, bf16[512,9,2,3,64]{0,4,3,2,1:T(8,128)(2,1)S(1)}, u32[]{:S(2)}) copy-start(bf16[512,9,2,3,64]{0,4,3,2,1:T(8,128)(2,1)S(1)} %pad_maximum_fusion) | copy-start | bytes 10616836
  96.9 10.1 %collective-permute-start.3 = (bf16[1024,192]{0,1:T(8,128)(2,1)S(1)}, bf16[1024,192]{0,1:T(8,128)(2,1)S(1)}, u32[]{:S(2)}, u32[]{:S(2)}) collective-permute-start(bf16[1024,192]{0,1:T(8,128)(2,1)S(1)} %bitcast.236), channel_id=1, source_target_pairs={{0,1},{1,0},{2,3},{3,2},{4,5},{5,4},{6,7},{7,6},{8,9},{9,8},{10,11... | collective-permute-start | bytes 1179656 | tf_op jit(solution)/shard_map/ppermute | solution.py:145
  106.9 1.6 copy-start.27
  113.8 1.5 copy-start.2
  116.4 20.1 %all-to-all-start.1 = ((bf16[16,32,2,192]{3,2,1,0:T(2,128)(2,1)}), bf16[16,32,2,192]{3,2,1,0:T(2,128)(2,1)}, u32[]{:S(2)}, u32[]{:S(2)}) async-start(bf16[16,32,2,192]{3,2,1,0:T(2,128)(2,1)} %reshape.206), calls=%async_computation.1 | async-start | bytes 1048576 | tf_op jit(solution)/shard_map/all_to_all | solution.py:274
  127.4 4.7 %copy-start.3 = (f32[1536,384]{1,0:T(8,128)S(1)}, f32[1536,384]{1,0:T(8,128)}, u32[]{:S(2)}) copy-start(f32[1536,384]{1,0:T(8,128)} %copy-done.2) | copy-start | bytes 7077892
  128.8 14.4 %copy-start.9 = (bf16[1024,1,192]{0,2,1:T(8,128)(2,1)}, bf16[1024,1,192]{0,2,1:T(8,128)(2,1)S(1)}, u32[]{:S(2)}) copy-start(bf16[1024,1,192]{0,2,1:T(8,128)(2,1)S(1)} %reshape_reshape.4) | copy-start | bytes 1179652
  128.8 3.3 %copy-start.13 = (bf16[512,1,384]{2,0,1:T(8,128)(2,1)S(1)}, bf16[512,1,384]{2,0,1:T(8,128)(2,1)}, u32[]{:S(2)}) copy-start(bf16[512,1,384]{2,0,1:T(8,128)(2,1)} %copy.190) | copy-start | bytes 1179652
  128.8 3.3 %copy-start.14 = (bf16[512,1,384]{2,0,1:T(8,128)(2,1)S(1)}, bf16[512,1,384]{2,0,1:T(8,128)(2,1)}, u32[]{:S(2)}) copy-start(bf16[512,1,384]{2,0,1:T(8,128)(2,1)} %copy.189) | copy-start | bytes 1179652
  140.5 3.5 %copy-start.20 = (bf16[1024,2,192]{0,2,1:T(8,128)(2,1)}, bf16[1024,2,192]{0,2,1:T(8,128)(2,1)S(1)}, u32[]{:S(2)}) copy-start(bf16[1024,2,192]{0,2,1:T(8,128)(2,1)S(1)} %add_convert_fusion) | copy-start | bytes 2359300
  141.8 28.2 %collective-permute-start.6 = (bf16[1024,3,192]{0,2,1:T(8,128)(2,1)}, bf16[1024,3,192]{0,2,1:T(8,128)(2,1)}, u32[]{:S(2)}, u32[]{:S(2)}) collective-permute-start(bf16[1024,3,192]{0,2,1:T(8,128)(2,1)} %pad_maximum_fusion.3), channel_id=1, source_target_pairs={{0,1},{1,0},{2,3},{3,2},{4,5},{5,4},{6,7},{7,6},{8,9},{9,8},{10,11... | collective-permute-start | bytes 3538952 | tf_op jit(solution)/shard_map/ppermute | solution.py:145
  147.1 1.3 copy-start.10
  147.1 1.3 copy-start.21
  147.1 1.4 copy-start.25
  148.2 2.4 %copy-start.15 = (f32[192,384]{1,0:T(8,128)S(1)}, f32[192,384]{1,0:T(8,128)}, u32[]{:S(2)}) copy-start(f32[192,384]{1,0:T(8,128)} %convolution_multiply_fusion.2) | copy-start | bytes 884740
  148.2 2.4 %collective-permute-start.7 = (f32[384,384]{1,0:T(8,128)S(1)}, f32[384,384]{1,0:T(8,128)S(1)}, u32[]{:S(2)}, u32[]{:S(2)}) collective-permute-start(f32[384,384]{1,0:T(8,128)S(1)} %broadcast_select_fusion.2), channel_id=1, source_target_pairs={{0,2},{2,0},{4,6},{6,4},{8,10},{10,8},{12,14},{14,12},{16,18},{18,... | collective-permute-start | bytes 1769480 | tf_op jit(solution)/shard_map/ppermute | solution.py:163
  150.7 19.3 %copy-start.23 = (bf16[1024,192]{1,0:T(8,128)(2,1)S(1)}, bf16[1024,192]{1,0:T(8,128)(2,1)}, u32[]{:S(2)}) copy-start(bf16[1024,192]{1,0:T(8,128)(2,1)} %copy-done.22) | copy-start | bytes 1179652
  151.6 25.0 %all-to-all-start.2 = ((f32[16,24,384]{2,1,0:T(8,128)}), f32[16,24,384]{2,1,0:T(8,128)S(1)}, u32[]{:S(2)}, u32[]{:S(2)}) async-start(f32[16,24,384]{2,1,0:T(8,128)} %bitcast.102), calls=%async_computation.2 | async-start | bytes 1179648 | tf_op jit(solution)/shard_map/all_to_all | solution.py:177
  156.6 16.8 %copy-start.7 = (bf16[1024,384]{1,0:T(8,128)(2,1)S(1)}, bf16[1024,384]{1,0:T(8,128)(2,1)}, u32[]{:S(2)}) copy-start(bf16[1024,384]{1,0:T(8,128)(2,1)} %param.11) | copy-start | bytes 2359300
  174.1 1.6 collective-permute-start.8
  176.5 17.2 %all-to-all-start.3 = ((f32[16,12,384]{2,1,0:T(8,128)}), f32[16,12,384]{2,1,0:T(8,128)S(1)}, u32[]{:S(2)}, u32[]{:S(2)}) async-start(f32[16,12,384]{2,1,0:T(8,128)} %reshape.210), calls=%async_computation.3 | async-start | bytes 786432 | tf_op jit(solution)/shard_map/all_to_all | solution.py:177
  193.7 29.1 %copy-start.12 = (bf16[2,24,8,512]{3,2,0,1:T(8,128)(2,1)S(1)}, bf16[2,24,8,512]{3,2,0,1:T(8,128)(2,1)}, u32[]{:S(2)}) copy-start(bf16[2,24,8,512]{3,2,0,1:T(8,128)(2,1)} %copy-done.11) | copy-start | bytes 1179652
  222.1 6.0 %collective-permute-start.9 = (f32[16,36,384]{2,0,1:T(8,128)}, f32[16,36,384]{2,0,1:T(8,128)}, u32[]{:S(2)}, u32[]{:S(2)}) collective-permute-start(f32[16,36,384]{2,0,1:T(8,128)} %copy.128), channel_id=1, source_target_pairs={{0,2},{2,0},{4,6},{6,4},{8,10},{10,8},{12,14},{14,12},{16,18},{18,... | collective-permute-start | bytes 2654216 | tf_op jit(solution)/shard_map/ppermute | solution.py:163
  222.8 3.7 %copy-start.17 = (bf16[384,384]{1,0:T(8,128)(2,1)S(1)}, bf16[384,384]{1,0:T(8,128)(2,1)}, u32[]{:S(2)}) copy-start(bf16[384,384]{1,0:T(8,128)(2,1)} %param.12) | copy-start | bytes 884740

commit v19 on v18

--- a/solution.py
+++ b/solution.py
@@ -270,6 +270,8 @@
     for attended_other, mix_other in zip(attended_others, mix_others):
         branch = branch + jnp.dot(attended_other, mix_other, preferred_element_type=f32)
     section_output = (pooled.astype(f32) + branch).astype(bf16)
+    query_part = query_grads.astype(bf16)
+    query_others = ch_exchange(query_part)
     remote_grads = carried[row_count:].reshape(peer_count, slot_count, 2, half_width)
     returned = lax.all_to_all(remote_grads, "pix", split_axis=0, concat_axis=0, tiled=True)
     returned_rows = jnp.einsum(
@@ -282,7 +284,7 @@
     grad_projected = jnp.concatenate(
         [query_grads.reshape(row_count, 1, half_width), local_grads], axis=1
     ).astype(bf16)
-    grad_others = ch_exchange(grad_projected)
+    grad_others = ch_exchange(local_grads.astype(bf16))
     projection_term = (
         jnp.einsum("rc,rkd->kcd", pooled_all, grad_projected, preferred_element_type=f32)
         * grad_scale
@@ -291,9 +293,12 @@
     pooled_sum = upstream.astype(f32) + jnp.einsum(
         "rkd,kcd->rc", grad_projected, projections, preferred_element_type=f32
     )
-    for grad_other, proj_other in zip(grad_others, proj_others):
+    for query_other, grad_other, proj_other in zip(query_others, grad_others, proj_others):
         pooled_sum = pooled_sum + jnp.einsum(
-            "rkd,kcd->rc", grad_other, proj_other, preferred_element_type=f32
+            "rd,cd->rc", query_other, proj_other[0], preferred_element_type=f32
+        )
+        pooled_sum = pooled_sum + jnp.einsum(
+            "rkd,kcd->rc", grad_other, proj_other[1:], preferred_element_type=f32
         )
     grad_pooled = pooled_sum.astype(bf16)
     kernel_term = jnp.dot(fine_pixels.T, grad_pooled, preferred_element_type=f32) * grad_scale

time: 238 us -> 248 us (1.042)
  waiting for transfers between devices: 62.7 us -> 68.9 us
    all_to_all x2, waiting for transfers between devices: 12.2 us -> 25.6 us  [pix_scatter(): lax.all_to_all(mine.reshape(size, chunk, width), 'pix', 0, 0, tiled=True)]
    ppermute x6 -> x7, waiting for transfers between devices: 47.8 us -> 43.1 us  [ch_exchange(): lax.ppermute(value, 'ch', [(i, (i + shift) % size) for i in range(size)])]
    unnamed x82 -> x81, local copies, waits for them, and re-layouts: 11.3 us -> 13.1 us
    dot_general x1 -> x2, matrix products: 3.41 us -> 5.06 us  [the longest x1 2.68 us: per_device(): jnp.einsum('rd,cd->rc', query_other, proj_other[0], preferred_element_typ...]
    ppermute x6 -> x7, starting transfers between devices: 9.1 us -> 9.98 us  [ch_exchange(): lax.ppermute(value, 'ch', [(i, (i + shift) % size) for i in range(size)])]
  transfers between devices with their start and end apart: 14 -> 15, of which waited for: 7 -> 7; matrix products, arithmetic and copies ran while one was open for 35% -> 35% of each run, Pallas kernels for 0% -> 0%
where the time goes in v19:
time: 248 us; the launch traced here: 243 us
  waiting for transfers between devices  68.9 us (28%)
  matrix products  59.5 us (24%)
  local copies, waits for them, and re-layouts  34.5 us (14%)
  starting transfers between devices  33.4 us (13%)
  blocking collectives  28.2 us (11%)
  other arithmetic  16.4 us (7%)
    ppermute x7, waiting for transfers between devices, ch_exchange(): lax.ppermute(value, 'ch', [(i, (i + shift) % size) for i in range(size)])  43.1 us
    all_to_all x1, blocking collectives, pix_gather(): lax.all_to_all(spread.reshape(size, total, width), 'pix', 0, 0, tiled=True)  28.2 us
    all_to_all x2, waiting for transfers between devices, pix_scatter(): lax.all_to_all(mine.reshape(size, chunk, width), 'pix', 0, 0, tiled=True)  25.6 us
    dot_general x16, matrix products, backward_block(): jnp.einsum('bx,bc->xc', pick_table(slot_rows[:, slot], ext_rows), contrib...  20.1 us
    dot_general x16, matrix products, forward_block(): jnp.dot(pick_table(slot_rows[:, slot], ext_rows), flattened, preferred_el...  16.9 us
    unnamed x81, local copies, waits for them, and re-layouts  13.1 us
    ppermute x7, starting transfers between devices, ch_exchange(): lax.ppermute(value, 'ch', [(i, (i + shift) % size) for i in range(size)])  9.98 us
    all_to_all x2, starting transfers between devices, pix_scatter(): lax.all_to_all(mine.reshape(size, chunk, width), 'pix', 0, 0, tiled=True)  9.33 us
  transfers between devices with their start and end apart: 15, of which 7 were waited for; matrix products, arithmetic and copies ran while one was open for 35% of the time, Pallas kernels for 0%

profile of v19, /device:TPU:0, one launch (start us, length us, event | category | flops | bytes accessed | tf_op | source)
XLA Modules:
  0.0 243.1 jit_solution(7370969560152138231)
XLA Ops:
  0.7 3.0 %collective-permute-start = (bf16[1024,384]{1,0:T(8,128)(2,1)}, bf16[1024,384]{1,0:T(8,128)(2,1)S(1)}, u32[]{:S(2)}, u32[]{:S(2)}) collective-permute-start(bf16[1024,384]{1,0:T(8,128)(2,1)} %param.11), channel_id=1, source_target_pairs={{0,1},{1,0},{2,3},{3,2},{4,5},{5,4},{6,7},{7,6},{8,9},{9,8},{10,11... | collective-permute-start | bytes 2359304 | tf_op jit(solution)/shard_map/ppermute | solution.py:145
  3.7 1.1 reshape.205
  6.1 1.2 broadcast_select_fusion
  8.7 1.2 copy.106
  10.7 17.1 %collective-permute-done.1 = bf16[384,384]{1,0:T(8,128)(2,1)S(1)} collective-permute-done((bf16[384,384]{1,0:T(8,128)(2,1)}, bf16[384,384]{1,0:T(8,128)(2,1)S(1)}, u32[]{:S(2)}, u32[]{:S(2)}) %collective-permute-start.1) | collective-permute-done | bytes 294944 | tf_op jit(solution)/shard_map/ppermute | solution.py:145
  31.1 1.1 reshape.206
  32.2 6.8 %all-to-all-start = ((bf16[16,32,2,192]{3,2,1,0:T(2,128)(2,1)}), bf16[16,32,2,192]{3,2,1,0:T(2,128)(2,1)}, u32[]{:S(2)}, u32[]{:S(2)}) async-start(bf16[16,32,2,192]{3,2,1,0:T(2,128)(2,1)} %reshape.206), calls=%async_computation | async-start | bytes 1048576 | tf_op jit(solution)/shard_map/all_to_all | solution.py:257
  38.9 1.0 copy.105
  39.9 1.5 collective-permute-start.2
  42.1 1.5 collective-permute-start.5
  44.6 10.3 %collective-permute-done.2 = bf16[1024,192]{1,0:T(8,128)(2,1)S(1)} collective-permute-done((bf16[1024,192]{1,0:T(8,128)(2,1)}, bf16[1024,192]{1,0:T(8,128)(2,1)S(1)}, u32[]{:S(2)}, u32[]{:S(2)}) %collective-permute-start.2) | collective-permute-done | bytes 393248 | tf_op jit(solution)/shard_map/ppermute | solution.py:145
  55.8 1.4 concatenate.45
  58.1 2.3 fusion.101
  60.4 1.0 fusion.109
  68.3 1.3 copy-done.4
  72.8 1.3 fusion.53
  74.2 1.2 fusion.51
  77.3 1.0 fusion.104
  86.1 1.2 fusion.40
  87.2 1.6 convolution_add_fusion.11
  88.8 1.2 convolution_add_fusion.10
  90.0 1.2 convolution_add_fusion.9
  91.2 1.2 convolution_add_fusion.8
  92.4 1.2 convolution_add_fusion.7
  93.6 1.2 convolution_add_fusion.6
  94.9 1.2 convolution_add_fusion.5
  96.1 1.5 collective-permute-start.3
  97.6 1.2 fusion.49
  99.1 7.0 %collective-permute-done.3 = bf16[1024,192]{0,1:T(8,128)(2,1)S(1)} collective-permute-done((bf16[1024,192]{0,1:T(8,128)(2,1)S(1)}, bf16[1024,192]{0,1:T(8,128)(2,1)S(1)}, u32[]{:S(2)}, u32[]{:S(2)}) %collective-permute-start.3) | collective-permute-done | bytes 393248 | tf_op jit(solution)/shard_map/ppermute | solution.py:145
  106.1 1.6 convolution_add_fusion.4
  107.7 1.2 convolution_add_fusion.3
  108.9 1.4 convolution_add_fusion.2
  110.3 1.2 convolution_add_fusion.1
  111.5 1.2 convolution_add_fusion
  112.7 1.5 copy-done.2
  114.2 1.1 reshape.208
  115.3 5.6 %all-to-all-start.1 = ((bf16[16,32,2,192]{3,2,1,0:T(2,128)(2,1)}), bf16[16,32,2,192]{3,2,1,0:T(2,128)(2,1)}, u32[]{:S(2)}, u32[]{:S(2)}) async-start(bf16[16,32,2,192]{3,2,1,0:T(2,128)(2,1)} %reshape.208), calls=%async_computation.1 | async-start | bytes 1048576 | tf_op jit(solution)/shard_map/all_to_all | solution.py:276
  121.2 1.0 slice.377
  122.3 1.0 slice.376
  124.4 1.0 reshape_reshape.4
  126.2 1.5 collective-permute-start.6
  129.6 3.2 %convolution_multiply_fusion.2 = f32[192,384]{1,0:T(8,128)} fusion(bf16[1024,192]{0,1:T(8,128)(2,1)} %bitcast.250, bf16[1024,192]{1,0:T(8,128)(2,1)} %copy-done.19, bf16[1024,192]{1,0:T(8,128)(2,1)} %copy-done.28, pred[]{:T(512)S(6)} %eq.213), kind=kOutput, calls=%fused_computation.153 | convolution fusion | flops 154607616 | bytes 1474561 | tf_op jit(solution)/shard_map/dot_general | solution.py:264
  132.7 1.4 slice_add_fusion
  134.1 1.9 copy.120
  136.0 1.4 convert_element_type.208
  137.5 1.6 add_convert_fusion
  140.1 2.7 %fusion.124 = f32[1024,384]{1,0:T(8,128)} fusion(bf16[1024,192]{0,1:T(8,128)(2,1)} %collective-permute-done.6, bf16[3,384,192]{1,2,0:T(8,128)(2,1)} %collective-permute-done.5), kind=kOutput, calls=%fused_computation.193 | convolution fusion | flops 150994944 | bytes 2113536 | tf_op jit(solution)/shard_map/rd,cd->rc/dot_general | solution.py:297
  142.8 1.9 fusion.97
  145.9 1.3 copy.122
  147.7 2.5 %fusion.120 = f32[1024,384,1]{1,0,2:T(8,128)S(1)} fusion(bf16[3,384,192]{1,2,0:T(8,128)(2,1)} %param.13, bf16[1024,2,192]{0,2,1:T(8,128)(2,1)} %add_convert_fusion, bf16[1024,1,192]{0,2,1:T(8,128)(2,1)} %reshape_reshape.4), kind=kOutput, calls=%fused_computation.162 | convolution fusion | flops 453574656 | bytes 3194880 | tf_op jit(solution)/shard_map/rkd,kcd->rc/dot_general | solution.py:293
  150.2 8.8 %collective-permute-done.7 = bf16[1024,2,192]{0,2,1:T(8,128)(2,1)} collective-permute-done((bf16[1024,2,192]{0,2,1:T(8,128)(2,1)}, bf16[1024,2,192]{0,2,1:T(8,128)(2,1)}, u32[]{:S(2)}, u32[]{:S(2)}) %collective-permute-start.7) | collective-permute-done | bytes 786464 | tf_op jit(solution)/shard_map/ppermute | solution.py:145
  159.0 2.4 fusion.60
  164.6 5.7 %all-to-all-start.3 = ((f32[16,12,384]{2,1,0:T(8,128)}), f32[16,12,384]{2,1,0:T(8,128)S(1)}, u32[]{:S(2)}, u32[]{:S(2)}) async-start(f32[16,12,384]{2,1,0:T(8,128)} %reshape.212), calls=%async_computation.3 | async-start | bytes 786432 | tf_op jit(solution)/shard_map/all_to_all | solution.py:177
  170.3 2.0 select_add_fusion
  172.4 10.1 %all-to-all-done.3 = f32[16,12,384]{2,1,0:T(8,128)S(1)} async-done(((f32[16,12,384]{2,1,0:T(8,128)}), f32[16,12,384]{2,1,0:T(8,128)S(1)}, u32[]{:S(2)}, u32[]{:S(2)}) %all-to-all-start.3) | async-done | bytes 294944 | tf_op jit(solution)/shard_map/all_to_all | solution.py:177
  182.5 3.6 %all-to-all-start.2 = ((f32[16,24,384]{2,1,0:T(8,128)}), f32[16,24,384]{2,1,0:T(8,128)S(1)}, u32[]{:S(2)}, u32[]{:S(2)}) async-start(f32[16,24,384]{2,1,0:T(8,128)} %bitcast.244), calls=%async_computation.2 | async-start | bytes 1179648 | tf_op jit(solution)/shard_map/all_to_all | solution.py:177
  186.2 15.5 %all-to-all-done.2 = f32[16,24,384]{2,1,0:T(8,128)S(1)} async-done(((f32[16,24,384]{2,1,0:T(8,128)}), f32[16,24,384]{2,1,0:T(8,128)S(1)}, u32[]{:S(2)}, u32[]{:S(2)}) %all-to-all-start.2) | async-done | bytes 589856 | tf_op jit(solution)/shard_map/all_to_all | solution.py:177
  201.8 28.2 %all_to_all.25 = f32[16,36,384]{2,1,0:T(8,128)S(1)} all-to-all(f32[16,36,384]{2,1,0:T(8,128)S(1)} %bitcast.241), channel_id=1, replica_groups=mesh['pix'=16,'ch'=2] {'pix'}, dimensions={0} | all-to-all | bytes 1769472 | tf_op jit(solution)/shard_map/all_to_all | solution.py:188
  230.0 1.1 copy.124
  232.2 2.3 fusion.98
  234.5 2.0 copy.127
  236.5 1.5 convolution_convert_fusion
  238.0 1.5 copy_select_fusion.1
  240.8 1.3 copy.128
  (183 shorter events, 43.5 us)
Async XLA Ops:
  0.6 9.4 %copy-start.6 = (bf16[1024,384]{1,0:T(8,128)(2,1)S(1)}, bf16[1024,384]{1,0:T(8,128)(2,1)}, u32[]{:S(2)}) copy-start(bf16[1024,384]{1,0:T(8,128)(2,1)} %param.11) | copy-start | bytes 2359300
  0.6 9.4 %copy-start.15 = (bf16[384,384]{1,0:T(8,128)(2,1)S(1)}, bf16[384,384]{1,0:T(8,128)(2,1)}, u32[]{:S(2)}) copy-start(bf16[384,384]{1,0:T(8,128)(2,1)} %param.12) | copy-start | bytes 884740
  0.7 27.1 %collective-permute-start = (bf16[1024,384]{1,0:T(8,128)(2,1)}, bf16[1024,384]{1,0:T(8,128)(2,1)S(1)}, u32[]{:S(2)}, u32[]{:S(2)}) collective-permute-start(bf16[1024,384]{1,0:T(8,128)(2,1)} %param.11), channel_id=1, source_target_pairs={{0,1},{1,0},{2,3},{3,2},{4,5},{5,4},{6,7},{7,6},{8,9},{9,8},{10,11... | collective-permute-start | bytes 2359304 | tf_op jit(solution)/shard_map/ppermute | solution.py:145
  3.7 24.1 %collective-permute-start.1 = (bf16[384,384]{1,0:T(8,128)(2,1)}, bf16[384,384]{1,0:T(8,128)(2,1)S(1)}, u32[]{:S(2)}, u32[]{:S(2)}) collective-permute-start(bf16[384,384]{1,0:T(8,128)(2,1)} %param.12), channel_id=1, source_target_pairs={{0,1},{1,0},{2,3},{3,2},{4,5},{5,4},{6,7},{7,6},{8,9},{9,8},{10,11... | collective-permute-start | bytes 884744 | tf_op jit(solution)/shard_map/ppermute | solution.py:145
  9.9 44.9 %copy-start.19 = (bf16[1024,192]{1,0:T(8,128)(2,1)}, bf16[1024,192]{1,0:T(8,128)(2,1)S(1)}, u32[]{:S(2)}) copy-start(bf16[1024,192]{1,0:T(8,128)(2,1)S(1)} %copy.106) | copy-start | bytes 1179652
  10.6 17.7 %copy-start.21 = (bf16[3,384,192]{1,2,0:T(8,128)(2,1)S(1)}, bf16[3,384,192]{1,2,0:T(8,128)(2,1)}, u32[]{:S(2)}) copy-start(bf16[3,384,192]{1,2,0:T(8,128)(2,1)} %param.13) | copy-start | bytes 1327108
  29.4 0.9 copy-start.17
  29.4 9.5 %copy-start.8 = (bf16[1024,192]{0,1:T(8,128)(2,1)S(1)}, bf16[1024,192]{0,1:T(8,128)(2,1)}, u32[]{:S(2)}) copy-start(bf16[1024,192]{0,1:T(8,128)(2,1)} %param.17) | copy-start | bytes 1179652
  32.2 23.6 %all-to-all-start = ((bf16[16,32,2,192]{3,2,1,0:T(2,128)(2,1)}), bf16[16,32,2,192]{3,2,1,0:T(2,128)(2,1)}, u32[]{:S(2)}, u32[]{:S(2)}) async-start(bf16[16,32,2,192]{3,2,1,0:T(2,128)(2,1)} %reshape.206), calls=%async_computation | async-start | bytes 1048576 | tf_op jit(solution)/shard_map/all_to_all | solution.py:257
  39.9 15.0 %copy-start.26 = (bf16[192,384]{1,0:T(8,128)(2,1)S(1)}, bf16[192,384]{1,0:T(8,128)(2,1)}, u32[]{:S(2)}) copy-start(bf16[192,384]{1,0:T(8,128)(2,1)} %param.14) | copy-start | bytes 442372
  39.9 15.0 %collective-permute-start.2 = (bf16[1024,192]{1,0:T(8,128)(2,1)}, bf16[1024,192]{1,0:T(8,128)(2,1)S(1)}, u32[]{:S(2)}, u32[]{:S(2)}) collective-permute-start(bf16[1024,192]{1,0:T(8,128)(2,1)} %copy.105), channel_id=1, source_target_pairs={{0,1},{1,0},{2,3},{3,2},{4,5},{5,4},{6,7},{7,6},{8,9},{9,8},{10,11... | collective-permute-start | bytes 1179656 | tf_op jit(solution)/shard_map/ppermute | solution.py:145
  41.5 57.6 %collective-permute-start.4 = (bf16[192,192]{1,0:T(8,128)(2,1)}, bf16[192,192]{1,0:T(8,128)(2,1)}, u32[]{:S(2)}, u32[]{:S(2)}) collective-permute-start(bf16[192,192]{1,0:T(8,128)(2,1)} %bitcast.296), channel_id=1, source_target_pairs={{0,1},{1,0},{2,3},{3,2},{4,5},{5,4},{6,7},{7,6},{8,9},{9,8},{10,11... | collective-permute-start | bytes 221192 | tf_op jit(solution)/shard_map/ppermute | solution.py:241
  42.1 57.0 %collective-permute-start.5 = (bf16[3,384,192]{1,2,0:T(8,128)(2,1)}, bf16[3,384,192]{1,2,0:T(8,128)(2,1)}, u32[]{:S(2)}, u32[]{:S(2)}) collective-permute-start(bf16[3,384,192]{1,2,0:T(8,128)(2,1)} %param.13), channel_id=1, source_target_pairs={{0,1},{1,0},{2,3},{3,2},{4,5},{5,4},{6,7},{7,6},{8,9},{9,8},{10,11... | collective-permute-start | bytes 1327112 | tf_op jit(solution)/shard_map/ppermute | solution.py:145
  54.9 0.8 copy-start.28
  58.1 2.3 copy-start.18
  58.1 2.3 copy-start.23
  61.4 1.0 copy-start.27
  66.3 2.0 copy-start.5
  67.3 2.3 copy-start.4
  72.8 38.7 %copy-start.1 = (bf16[512,9,2,3,64]{0,4,3,2,1:T(8,128)(2,1)}, bf16[512,9,2,3,64]{0,4,3,2,1:T(8,128)(2,1)S(1)}, u32[]{:S(2)}) copy-start(bf16[512,9,2,3,64]{0,4,3,2,1:T(8,128)(2,1)S(1)} %pad_maximum_fusion.1) | copy-start | bytes 10616836
  84.7 11.4 %copy-start.10 = (bf16[2,24,8,512]{3,2,0,1:T(8,128)(2,1)}, bf16[2,24,8,512]{3,2,0,1:T(8,128)(2,1)S(1)}, u32[]{:S(2)}) copy-start(bf16[2,24,8,512]{3,2,0,1:T(8,128)(2,1)S(1)} %copy.197) | copy-start | bytes 1179652
  86.0 8.8 %copy-start = (bf16[512,9,2,3,64]{0,4,3,2,1:T(8,128)(2,1)}, bf16[512,9,2,3,64]{0,4,3,2,1:T(8,128)(2,1)S(1)}, u32[]{:S(2)}) copy-start(bf16[512,9,2,3,64]{0,4,3,2,1:T(8,128)(2,1)S(1)} %pad_maximum_fusion) | copy-start | bytes 10616836
  96.1 10.1 %collective-permute-start.3 = (bf16[1024,192]{0,1:T(8,128)(2,1)S(1)}, bf16[1024,192]{0,1:T(8,128)(2,1)S(1)}, u32[]{:S(2)}, u32[]{:S(2)}) collective-permute-start(bf16[1024,192]{0,1:T(8,128)(2,1)S(1)} %bitcast.249), channel_id=1, source_target_pairs={{0,1},{1,0},{2,3},{3,2},{4,5},{5,4},{6,7},{7,6},{8,9},{9,8},{10,11... | collective-permute-start | bytes 1179656 | tf_op jit(solution)/shard_map/ppermute | solution.py:145
  106.1 1.6 copy-start.25
  112.7 1.5 copy-start.2
  115.3 20.7 %all-to-all-start.1 = ((bf16[16,32,2,192]{3,2,1,0:T(2,128)(2,1)}), bf16[16,32,2,192]{3,2,1,0:T(2,128)(2,1)}, u32[]{:S(2)}, u32[]{:S(2)}) async-start(bf16[16,32,2,192]{3,2,1,0:T(2,128)(2,1)} %reshape.208), calls=%async_computation.1 | async-start | bytes 1048576 | tf_op jit(solution)/shard_map/all_to_all | solution.py:276
  126.2 13.9 %collective-permute-start.6 = (bf16[1024,192]{0,1:T(8,128)(2,1)}, bf16[1024,192]{0,1:T(8,128)(2,1)}, u32[]{:S(2)}, u32[]{:S(2)}) collective-permute-start(bf16[1024,192]{0,1:T(8,128)(2,1)} %bitcast.125), channel_id=1, source_target_pairs={{0,1},{1,0},{2,3},{3,2},{4,5},{5,4},{6,7},{7,6},{8,9},{9,8},{10,11... | collective-permute-start | bytes 1179656 | tf_op jit(solution)/shard_map/ppermute | solution.py:145
  128.6 4.1 %copy-start.3 = (f32[1536,384]{1,0:T(8,128)S(1)}, f32[1536,384]{1,0:T(8,128)}, u32[]{:S(2)}) copy-start(f32[1536,384]{1,0:T(8,128)} %copy-done.2) | copy-start | bytes 7077892
  129.6 3.2 %copy-start.12 = (bf16[512,1,384]{2,0,1:T(8,128)(2,1)S(1)}, bf16[512,1,384]{2,0,1:T(8,128)(2,1)}, u32[]{:S(2)}) copy-start(bf16[512,1,384]{2,0,1:T(8,128)(2,1)} %copy.186) | copy-start | bytes 1179652
  129.6 3.2 %copy-start.13 = (bf16[512,1,384]{2,0,1:T(8,128)(2,1)S(1)}, bf16[512,1,384]{2,0,1:T(8,128)(2,1)}, u32[]{:S(2)}) copy-start(bf16[512,1,384]{2,0,1:T(8,128)(2,1)} %copy.185) | copy-start | bytes 1179652
  137.5 5.2 %copy-start.24 = (bf16[1024,1,192]{0,2,1:T(8,128)(2,1)S(1)}, bf16[1024,1,192]{0,2,1:T(8,128)(2,1)}, u32[]{:S(2)}) copy-start(bf16[1024,1,192]{0,2,1:T(8,128)(2,1)} %reshape_reshape.4) | copy-start | bytes 1179652
  139.2 19.8 %collective-permute-start.7 = (bf16[1024,2,192]{0,2,1:T(8,128)(2,1)}, bf16[1024,2,192]{0,2,1:T(8,128)(2,1)}, u32[]{:S(2)}, u32[]{:S(2)}) collective-permute-start(bf16[1024,2,192]{0,2,1:T(8,128)(2,1)} %add_convert_fusion), channel_id=1, source_target_pairs={{0,1},{1,0},{2,3},{3,2},{4,5},{5,4},{6,7},{7,6},{8,9},{9,8},{10,11... | collective-permute-start | bytes 2359304 | tf_op jit(solution)/shard_map/ppermute | solution.py:145
  147.7 11.3 %copy-start.9 = (f32[1024,384]{1,0:T(8,128)S(1)}, f32[1024,384]{1,0:T(8,128)}, u32[]{:S(2)}) copy-start(f32[1024,384]{1,0:T(8,128)} %fusion.124) | copy-start | bytes 4718596
  147.7 11.3 %copy-start.20 = (bf16[1024,192]{1,0:T(8,128)(2,1)S(1)}, bf16[1024,192]{1,0:T(8,128)(2,1)}, u32[]{:S(2)}) copy-start(bf16[1024,192]{1,0:T(8,128)(2,1)} %copy-done.19) | copy-start | bytes 1179652
  147.7 11.3 %copy-start.29 = (bf16[1024,192]{1,0:T(8,128)(2,1)S(1)}, bf16[1024,192]{1,0:T(8,128)(2,1)}, u32[]{:S(2)}) copy-start(bf16[1024,192]{1,0:T(8,128)(2,1)} %copy-done.28) | copy-start | bytes 1179652
  150.2 11.2 %copy-start.7 = (bf16[1024,384]{1,0:T(8,128)(2,1)S(1)}, bf16[1024,384]{1,0:T(8,128)(2,1)}, u32[]{:S(2)}) copy-start(bf16[1024,384]{1,0:T(8,128)(2,1)} %param.11) | copy-start | bytes 2359300
  161.4 1.0 copy-start.14
  162.1 1.6 collective-permute-start.9
  163.2 7.1 %collective-permute-start.8 = (f32[384,384]{1,0:T(8,128)}, f32[384,384]{1,0:T(8,128)}, u32[]{:S(2)}, u32[]{:S(2)}) collective-permute-start(f32[384,384]{1,0:T(8,128)} %broadcast_select_fusion.2), channel_id=1, source_target_pairs={{0,2},{2,0},{4,6},{6,4},{8,10},{10,8},{12,14},{14,12},{16,18},{18,... | collective-permute-start | bytes 1769480 | tf_op jit(solution)/shard_map/ppermute | solution.py:163
  164.6 18.0 %all-to-all-start.3 = ((f32[16,12,384]{2,1,0:T(8,128)}), f32[16,12,384]{2,1,0:T(8,128)S(1)}, u32[]{:S(2)}, u32[]{:S(2)}) async-start(f32[16,12,384]{2,1,0:T(8,128)} %reshape.212), calls=%async_computation.3 | async-start | bytes 786432 | tf_op jit(solution)/shard_map/all_to_all | solution.py:177
  182.5 19.1 %all-to-all-start.2 = ((f32[16,24,384]{2,1,0:T(8,128)}), f32[16,24,384]{2,1,0:T(8,128)S(1)}, u32[]{:S(2)}, u32[]{:S(2)}) async-start(f32[16,24,384]{2,1,0:T(8,128)} %bitcast.244), calls=%async_computation.2 | async-start | bytes 1179648 | tf_op jit(solution)/shard_map/all_to_all | solution.py:177
  201.7 30.2 %copy-start.11 = (bf16[2,24,8,512]{3,2,0,1:T(8,128)(2,1)S(1)}, bf16[2,24,8,512]{3,2,0,1:T(8,128)(2,1)}, u32[]{:S(2)}) copy-start(bf16[2,24,8,512]{3,2,0,1:T(8,128)(2,1)} %copy-done.10) | copy-start | bytes 1179652
  201.7 30.2 %copy-start.22 = (bf16[192,1,192]{2,1,0:T(2,128)(2,1)S(1)}, bf16[192,1,192]{2,1,0:T(2,128)(2,1)}, u32[]{:S(2)}) copy-start(bf16[192,1,192]{2,1,0:T(2,128)(2,1)} %get-tuple-element.94) | copy-start | bytes 221188
  231.1 6.9 %collective-permute-start.10 = (f32[16,36,384]{2,0,1:T(8,128)}, f32[16,36,384]{2,0,1:T(8,128)}, u32[]{:S(2)}, u32[]{:S(2)}) collective-permute-start(f32[16,36,384]{2,0,1:T(8,128)} %copy.124), channel_id=1, source_target_pairs={{0,2},{2,0},{4,6},{6,4},{8,10},{10,8},{12,14},{14,12},{16,18},{18,... | collective-permute-start | bytes 2654216 | tf_op jit(solution)/shard_map/ppermute | solution.py:163
  231.9 4.6 %copy-start.16 = (bf16[384,384]{1,0:T(8,128)(2,1)S(1)}, bf16[384,384]{1,0:T(8,128)(2,1)}, u32[]{:S(2)}) copy-start(bf16[384,384]{1,0:T(8,128)(2,1)} %param.12) | copy-start | bytes 884740

commit v20 on v16

--- a/solution.py
+++ b/solution.py
@@ -288,7 +288,6 @@
         * grad_scale
     )
     early_reduced = pix_scatter((projection_term, mixing_term), mixing_weight.shape[1])
-    early_reduced, grad_others = lax.optimization_barrier((early_reduced, grad_others))
     pooled_sum = upstream.astype(f32) + jnp.einsum(
         "rkd,kcd->rc", grad_projected, projections, preferred_element_type=f32
     )

time: 242 us -> 238 us (0.983)
  blocking collectives: 44.8 us -> 27.2 us
  waiting for transfers between devices: 50.6 us -> 60.4 us
  starting transfers between devices: 28.8 us -> 32.6 us
    all_to_all x1 -> x0, blocking collectives: 17.6 us -> none  [pix_scatter(): lax.all_to_all(mine.reshape(size, chunk, width), 'pix', 0, 0, tiled=True)]
    ppermute x6, waiting for transfers between devices: 36.7 us -> 45.4 us  [ch_exchange(): lax.ppermute(value, 'ch', [(i, (i + shift) % size) for i in range(size)])]
    all_to_all x1 -> x2, starting transfers between devices: 5.94 us -> 9.79 us  [pix_scatter(): lax.all_to_all(mine.reshape(size, chunk, width), 'pix', 0, 0, tiled=True)]
    unnamed x116 -> x120, local copies, waits for them, and re-layouts: 12.5 us -> 12.3 us
    all_to_all x1 -> x2, waiting for transfers between devices: 12 us -> 12.2 us  [pix_scatter(): lax.all_to_all(mine.reshape(size, chunk, width), 'pix', 0, 0, tiled=True)]
  transfers between devices with their start and end apart: 13 -> 14, of which waited for: 7 -> 7; matrix products, arithmetic and copies ran while one was open for 35% -> 38% of each run, Pallas kernels for 0% -> 0%
where the time goes in v20:
time: 238 us; the launch traced here: 233 us
  waiting for transfers between devices  60.4 us (25%)
  matrix products  57.5 us (24%)
  local copies, waits for them, and re-layouts  35.5 us (15%)
  starting transfers between devices  32.6 us (14%)
  blocking collectives  27.2 us (11%)
  other arithmetic  17.5 us (7%)
    ppermute x6, waiting for transfers between devices, ch_exchange(): lax.ppermute(value, 'ch', [(i, (i + shift) % size) for i in range(size)])  45.4 us
    all_to_all x1, blocking collectives, pix_gather(): lax.all_to_all(spread.reshape(size, total, width), 'pix', 0, 0, tiled=True)  27.2 us
    dot_general x16, matrix products, backward_block(): jnp.einsum('bx,bc->xc', pick_table(slot_rows[:, slot], ext_rows), contrib...  19.7 us
    dot_general x16, matrix products, forward_block(): jnp.dot(pick_table(slot_rows[:, slot], ext_rows), flattened, preferred_el...  17.2 us
    unnamed x120, local copies, waits for them, and re-layouts  12.3 us
    all_to_all x2, waiting for transfers between devices, pix_scatter(): lax.all_to_all(mine.reshape(size, chunk, width), 'pix', 0, 0, tiled=True)  12.2 us
    all_to_all x2, starting transfers between devices, pix_scatter(): lax.all_to_all(mine.reshape(size, chunk, width), 'pix', 0, 0, tiled=True)  9.79 us
    ppermute x6, starting transfers between devices, ch_exchange(): lax.ppermute(value, 'ch', [(i, (i + shift) % size) for i in range(size)])  8.18 us
  transfers between devices with their start and end apart: 14, of which 7 were waited for; matrix products, arithmetic and copies ran while one was open for 38% of the time, Pallas kernels for 0%

profile of v20, /device:TPU:0, one launch (start us, length us, event | category | flops | bytes accessed | tf_op | source)
XLA Modules:
  0.0 232.9 jit_solution(4964519904952244616)
XLA Ops:
  0.7 3.0 %collective-permute-start = (bf16[1024,384]{1,0:T(8,128)(2,1)}, bf16[1024,384]{1,0:T(8,128)(2,1)S(1)}, u32[]{:S(2)}, u32[]{:S(2)}) collective-permute-start(bf16[1024,384]{1,0:T(8,128)(2,1)} %param.11), channel_id=1, source_target_pairs={{0,1},{1,0},{2,3},{3,2},{4,5},{5,4},{6,7},{7,6},{8,9},{9,8},{10,11... | collective-permute-start | bytes 2359304 | tf_op jit(solution)/shard_map/ppermute | solution.py:145
  3.7 1.1 reshape.203
  6.8 1.2 broadcast_select_fusion
  9.4 1.2 copy.77
  12.6 15.3 %collective-permute-done.1 = bf16[384,384]{1,0:T(8,128)(2,1)} collective-permute-done((bf16[384,384]{1,0:T(8,128)(2,1)}, bf16[384,384]{1,0:T(8,128)(2,1)}, u32[]{:S(2)}, u32[]{:S(2)}) %collective-permute-start.1) | collective-permute-done | bytes 294944 | tf_op jit(solution)/shard_map/ppermute | solution.py:145
  27.8 1.6 add_convert_fusion.1
  32.1 1.1 reshape.204
  33.2 6.7 %all-to-all-start = ((bf16[16,32,2,192]{3,2,1,0:T(2,128)(2,1)}), bf16[16,32,2,192]{3,2,1,0:T(2,128)(2,1)S(1)}, u32[]{:S(2)}, u32[]{:S(2)}) async-start(bf16[16,32,2,192]{3,2,1,0:T(2,128)(2,1)} %reshape.204), calls=%async_computation | async-start | bytes 1048576 | tf_op jit(solution)/shard_map/all_to_all | solution.py:257
  40.0 1.0 copy.76
  41.0 1.5 collective-permute-start.2
  43.9 1.5 collective-permute-start.4
  46.3 9.6 %collective-permute-done.2 = bf16[1024,192]{1,0:T(8,128)(2,1)S(1)} collective-permute-done((bf16[1024,192]{1,0:T(8,128)(2,1)}, bf16[1024,192]{1,0:T(8,128)(2,1)S(1)}, u32[]{:S(2)}, u32[]{:S(2)}) %collective-permute-start.2) | collective-permute-done | bytes 393248 | tf_op jit(solution)/shard_map/ppermute | solution.py:145
  58.1 2.2 fusion.105
  62.3 1.0 fusion.99
  65.3 1.0 fusion.102
  68.4 1.3 copy-done.4
  72.9 1.2 fusion.108
  83.6 1.2 fusion.40
  84.8 1.2 convolution_add_fusion.14
  86.0 1.2 convolution_add_fusion.13
  87.2 1.2 convolution_add_fusion.12
  88.4 1.4 convolution_add_fusion.11
  89.9 1.2 convolution_add_fusion.10
  91.1 1.2 convolution_add_fusion.9
  92.3 1.2 convolution_add_fusion.8
  93.8 1.2 convolution_add_fusion.7
  95.0 1.2 convolution_add_fusion.6
  96.2 1.2 convolution_add_fusion.5
  97.4 1.2 convolution_add_fusion.4
  98.6 1.2 convolution_add_fusion.3
  99.8 1.2 convolution_add_fusion.2
  101.0 1.6 convolution_add_fusion.1
  103.5 1.6 collective-permute-start.3
  105.0 1.2 convolution_add_fusion
  106.6 7.0 %collective-permute-done.3 = bf16[1024,192]{0,1:T(8,128)(2,1)S(1)} collective-permute-done((bf16[1024,192]{0,1:T(8,128)(2,1)S(1)}, bf16[1024,192]{0,1:T(8,128)(2,1)S(1)}, u32[]{:S(2)}, u32[]{:S(2)}) %collective-permute-start.3) | collective-permute-done | bytes 393248 | tf_op jit(solution)/shard_map/ppermute | solution.py:145
  114.4 1.1 reshape.206
  115.5 5.5 %all-to-all-start.1 = ((bf16[16,32,2,192]{3,2,1,0:T(2,128)(2,1)}), bf16[16,32,2,192]{3,2,1,0:T(2,128)(2,1)}, u32[]{:S(2)}, u32[]{:S(2)}) async-start(bf16[16,32,2,192]{3,2,1,0:T(2,128)(2,1)} %reshape.206), calls=%async_computation.1 | async-start | bytes 1048576 | tf_op jit(solution)/shard_map/all_to_all | solution.py:274
  121.4 1.0 slice.368
  122.4 1.8 slice.367
  125.8 2.1 copy.141
  127.9 3.2 %convolution_multiply_fusion.2 = f32[192,384]{1,0:T(8,128)} fusion(bf16[1024,192]{0,1:T(8,128)(2,1)} %bitcast.237, bf16[1024,192]{1,0:T(8,128)(2,1)} %copy-done.23, bf16[1024,192]{1,0:T(8,128)(2,1)} %copy-done.49, pred[]{:T(512)S(6)} %eq.213), kind=kOutput, calls=%fused_computation.152 | convolution fusion | flops 154607616 | bytes 1474561 | tf_op jit(solution)/shard_map/dot_general | solution.py:264
  131.1 1.4 convert_add_fusion
  132.4 1.9 copy.84
  134.3 1.2 all-to-all-done.1
  135.5 1.4 convert_element_type.203
  137.8 1.7 add_convert_fusion
  139.6 1.2 pad_maximum_fusion.3
  140.8 1.5 collective-permute-start.6
  144.6 1.3 copy.86
  146.1 1.1 broadcast_select_fusion.2
  147.4 2.1 fusion.125
  150.5 4.9 %all-to-all-start.2 = ((f32[16,24,384]{2,1,0:T(8,128)}), f32[16,24,384]{2,1,0:T(8,128)S(1)}, u32[]{:S(2)}, u32[]{:S(2)}) async-start(f32[16,24,384]{2,1,0:T(8,128)} %bitcast.102), calls=%async_computation.2 | async-start | bytes 1179648 | tf_op jit(solution)/shard_map/all_to_all | solution.py:177
  155.4 13.6 %collective-permute-done.6 = bf16[1024,3,192]{0,2,1:T(8,128)(2,1)} collective-permute-done((bf16[1024,3,192]{0,2,1:T(8,128)(2,1)}, bf16[1024,3,192]{0,2,1:T(8,128)(2,1)}, u32[]{:S(2)}, u32[]{:S(2)}) %collective-permute-start.6) | collective-permute-done | bytes 1179680 | tf_op jit(solution)/shard_map/ppermute | solution.py:145
  169.0 3.4 %fusion.57 = bf16[1024,384]{1,0:T(8,128)(2,1)S(1)} fusion(f32[1024,384,1]{1,0,2:T(8,128)} %fusion.125, bf16[1024,3,192]{0,2,1:T(8,128)(2,1)} %collective-permute-done.6, bf16[3,384,192]{1,2,0:T(8,128)(2,1)} %collective-permute-done.5, bf16[1024,192]{1,0:T(8,128)(2,1)} %copy-done.49, bf16[1024,192]{1,0:T(8,128)(2,1)S(1)} %copy-done.24, pred[]{:T(512)S(6)} %eq.213), kind=kOutput, calls=%fused_computation.87 | convolution fusion | flops 458096640 | bytes 4767745 | tf_op jit(solution)/shard_map/rkd,kcd->rc/dot_general | solution.py:295
  173.2 1.6 collective-permute-done.8
  175.6 4.9 %all-to-all-start.3 = ((f32[16,12,384]{2,1,0:T(8,128)}), f32[16,12,384]{2,1,0:T(8,128)S(1)}, u32[]{:S(2)}, u32[]{:S(2)}) async-start(f32[16,12,384]{2,1,0:T(8,128)} %reshape.210), calls=%async_computation.3 | async-start | bytes 786432 | tf_op jit(solution)/shard_map/all_to_all | solution.py:177
  180.5 12.2 %all-to-all-done.3 = f32[16,12,384]{2,1,0:T(8,128)S(1)} async-done(((f32[16,12,384]{2,1,0:T(8,128)}), f32[16,12,384]{2,1,0:T(8,128)S(1)}, u32[]{:S(2)}, u32[]{:S(2)}) %all-to-all-start.3) | async-done | bytes 294944 | tf_op jit(solution)/shard_map/all_to_all | solution.py:177
  192.8 27.2 %all_to_all.25 = f32[16,36,384]{2,1,0:T(8,128)S(1)} all-to-all(f32[16,36,384]{2,1,0:T(8,128)S(1)} %bitcast.230), channel_id=1, replica_groups=mesh['pix'=16,'ch'=2] {'pix'}, dimensions={0} | all-to-all | bytes 1769472 | tf_op jit(solution)/shard_map/all_to_all | solution.py:188
  220.0 1.1 copy.88
  221.8 1.3 fusion.118
  223.1 1.5 fusion.94
  225.5 1.5 convolution_convert_fusion
  227.1 1.5 copy_select_fusion.1
  230.5 1.3 copy.92
  (219 shorter events, 45.8 us)
Async XLA Ops:
  0.6 11.3 %copy-start.8 = (bf16[1024,384]{1,0:T(8,128)(2,1)S(1)}, bf16[1024,384]{1,0:T(8,128)(2,1)}, u32[]{:S(2)}) copy-start(bf16[1024,384]{1,0:T(8,128)(2,1)} %param.11) | copy-start | bytes 2359300
  0.6 11.3 %copy-start.17 = (bf16[384,384]{1,0:T(8,128)(2,1)S(1)}, bf16[384,384]{1,0:T(8,128)(2,1)}, u32[]{:S(2)}) copy-start(bf16[384,384]{1,0:T(8,128)(2,1)} %param.12) | copy-start | bytes 884740
  0.7 27.2 %collective-permute-start = (bf16[1024,384]{1,0:T(8,128)(2,1)}, bf16[1024,384]{1,0:T(8,128)(2,1)S(1)}, u32[]{:S(2)}, u32[]{:S(2)}) collective-permute-start(bf16[1024,384]{1,0:T(8,128)(2,1)} %param.11), channel_id=1, source_target_pairs={{0,1},{1,0},{2,3},{3,2},{4,5},{5,4},{6,7},{7,6},{8,9},{9,8},{10,11... | collective-permute-start | bytes 2359304 | tf_op jit(solution)/shard_map/ppermute | solution.py:145
  3.7 24.2 %collective-permute-start.1 = (bf16[384,384]{1,0:T(8,128)(2,1)}, bf16[384,384]{1,0:T(8,128)(2,1)}, u32[]{:S(2)}, u32[]{:S(2)}) collective-permute-start(bf16[384,384]{1,0:T(8,128)(2,1)} %param.12), channel_id=1, source_target_pairs={{0,1},{1,0},{2,3},{3,2},{4,5},{5,4},{6,7},{7,6},{8,9},{9,8},{10,11... | collective-permute-start | bytes 884744 | tf_op jit(solution)/shard_map/ppermute | solution.py:145
  9.4 21.1 %copy-start.46 = (s32[512]{0:T(512)}, s32[512]{0:T(512)S(1)}, u32[]{:S(2)}) copy-start(s32[512]{0:T(512)S(1)} %eq.149) | copy-start | bytes 6148
  10.6 45.3 %copy-start.23 = (bf16[1024,192]{1,0:T(8,128)(2,1)}, bf16[1024,192]{1,0:T(8,128)(2,1)S(1)}, u32[]{:S(2)}) copy-start(bf16[1024,192]{1,0:T(8,128)(2,1)S(1)} %copy.77) | copy-start | bytes 1179652
  12.5 16.9 %copy-start.25 = (bf16[3,384,192]{1,2,0:T(8,128)(2,1)S(1)}, bf16[3,384,192]{1,2,0:T(8,128)(2,1)}, u32[]{:S(2)}) copy-start(bf16[3,384,192]{1,2,0:T(8,128)(2,1)} %param.13) | copy-start | bytes 1327108
  30.5 0.9 copy-start.19
  30.5 9.4 %copy-start.10 = (bf16[1024,192]{0,1:T(8,128)(2,1)S(1)}, bf16[1024,192]{0,1:T(8,128)(2,1)}, u32[]{:S(2)}) copy-start(bf16[1024,192]{0,1:T(8,128)(2,1)} %param.17) | copy-start | bytes 1179652
  33.2 24.4 %all-to-all-start = ((bf16[16,32,2,192]{3,2,1,0:T(2,128)(2,1)}), bf16[16,32,2,192]{3,2,1,0:T(2,128)(2,1)S(1)}, u32[]{:S(2)}, u32[]{:S(2)}) async-start(bf16[16,32,2,192]{3,2,1,0:T(2,128)(2,1)} %reshape.204), calls=%async_computation | async-start | bytes 1048576 | tf_op jit(solution)/shard_map/all_to_all | solution.py:257
  39.9 16.0 %copy-start.28 = (bf16[192,384]{1,0:T(8,128)(2,1)S(1)}, bf16[192,384]{1,0:T(8,128)(2,1)}, u32[]{:S(2)}) copy-start(bf16[192,384]{1,0:T(8,128)(2,1)} %param.14) | copy-start | bytes 442372
  41.0 15.0 %collective-permute-start.2 = (bf16[1024,192]{1,0:T(8,128)(2,1)}, bf16[1024,192]{1,0:T(8,128)(2,1)S(1)}, u32[]{:S(2)}, u32[]{:S(2)}) collective-permute-start(bf16[1024,192]{1,0:T(8,128)(2,1)} %copy.76), channel_id=1, source_target_pairs={{0,1},{1,0},{2,3},{3,2},{4,5},{5,4},{6,7},{7,6},{8,9},{9,8},{10,11... | collective-permute-start | bytes 1179656 | tf_op jit(solution)/shard_map/ppermute | solution.py:145
  43.4 63.2 %collective-permute-start.5 = (bf16[3,384,192]{1,2,0:T(8,128)(2,1)}, bf16[3,384,192]{1,2,0:T(8,128)(2,1)}, u32[]{:S(2)}, u32[]{:S(2)}) collective-permute-start(bf16[3,384,192]{1,2,0:T(8,128)(2,1)} %param.13), channel_id=1, source_target_pairs={{0,1},{1,0},{2,3},{3,2},{4,5},{5,4},{6,7},{7,6},{8,9},{9,8},{10,11... | collective-permute-start | bytes 1327112 | tf_op jit(solution)/shard_map/ppermute | solution.py:145
  43.9 62.7 %collective-permute-start.4 = (bf16[192,192]{1,0:T(8,128)(2,1)}, bf16[192,192]{1,0:T(8,128)(2,1)}, u32[]{:S(2)}, u32[]{:S(2)}) collective-permute-start(bf16[192,192]{1,0:T(8,128)(2,1)} %bitcast.285), channel_id=1, source_target_pairs={{0,1},{1,0},{2,3},{3,2},{4,5},{5,4},{6,7},{7,6},{8,9},{9,8},{10,11... | collective-permute-start | bytes 221192 | tf_op jit(solution)/shard_map/ppermute | solution.py:241
  55.9 0.8 copy-start.49
  56.7 1.4 copy-start.38
  58.1 2.2 copy-start.20
  58.1 2.2 copy-start.48
  60.3 1.0 copy-start.45
  61.3 1.0 copy-start.44
  62.3 1.0 copy-start.43
  63.3 1.0 copy-start.42
  64.3 1.0 copy-start.41
  65.3 1.0 copy-start.40
  66.4 1.0 copy-start.39
  66.4 2.0 copy-start.5
  67.4 2.3 copy-start.4
  70.0 0.8 copy-start.29
  70.3 0.6 copy-start.37
  70.9 1.0 copy-start.36
  71.9 1.0 copy-start.35
  72.9 1.2 copy-start.34
  74.2 1.0 copy-start.33
  75.2 1.0 copy-start.32
  76.2 1.0 copy-start.31
  78.4 1.0 copy-start.6
  78.5 1.4 copy-start.30
  78.7 1.3 copy-start.7
  83.6 8.6 %copy-start.1 = (bf16[512,9,2,3,64]{0,4,3,2,1:T(8,128)(2,1)}, bf16[512,9,2,3,64]{0,4,3,2,1:T(8,128)(2,1)S(1)}, u32[]{:S(2)}) copy-start(bf16[512,9,2,3,64]{0,4,3,2,1:T(8,128)(2,1)S(1)} %pad_maximum_fusion) | copy-start | bytes 10616836
  93.8 11.2 %copy-start = (bf16[512,9,2,3,64]{0,4,3,2,1:T(8,128)(2,1)}, bf16[512,9,2,3,64]{0,4,3,2,1:T(8,128)(2,1)S(1)}, u32[]{:S(2)}) copy-start(bf16[512,9,2,3,64]{0,4,3,2,1:T(8,128)(2,1)S(1)} %pad_maximum_fusion.1) | copy-start | bytes 10616836
  103.4 2.8 %copy-start.11 = (bf16[2,24,8,512]{3,2,0,1:T(8,128)(2,1)}, bf16[2,24,8,512]{3,2,0,1:T(8,128)(2,1)S(1)}, u32[]{:S(2)}) copy-start(bf16[2,24,8,512]{3,2,0,1:T(8,128)(2,1)S(1)} %copy.153) | copy-start | bytes 1179652
  103.5 10.1 %collective-permute-start.3 = (bf16[1024,192]{0,1:T(8,128)(2,1)S(1)}, bf16[1024,192]{0,1:T(8,128)(2,1)S(1)}, u32[]{:S(2)}, u32[]{:S(2)}) collective-permute-start(bf16[1024,192]{0,1:T(8,128)(2,1)S(1)} %bitcast.236), channel_id=1, source_target_pairs={{0,1},{1,0},{2,3},{3,2},{4,5},{5,4},{6,7},{7,6},{8,9},{9,8},{10,11... | collective-permute-start | bytes 1179656 | tf_op jit(solution)/shard_map/ppermute | solution.py:145
  106.2 7.4 %copy-start.2 = (f32[1536,384]{1,0:T(8,128)}, f32[1536,384]{1,0:T(8,128)S(1)}, u32[]{:S(2)}) copy-start(f32[1536,384]{1,0:T(8,128)S(1)} %convolution_add_fusion) | copy-start | bytes 7077892
  113.6 0.8 copy-start.27
  115.5 20.0 %all-to-all-start.1 = ((bf16[16,32,2,192]{3,2,1,0:T(2,128)(2,1)}), bf16[16,32,2,192]{3,2,1,0:T(2,128)(2,1)}, u32[]{:S(2)}, u32[]{:S(2)}) async-start(bf16[16,32,2,192]{3,2,1,0:T(2,128)(2,1)} %reshape.206), calls=%async_computation.1 | async-start | bytes 1048576 | tf_op jit(solution)/shard_map/all_to_all | solution.py:274
  125.8 5.2 %copy-start.3 = (f32[1536,384]{1,0:T(8,128)S(1)}, f32[1536,384]{1,0:T(8,128)}, u32[]{:S(2)}) copy-start(f32[1536,384]{1,0:T(8,128)} %copy-done.2) | copy-start | bytes 7077892
  127.9 3.2 %copy-start.14 = (bf16[512,1,384]{2,0,1:T(8,128)(2,1)S(1)}, bf16[512,1,384]{2,0,1:T(8,128)(2,1)}, u32[]{:S(2)}) copy-start(bf16[512,1,384]{2,0,1:T(8,128)(2,1)} %copy.142) | copy-start | bytes 1179652
  127.9 3.2 %copy-start.15 = (bf16[512,1,384]{2,0,1:T(8,128)(2,1)S(1)}, bf16[512,1,384]{2,0,1:T(8,128)(2,1)}, u32[]{:S(2)}) copy-start(bf16[512,1,384]{2,0,1:T(8,128)(2,1)} %copy.141) | copy-start | bytes 1179652
  132.4 5.4 %copy-start.47 = (s32[512]{0:T(512)S(1)}, s32[512]{0:T(512)}, u32[]{:S(2)}) copy-start(s32[512]{0:T(512)} %copy-done.46) | copy-start | bytes 6148
  139.6 2.7 %copy-start.21 = (bf16[1024,2,192]{0,2,1:T(8,128)(2,1)}, bf16[1024,2,192]{0,2,1:T(8,128)(2,1)S(1)}, u32[]{:S(2)}) copy-start(bf16[1024,2,192]{0,2,1:T(8,128)(2,1)S(1)} %add_convert_fusion) | copy-start | bytes 2359300
  140.8 28.2 %collective-permute-start.6 = (bf16[1024,3,192]{0,2,1:T(8,128)(2,1)}, bf16[1024,3,192]{0,2,1:T(8,128)(2,1)}, u32[]{:S(2)}, u32[]{:S(2)}) collective-permute-start(bf16[1024,3,192]{0,2,1:T(8,128)(2,1)} %pad_maximum_fusion.3), channel_id=1, source_target_pairs={{0,1},{1,0},{2,3},{3,2},{4,5},{5,4},{6,7},{7,6},{8,9},{9,8},{10,11... | collective-permute-start | bytes 3538952 | tf_op jit(solution)/shard_map/ppermute | solution.py:145
  146.1 1.2 copy-start.22
  146.1 1.3 copy-start.26
  147.3 2.3 %copy-start.16 = (f32[192,384]{1,0:T(8,128)S(1)}, f32[192,384]{1,0:T(8,128)}, u32[]{:S(2)}) copy-start(f32[192,384]{1,0:T(8,128)} %convolution_multiply_fusion.2) | copy-start | bytes 884740
  147.3 2.3 collective-permute-start.7
  149.6 19.4 %copy-start.24 = (bf16[1024,192]{1,0:T(8,128)(2,1)S(1)}, bf16[1024,192]{1,0:T(8,128)(2,1)}, u32[]{:S(2)}) copy-start(bf16[1024,192]{1,0:T(8,128)(2,1)} %copy-done.23) | copy-start | bytes 1179652
  150.5 25.1 %all-to-all-start.2 = ((f32[16,24,384]{2,1,0:T(8,128)}), f32[16,24,384]{2,1,0:T(8,128)S(1)}, u32[]{:S(2)}, u32[]{:S(2)}) async-start(f32[16,24,384]{2,1,0:T(8,128)} %bitcast.102), calls=%async_computation.2 | async-start | bytes 1179648 | tf_op jit(solution)/shard_map/all_to_all | solution.py:177
  155.4 17.0 %copy-start.9 = (bf16[1024,384]{1,0:T(8,128)(2,1)S(1)}, bf16[1024,384]{1,0:T(8,128)(2,1)}, u32[]{:S(2)}) copy-start(bf16[1024,384]{1,0:T(8,128)(2,1)} %param.11) | copy-start | bytes 2359300
  173.1 1.6 collective-permute-start.8
  175.6 17.1 %all-to-all-start.3 = ((f32[16,12,384]{2,1,0:T(8,128)}), f32[16,12,384]{2,1,0:T(8,128)S(1)}, u32[]{:S(2)}, u32[]{:S(2)}) async-start(f32[16,12,384]{2,1,0:T(8,128)} %reshape.210), calls=%async_computation.3 | async-start | bytes 786432 | tf_op jit(solution)/shard_map/all_to_all | solution.py:177
  192.7 29.1 %copy-start.12 = (bf16[2,24,8,512]{3,2,0,1:T(8,128)(2,1)S(1)}, bf16[2,24,8,512]{3,2,0,1:T(8,128)(2,1)}, u32[]{:S(2)}) copy-start(bf16[2,24,8,512]{3,2,0,1:T(8,128)(2,1)} %copy-done.11) | copy-start | bytes 1179652
  221.0 6.0 %collective-permute-start.9 = (f32[16,36,384]{2,0,1:T(8,128)}, f32[16,36,384]{2,0,1:T(8,128)}, u32[]{:S(2)}, u32[]{:S(2)}) collective-permute-start(f32[16,36,384]{2,0,1:T(8,128)} %copy.88), channel_id=1, source_target_pairs={{0,2},{2,0},{4,6},{6,4},{8,10},{10,8},{12,14},{14,12},{16,18},{18,... | collective-permute-start | bytes 2654216 | tf_op jit(solution)/shard_map/ppermute | solution.py:163
  221.8 3.7 %copy-start.18 = (bf16[384,384]{1,0:T(8,128)(2,1)S(1)}, bf16[384,384]{1,0:T(8,128)(2,1)}, u32[]{:S(2)}) copy-start(bf16[384,384]{1,0:T(8,128)(2,1)} %param.12) | copy-start | bytes 884740
  230.2 1.6 copy-start.13
